TPU v7x, 32 devices: a whole 2x2x4 slice. The times are simulated.
32 devices in a mesh: groups: 2 (over x), seq: 8 (over z, y), head: 2 (over core).
Axes of the slice: x: 2, y: 2, z: 4, core: 2. Of those that a mesh axis runs over, the one named last changes fastest.
Arguments:
- x_input: bfloat16 [2048, 4096], P(('groups', 'seq'), 'head'), parts along dimension 0, may hold values from -6 to 6
- b_rows: bfloat16 [2048, 128], P(('groups', 'seq')), parts along dimension 0, may hold values from -0.5 to 0.5
- c_rows: bfloat16 [2048, 128], P(('groups', 'seq')), parts along dimension 0, may hold values from -0.5 to 0.5
- decay_log: float32 [64, 1024], P(('groups', 'head'), 'seq'), parts along dimension 0, may hold values from -1 to 0
- skip_gain: float32 [32], P('head'), may hold values from 0.5 to 1.5
- doc_lengths: int32 [8], P('groups'), parts along dimension 0, may hold values from 1 to 512, 1024 in all
- queries: bfloat16 [2048, 2048], P(('groups', 'seq'), 'head'), parts along dimension 0, may hold values from -9 to 9
- attention_key_rows: bfloat16 [2048, 512], P(('groups', 'seq'), 'head'), parts along dimension 0, may hold values from -9 to 9
- values: bfloat16 [2048, 512], P(('groups', 'seq'), 'head'), parts along dimension 0, may hold values from -6 to 6
- mixer_cot: bfloat16 [2048, 4096], P(('groups', 'seq'), 'head'), parts along dimension 0, may hold values from -6 to 6
- attention_output_cotangent: bfloat16 [2048, 2048], P(('groups', 'seq'), 'head'), parts along dimension 0, may hold values from -6 to 6
Outputs:
- mixer_out: bfloat16 [2048, 4096], P(('groups', 'seq'), 'head'), parts along dimension 0
- attn_out: bfloat16 [2048, 2048], P(('groups', 'seq'), 'head'), parts along dimension 0
- x_grad: bfloat16 [2048, 4096], P(('groups', 'seq'), 'head'), parts along dimension 0
- b_grad: float32 [2048, 128], P(('groups', 'seq')), parts along dimension 0
- c_grad: float32 [2048, 128], P(('groups', 'seq')), parts along dimension 0
- decay_grad: float32 [64, 1024], P(('groups', 'head'), 'seq'), parts along dimension 0
- q_grad: bfloat16 [2048, 2048], P(('groups', 'seq'), 'head'), parts along dimension 0
- key_gradient: bfloat16 [2048, 512], P(('groups', 'seq'), 'head'), parts along dimension 0
- value_gradient: bfloat16 [2048, 512], P(('groups', 'seq'), 'head'), parts along dimension 0
There are 2 independent parts, one for each index of `groups`. A program takes and returns all parts, laid end to end along the dimension named above; an argument that names none is the same for every part. Nothing has to cross between parts.
Inputs may be any that keep to these rules, and one draw needn't show every extreme that they name: `doc_lengths`: the lengths of the documents packed into the stream, in order; they sum to 1024.
All inputs are finite; a program needn't handle non-finite values.
Results may differ from a plain program's by a relative error of at most 0.023.
Values may be sent and summed in bfloat16 or wider, within the bound.
No kernel may reach another device: no remote copies, remote signals or barrier semaphores. Data moves between devices by JAX's collectives and lax.ppermute only.
A program may use at most 128 MiB of HBM per device.

v0:
```python
import math

import jax
import jax.numpy as jnp
from jax import lax
from jax.sharding import PartitionSpec as P

P_SIZE = 128
HEAD_SIZE = 128


precise = lax.Precision.HIGHEST
big_negative = -1e30


def entering_2(part, axis, combine, identity, reverse):
    count = lax.axis_size(axis)
    place = lax.axis_index(axis)
    ahead = count - 1 - place if reverse else place
    gathered = jax.tree.map(lambda a: lax.all_gather(a, axis), part)
    state = jax.tree.map(lambda a, e: jnp.zeros_like(a) + jnp.asarray(e, a.dtype), part, identity)

    def one(step, state):
        source = count - 1 - step if reverse else step
        return combine(
            state, jax.tree.map(lambda a: lax.dynamic_index_in_dim(a, source, 0, False), gathered)
        )

    return lax.fori_loop(0, ahead, one, state)


def doc_index(positions, lengths):
    ends = jnp.cumsum(lengths)
    return jnp.sum((positions[:, None] >= ends[None, :]).astype(jnp.int32), axis=1)


def cumulate(decay):
    return jnp.cumsum(decay, axis=1)


def local_state(inputs, b_float, cumulated, segment):
    weights = (
        jnp.exp(cumulated[:, -1:] - cumulated)
        * (segment == segment[-1]).astype(inputs.dtype)[None, :]
    )
    return jnp.einsum("hs,sn,shp->hnp", weights, b_float, inputs, precision=precise)


def carry_factor(cumulated, segment, before):
    return jnp.exp(cumulated[:, -1]) * (segment[-1] == before).astype(cumulated.dtype)


def mixer_stretch(inputs, b_float, c_float, decay, gains, segment, before, state_in):
    cumulated = cumulate(decay)
    width = inputs.shape[0]
    steps = jnp.arange(width)
    allowed = (steps[:, None] >= steps[None, :]) & (segment[:, None] == segment[None, :])
    gaps = jnp.where(allowed[None], cumulated[:, :, None] - cumulated[:, None, :], big_negative)
    kernel = jnp.exp(gaps) * jnp.dot(c_float, b_float.T, precision=precise)[None]
    inner = jnp.einsum("hts,shp->thp", kernel, inputs, precision=precise)
    keeps = (segment == before).astype(inputs.dtype)
    entering = jnp.einsum("tn,hnp->thp", c_float, state_in, precision=precise)
    reach = jnp.exp(cumulated).T * keeps[:, None]
    outputs = inner + reach[:, :, None] * entering + gains[None, :, None] * inputs
    factor = carry_factor(cumulated, segment, before)
    state_out = factor[:, None, None] * state_in + local_state(inputs, b_float, cumulated, segment)
    return (outputs, state_out)


def combine_states(earlier, later):
    return (earlier[0] * later[0], later[0][:, None, None] * earlier[1] + later[1])


def on_device(
    x_input,
    b_rows,
    c_rows,
    decay_log,
    skip_gain,
    doc_lengths,
    queries,
    attention_key_rows,
    values,
    mixer_cot,
    attention_output_cotangent,
):
    tokens = x_input.shape[0]
    offset = lax.axis_index("seq") * tokens
    total_len = tokens * lax.axis_size("seq")
    positions = offset + jnp.arange(tokens, dtype=jnp.int32)
    segment = doc_index(positions, doc_lengths)
    previous = doc_index(jnp.reshape(offset - 1, (1,)), doc_lengths)[0]
    before = jnp.where(offset > 0, previous, -1)
    heads_here = skip_gain.shape[0]
    inputs = x_input.astype(jnp.float32).reshape(tokens, heads_here, P_SIZE)
    b_float = b_rows.astype(jnp.float32)
    c_float = c_rows.astype(jnp.float32)
    cot_float = mixer_cot.astype(jnp.float32).reshape(tokens, heads_here, P_SIZE)

    def stretch_of(inp, brow, crow, decay, state_in):
        return mixer_stretch(inp, brow, crow, decay, skip_gain, segment, before, state_in)

    cumulated = cumulate(decay_log)
    factor = carry_factor(cumulated, segment, before)
    summary = local_state(inputs, b_float, cumulated, segment)
    zero_state = jnp.zeros_like(summary)
    identity = (jnp.ones_like(factor), zero_state)
    state_in = entering_2((factor, summary), "seq", combine_states, identity, False)[1]
    (mixed, state_out), pull = jax.vjp(stretch_of, inputs, b_float, c_float, decay_log, state_in)
    adjoint_local = pull((cot_float, zero_state))[4]
    adjoint_out = entering_2((factor, adjoint_local), "seq", combine_states, identity, True)[1]
    grad_x, grad_b, grad_c, grad_decay, unused = pull((cot_float, adjoint_out))
    grad_b, grad_c = lax.psum((grad_b, grad_c), "head")
    mixer_out = mixed.reshape(tokens, heads_here * P_SIZE).astype(jnp.bfloat16)
    x_grad = grad_x.reshape(tokens, heads_here * P_SIZE).astype(jnp.bfloat16)
    logit_scale = 1.0 / math.sqrt(HEAD_SIZE)
    groups = attention_key_rows.shape[1] // HEAD_SIZE
    heads_per_group = queries.shape[1] // HEAD_SIZE // groups
    key_span = min(512, total_len)
    blocks = total_len // key_span
    last_pos = offset + tokens - 1
    query_grid = queries.reshape(tokens, groups, heads_per_group, HEAD_SIZE)
    cotangent_table = attention_output_cotangent.reshape(tokens, groups, heads_per_group, HEAD_SIZE)
    key_all, value_all = (
        lax.all_gather(attention_key_rows, "seq", axis=0, tiled=True),
        lax.all_gather(values, "seq", axis=0, tiled=True),
    )

    def block_view(number):
        anchor = number * key_span
        key_blk = lax.dynamic_slice_in_dim(key_all, anchor, key_span, 0).reshape(
            key_span, groups, HEAD_SIZE
        )
        value_blk = lax.dynamic_slice_in_dim(value_all, anchor, key_span, 0).reshape(
            key_span, groups, HEAD_SIZE
        )
        key_pos = anchor + jnp.arange(key_span, dtype=jnp.int32)
        allowed = (key_pos[None, :] <= positions[:, None]) & (
            doc_index(key_pos, doc_lengths)[None, :] == segment[:, None]
        )
        scores = (
            jnp.einsum("tgrd,kgd->grtk", query_grid, key_blk, preferred_element_type=jnp.float32)
            * logit_scale
        )
        scores = jnp.where(allowed[None, None], scores, big_negative)
        return (anchor, key_blk, value_blk, allowed, scores)

    def visit(number, carried, work):
        return lax.cond(
            number * key_span <= last_pos,
            lambda inner: work(number, inner),
            lambda inner: inner,
            carried,
        )

    def stats_step(number, carried):
        row_peak, row_total = carried
        anchor, key_blk, value_blk, allowed, scores = block_view(number)
        new_peak = jnp.maximum(row_peak, jnp.max(scores, axis=-1))
        fresh = jnp.sum(
            jnp.where(allowed[None, None], jnp.exp(scores - new_peak[..., None]), 0.0), axis=-1
        )
        return (new_peak, row_total * jnp.exp(row_peak - new_peak) + fresh)

    stat_shape = (groups, heads_per_group, tokens)
    row_peak, row_total = lax.fori_loop(
        0,
        blocks,
        lambda number, carried: visit(number, carried, stats_step),
        (jnp.full(stat_shape, big_negative, jnp.float32), jnp.zeros(stat_shape, jnp.float32)),
    )
    log_norm = row_peak + jnp.log(row_total)

    def output_step(number, totals):
        anchor, key_blk, value_blk, allowed, scores = block_view(number)
        weights = jnp.where(allowed[None, None], jnp.exp(scores - log_norm[..., None]), 0.0).astype(
            jnp.bfloat16
        )
        return totals + jnp.einsum(
            "grtk,kgd->tgrd", weights, value_blk, preferred_element_type=jnp.float32
        )

    attention_table = lax.fori_loop(
        0,
        blocks,
        lambda number, carried: visit(number, carried, output_step),
        jnp.zeros((tokens, groups, heads_per_group, HEAD_SIZE), jnp.float32),
    ).astype(jnp.bfloat16)
    row_products = jnp.einsum(
        "bkfh,bkfh->kfb", cotangent_table, attention_table, preferred_element_type=jnp.float32
    )

    def grad_terms(allowed, scores, value_blk):
        probs_full = jnp.where(allowed[None, None], jnp.exp(scores - log_norm[..., None]), 0.0)
        grad_prob = jnp.einsum(
            "tgrd,kgd->grtk", cotangent_table, value_blk, preferred_element_type=jnp.float32
        )
        grad_score = (probs_full * (grad_prob - row_products[..., None])).astype(jnp.bfloat16)
        return (probs_full.astype(jnp.bfloat16), grad_score)

    query_zero = jnp.zeros((tokens, groups, heads_per_group, HEAD_SIZE), jnp.float32)

    def full_step(number, carried):
        grad_query, term_key, term_value = carried
        anchor, key_blk, value_blk, allowed, scores = block_view(number)
        weights, grad_score = grad_terms(allowed, scores, value_blk)
        grad_query = grad_query + jnp.einsum(
            "grtk,kgd->tgrd", grad_score, key_blk, preferred_element_type=jnp.float32
        )
        key_part = jnp.einsum(
            "grtk,tgrd->kgd", grad_score, query_grid, preferred_element_type=jnp.float32
        ).reshape(key_span, groups * HEAD_SIZE)
        value_part = jnp.einsum(
            "grtk,tgrd->kgd", weights, cotangent_table, preferred_element_type=jnp.float32
        ).reshape(key_span, groups * HEAD_SIZE)
        term_key = lax.dynamic_update_slice_in_dim(term_key, key_part, anchor, 0)
        term_value = lax.dynamic_update_slice_in_dim(term_value, value_part, anchor, 0)
        return (grad_query, term_key, term_value)

    term_zero = jnp.zeros((total_len, groups * HEAD_SIZE), jnp.float32)
    grad_query, term_key, term_value = lax.fori_loop(
        0,
        blocks,
        lambda number, carried: visit(number, carried, full_step),
        (query_zero, term_zero, term_zero),
    )
    key_gradient_total, value_gradient_total = (
        lax.psum_scatter(term_key, "seq", scatter_dimension=0, tiled=True),
        lax.psum_scatter(term_value, "seq", scatter_dimension=0, tiled=True),
    )
    attn_out = attention_table.reshape(tokens, groups * heads_per_group * HEAD_SIZE)
    q_grad = (
        (grad_query * logit_scale)
        .reshape(tokens, groups * heads_per_group * HEAD_SIZE)
        .astype(jnp.bfloat16)
    )
    key_gradient = (key_gradient_total * logit_scale).astype(jnp.bfloat16)
    value_gradient = value_gradient_total.astype(jnp.bfloat16)
    return (
        mixer_out,
        attn_out,
        x_grad,
        grad_b,
        grad_c,
        grad_decay,
        q_grad,
        key_gradient,
        value_gradient,
    )


def solution(mesh):
    placed = (
        P(("groups", "seq"), "head"),
        P(("groups", "seq"), None),
        P(("groups", "seq"), None),
        P(("groups", "head"), "seq"),
        P("head"),
        P("groups"),
        P(("groups", "seq"), "head"),
        P(("groups", "seq"), "head"),
        P(("groups", "seq"), "head"),
        P(("groups", "seq"), "head"),
        P(("groups", "seq"), "head"),
    )
    return jax.shard_map(
        on_device,
        mesh=mesh,
        in_specs=placed,
        out_specs=(
            P(("groups", "seq"), "head"),
            P(("groups", "seq"), "head"),
            P(("groups", "seq"), "head"),
            P(("groups", "seq"), None),
            P(("groups", "seq"), None),
            P(("groups", "head"), "seq"),
            P(("groups", "seq"), "head"),
            P(("groups", "seq"), "head"),
            P(("groups", "seq"), "head"),
        ),
        check_vma=False,
    )
```

profile of v0, /device:TPU:0, one launch (start us, length us, event | category | flops | bytes accessed | tf_op | source)
XLA Modules:
  0.0 459.2 jit_solution(4572568857524987816)
XLA Ops:
  16.9 32.1 %all_gather.28 = bf16[1024,256]{0,1:T(8,128)(2,1)S(1)} all-gather(bf16[128,256]{0,1:T(8,128)(2,1)S(1)} %copy.169), channel_id=1, replica_groups=mesh['groups'=2,'seq'=8,'head'=2] {'seq'}, dimensions={0}, use_global_device_ids=true | all-gather | bytes 589824 | tf_op jit(solution)/shard_map/all_gather | solution.py:125
  49.0 1.7 while.79
  49.1 1.6 conditional.9
  50.8 35.4 %all_gather.27 = bf16[1024,256]{0,1:T(8,128)(2,1)S(1)} all-gather(bf16[128,256]{0,1:T(8,128)(2,1)S(1)} %copy.168), channel_id=1, replica_groups=mesh['groups'=2,'seq'=8,'head'=2] {'seq'}, dimensions={0}, use_global_device_ids=true | all-gather | bytes 589824 | tf_op jit(solution)/shard_map/all_gather | solution.py:126
  86.2 1.6 while.80
  86.2 1.6 conditional.10
  90.8 4.8 %while.81 = (s32[]{:T(128)}, f32[128,2,4,128]{0,3,2,1:T(8,128)S(1)}, f32[1024,256]{0,1:T(8,128)}, f32[1024,256]{0,1:T(8,128)}, s32[]{:T(128)}, /*index=5*/bf16[1...) while((s32[]{:T(128)}, ...), condition=%wide.region_36.37_spmd.clone, body=%wide.region_31.36_spmd.clone.sunk | while | flops 675616896 | bytes 33444924 | solution.py:221
  90.9 4.8 %conditional.11 = ((f32[128,2,4,128]{0,3,2,1:T(8,128)S(1)}, f32[1024,256]{0,1:T(8,128)}, f32[1024,256]{0,1:T(8,128)})) conditional(s32[]{:T(128)} %convert_element_type.150, (f32[128,2,4,128]{0,3,2,1:T(8,128)S(1)}, f32[1024,256]{0,1:T(8,128)}, f32[1024,256]{0,1:T(8,128)}) %tuple.194, (s32[]{:T(128)}, bf16[1024,256]{0,1:T(8,128)(2,1)S(1)}, ...), branch_computations={%region_32.32_spmd, %region_33.35_spmd} | conditional | flops 675616896 | bytes 33444102 | solution.py:149
  95.7 2.6 copy.186
  101.4 26.3 %all-reduce.2 = f32[128]{0:T(128)S(1)} all-reduce(f32[128]{0:T(128)S(1)} %dynamic-update-slice), channel_id=2, replica_groups=mesh['groups'=2,'seq'=8,'head'=2] {'seq'}, use_global_device_ids=true, to_apply=%add.2 | all-reduce | flops 128 | bytes 1024
  128.0 30.1 %all-gather.8.cloned.1.call-done = f32[128,128,128]{2,1,0:T(8,128)} async-done(((f32[16,128,128]{2,1,0:T(8,128)}), f32[128,128,128]{2,1,0:T(8,128)}) %all-gather.8.cloned.1.call-update) | async-done | bytes 8388624 | tf_op jit(solution)/shard_map/all_gather | solution.py:20
  158.3 10.5 %while.78 = (s32[]{:T(128)}, f32[16,128,128]{2,1,0:T(8,128)S(1)}, s32[]{:T(128)}, f32[8,16]{1,0:T(8,128)S(1)}, f32[8,16,128,128]{3,2,1,0:T(8,128)}, /*index=5*/s32[]{:T(128)}, s32[]{:T(128)}, s32[]{:T(128)}, s32[]{:T(128)}) while((s32[]{:T(128)}, f32[16,128,128]{2,1,0:T(8,128)S(1)}, s32[]{:T(128)}, f32[8,16]{1,0:T(8,128)S(1)}, ...), condition=%wide.region_21.22_spmd, body=%wide.region_20.21_spmd.sunk | while | flops 524294 | bytes 3146067 | solution.py:29
  162.8 1.4 bitcast_add_fusion.5
  164.3 1.4 bitcast_add_fusion.5
  165.8 1.5 bitcast_add_fusion.5
  167.3 1.5 bitcast_add_fusion.5
  168.8 1.6 fusion.41
  170.6 2.4 fusion.43
  175.2 1.5 fusion.51
  176.7 2.0 convolution_bitcast_fusion.3
  178.7 45.5 %reduce-scatter.5.cloned.1.call-done = f32[128,256]{1,0:T(8,128)} async-done(((f32[1024,256]{1,0:T(8,128)}), f32[128,256]{1,0:T(8,128)}) %reduce-scatter.5.cloned.1.call-update) | async-done | bytes 131088 | tf_op jit(solution)/shard_map/reduce_scatter | solution.py:229
  224.2 1.5 convert_element_type.117
  225.7 65.1 %reduce-scatter.3.cloned.1.call-done = f32[128,256]{1,0:T(8,128)} async-done(((f32[1024,256]{1,0:T(8,128)}), f32[128,256]{1,0:T(8,128)}) %reduce-scatter.3.cloned.1.call-update) | async-done | bytes 131088 | tf_op jit(solution)/shard_map/reduce_scatter | solution.py:228
  290.8 1.5 multiply_convert_fusion.1
  292.6 3.5 fusion.36
  298.0 118.3 %all-gather.6.cloned.1.call-done = f32[128,128,128]{2,1,0:T(8,128)} async-done(((f32[16,128,128]{2,1,0:T(8,128)}), f32[128,128,128]{2,1,0:T(8,128)}) %all-gather.6.cloned.1.call-update) | async-done | bytes 8388624 | tf_op jit(solution)/shard_map/all_gather | solution.py:20
  417.7 1.8 fusion.38
  420.5 1.5 fusion.35
  423.2 1.8 reduce_window_sum.39
  425.0 24.7 %all-reduce.6.cloned.1.call-done = (f32[128,128]{1,0:T(8,128)}, f32[128,128]{1,0:T(8,128)}) async-done(((f32[128,128]{1,0:T(8,128)}, f32[128,128]{1,0:T(8,128)}), (f32[128,128]{1,0:T(8,128)}, f32[128,128]{1,0:T(8,128)})) %all-reduce.6.cloned.1.call-update) | async-done | bytes 131088 | tf_op jit(solution)/shard_map/psum | solution.py:113
  449.7 1.5 copy.302
  451.1 1.5 copy.303
  (172 shorter events, 34.2 us)
Async XLA Ops:
  7.2 6.7 %copy-start = (bf16[128,128]{1,0:T(8,128)(2,1)S(1)}, bf16[128,128]{1,0:T(8,128)(2,1)}, u32[]{:S(2)}) copy-start(bf16[128,128]{1,0:T(8,128)(2,1)} %param.29) | copy-start | bytes 98308
  7.2 151.0 %all-gather.8.cloned.1.call-start = ((), (), s32[]{:S(2)}) async-start(), calls=%async_computation.5 | async-start | bytes 9437184 | tf_op jit(solution)/shard_map/all_gather | solution.py:20
  11.3 2.6 copy-start.20
  11.4 159.0 %copy-start.16 = (f32[128]{0:T(128)}, f32[128]{0:T(128)S(1)}, u32[]{:S(2)}) copy-start(f32[128]{0:T(128)S(1)} %get-tuple-element.1166) | copy-start | bytes 1540
  12.5 157.9 %copy-start.22 = (f32[16]{0:T(128)}, f32[16]{0:T(128)S(1)}, u32[]{:S(2)}) copy-start(f32[16]{0:T(128)S(1)} %get-tuple-element.1065) | copy-start | bytes 196
  13.9 2.2 copy-start.12
  13.9 2.3 copy-start.10
  14.6 2.0 copy-start.13
  14.6 2.1 copy-start.11
  16.0 33.0 %copy-start.26 = (s32[4]{0:T(128)S(1)}, s32[4]{0:T(128)}, u32[]{:S(2)}) copy-start(s32[4]{0:T(128)} %param.32) | copy-start | bytes 52
  16.1 208.1 %reduce-scatter.5.cloned.1.call-start = ((), (), s32[]{:S(2)}) async-start(), calls=%async_computation.3 | async-start | bytes 1179648 | tf_op jit(solution)/shard_map/reduce_scatter | solution.py:229
  92.7 1.2 copy-start.1
  92.7 1.5 copy-start.4
  94.3 1.3 copy-start.5
  95.7 2.7 copy-start.3
  98.3 1.5 copy-start.8
  98.3 1.6 copy-start.27
  98.3 29.5 %copy-start.9 = (bf16[128,2048]{1,0:T(8,128)(2,1)S(1)}, bf16[128,2048]{1,0:T(8,128)(2,1)}, u32[]{:S(2)}) copy-start(bf16[128,2048]{1,0:T(8,128)(2,1)} %param.27) | copy-start | bytes 1572868
  98.3 192.5 %reduce-scatter.3.cloned.1.call-start = ((), (), s32[]{:S(2)}) async-start(), calls=%async_computation.2 | async-start | bytes 1179648 | tf_op jit(solution)/shard_map/reduce_scatter | solution.py:228
  99.7 316.6 %all-gather.6.cloned.1.call-start = ((), (), s32[]{:S(2)}) async-start(), calls=%async_computation.4 | async-start | bytes 9437184 | tf_op jit(solution)/shard_map/all_gather | solution.py:20
  170.4 3.7 copy-start.7
  173.0 276.7 %all-reduce.6.cloned.1.call-start = ((), (), s32[]{:S(2)}) async-start(), calls=%async_computation.6 | async-start | bytes 262144 | tf_op jit(solution)/shard_map/psum | solution.py:113
  175.2 3.5 copy-start.14
  175.2 117.2 %copy-start.6 = (f32[16,128,128]{2,1,0:T(8,128)S(1)}, f32[16,128,128]{2,1,0:T(8,128)}, u32[]{:S(2)}) copy-start(f32[16,128,128]{2,1,0:T(8,128)} %get-tuple-element.1168) | copy-start | bytes 3145732
  176.7 115.9 %copy-start.24 = (f32[16]{0:T(128)S(1)}, f32[16]{0:T(128)}, u32[]{:S(2)}) copy-start(f32[16]{0:T(128)} %param.31) | copy-start | bytes 196
  416.7 3.8 copy-start.15
  416.7 3.8 copy-start.25
  420.5 2.5 copy-start.17
  420.5 2.5 copy-start.18
  420.5 2.5 copy-start.19
  420.5 2.5 copy-start.21
  420.5 2.5 copy-start.23
  (1 other events, 1.0 us)
Sparse Core Ops, SparseCore 0:
  16.2 141.9 all-gather.7
  161.6 62.5 reduce-scatter.4
  227.6 63.1 reduce-scatter.2
  292.8 123.4 all-gather.5
  423.1 26.4 all-reduce.5
where the time goes:
time: 460 us; the launch traced here: 459 us
  waiting for transfers between devices  284 us (62%)
  blocking collectives  93.7 us (20%)
  other arithmetic  22 us (5%)
  matrix products  21.7 us (5%)
  local copies, waits for them, and re-layouts  20.6 us (4%)
  between operations  16.3 us (4%)
    all_gather x2, waiting for transfers between devices, entering_2(): gathered = jax.tree.map(lambda a: lax.all_gather(a, axis), part)  148 us
    reduce_scatter x1, waiting for transfers between devices, on_device(): lax.psum_scatter(term_key, 'seq', scatter_dimension=0, tiled=True)  65.1 us
    reduce_scatter x1, waiting for transfers between devices, on_device(): lax.psum_scatter(term_value, 'seq', scatter_dimension=0, tiled=True)  45.5 us
    all_gather x1, blocking collectives, on_device(): lax.all_gather(values, 'seq', axis=0, tiled=True)  35.4 us
    all_gather x1, blocking collectives, on_device(): lax.all_gather(attention_key_rows, 'seq', axis=0, tiled=True)  32.1 us
    unnamed x1, blocking collectives  26.3 us
    psum x1, waiting for transfers between devices, on_device(): grad_b, grad_c = lax.psum((grad_b, grad_c), 'head')  24.7 us
    add x7, other arithmetic, combine_states(): later[0][:, None, None] * earlier[1] + later[1]  10.1 us
  transfers between devices with their start and end apart: 5, of which 5 were waited for; matrix products, arithmetic and copies ran while one was open for 10% of the time, Pallas kernels for 0%

commit v1 on v0

--- a/solution.py
+++ b/solution.py
@@ -17,16 +17,22 @@
     count = lax.axis_size(axis)
     place = lax.axis_index(axis)
     ahead = count - 1 - place if reverse else place
-    gathered = jax.tree.map(lambda a: lax.all_gather(a, axis), part)
-    state = jax.tree.map(lambda a, e: jnp.zeros_like(a) + jnp.asarray(e, a.dtype), part, identity)
-
-    def one(step, state):
-        source = count - 1 - step if reverse else step
-        return combine(
-            state, jax.tree.map(lambda a: lax.dynamic_index_in_dim(a, source, 0, False), gathered)
-        )
-
-    return lax.fori_loop(0, ahead, one, state)
+    early = jax.tree.map(lambda a, e: jnp.zeros_like(a) + jnp.asarray(e, a.dtype), part, identity)
+    span = part
+    shift = 1
+    while shift < count:
+        if reverse:
+            pairs = [(i, i - shift) for i in range(shift, count)]
+        else:
+            pairs = [(i, i + shift) for i in range(count - shift)]
+        got = lax.ppermute(span, axis, pairs)
+        have = ahead >= shift
+        got = jax.tree.map(lambda g, e: jnp.where(have, g, jnp.asarray(e, g.dtype)), got, identity)
+        early = combine(got, early)
+        if 2 * shift < count:
+            span = combine(got, span)
+        shift *= 2
+    return early
 
 
 def doc_index(positions, lengths):
@@ -110,7 +116,12 @@
     adjoint_local = pull((cot_float, zero_state))[4]
     adjoint_out = entering_2((factor, adjoint_local), "seq", combine_states, identity, True)[1]
     grad_x, grad_b, grad_c, grad_decay, unused = pull((cot_float, adjoint_out))
-    grad_b, grad_c = lax.psum((grad_b, grad_c), "head")
+    head_count = lax.axis_size("head")
+    if head_count == 2:
+        other_b, other_c = lax.ppermute((grad_b, grad_c), "head", [(0, 1), (1, 0)])
+        grad_b, grad_c = grad_b + other_b, grad_c + other_c
+    else:
+        grad_b, grad_c = lax.psum((grad_b, grad_c), "head")
     mixer_out = mixed.reshape(tokens, heads_here * P_SIZE).astype(jnp.bfloat16)
     x_grad = grad_x.reshape(tokens, heads_here * P_SIZE).astype(jnp.bfloat16)
     logit_scale = 1.0 / math.sqrt(HEAD_SIZE)
@@ -121,10 +132,11 @@
     last_pos = offset + tokens - 1
     query_grid = queries.reshape(tokens, groups, heads_per_group, HEAD_SIZE)
     cotangent_table = attention_output_cotangent.reshape(tokens, groups, heads_per_group, HEAD_SIZE)
-    key_all, value_all = (
-        lax.all_gather(attention_key_rows, "seq", axis=0, tiled=True),
-        lax.all_gather(values, "seq", axis=0, tiled=True),
-    )
+    key_width = attention_key_rows.shape[1]
+    kv_all = lax.all_gather(
+        jnp.concatenate([attention_key_rows, values], axis=1), "seq", axis=0, tiled=True
+    )
+    key_all, value_all = kv_all[:, :key_width], kv_all[:, key_width:]
 
     def block_view(number):
         anchor = number * key_span
@@ -224,10 +236,11 @@
         lambda number, carried: visit(number, carried, full_step),
         (query_zero, term_zero, term_zero),
     )
-    key_gradient_total, value_gradient_total = (
-        lax.psum_scatter(term_key, "seq", scatter_dimension=0, tiled=True),
-        lax.psum_scatter(term_value, "seq", scatter_dimension=0, tiled=True),
-    )
+    kv_total = lax.psum_scatter(
+        jnp.concatenate([term_key, term_value], axis=1), "seq", scatter_dimension=0, tiled=True
+    )
+    key_gradient_total = kv_total[:, : groups * HEAD_SIZE]
+    value_gradient_total = kv_total[:, groups * HEAD_SIZE :]
     attn_out = attention_table.reshape(tokens, groups * heads_per_group * HEAD_SIZE)
     q_grad = (
         (grad_query * logit_scale)

time: 460 us -> 239 us (0.52)
  waiting for transfers between devices: 284 us -> 100 us
  blocking collectives: 93.7 us -> 0 us
  starting transfers between devices: 0.38 us -> 47.2 us
  other arithmetic: 22 us -> 32.4 us
    all_gather x2 -> x1, waiting for transfers between devices: 148 us -> 1.94 us  [on_device(): lax.all_gather(jnp.concatenate([attention_key_rows, values], axis=1), 'se...]
    reduce_scatter x2 -> x1, waiting for transfers between devices: 111 us -> 20.7 us  [on_device(): lax.psum_scatter(jnp.concatenate([term_key, term_value], axis=1), 'seq',...]
    ppermute x0 -> x12, waiting for transfers between devices: none -> 77.3 us  [the longest x10 77.3 us: entering_2(): got = lax.ppermute(span, axis, pairs)]
    all_gather x2 -> x0, blocking collectives: 67.4 us -> none  [the longest x1 35.4 us: on_device(): lax.all_gather(values, 'seq', axis=0, tiled=True)]
    ppermute x0 -> x12, starting transfers between devices: none -> 47.2 us  [the longest x10 46.5 us: entering_2(): got = lax.ppermute(span, axis, pairs)]
    unnamed x1 -> x0, blocking collectives: 26.3 us -> none
    psum x1 -> x0, waiting for transfers between devices: 24.7 us -> none  [on_device(): grad_b, grad_c = lax.psum((grad_b, grad_c), 'head')]
    add x7 -> x3, other arithmetic: 10.1 us -> 7.47 us  [combine_states(): later[0][:, None, None] * earlier[1] + later[1]]
  transfers between devices with their start and end apart: 5 -> 14, of which waited for: 5 -> 6; matrix products, arithmetic and copies ran while one was open for 10% -> 26% of each run, Pallas kernels for 0% -> 0%
where the time goes in v1:
time: 239 us; the launch traced here: 238 us
  waiting for transfers between devices  100 us (42%)
  starting transfers between devices  47.2 us (20%)
  other arithmetic  32.4 us (14%)
  local copies, waits for them, and re-layouts  21.1 us (9%)
  matrix products  20.8 us (9%)
  between operations  16.2 us (7%)
    ppermute x10, waiting for transfers between devices, entering_2(): got = lax.ppermute(span, axis, pairs)  77.3 us
    ppermute x10, starting transfers between devices, entering_2(): got = lax.ppermute(span, axis, pairs)  46.5 us
    reduce_scatter x1, waiting for transfers between devices, on_device(): lax.psum_scatter(jnp.concatenate([term_key, term_value], axis=1), 'seq',...  20.7 us
    add x3, other arithmetic, combine_states(): later[0][:, None, None] * earlier[1] + later[1]  7.47 us
    dot_general x3, matrix products, local_state(): jnp.einsum('hs,sn,shp->hnp', weights, b_float, inputs, precision=precise)  6.26 us
    dot_general x3, matrix products, mixer_stretch(): inner = jnp.einsum('hts,shp->thp', kernel, inputs, precision=precise)  5.7 us
    unnamed x90, local copies, waits for them, and re-layouts  5.22 us
  transfers between devices with their start and end apart: 14, of which 6 were waited for; matrix products, arithmetic and copies ran while one was open for 26% of the time, Pallas kernels for 0%

profile of v1, /device:TPU:0, one launch (start us, length us, event | category | flops | bytes accessed | tf_op | source)
XLA Modules:
  0.0 238.2 jit_solution(8153878694560694745)
XLA Ops:
  18.2 2.3 fusion.41
  20.5 6.5 %collective-permute-start.2 = (f32[16,128,128]{2,1,0:T(8,128)}, f32[16,128,128]{2,1,0:T(8,128)}, u32[]{:S(2)}, u32[]{:S(2)}) collective-permute-start(f32[16,128,128]{2,1,0:T(8,128)} %fusion.41), channel_id=1, source_target_pairs={{0,2},{2,4},{4,6},{6,8},{8,10},{10,12},{12,14},{1,3},{3,5},{5,7},{... | collective-permute-start | bytes 3145736 | tf_op jit(solution)/shard_map/ppermute | solution.py:28
  27.1 3.8 %collective-permute-start = (f32[16]{0:T(128)}, f32[16]{0:T(128)S(1)}, u32[]{:S(2)}, u32[]{:S(2)}) collective-permute-start(f32[16]{0:T(128)} %get-tuple-element.971), channel_id=1, source_target_pairs={{0,2},{2,4},{4,6},{6,8},{8,10},{10,12},{12,14},{1,3},{3,5},{5,7},{... | collective-permute-start | bytes 200 | tf_op jit(solution)/shard_map/ppermute | solution.py:28
  34.5 10.6 %collective-permute-done.7 = f32[16,128,128]{2,1,0:T(8,128)} collective-permute-done((f32[16,128,128]{2,1,0:T(8,128)S(1)}, f32[16,128,128]{2,1,0:T(8,128)}, u32[]{:S(2)}, u32[]{:S(2)}) %collective-permute-start.7) | collective-permute-done | bytes 1048608 | tf_op jit(solution)/shard_map/ppermute | solution.py:28
  45.1 24.0 %collective-permute-done.2 = f32[16,128,128]{2,1,0:T(8,128)} collective-permute-done((f32[16,128,128]{2,1,0:T(8,128)}, f32[16,128,128]{2,1,0:T(8,128)}, u32[]{:S(2)}, u32[]{:S(2)}) %collective-permute-start.2) | collective-permute-done | bytes 1048608 | tf_op jit(solution)/shard_map/ppermute | solution.py:28
  69.1 3.4 %multiply_add_fusion.4 = (f32[16,128,128]{2,1,0:T(8,128)}, f32[16,128,128]{2,1,0:T(8,128)}) fusion(f32[16,128,128]{2,1,0:T(8,128)} %fusion.41, f32[16,128,128]{2,1,0:T(8,128)} %collective-permute-done.2, f32[16]{0:T(128)} %get-tuple-element.971, pred[]{:T(512)S(6)} %ge.116, f32[16,128,128]{2,1,0:T(8,128)S(1)} %fusion.32, ...), kind=kLoop, calls=%fused_computation.89 | loop fusion | flops 1572864 | bytes 6291522 | tf_op jit(solution)/shard_map/add | solution.py:77
  74.9 5.5 %collective-permute-start.3 = (f32[16,128,128]{2,1,0:T(8,128)}, f32[16,128,128]{2,1,0:T(8,128)}, u32[]{:S(2)}, u32[]{:S(2)}) collective-permute-start(f32[16,128,128]{2,1,0:T(8,128)} %get-tuple-element.986), channel_id=1, source_target_pairs={{0,4},{2,6},{4,8},{6,10},{8,12},{10,14},{1,5},{3,7},{5,9},{7,11},{... | collective-permute-start | bytes 3145736 | tf_op jit(solution)/shard_map/ppermute | solution.py:28
  80.5 1.9 all-gather.2.cloned.1.call-done
  83.7 2.4 %while.51 = (s32[]{:T(128)}, f32[2,4,128]{2,1,0:T(4,128)S(1)}, f32[2,4,128]{2,1,0:T(4,128)S(1)}, s32[]{:T(128)}, s32[4]{0:T(128)}, /*index=5*/s32[128]{0:T(128)S...) while((s32[]{:T(128)}, f32[2,4,128]{2,1,0:T(4,128)S(1)}, ...), condition=%wide.region_11.12_spmd.clone, body=%wide.region_4.11_spmd.clone.sunk | while | flops 138616976 | bytes 5505901 | solution.py:178
  83.7 2.3 conditional.9
  86.8 4.2 %while.52 = (s32[]{:T(128)}, f32[128,2,4,128]{0,3,2,1:T(8,128)S(1)}, s32[]{:T(128)}, bf16[1024,256]{0,1:T(8,128)(2,1)S(1)}, s32[4]{0:T(128)}, /*index=5*/s32[128...) while((s32[]{:T(128)}, ...), condition=%wide.region_17.18_spmd.clone, body=%wide.region_12.17_spmd.clone.sunk | while | flops 271390848 | bytes 3031901 | solution.py:195
  86.8 4.1 %conditional.10 = (f32[128,2,4,128]{0,3,2,1:T(8,128)S(1)}) conditional(s32[]{:T(128)} %convert_element_type.146, f32[128,2,4,128]{0,3,2,1:T(8,128)S(1)} %get-tuple-element.1261, (s32[]{:T(128)}, bf16[1024,256]{0,1:T(8,128)(2,1)S(1)}, s32[]{:T(128)}, s32[4]{0:T(128)}, s32[128]{0:T(128)S(1)}, /*index=5*/bf16[1024,256]{0,1:T(8,128)(2,1)S(1)}, ...), branch_computations={%region_13.13_spmd, %region_14.16_spmd} | conditional | flops 271390848 | bytes 3031158 | solution.py:161
  89.2 1.7 fusion.13
  94.0 6.4 %while.53 = (s32[]{:T(128)}, f32[128,2,4,128]{0,3,2,1:T(8,128)S(1)}, f32[1024,256]{0,1:T(8,128)}, f32[1024,256]{0,1:T(8,128)}, s32[]{:T(128)}, /*index=5*/bf16[1...) while((s32[]{:T(128)}, ...), condition=%wide.region_30.31_spmd.clone, body=%wide.region_25.30_spmd.clone.sunk | while | flops 675616896 | bytes 33444932 | solution.py:233
  94.0 6.4 %conditional.11 = ((f32[128,2,4,128]{0,3,2,1:T(8,128)S(1)}, f32[1024,256]{0,1:T(8,128)}, f32[1024,256]{0,1:T(8,128)})) conditional(s32[]{:T(128)} %convert_element_type.147, (f32[128,2,4,128]{0,3,2,1:T(8,128)S(1)}, f32[1024,256]{0,1:T(8,128)}, f32[1024,256]{0,1:T(8,128)}) %tuple.157, (s32[]{:T(128)}, bf16[1024,256]{0,1:T(8,128)(2,1)S(1)}, ...), branch_computations={%region_26.26_spmd, %region_27.29_spmd} | conditional | flops 675616896 | bytes 33444102 | solution.py:161
  100.5 2.7 %copy.151 = f32[1024,256]{1,0:T(8,128)} copy(f32[1024,256]{0,1:T(8,128)} %get-tuple-element.692) | data formatting | bytes 2097152 | tf_op jit(solution)/shard_map/while | solution.py:233
  104.5 3.1 %pad_maximum_fusion = f32[1024,512]{1,0:T(8,128)} fusion(f32[1024,256]{1,0:T(8,128)} %copy.151, f32[1024,256]{1,0:T(8,128)} %copy.150), kind=kLoop, calls=%fused_computation.53 | loop fusion | flops 524288 | bytes 4194304 | tf_op jit(solution)/shard_map/concatenate | solution.py:240
  108.2 1.7 multiply_add_fusion.1
  111.5 2.4 %multiply_add_fusion.3 = f32[16,128,128]{2,1,0:T(8,128)} fusion(f32[16,128,128]{2,1,0:T(8,128)} %get-tuple-element.986, f32[16,128,128]{2,1,0:T(8,128)} %collective-permute-done.3, f32[16]{0:T(128)S(1)} %copy-done.41, pred[]{:T(512)S(6)} %ge.115), kind=kLoop, calls=%fused_computation.88 | loop fusion | flops 786432 | bytes 3145793 | tf_op jit(solution)/shard_map/add | solution.py:77
  113.9 19.4 %collective-permute-start.4 = (f32[16,128,128]{2,1,0:T(8,128)}, f32[16,128,128]{2,1,0:T(8,128)}, u32[]{:S(2)}, u32[]{:S(2)}) collective-permute-start(f32[16,128,128]{2,1,0:T(8,128)} %multiply_add_fusion.3), channel_id=1, source_target_pairs={{0,8},{2,10},{4,12},{6,14},{1,9},{3,11},{5,13},{7,15},{16,24},{18,... | collective-permute-start | bytes 3145736 | tf_op jit(solution)/shard_map/ppermute | solution.py:28
  133.6 1.9 convolution_bitcast_fusion.3
  136.8 4.5 %collective-permute-start.1 = (f32[16]{0:T(128)S(1)}, f32[16]{0:T(128)S(1)}, u32[]{:S(2)}, u32[]{:S(2)}) collective-permute-start(f32[16]{0:T(128)S(1)} %copy-done.41), channel_id=1, source_target_pairs={{0,4},{2,6},{4,8},{6,10},{8,12},{10,14},{1,5},{3,7},{5,9},{7,11},{... | collective-permute-start | bytes 200 | tf_op jit(solution)/shard_map/ppermute | solution.py:28
  141.4 17.6 %collective-permute-done.1 = f32[16]{0:T(128)S(1)} collective-permute-done((f32[16]{0:T(128)S(1)}, f32[16]{0:T(128)S(1)}, u32[]{:S(2)}, u32[]{:S(2)}) %collective-permute-start.1) | collective-permute-done | bytes 96 | tf_op jit(solution)/shard_map/ppermute | solution.py:28
  160.8 25.1 %collective-permute-done.9 = f32[16,128,128]{2,1,0:T(8,128)} collective-permute-done((f32[16,128,128]{2,1,0:T(8,128)S(1)}, f32[16,128,128]{2,1,0:T(8,128)}, u32[]{:S(2)}, u32[]{:S(2)}) %collective-permute-start.9) | collective-permute-done | bytes 1048608 | tf_op jit(solution)/shard_map/ppermute | solution.py:28
  186.0 2.6 %multiply_reduce_fusion = (f32[16]{0:T(128)S(1)}, f32[16,128,128]{2,1,0:T(8,128)S(1)}, f32[16,128,128]{2,1,0:T(8,128)S(1)}) fusion(f32[16,128,128]{2,1,0:T(8,128)} %collective-permute-done.7, pred[]{:T(512)S(6)} %ge.119, f32[16,128,128]{2,1,0:T(8,128)} %collective-permute-done.8, pred[]{:T(512)S(6)} %ge.118, f32[16]{0:T(128)S(1)} %copy-done.39, ...), kind=kLoop, calls=%fused_computation.81 | loop fusion | flops 4194288 | bytes 8388934 | tf_op jit(solution)/shard_map/transpose(jvp())/reduce_sum | solution.py:72
  188.6 1.6 fusion.38
  190.6 1.8 fusion.36
  197.6 2.2 add_convert_fusion
  199.9 2.3 fusion.33
  204.4 1.8 reduce_window_sum.39
  207.5 20.7 %reduce-scatter.2.cloned.1.call-done = f32[128,512]{1,0:T(8,128)} async-done(((f32[1024,512]{1,0:T(8,128)}), f32[128,512]{1,0:T(8,128)}) %reduce-scatter.2.cloned.1.call-update) | async-done | bytes 262160 | tf_op jit(solution)/shard_map/reduce_scatter | solution.py:239
  228.3 1.5 fusion.69
  (202 shorter events, 48.6 us)
Async XLA Ops:
  7.2 7.4 %copy-start = (bf16[128,128]{1,0:T(8,128)(2,1)S(1)}, bf16[128,128]{1,0:T(8,128)(2,1)}, u32[]{:S(2)}) copy-start(bf16[128,128]{1,0:T(8,128)(2,1)} %param.25) | copy-start | bytes 98308
  7.2 9.7 %copy-start.21 = (bf16[128,256]{1,0:T(8,128)(2,1)S(1)}, bf16[128,256]{1,0:T(8,128)(2,1)}, u32[]{:S(2)}) copy-start(bf16[128,256]{1,0:T(8,128)(2,1)} %param.31) | copy-start | bytes 196612
  7.2 9.8 %copy-start.22 = (bf16[128,256]{1,0:T(8,128)(2,1)S(1)}, bf16[128,256]{1,0:T(8,128)(2,1)}, u32[]{:S(2)}) copy-start(bf16[128,256]{1,0:T(8,128)(2,1)} %param.30) | copy-start | bytes 196612
  7.2 10.7 %copy-start.13 = (bf16[128,2048]{1,0:T(8,128)(2,1)S(1)}, bf16[128,2048]{1,0:T(8,128)(2,1)}, u32[]{:S(2)}) copy-start(bf16[128,2048]{1,0:T(8,128)(2,1)} %param.23) | copy-start | bytes 1572868
  7.2 75.2 %all-gather.2.cloned.1.call-start = ((), (), s32[]{:S(2)}) async-start(), calls=%async_computation.1 | async-start | bytes 1179648 | tf_op jit(solution)/shard_map/all_gather | solution.py:136
  15.4 16.8 %copy-start.15 = (bf16[128,1024]{1,0:T(8,128)(2,1)S(1)}, bf16[128,1024]{1,0:T(8,128)(2,1)}, u32[]{:S(2)}) copy-start(bf16[128,1024]{1,0:T(8,128)(2,1)} %param.33) | copy-start | bytes 786436
  15.4 17.0 %copy-start.16 = (bf16[128,1024]{1,0:T(8,128)(2,1)S(1)}, bf16[128,1024]{1,0:T(8,128)(2,1)}, u32[]{:S(2)}) copy-start(bf16[128,1024]{1,0:T(8,128)(2,1)} %param.29) | copy-start | bytes 786436
  15.4 29.7 %collective-permute-start.7 = (f32[16,128,128]{2,1,0:T(8,128)S(1)}, f32[16,128,128]{2,1,0:T(8,128)}, u32[]{:S(2)}, u32[]{:S(2)}) collective-permute-start(f32[16,128,128]{2,1,0:T(8,128)S(1)} %fusion.32), channel_id=1, source_target_pairs={{2,0},{4,2},{6,4},{8,6},{10,8},{12,10},{14,12},{3,1},{5,3},{7,5},{... | collective-permute-start | bytes 3145736 | tf_op jit(solution)/shard_map/ppermute | solution.py:28
  17.8 210.5 %reduce-scatter.2.cloned.1.call-start = ((), (), s32[]{:S(2)}) async-start(), calls=%async_computation.2 | async-start | bytes 2359296 | tf_op jit(solution)/shard_map/reduce_scatter | solution.py:239
  18.2 16.4 %copy-start.1 = (bf16[128,2048]{0,1:T(8,128)(2,1)}, bf16[128,2048]{0,1:T(8,128)(2,1)S(1)}, u32[]{:S(2)}) copy-start(bf16[128,2048]{0,1:T(8,128)(2,1)S(1)} %copy.129) | copy-start | bytes 1572868
  18.2 14.4 %copy-start.10 = (f32[128,128]{1,0:T(8,128)}, f32[128,128]{1,0:T(8,128)S(1)}, u32[]{:S(2)}) copy-start(f32[128,128]{1,0:T(8,128)S(1)} %convert.8) | copy-start | bytes 196612
  20.5 48.5 %collective-permute-start.2 = (f32[16,128,128]{2,1,0:T(8,128)}, f32[16,128,128]{2,1,0:T(8,128)}, u32[]{:S(2)}, u32[]{:S(2)}) collective-permute-start(f32[16,128,128]{2,1,0:T(8,128)} %fusion.41), channel_id=1, source_target_pairs={{0,2},{2,4},{4,6},{6,8},{8,10},{10,12},{12,14},{1,3},{3,5},{5,7},{... | collective-permute-start | bytes 3145736 | tf_op jit(solution)/shard_map/ppermute | solution.py:28
  27.1 46.7 %collective-permute-start = (f32[16]{0:T(128)}, f32[16]{0:T(128)S(1)}, u32[]{:S(2)}, u32[]{:S(2)}) collective-permute-start(f32[16]{0:T(128)} %get-tuple-element.971), channel_id=1, source_target_pairs={{0,2},{2,4},{4,6},{6,8},{8,10},{10,12},{12,14},{1,3},{3,5},{5,7},{... | collective-permute-start | bytes 200 | tf_op jit(solution)/shard_map/ppermute | solution.py:28
  30.9 42.9 %collective-permute-start.5 = (f32[16]{0:T(128)}, f32[16]{0:T(128)S(1)}, u32[]{:S(2)}, u32[]{:S(2)}) collective-permute-start(f32[16]{0:T(128)} %get-tuple-element.971), channel_id=1, source_target_pairs={{2,0},{4,2},{6,4},{8,6},{10,8},{12,10},{14,12},{3,1},{5,3},{7,5},{... | collective-permute-start | bytes 200 | tf_op jit(solution)/shard_map/ppermute | solution.py:28
  32.9 39.6 %copy-start.27 = (pred[128,128]{1,0:T(8,128)(4,1)}, pred[128,128]{1,0:T(8,128)(4,1)S(1)}, u32[]{:S(2)}) copy-start(pred[128,128]{1,0:T(8,128)(4,1)S(1)} %fusion.70) | copy-start | bytes 49156
  33.0 39.4 %copy-start.23 = (f32[128,128]{1,0:T(8,128)}, f32[128,128]{1,0:T(8,128)S(1)}, u32[]{:S(2)}) copy-start(f32[128,128]{1,0:T(8,128)S(1)} %fusion.86) | copy-start | bytes 196612
  72.4 35.2 %collective-permute-start.8 = (f32[16,128,128]{2,1,0:T(8,128)}, f32[16,128,128]{2,1,0:T(8,128)}, u32[]{:S(2)}, u32[]{:S(2)}) collective-permute-start(f32[16,128,128]{2,1,0:T(8,128)} %get-tuple-element.987), channel_id=1, source_target_pairs={{4,0},{6,2},{8,4},{10,6},{12,8},{14,10},{5,1},{7,3},{9,5},{11,7},{... | collective-permute-start | bytes 3145736 | tf_op jit(solution)/shard_map/ppermute | solution.py:28
  74.9 36.5 %collective-permute-start.3 = (f32[16,128,128]{2,1,0:T(8,128)}, f32[16,128,128]{2,1,0:T(8,128)}, u32[]{:S(2)}, u32[]{:S(2)}) collective-permute-start(f32[16,128,128]{2,1,0:T(8,128)} %get-tuple-element.986), channel_id=1, source_target_pairs={{0,4},{2,6},{4,8},{6,10},{8,12},{10,14},{1,5},{3,7},{5,9},{7,11},{... | collective-permute-start | bytes 3145736 | tf_op jit(solution)/shard_map/ppermute | solution.py:28
  110.0 23.3 %copy-start.14 = (f32[128,128]{1,0:T(8,128)S(1)}, f32[128,128]{1,0:T(8,128)}, u32[]{:S(2)}) copy-start(f32[128,128]{1,0:T(8,128)} %get-tuple-element.896) | copy-start | bytes 196612
  110.0 23.6 %copy-start.24 = (f32[128,128]{1,0:T(8,128)S(1)}, f32[128,128]{1,0:T(8,128)}, u32[]{:S(2)}) copy-start(f32[128,128]{1,0:T(8,128)} %copy-done.23) | copy-start | bytes 196612
  110.0 23.6 %copy-start.28 = (pred[128,128]{1,0:T(8,128)(4,1)S(1)}, pred[128,128]{1,0:T(8,128)(4,1)}, u32[]{:S(2)}) copy-start(pred[128,128]{1,0:T(8,128)(4,1)} %copy-done.27) | copy-start | bytes 49156
  110.0 76.0 %collective-permute-start.9 = (f32[16,128,128]{2,1,0:T(8,128)S(1)}, f32[16,128,128]{2,1,0:T(8,128)}, u32[]{:S(2)}, u32[]{:S(2)}) collective-permute-start(f32[16,128,128]{2,1,0:T(8,128)S(1)} %multiply_add_fusion.1), channel_id=1, source_target_pairs={{8,0},{10,2},{12,4},{14,6},{9,1},{11,3},{13,5},{15,7},{24,16},{26,... | collective-permute-start | bytes 3145736 | tf_op jit(solution)/shard_map/ppermute | solution.py:28
  111.4 30.0 %copy-start.39 = (f32[16]{0:T(128)S(1)}, f32[16]{0:T(128)}, u32[]{:S(2)}) copy-start(f32[16]{0:T(128)} %get-tuple-element.985) | copy-start | bytes 196
  111.5 47.6 %copy-start.38 = (f32[16]{0:T(128)S(1)}, f32[16]{0:T(128)}, u32[]{:S(2)}) copy-start(f32[16]{0:T(128)} %get-tuple-element.973) | copy-start | bytes 196
  111.5 47.6 %copy-start.9 = (bf16[128,2,4,128]{0,3,2,1:T(8,128)(2,1)S(1)}, bf16[128,2,4,128]{0,3,2,1:T(8,128)(2,1)}, u32[]{:S(2)}) copy-start(bf16[128,2,4,128]{0,3,2,1:T(8,128)(2,1)} %get-tuple-element.964) | copy-start | bytes 786436
  113.9 72.1 %collective-permute-start.4 = (f32[16,128,128]{2,1,0:T(8,128)}, f32[16,128,128]{2,1,0:T(8,128)}, u32[]{:S(2)}, u32[]{:S(2)}) collective-permute-start(f32[16,128,128]{2,1,0:T(8,128)} %multiply_add_fusion.3), channel_id=1, source_target_pairs={{0,8},{2,10},{4,12},{6,14},{1,9},{3,11},{5,13},{7,15},{16,24},{18,... | collective-permute-start | bytes 3145736 | tf_op jit(solution)/shard_map/ppermute | solution.py:28
  135.5 5.8 %collective-permute-start.6 = (f32[16]{0:T(128)S(1)}, f32[16]{0:T(128)S(1)}, u32[]{:S(2)}, u32[]{:S(2)}) collective-permute-start(f32[16]{0:T(128)S(1)} %copy-done.42), channel_id=1, source_target_pairs={{4,0},{6,2},{8,4},{10,6},{12,8},{14,10},{5,1},{7,3},{9,5},{11,7},{... | collective-permute-start | bytes 200 | tf_op jit(solution)/shard_map/ppermute | solution.py:28
  136.8 22.2 %collective-permute-start.1 = (f32[16]{0:T(128)S(1)}, f32[16]{0:T(128)S(1)}, u32[]{:S(2)}, u32[]{:S(2)}) collective-permute-start(f32[16]{0:T(128)S(1)} %copy-done.41), channel_id=1, source_target_pairs={{0,4},{2,6},{4,8},{6,10},{8,12},{10,14},{1,5},{3,7},{5,9},{7,11},{... | collective-permute-start | bytes 200 | tf_op jit(solution)/shard_map/ppermute | solution.py:28
  160.8 27.7 %copy-start.2 = (bf16[128,2048]{0,1:T(8,128)(2,1)S(1)}, bf16[128,2048]{0,1:T(8,128)(2,1)}, u32[]{:S(2)}) copy-start(bf16[128,2048]{0,1:T(8,128)(2,1)} %copy-done.1) | copy-start | bytes 1572868
  160.8 27.7 %copy-start.18 = (f32[128,16]{0,1:T(8,128)S(1)}, f32[128,16]{0,1:T(8,128)}, u32[]{:S(2)}) copy-start(f32[128,16]{0,1:T(8,128)} %copy-done.17) | copy-start | bytes 24580
  190.5 15.7 %collective-permute-start.10 = (f32[128,128]{1,0:T(8,128)S(1)}, f32[128,128]{1,0:T(8,128)S(1)}, u32[]{:S(2)}, u32[]{:S(2)}) collective-permute-start(f32[128,128]{1,0:T(8,128)S(1)} %convolution_add_fusion.1), channel_id=1, source_target_pairs={{0,1},{1,0},{2,3},{3,2},{4,5},{5,4},{6,7},{7,6},{8,9},{9,8},{10,11... | collective-permute-start | bytes 196616 | tf_op jit(solution)/shard_map/ppermute | solution.py:121
  192.5 14.4 %collective-permute-start.11 = (f32[128,128]{1,0:T(8,128)S(1)}, f32[128,128]{1,0:T(8,128)S(1)}, u32[]{:S(2)}, u32[]{:S(2)}) collective-permute-start(f32[128,128]{1,0:T(8,128)S(1)} %fusion.36), channel_id=1, source_target_pairs={{0,1},{1,0},{2,3},{3,2},{4,5},{5,4},{6,7},{7,6},{8,9},{9,8},{10,11... | collective-permute-start | bytes 196616 | tf_op jit(solution)/shard_map/ppermute | solution.py:121
  (26 other events, 78.4 us)
Sparse Core Ops, SparseCore 0:
  17.9 64.4 all-gather.1
  107.8 120.4 reduce-scatter.1

commit v2 on v1

--- a/solution.py
+++ b/solution.py
@@ -7,6 +7,7 @@
 
 P_SIZE = 128
 HEAD_SIZE = 128
+TOK_SPAN = 128
 
 
 precise = lax.Precision.HIGHEST
@@ -77,6 +78,103 @@
     return (earlier[0] * later[0], later[0][:, None, None] * earlier[1] + later[1])
 
 
+def mixer_whole(inputs, b_float, c_float, decay, gains, segment):
+    width = TOK_SPAN
+    count = inputs.shape[0] // width
+    heads = inputs.shape[1]
+    inp = inputs.reshape(count, width, heads, P_SIZE)
+    b_blocks = b_float.reshape(count, width, -1)
+    c_blocks = c_float.reshape(count, width, -1)
+    dec = decay.reshape(heads, count, width).transpose(1, 0, 2)
+    seg = segment.reshape(count, width)
+    befores = jnp.concatenate([jnp.full((1,), -1, seg.dtype), seg[:-1, -1]])
+    cumulated = jnp.cumsum(dec, axis=2)
+    factor = jax.vmap(carry_factor)(cumulated, seg, befores)
+    summary = jax.vmap(local_state)(inp, b_blocks, cumulated, seg)
+
+    def advance(carried, pieces):
+        fac, summ = pieces
+        return (fac[:, None, None] * carried + summ, carried)
+
+    unused, state_in = lax.scan(advance, jnp.zeros_like(summary[0]), (factor, summary))
+
+    def stretch(i, brow, crow, d, sg, bf, st):
+        return mixer_stretch(i, brow, crow, d, gains, sg, bf, st)[0]
+
+    outputs = jax.vmap(stretch)(inp, b_blocks, c_blocks, dec, seg, befores, state_in)
+    return outputs.reshape(count * width, heads, P_SIZE)
+
+
+def mamba_by_heads(x_input, b_all, c_all, decay_log, skip_gain, doc_lengths, mixer_cot):
+    seq_count = lax.axis_size("seq")
+    place = lax.axis_index("seq")
+    tokens = x_input.shape[0]
+    heads_here = skip_gain.shape[0]
+    own = heads_here // seq_count
+    total = tokens * seq_count
+    pair = lax.all_to_all(
+        jnp.stack([x_input, mixer_cot]), "seq", split_axis=2, concat_axis=1, tiled=True
+    )
+    decay = lax.all_to_all(decay_log, "seq", split_axis=0, concat_axis=1, tiled=True)
+    gains = lax.dynamic_slice_in_dim(skip_gain, place * own, own)
+    segment = doc_index(jnp.arange(total, dtype=jnp.int32), doc_lengths)
+    inputs = pair[0].astype(jnp.float32).reshape(total, own, P_SIZE)
+    cot = pair[1].astype(jnp.float32).reshape(total, own, P_SIZE)
+
+    def whole_of(i, brow, crow, d):
+        return mixer_whole(i, brow, crow, d, gains, segment)
+
+    mixed, pull = jax.vjp(
+        whole_of, inputs, b_all.astype(jnp.float32), c_all.astype(jnp.float32), decay
+    )
+    grad_x, grad_b, grad_c, grad_decay = pull(cot)
+    back = jnp.stack(
+        [
+            mixed.reshape(total, own * P_SIZE).astype(jnp.bfloat16),
+            grad_x.reshape(total, own * P_SIZE).astype(jnp.bfloat16),
+        ]
+    )
+    back = lax.all_to_all(back, "seq", split_axis=1, concat_axis=2, tiled=True)
+    grad_decay = lax.all_to_all(grad_decay, "seq", split_axis=1, concat_axis=0, tiled=True)
+    return back[0], back[1], jnp.concatenate([grad_b, grad_c], axis=1), grad_decay
+
+
+def mamba_by_stretch(
+    x_input, b_rows, c_rows, decay_log, skip_gain, doc_lengths, mixer_cot, segment, offset
+):
+    tokens = x_input.shape[0]
+    previous = doc_index(jnp.reshape(offset - 1, (1,)), doc_lengths)[0]
+    before = jnp.where(offset > 0, previous, -1)
+    heads_here = skip_gain.shape[0]
+    inputs = x_input.astype(jnp.float32).reshape(tokens, heads_here, P_SIZE)
+    b_float = b_rows.astype(jnp.float32)
+    c_float = c_rows.astype(jnp.float32)
+    cot_float = mixer_cot.astype(jnp.float32).reshape(tokens, heads_here, P_SIZE)
+
+    def stretch_of(inp, brow, crow, decay, state_in):
+        return mixer_stretch(inp, brow, crow, decay, skip_gain, segment, before, state_in)
+
+    cumulated = cumulate(decay_log)
+    factor = carry_factor(cumulated, segment, before)
+    summary = local_state(inputs, b_float, cumulated, segment)
+    zero_state = jnp.zeros_like(summary)
+    identity = (jnp.ones_like(factor), zero_state)
+    state_in = entering_2((factor, summary), "seq", combine_states, identity, False)[1]
+    (mixed, state_out), pull = jax.vjp(stretch_of, inputs, b_float, c_float, decay_log, state_in)
+    adjoint_local = pull((cot_float, zero_state))[4]
+    adjoint_out = entering_2((factor, adjoint_local), "seq", combine_states, identity, True)[1]
+    grad_x, grad_b, grad_c, grad_decay, unused = pull((cot_float, adjoint_out))
+    head_count = lax.axis_size("head")
+    if head_count == 2:
+        other_b, other_c = lax.ppermute((grad_b, grad_c), "head", [(0, 1), (1, 0)])
+        grad_b, grad_c = grad_b + other_b, grad_c + other_c
+    else:
+        grad_b, grad_c = lax.psum((grad_b, grad_c), "head")
+    mixer_out = mixed.reshape(tokens, heads_here * P_SIZE).astype(jnp.bfloat16)
+    x_grad = grad_x.reshape(tokens, heads_here * P_SIZE).astype(jnp.bfloat16)
+    return (mixer_out, x_grad, grad_b, grad_c, grad_decay)
+
+
 def on_device(
     x_input,
     b_rows,
@@ -95,35 +193,23 @@
     total_len = tokens * lax.axis_size("seq")
     positions = offset + jnp.arange(tokens, dtype=jnp.int32)
     segment = doc_index(positions, doc_lengths)
-    previous = doc_index(jnp.reshape(offset - 1, (1,)), doc_lengths)[0]
-    before = jnp.where(offset > 0, previous, -1)
     heads_here = skip_gain.shape[0]
-    inputs = x_input.astype(jnp.float32).reshape(tokens, heads_here, P_SIZE)
-    b_float = b_rows.astype(jnp.float32)
-    c_float = c_rows.astype(jnp.float32)
-    cot_float = mixer_cot.astype(jnp.float32).reshape(tokens, heads_here, P_SIZE)
-
-    def stretch_of(inp, brow, crow, decay, state_in):
-        return mixer_stretch(inp, brow, crow, decay, skip_gain, segment, before, state_in)
-
-    cumulated = cumulate(decay_log)
-    factor = carry_factor(cumulated, segment, before)
-    summary = local_state(inputs, b_float, cumulated, segment)
-    zero_state = jnp.zeros_like(summary)
-    identity = (jnp.ones_like(factor), zero_state)
-    state_in = entering_2((factor, summary), "seq", combine_states, identity, False)[1]
-    (mixed, state_out), pull = jax.vjp(stretch_of, inputs, b_float, c_float, decay_log, state_in)
-    adjoint_local = pull((cot_float, zero_state))[4]
-    adjoint_out = entering_2((factor, adjoint_local), "seq", combine_states, identity, True)[1]
-    grad_x, grad_b, grad_c, grad_decay, unused = pull((cot_float, adjoint_out))
-    head_count = lax.axis_size("head")
-    if head_count == 2:
-        other_b, other_c = lax.ppermute((grad_b, grad_c), "head", [(0, 1), (1, 0)])
-        grad_b, grad_c = grad_b + other_b, grad_c + other_c
+    by_heads = heads_here % lax.axis_size("seq") == 0
+    key_width = attention_key_rows.shape[1]
+    state_width = b_rows.shape[1]
+    pieces = [attention_key_rows, values] + ([b_rows, c_rows] if by_heads else [])
+    gathered = lax.all_gather(jnp.concatenate(pieces, axis=1), "seq", axis=0, tiled=True)
+    key_all, value_all = gathered[:, :key_width], gathered[:, key_width : 2 * key_width]
+    if by_heads:
+        b_all = gathered[:, 2 * key_width : 2 * key_width + state_width]
+        c_all = gathered[:, 2 * key_width + state_width :]
+        mixer_out, x_grad, bc_part, grad_decay = mamba_by_heads(
+            x_input, b_all, c_all, decay_log, skip_gain, doc_lengths, mixer_cot
+        )
     else:
-        grad_b, grad_c = lax.psum((grad_b, grad_c), "head")
-    mixer_out = mixed.reshape(tokens, heads_here * P_SIZE).astype(jnp.bfloat16)
-    x_grad = grad_x.reshape(tokens, heads_here * P_SIZE).astype(jnp.bfloat16)
+        mixer_out, x_grad, grad_b, grad_c, grad_decay = mamba_by_stretch(
+            x_input, b_rows, c_rows, decay_log, skip_gain, doc_lengths, mixer_cot, segment, offset
+        )
     logit_scale = 1.0 / math.sqrt(HEAD_SIZE)
     groups = attention_key_rows.shape[1] // HEAD_SIZE
     heads_per_group = queries.shape[1] // HEAD_SIZE // groups
@@ -132,11 +218,6 @@
     last_pos = offset + tokens - 1
     query_grid = queries.reshape(tokens, groups, heads_per_group, HEAD_SIZE)
     cotangent_table = attention_output_cotangent.reshape(tokens, groups, heads_per_group, HEAD_SIZE)
-    key_width = attention_key_rows.shape[1]
-    kv_all = lax.all_gather(
-        jnp.concatenate([attention_key_rows, values], axis=1), "seq", axis=0, tiled=True
-    )
-    key_all, value_all = kv_all[:, :key_width], kv_all[:, key_width:]
 
     def block_view(number):
         anchor = number * key_span
@@ -236,11 +317,19 @@
         lambda number, carried: visit(number, carried, full_step),
         (query_zero, term_zero, term_zero),
     )
+    sums = [term_key, term_value] + ([bc_part] if by_heads else [])
     kv_total = lax.psum_scatter(
-        jnp.concatenate([term_key, term_value], axis=1), "seq", scatter_dimension=0, tiled=True
+        jnp.concatenate(sums, axis=1), "seq", scatter_dimension=0, tiled=True
     )
     key_gradient_total = kv_total[:, : groups * HEAD_SIZE]
-    value_gradient_total = kv_total[:, groups * HEAD_SIZE :]
+    value_gradient_total = kv_total[:, groups * HEAD_SIZE : 2 * groups * HEAD_SIZE]
+    if by_heads:
+        bc_sum = kv_total[:, 2 * groups * HEAD_SIZE :]
+        if lax.axis_size("head") == 2:
+            bc_sum = bc_sum + lax.ppermute(bc_sum, "head", [(0, 1), (1, 0)])
+        else:
+            bc_sum = lax.psum(bc_sum, "head")
+        grad_b, grad_c = bc_sum[:, :state_width], bc_sum[:, state_width:]
     attn_out = attention_table.reshape(tokens, groups * heads_per_group * HEAD_SIZE)
     q_grad = (
         (grad_query * logit_scale)

time: 239 us -> 269 us (1.13)
  local copies, waits for them, and re-layouts: 21.1 us -> 68.2 us
  starting transfers between devices: 47.2 us -> 29 us
  matrix products: 20.8 us -> 32.8 us
  waiting for transfers between devices: 100 us -> 93.5 us
  other arithmetic: 32.4 us -> 27.9 us
    ppermute x12 -> x1, waiting for transfers between devices: 77.3 us -> 0.01 us  [on_device(): bc_sum = bc_sum + lax.ppermute(bc_sum, 'head', [(0, 1), (1, 0)])]
    all_to_all x0 -> x4, waiting for transfers between devices: none -> 65.7 us  [the longest x1 34.7 us: mamba_by_heads(): lax.all_to_all(jnp.stack([x_input, mixer_cot]), 'seq', split_axis=2, conc...]
    ppermute x12 -> x1, starting transfers between devices: 47.2 us -> 0.07 us  [on_device(): bc_sum = bc_sum + lax.ppermute(bc_sum, 'head', [(0, 1), (1, 0)])]
    all_to_all x0 -> x4, starting transfers between devices: none -> 28.9 us  [the longest x1 14.3 us: mamba_by_heads(): lax.all_to_all(grad_decay, 'seq', split_axis=1, concat_axis=0, tiled=True)]
    mul x1 -> x18, local copies, waits for them, and re-layouts: 0.09 us -> 10.9 us  [the longest x16 10.9 us: advance(): return (fac[:, None, None] * carried + summ, carried)]
    dynamic_update_slice x0 -> x16, local copies, waits for them, and re-layouts: none -> 9.87 us  [mixer_whole(): lax.scan(advance, jnp.zeros_like(summary[0]), (factor, summary))]
    dynamic_slice x0 -> x17, local copies, waits for them, and re-layouts: none -> 8.14 us  [the longest x16 8.06 us: mixer_whole(): lax.scan(advance, jnp.zeros_like(summary[0]), (factor, summary))]
    reduce_scatter x1, waiting for transfers between devices: 20.7 us -> 27 us  [on_device(): lax.psum_scatter(jnp.concatenate(sums, axis=1), 'seq', scatter_dimension=...]
  transfers between devices with their start and end apart: 14 -> 7, of which waited for: 6 -> 6; matrix products, arithmetic and copies ran while one was open for 26% -> 13% of each run, Pallas kernels for 0% -> 0%
where the time goes in v2:
time: 269 us; the launch traced here: 267 us
  waiting for transfers between devices  93.5 us (35%)
  local copies, waits for them, and re-layouts  68.2 us (25%)
  matrix products  32.8 us (12%)
  starting transfers between devices  29 us (11%)
  other arithmetic  27.9 us (10%)
  between operations  14.7 us (5%)
    all_to_all x1, waiting for transfers between devices, mamba_by_heads(): lax.all_to_all(jnp.stack([x_input, mixer_cot]), 'seq', split_axis=2, conc...  34.7 us
    reduce_scatter x1, waiting for transfers between devices, on_device(): lax.psum_scatter(jnp.concatenate(sums, axis=1), 'seq', scatter_dimension=...  27 us
    all_to_all x1, waiting for transfers between devices, mamba_by_heads(): back = lax.all_to_all(back, 'seq', split_axis=1, concat_axis=2, tiled=True)  24.1 us
    all_to_all x1, starting transfers between devices, mamba_by_heads(): lax.all_to_all(grad_decay, 'seq', split_axis=1, concat_axis=0, tiled=True)  14.3 us
    mul x16, local copies, waits for them, and re-layouts, advance(): return (fac[:, None, None] * carried + summ, carried)  10.9 us
    unnamed x86, local copies, waits for them, and re-layouts  10.1 us
    dynamic_update_slice x16, local copies, waits for them, and re-layouts, mixer_whole(): lax.scan(advance, jnp.zeros_like(summary[0]), (factor, summary))  9.87 us
    dot_general x3, matrix products, local_state(): jnp.einsum('hs,sn,shp->hnp', weights, b_float, inputs, precision=precise)  8.09 us
  transfers between devices with their start and end apart: 7, of which 6 were waited for; matrix products, arithmetic and copies ran while one was open for 13% of the time, Pallas kernels for 0%

profile of v2, /device:TPU:0, one launch (start us, length us, event | category | flops | bytes accessed | tf_op | source)
XLA Modules:
  0.0 266.9 jit_solution(8798041764163728764)
XLA Ops:
  11.6 7.3 %all-to-all-start.1 = ((f32[8,2,128]{2,1,0:T(2,128)}), f32[8,2,128]{2,1,0:T(2,128)S(1)}, u32[]{:S(2)}, u32[]{:S(2)}) async-start(f32[8,2,128]{2,1,0:T(2,128)} %bitcast.332), calls=%async_computation.1 | async-start | bytes 16384 | tf_op jit(solution)/shard_map/all_to_all | solution.py:118
  21.2 2.0 copy.341
  23.2 2.3 all-to-all-done.1
  25.5 3.7 %all-to-all-start = ((bf16[2,128,2048]{1,0,2:T(2,128)(2,1)}), bf16[2,128,2048]{1,0,2:T(2,128)(2,1)S(1)}, u32[]{:S(2)}, u32[]{:S(2)}) async-start(bf16[2,128,2048]{1,0,2:T(2,128)(2,1)} %copy.341), calls=%async_computation | async-start | bytes 2097152 | tf_op jit(solution)/shard_map/all_to_all | solution.py:115
  34.7 34.7 %all-to-all-done = bf16[2,128,2048]{1,0,2:T(2,128)(2,1)S(1)} async-done(((bf16[2,128,2048]{1,0,2:T(2,128)(2,1)}), bf16[2,128,2048]{1,0,2:T(2,128)(2,1)S(1)}, u32[]{:S(2)}, u32[]{:S(2)}) %all-to-all-start) | async-done | bytes 1048608 | tf_op jit(solution)/shard_map/all_to_all | solution.py:115
  73.2 2.3 fusion.35
  75.6 23.3 %while.88 = (s32[]{:T(128)}, f32[2,128,128]{2,1,0:T(8,128)S(1)}, f32[8,2,128,128]{3,2,1,0:T(8,128)S(1)}, f32[8,2,1,1]{1,3,2,0:T(1,128)}, f32[8,2]{1,0:T(8,128)},...) while((s32[]{:T(128)}, f32[2,128,128]{2,1,0:T(8,128)S(1)}, ...), condition=%wide.region_4.5_spmd.clone, body=%wide.region_3.4_spmd.clone.sunk | while | flops 131075 | bytes 656528 | solution.py:99
  100.2 2.9 %fusion.52 = (f32[8,128,2]{1,2,0:T(2,128)S(1)}, f32[8,128,256]{1,2,0}) fusion(bf16[8,128,2,128]{1,3,2,0:T(8,128)(2,1)S(1)} %bitcast.283, bf16[8,128,128]{2,1,0:T(8,128)(2,1)S(1)} %bitcast.294, f32[8,128,256]{1,2,0:T(8,128)} %bitcast.306), kind=kOutput, calls=%fused_computation.87 | convolution fusion | flops 403437568 | bytes 2891776
  104.7 2.7 %fusion.51 = f32[8,128,128]{2,1,0:T(8,128)} fusion(f32[8,2,128,128]{3,2,1,0:T(8,128)S(1)} %get-tuple-element.1737, bf16[8,128,2,128]{1,3,2,0:T(8,128)(2,1)S(1)} %bitcast.285, f32[8,128,2]{1,2,0:T(2,128)S(1)} %copy.352), kind=kOutput, calls=%fused_computation.84 | convolution fusion | flops 403177472 | bytes 2105344 | tf_op jit(solution)/shard_map/transpose(jvp(vmap(tn,hnp->thp)))/dot_general | solution.py:69
  109.1 14.9 %while.89 = (s32[]{:T(128)}, f32[2,128,128]{2,1,0:T(8,128)S(1)}, f32[8,2]{1,0:T(8,128)S(1)}, f32[8,2,128,128]{3,2,1,0:T(8,128)S(1)}, f32[8,2,128,128]{2,3,1,0:T(...) while((s32[]{:T(128)}, f32[2,128,128]{2,1,0:T(8,128)S(1)}, ...), condition=%wide.region_7.8_spmd.clone, body=%wide.region_5.7_spmd.clone.sunk | while | flops 196610 | bytes 1310920 | solution.py:99
  128.1 3.3 %while.86 = (s32[]{:T(128)}, f32[128,2,4,128]{0,3,2,1:T(8,128)}, s32[]{:T(128)}, bf16[1024,256]{0,1:T(8,128)(2,1)S(1)}, s32[4]{0:T(128)S(1)}, /*index=5*/s32[128...) while((s32[]{:T(128)}, f32[128,2,4,128]{0,3,2,1:T(8,128)}, ...), condition=%wide.region_22.23_spmd.clone, body=%wide.region_17.22_spmd.clone.sunk | while | flops 271390848 | bytes 3031901 | solution.py:276
  128.1 3.3 %conditional.10 = (f32[128,2,4,128]{0,3,2,1:T(8,128)}) conditional(s32[]{:T(128)} %convert_element_type.165, f32[128,2,4,128]{0,3,2,1:T(8,128)} %get-tuple-element.1807, (s32[]{:T(128)}, bf16[1024,256]{0,1:T(8,128)(2,1)S(1)}, s32[]{:T(128)}, s32[4]{0:T(128)S(1)}, s32[128]{0:T(128)S(1)}, /*index=5*/bf16[1024,256]{0,1:T(8,128)(2,1)S(1)}, ...), branch_computations={%region_18.18_spmd, %region_19.21_spmd} | conditional | flops 271390848 | bytes 3031158 | solution.py:242
  128.7 2.8 %fusion.13 = f32[128,2,4,128]{0,3,2,1:T(8,128)} fusion(f32[128,2,4,128]{0,3,2,1:T(8,128)} %get-tuple-element.792, bf16[512,2,128,1]{0,2,3,1:T(8,128)(2,1)S(1)} %bitcast.298, bf16[512,2,128,1]{0,2,3,1:T(8,128)(2,1)S(1)} %bitcast.297, bf16[128,2,4,128]{3,0,2,1:T(8,128)(2,1)S(1)} %get-tuple-element.799, f32[2,4,128]{2,1,0:T(4,128)S(1)} %get-tuple-element.800, ...), kind=kOutput, calls=%fused_computation.19 | convolution fusion | flops 271187968 | bytes 1904640 | tf_op jit(solution)/shard_map/while/body/eval_jaxpr/cond/branch_1_fun/grtk,kgd->tgrd/dot_general | solution.py:272
  131.4 3.5 %fusion.53 = (f32[8,128,128]{1,2,0:T(8,128)}, f32[8,2,128,128]{3,2,1,0:T(8,128)}) fusion(f32[8,128,2]{1,2,0:T(2,128)S(1)} %copy.353, f32[8,2,128,128]{3,2,1,0:T(8,128)S(1)} %get-tuple-element.864, bf16[8,128,2,128]{1,3,2,0:T(8,128)(2,1)} %bitcast.301), kind=kOutput, calls=%fused_computation.91 | convolution fusion | flops 403046400 | bytes 3153920 | tf_op jit(solution)/shard_map/transpose(jvp(vmap(hs,sn,shp->hnp)))/dot_general | solution.py:53
  134.9 2.1 copy.423
  137.1 2.5 convolution_add_fusion
  141.0 1.8 fusion.60
  145.1 5.8 %while.87 = (s32[]{:T(128)}, f32[128,2,4,128]{0,3,2,1:T(8,128)S(1)}, f32[1024,256]{0,1:T(8,128)}, f32[1024,256]{0,1:T(8,128)}, s32[]{:T(128)}, /*index=5*/bf16[1...) while((s32[]{:T(128)}, ...), condition=%wide.region_28.29_spmd.clone, body=%wide.region_23.28_spmd.clone.sunk | while | flops 675616896 | bytes 33444932 | solution.py:314
  145.1 5.8 %conditional.11 = ((f32[128,2,4,128]{0,3,2,1:T(8,128)S(1)}, f32[1024,256]{0,1:T(8,128)}, f32[1024,256]{0,1:T(8,128)})) conditional(s32[]{:T(128)} %convert_element_type.166, (f32[128,2,4,128]{0,3,2,1:T(8,128)S(1)}, f32[1024,256]{0,1:T(8,128)}, f32[1024,256]{0,1:T(8,128)}) %tuple.226, (s32[]{:T(128)}, bf16[1024,256]{0,1:T(8,128)(2,1)S(1)}, ...), branch_computations={%region_24.24_spmd, %region_25.27_spmd} | conditional | flops 675616896 | bytes 33444102 | solution.py:242
  150.9 2.7 %copy.377 = f32[1024,256]{1,0:T(8,128)} copy(f32[1024,256]{0,1:T(8,128)} %get-tuple-element.869) | data formatting | bytes 2097152 | tf_op jit(solution)/shard_map/while | solution.py:314
  154.9 3.6 %pad_maximum_fusion = f32[1024,768]{1,0:T(8,128)} fusion(f32[1024,128]{1,0:T(8,128)S(1)} %bitcast.307, f32[1024,128]{1,0:T(8,128)} %bitcast.308, f32[1024,256]{1,0:T(8,128)} %copy.377, f32[1024,256]{1,0:T(8,128)} %copy.376), kind=kLoop, calls=%fused_computation.65 | loop fusion | flops 2359296 | bytes 6291456 | tf_op jit(solution)/shard_map/concatenate | solution.py:322
  160.5 2.1 fusion.43
  162.6 2.3 fusion.47
  165.5 3.0 %fusion.46 = bf16[8,128,2,128]{1,3,2,0:T(8,128)(2,1)S(1)} fusion(bf16[8,128,2,128]{1,3,2,0:T(8,128)(2,1)S(1)} %bitcast.302, f32[8,128,2,128]{1,3,2,0:T(8,128)} %bitcast.314, f32[2]{0:T(128)S(1)} %dynamic_slice.54, f32[8,128,2]{1,2,0:T(2,128)S(1)} %copy.352, f32[8,128,128]{2,1,0:T(8,128)} %fusion.90, f32[8,2,128]{2,1,0:T(2,128)S(1)} %copy-done.36, ...), kind=kOutput, calls=%fused_computation.81 | convolution fusion | flops 405012480 | bytes 2768904 | tf_op jit(solution)/shard_map/jvp(vmap(hts,shp->thp))/dot_general | solution.py:67
  170.5 2.5 reduce_window_sum.46
  173.0 2.5 reduce_window_sum.47
  176.1 14.3 %all-to-all-start.3 = ((f32[2,8,128]{2,0,1:T(2,128)}), f32[2,8,128]{2,0,1:T(2,128)S(1)}, u32[]{:S(2)}, u32[]{:S(2)}) async-start(f32[2,8,128]{2,0,1:T(2,128)} %copy.384), calls=%async_computation.4 | async-start | bytes 16384 | tf_op jit(solution)/shard_map/all_to_all | solution.py:138
  190.6 2.1 copy.362
  192.6 4.6 %all-to-all-done.3 = f32[2,8,128]{2,0,1:T(2,128)S(1)} async-done(((f32[2,8,128]{2,0,1:T(2,128)}), f32[2,8,128]{2,0,1:T(2,128)S(1)}, u32[]{:S(2)}, u32[]{:S(2)}) %all-to-all-start.3) | async-done | bytes 8224 | tf_op jit(solution)/shard_map/all_to_all | solution.py:138
  197.2 3.6 %all-to-all-start.2 = ((bf16[2,1024,256]{2,0,1:T(2,128)(2,1)}), bf16[2,1024,256]{2,0,1:T(2,128)(2,1)S(1)}, u32[]{:S(2)}, u32[]{:S(2)}) async-start(bf16[2,1024,256]{2,0,1:T(2,128)(2,1)} %copy.362), calls=%async_computation.2 | async-start | bytes 2097152 | tf_op jit(solution)/shard_map/all_to_all | solution.py:137
  202.6 24.1 %all-to-all-done.2 = bf16[2,1024,256]{2,0,1:T(2,128)(2,1)S(1)} async-done(((bf16[2,1024,256]{2,0,1:T(2,128)(2,1)}), bf16[2,1024,256]{2,0,1:T(2,128)(2,1)S(1)}, u32[]{:S(2)}, u32[]{:S(2)}) %all-to-all-start.2) | async-done | bytes 1048608 | tf_op jit(solution)/shard_map/all_to_all | solution.py:137
  226.8 27.0 %reduce-scatter.2.cloned.1.call-done = f32[128,768]{1,0:T(8,128)} async-done(((f32[1024,768]{1,0:T(8,128)}), f32[128,768]{1,0:T(8,128)}) %reduce-scatter.2.cloned.1.call-update) | async-done | bytes 393232 | tf_op jit(solution)/shard_map/reduce_scatter | solution.py:321
  (296 shorter events, 90.0 us)
Async XLA Ops:
  7.2 63.4 %all-gather.2.cloned.1.call-start = ((), (), s32[]{:S(2)}) async-start(), calls=%async_computation.5 | async-start | bytes 1769472 | tf_op jit(solution)/shard_map/all_gather | solution.py:201
  11.6 13.8 %all-to-all-start.1 = ((f32[8,2,128]{2,1,0:T(2,128)}), f32[8,2,128]{2,1,0:T(2,128)S(1)}, u32[]{:S(2)}, u32[]{:S(2)}) async-start(f32[8,2,128]{2,1,0:T(2,128)} %bitcast.332), calls=%async_computation.1 | async-start | bytes 16384 | tf_op jit(solution)/shard_map/all_to_all | solution.py:118
  21.1 8.1 %copy-start.26 = (bf16[128,1024]{1,0:T(8,128)(2,1)S(1)}, bf16[128,1024]{1,0:T(8,128)(2,1)}, u32[]{:S(2)}) copy-start(bf16[128,1024]{1,0:T(8,128)(2,1)} %param.37) | copy-start | bytes 786436
  21.2 8.3 %copy-start.27 = (bf16[128,1024]{1,0:T(8,128)(2,1)S(1)}, bf16[128,1024]{1,0:T(8,128)(2,1)}, u32[]{:S(2)}) copy-start(bf16[128,1024]{1,0:T(8,128)(2,1)} %param.33) | copy-start | bytes 786436
  25.5 44.0 %all-to-all-start = ((bf16[2,128,2048]{1,0,2:T(2,128)(2,1)}), bf16[2,128,2048]{1,0,2:T(2,128)(2,1)S(1)}, u32[]{:S(2)}, u32[]{:S(2)}) async-start(bf16[2,128,2048]{1,0,2:T(2,128)(2,1)} %copy.341), calls=%async_computation | async-start | bytes 2097152 | tf_op jit(solution)/shard_map/all_to_all | solution.py:115
  29.2 224.6 %reduce-scatter.2.cloned.1.call-start = ((), (), s32[]{:S(2)}) async-start(), calls=%async_computation.6 | async-start | bytes 3538944 | tf_op jit(solution)/shard_map/reduce_scatter | solution.py:321
  31.1 38.5 %copy-start.37 = (f32[8]{0:T(128)}, f32[8]{0:T(128)S(1)}, u32[]{:S(2)}) copy-start(f32[8]{0:T(128)S(1)} %convert_reduce_fusion.4) | copy-start | bytes 100
  32.4 37.3 %copy-start.31 = (f32[8,128]{1,0:T(8,128)}, f32[8,128]{1,0:T(8,128)S(1)}, u32[]{:S(2)}) copy-start(f32[8,128]{1,0:T(8,128)S(1)} %get-tuple-element.1394) | copy-start | bytes 12292
  32.6 70.5 %copy-start.28 = (pred[8,128,128]{2,1,0:T(8,128)(4,1)}, pred[8,128,128]{2,1,0:T(8,128)(4,1)S(1)}, u32[]{:S(2)}) copy-start(pred[8,128,128]{2,1,0:T(8,128)(4,1)S(1)} %compare_and_fusion.3) | copy-start | bytes 393220
  34.0 35.7 %copy-start.34 = (f32[8,2]{0,1:T(2,128)}, f32[8,2]{0,1:T(2,128)S(1)}, u32[]{:S(2)}) copy-start(f32[8,2]{0,1:T(2,128)S(1)} %slice_reduce_fusion) | copy-start | bytes 196
  69.8 33.3 %copy-start.10 = (bf16[1,8,128,256]{2,3,1,0:T(8,128)(2,1)}, bf16[1,8,128,256]{2,3,1,0:T(8,128)(2,1)S(1)}, u32[]{:S(2)}) copy-start(bf16[1,8,128,256]{2,3,1,0:T(8,128)(2,1)S(1)} %get-tuple-element.1386) | copy-start | bytes 1572868
  69.8 37.6 %copy-start.1 = (bf16[1,8,128,256]{2,3,1,0:T(8,128)(2,1)}, bf16[1,8,128,256]{2,3,1,0:T(8,128)(2,1)S(1)}, u32[]{:S(2)}) copy-start(bf16[1,8,128,256]{2,3,1,0:T(8,128)(2,1)S(1)} %get-tuple-element.1387) | copy-start | bytes 1572868
  71.8 35.6 %copy-start.6 = (bf16[1024,128]{1,0:T(8,128)(2,1)}, bf16[1024,128]{1,0:T(8,128)(2,1)S(1)}, u32[]{:S(2)}) copy-start(bf16[1024,128]{1,0:T(8,128)(2,1)S(1)} %copy.350) | copy-start | bytes 786436
  72.0 3.5 %copy-start.3 = (bf16[1024,128]{1,0:T(8,128)(2,1)}, bf16[1024,128]{1,0:T(8,128)(2,1)S(1)}, u32[]{:S(2)}) copy-start(bf16[1024,128]{1,0:T(8,128)(2,1)S(1)} %copy.351) | copy-start | bytes 786436
  98.9 4.3 %copy-start.36 = (f32[8,2,128]{2,1,0:T(2,128)S(1)}, f32[8,2,128]{2,1,0:T(2,128)}, u32[]{:S(2)}) copy-start(f32[8,2,128]{2,1,0:T(2,128)} %copy.344) | copy-start | bytes 24580
  100.2 3.0 %copy-start.25 = (f32[8,128,128]{2,1,0:T(8,128)S(1)}, f32[8,128,128]{2,1,0:T(8,128)}, u32[]{:S(2)}) copy-start(f32[8,128,128]{2,1,0:T(8,128)} %fusion.90) | copy-start | bytes 1572868
  131.4 5.6 %copy-start.4 = (bf16[1024,128]{1,0:T(8,128)(2,1)S(1)}, bf16[1024,128]{1,0:T(8,128)(2,1)}, u32[]{:S(2)}) copy-start(bf16[1024,128]{1,0:T(8,128)(2,1)} %copy-done.3) | copy-start | bytes 786436
  134.9 4.6 %copy-start.7 = (bf16[1024,128]{1,0:T(8,128)(2,1)S(1)}, bf16[1024,128]{1,0:T(8,128)(2,1)}, u32[]{:S(2)}) copy-start(bf16[1024,128]{1,0:T(8,128)(2,1)} %copy-done.6) | copy-start | bytes 786436
  150.9 2.7 %copy-start.15 = (f32[1024,256]{0,1:T(8,128)S(1)}, f32[1024,256]{0,1:T(8,128)}, u32[]{:S(2)}) copy-start(f32[1024,256]{0,1:T(8,128)} %get-tuple-element.868) | copy-start | bytes 3145732
  150.9 4.0 %copy-start.19 = (f32[8,128,128]{2,1,0:T(8,128)S(1)}, f32[8,128,128]{2,1,0:T(8,128)}, u32[]{:S(2)}) copy-start(f32[8,128,128]{2,1,0:T(8,128)} %convolution_add_fusion) | copy-start | bytes 1572868
  158.6 4.0 %copy-start.9 = (f32[8,128,128]{2,1,0:T(8,128)S(1)}, f32[8,128,128]{2,1,0:T(8,128)}, u32[]{:S(2)}) copy-start(f32[8,128,128]{2,1,0:T(8,128)} %copy-done.8) | copy-start | bytes 1572868
  162.6 2.9 %copy-start.11 = (bf16[1,8,128,256]{2,3,1,0:T(8,128)(2,1)S(1)}, bf16[1,8,128,256]{2,3,1,0:T(8,128)(2,1)}, u32[]{:S(2)}) copy-start(bf16[1,8,128,256]{2,3,1,0:T(8,128)(2,1)} %copy-done.10) | copy-start | bytes 1572868
  165.5 4.5 %copy-start.35 = (f32[8,2]{0,1:T(2,128)S(1)}, f32[8,2]{0,1:T(2,128)}, u32[]{:S(2)}) copy-start(f32[8,2]{0,1:T(2,128)} %copy-done.34) | copy-start | bytes 196
  165.5 4.5 %copy-start.38 = (f32[8]{0:T(128)S(1)}, f32[8]{0:T(128)}, u32[]{:S(2)}) copy-start(f32[8]{0:T(128)} %copy-done.37) | copy-start | bytes 100
  165.5 4.6 %copy-start.12 = (f32[8,2,128,128]{3,2,1,0:T(8,128)S(1)}, f32[8,2,128,128]{3,2,1,0:T(8,128)}, u32[]{:S(2)}) copy-start(f32[8,2,128,128]{3,2,1,0:T(8,128)} %get-tuple-element.1401) | copy-start | bytes 3145732
  165.5 4.6 %copy-start.20 = (f32[8,128,128]{1,2,0:T(8,128)S(1)}, f32[8,128,128]{1,2,0:T(8,128)}, u32[]{:S(2)}) copy-start(f32[8,128,128]{1,2,0:T(8,128)} %copy.446) | copy-start | bytes 1572868
  169.9 20.6 %copy-start.22 = (bf16[1,1024,256]{1,2,0:T(8,128)(2,1)S(1)}, bf16[1,1024,256]{1,2,0:T(8,128)(2,1)}, u32[]{:S(2)}) copy-start(bf16[1,1024,256]{1,2,0:T(8,128)(2,1)} %convert_element_type.115) | copy-start | bytes 1572868
  176.1 21.1 %all-to-all-start.3 = ((f32[2,8,128]{2,0,1:T(2,128)}), f32[2,8,128]{2,0,1:T(2,128)S(1)}, u32[]{:S(2)}, u32[]{:S(2)}) async-start(f32[2,8,128]{2,0,1:T(2,128)} %copy.384), calls=%async_computation.4 | async-start | bytes 16384 | tf_op jit(solution)/shard_map/all_to_all | solution.py:138
  190.6 10.3 %copy-start.23 = (bf16[128,2,4,128]{0,3,2,1:T(8,128)(2,1)S(1)}, bf16[128,2,4,128]{0,3,2,1:T(8,128)(2,1)}, u32[]{:S(2)}) copy-start(bf16[128,2,4,128]{0,3,2,1:T(8,128)(2,1)} %get-tuple-element.1371) | copy-start | bytes 786436
  197.2 29.4 %all-to-all-start.2 = ((bf16[2,1024,256]{2,0,1:T(2,128)(2,1)}), bf16[2,1024,256]{2,0,1:T(2,128)(2,1)S(1)}, u32[]{:S(2)}, u32[]{:S(2)}) async-start(bf16[2,1024,256]{2,0,1:T(2,128)(2,1)} %copy.362), calls=%async_computation.2 | async-start | bytes 2097152 | tf_op jit(solution)/shard_map/all_to_all | solution.py:137
  254.7 3.4 %collective-permute-start = (f32[128,256]{1,0:T(8,128)S(1)}, f32[128,256]{1,0:T(8,128)S(1)}, u32[]{:S(2)}, u32[]{:S(2)}) collective-permute-start(f32[128,256]{1,0:T(8,128)S(1)} %slice.80), channel_id=1, source_target_pairs={{0,1},{1,0},{2,3},{3,2},{4,5},{5,4},{6,7},{7,6},{8,9},{9,8},{10,11... | collective-permute-start | bytes 393224 | tf_op jit(solution)/shard_map/ppermute | solution.py:329
  254.9 2.6 copy-start.24
  (16 other events, 23.8 us)
Sparse Core Ops, SparseCore 0:
  11.7 58.8 all-gather.1
  158.7 95.0 reduce-scatter.1

commit v3 on v2

--- a/solution.py
+++ b/solution.py
@@ -92,11 +92,14 @@
     factor = jax.vmap(carry_factor)(cumulated, seg, befores)
     summary = jax.vmap(local_state)(inp, b_blocks, cumulated, seg)
 
-    def advance(carried, pieces):
-        fac, summ = pieces
-        return (fac[:, None, None] * carried + summ, carried)
-
-    unused, state_in = lax.scan(advance, jnp.zeros_like(summary[0]), (factor, summary))
+    columns = jnp.arange(count)[:, None]
+    row = jnp.zeros((count, heads), factor.dtype)
+    rows = [row]
+    for k in range(1, count):
+        row = jnp.where(columns < k - 1, row * factor[k - 1][None, :], (columns == k - 1).astype(factor.dtype))
+        rows.append(row)
+    reach = jnp.stack(rows)
+    state_in = jnp.einsum("kjh,jhnp->khnp", reach, summary, precision=precise)
 
     def stretch(i, brow, crow, d, sg, bf, st):
         return mixer_stretch(i, brow, crow, d, gains, sg, bf, st)[0]
@@ -317,14 +320,13 @@
         lambda number, carried: visit(number, carried, full_step),
         (query_zero, term_zero, term_zero),
     )
-    sums = [term_key, term_value] + ([bc_part] if by_heads else [])
     kv_total = lax.psum_scatter(
-        jnp.concatenate(sums, axis=1), "seq", scatter_dimension=0, tiled=True
+        jnp.concatenate([term_key, term_value], axis=1), "seq", scatter_dimension=0, tiled=True
     )
     key_gradient_total = kv_total[:, : groups * HEAD_SIZE]
-    value_gradient_total = kv_total[:, groups * HEAD_SIZE : 2 * groups * HEAD_SIZE]
+    value_gradient_total = kv_total[:, groups * HEAD_SIZE :]
     if by_heads:
-        bc_sum = kv_total[:, 2 * groups * HEAD_SIZE :]
+        bc_sum = lax.psum_scatter(bc_part, "seq", scatter_dimension=0, tiled=True)
         if lax.axis_size("head") == 2:
             bc_sum = bc_sum + lax.ppermute(bc_sum, "head", [(0, 1), (1, 0)])
         else:

time: 269 us -> 264 us (0.981)
  local copies, waits for them, and re-layouts: 68.2 us -> 44 us
  waiting for transfers between devices: 93.5 us -> 114 us
  starting transfers between devices: 29 us -> 33.1 us
    all_gather x1, waiting for transfers between devices: 0.8 us -> 17.2 us  [on_device(): lax.all_gather(jnp.concatenate(pieces, axis=1), 'seq', axis=0, tiled=True)]
    all_to_all x1, waiting for transfers between devices: 24.1 us -> 36.1 us  [mamba_by_heads(): back = lax.all_to_all(back, 'seq', split_axis=1, concat_axis=2, tiled=True)]
    mul x16 -> x0, local copies, waits for them, and re-layouts: 10.9 us -> none  [advance(): return (fac[:, None, None] * carried + summ, carried)]
    dynamic_update_slice x16 -> x0, local copies, waits for them, and re-layouts: 9.87 us -> none  [mixer_whole(): lax.scan(advance, jnp.zeros_like(summary[0]), (factor, summary))]
    dynamic_slice x16 -> x0, local copies, waits for them, and re-layouts: 8.06 us -> none  [mixer_whole(): lax.scan(advance, jnp.zeros_like(summary[0]), (factor, summary))]
    add x8 -> x1, other arithmetic: 7.87 us -> 0.02 us  [on_device(): bc_sum = bc_sum + lax.ppermute(bc_sum, 'head', [(0, 1), (1, 0)])]
    all_to_all x1, waiting for transfers between devices: 34.7 us -> 27.5 us  [mamba_by_heads(): lax.all_to_all(jnp.stack([x_input, mixer_cot]), 'seq', split_axis=2, conc...]
    dot_general x0 -> x3, matrix products: none -> 6.37 us  [mixer_whole(): state_in = jnp.einsum('kjh,jhnp->khnp', reach, summary, precision=precise)]
  transfers between devices with their start and end apart: 7 -> 8, of which waited for: 6 -> 5; matrix products, arithmetic and copies ran while one was open for 13% -> 26% of each run, Pallas kernels for 0% -> 0%
where the time goes in v3:
time: 264 us; the launch traced here: 263 us
  waiting for transfers between devices  114 us (43%)
  local copies, waits for them, and re-layouts  44 us (17%)
  starting transfers between devices  33.1 us (13%)
  matrix products  30.6 us (12%)
  other arithmetic  26.9 us (10%)
  between operations  14.7 us (6%)
    all_to_all x1, waiting for transfers between devices, mamba_by_heads(): back = lax.all_to_all(back, 'seq', split_axis=1, concat_axis=2, tiled=True)  36.1 us
    reduce_scatter x1, waiting for transfers between devices, on_device(): lax.psum_scatter(jnp.concatenate([term_key, term_value], axis=1), 'seq',...  28.5 us
    all_to_all x1, waiting for transfers between devices, mamba_by_heads(): lax.all_to_all(jnp.stack([x_input, mixer_cot]), 'seq', split_axis=2, conc...  27.5 us
    all_gather x1, waiting for transfers between devices, on_device(): lax.all_gather(jnp.concatenate(pieces, axis=1), 'seq', axis=0, tiled=True)  17.2 us
    all_to_all x1, starting transfers between devices, mamba_by_heads(): lax.all_to_all(grad_decay, 'seq', split_axis=1, concat_axis=0, tiled=True)  15.7 us
    unnamed x115, local copies, waits for them, and re-layouts  9.71 us
    all_to_all x1, starting transfers between devices, mamba_by_heads(): lax.all_to_all(decay_log, 'seq', split_axis=0, concat_axis=1, tiled=True)  7.32 us
    dot_general x3, matrix products, mixer_whole(): state_in = jnp.einsum('kjh,jhnp->khnp', reach, summary, precision=precise)  6.37 us
  transfers between devices with their start and end apart: 8, of which 5 were waited for; matrix products, arithmetic and copies ran while one was open for 26% of the time, Pallas kernels for 0%

profile of v3, /device:TPU:0, one launch (start us, length us, event | category | flops | bytes accessed | tf_op | source)
XLA Modules:
  0.0 263.1 jit_solution(6910812292293547144)
XLA Ops:
  7.2 7.3 %all-to-all-start.1 = ((f32[8,2,128]{2,1,0:T(2,128)}), f32[8,2,128]{2,1,0:T(2,128)S(1)}, u32[]{:S(2)}, u32[]{:S(2)}) async-start(f32[8,2,128]{2,1,0:T(2,128)} %bitcast.327), calls=%async_computation.1 | async-start | bytes 16384 | tf_op jit(solution)/shard_map/all_to_all | solution.py:121
  21.6 2.0 copy.401
  23.6 6.1 %all-to-all-start = ((bf16[2,128,2048]{1,0,2:T(2,128)(2,1)}), bf16[2,128,2048]{1,0,2:T(2,128)(2,1)S(1)}, u32[]{:S(2)}, u32[]{:S(2)}) async-start(bf16[2,128,2048]{1,0,2:T(2,128)(2,1)} %copy.401), calls=%async_computation | async-start | bytes 2097152 | tf_op jit(solution)/shard_map/all_to_all | solution.py:118
  33.6 27.5 %all-to-all-done = bf16[2,128,2048]{1,0,2:T(2,128)(2,1)S(1)} async-done(((bf16[2,128,2048]{1,0,2:T(2,128)(2,1)}), bf16[2,128,2048]{1,0,2:T(2,128)(2,1)S(1)}, u32[]{:S(2)}, u32[]{:S(2)}) %all-to-all-start) | async-done | bytes 1048608 | tf_op jit(solution)/shard_map/all_to_all | solution.py:118
  62.2 17.2 %all-gather.2.cloned.1.call-done = bf16[1024,768]{0,1:T(8,128)(2,1)} async-done(((bf16[128,768]{0,1:T(8,128)(2,1)}), bf16[1024,768]{0,1:T(8,128)(2,1)}) %all-gather.2.cloned.1.call-update) | async-done | bytes 1572880 | tf_op jit(solution)/shard_map/all_gather | solution.py:204
  87.9 2.1 copy.488
  90.0 2.5 fusion.32
  93.4 2.6 convolution_bitcast_fusion.3
  96.0 2.5 copy.417
  98.6 3.2 %fusion.48 = f32[8,128,128]{2,1,0:T(8,128)S(1)} fusion(f32[8,2,128,128]{2,3,1,0:T(8,128)} %copy.417, bf16[8,128,2,128]{1,3,2,0:T(8,128)(2,1)S(1)} %bitcast.281, f32[8,128,2]{1,2,0:T(2,128)S(1)} %copy.412), kind=kOutput, calls=%fused_computation.74 | convolution fusion | flops 403177472 | bytes 2105344 | tf_op jit(solution)/shard_map/transpose(jvp(vmap(tn,hnp->thp)))/dot_general | solution.py:69
  106.5 2.2 fusion.40
  108.7 2.3 fusion.44
  113.7 2.4 while.51
  113.8 2.3 conditional.9
  117.6 4.0 %while.52 = (s32[]{:T(128)}, f32[128,2,4,128]{0,3,2,1:T(8,128)}, s32[]{:T(128)}, bf16[1024,256]{0,1:T(8,128)(2,1)S(1)}, s32[4]{0:T(128)}, /*index=5*/s32[128]{0:...) while((s32[]{:T(128)}, f32[128,2,4,128]{0,3,2,1:T(8,128)}, ...), condition=%wide.region_17.18_spmd.clone, body=%wide.region_12.17_spmd.clone.sunk | while | flops 271390848 | bytes 3031901 | solution.py:279
  117.6 4.0 %conditional.10 = (f32[128,2,4,128]{0,3,2,1:T(8,128)}) conditional(s32[]{:T(128)} %convert_element_type.251, f32[128,2,4,128]{0,3,2,1:T(8,128)} %get-tuple-element.1369, (s32[]{:T(128)}, bf16[1024,256]{0,1:T(8,128)(2,1)S(1)}, s32[]{:T(128)}, s32[4]{0:T(128)}, s32[128]{0:T(128)S(1)}, /*index=5*/bf16[1024,256]{0,1:T(8,128)(2,1)S(1)}, ...), branch_computations={%region_13.13_spmd, %region_14.16_spmd} | conditional | flops 271390848 | bytes 3031158 | solution.py:245
  118.8 2.8 %fusion.13 = f32[128,2,4,128]{0,3,2,1:T(8,128)} fusion(f32[128,2,4,128]{0,3,2,1:T(8,128)} %get-tuple-element.621, bf16[512,2,128,1]{0,2,3,1:T(8,128)(2,1)S(1)} %bitcast.295, bf16[512,2,128,1]{0,2,3,1:T(8,128)(2,1)S(1)} %bitcast.294, bf16[128,2,4,128]{3,0,2,1:T(8,128)(2,1)S(1)} %get-tuple-element.628, f32[2,4,128]{2,1,0:T(4,128)} %get-tuple-element.629, ...), kind=kOutput, calls=%fused_computation.19 | convolution fusion | flops 271187968 | bytes 1904640 | tf_op jit(solution)/shard_map/while/body/eval_jaxpr/cond/branch_1_fun/grtk,kgd->tgrd/dot_general | solution.py:275
  121.5 1.8 fusion.62
  125.7 6.6 %while.53 = (s32[]{:T(128)}, f32[128,2,4,128]{0,3,2,1:T(8,128)S(1)}, f32[1024,256]{0,1:T(8,128)}, f32[1024,256]{0,1:T(8,128)}, s32[]{:T(128)}, /*index=5*/bf16[1...) while((s32[]{:T(128)}, ...), condition=%wide.region_37.38_spmd.clone, body=%wide.region_32.37_spmd.clone.sunk | while | flops 675616896 | bytes 33444932 | solution.py:317
  125.7 6.6 %conditional.11 = ((f32[128,2,4,128]{0,3,2,1:T(8,128)S(1)}, f32[1024,256]{0,1:T(8,128)}, f32[1024,256]{0,1:T(8,128)})) conditional(s32[]{:T(128)} %convert_element_type.252, (f32[128,2,4,128]{0,3,2,1:T(8,128)S(1)}, f32[1024,256]{0,1:T(8,128)}, f32[1024,256]{0,1:T(8,128)}) %tuple.199, (s32[]{:T(128)}, bf16[1024,256]{0,1:T(8,128)(2,1)S(1)}, ...), branch_computations={%region_33.33_spmd, %region_34.36_spmd} | conditional | flops 675616896 | bytes 33444102 | solution.py:245
  132.3 2.7 %copy.455 = f32[1024,256]{1,0:T(8,128)} copy(f32[1024,256]{0,1:T(8,128)} %get-tuple-element.692) | data formatting | bytes 2097152 | tf_op jit(solution)/shard_map/while | solution.py:317
  136.3 3.2 %pad_maximum_fusion = f32[1024,512]{1,0:T(8,128)} fusion(f32[1024,256]{1,0:T(8,128)} %copy.455, f32[1024,256]{1,0:T(8,128)} %copy.454), kind=kLoop, calls=%fused_computation.53 | loop fusion | flops 524288 | bytes 4194304 | tf_op jit(solution)/shard_map/concatenate | solution.py:324
  139.6 2.8 %convolution_bitcast_fusion.6 = f32[8,8,2]{1,0,2:T(8,128)S(1)} fusion(f32[2,128,128,8]{2,3,1,0:T(8,128)S(1)} %copy.419, f32[8,2,128,128]{3,2,1,0:T(8,128)S(1)} %copy-done.1), kind=kOutput, calls=%fused_computation.77 | convolution fusion | flops 25165824 | bytes 2097664 | tf_op jit(solution)/shard_map/transpose(jvp(kjh,jhnp->khnp))/dot_general | solution.py:102
  148.2 2.5 fusion.43
  151.3 2.5 reduce_window_sum.47
  153.8 2.7 %reduce_window_sum.46 = f32[8,2,128]{2,0,1:T(8,128)S(1)} reduce-window(f32[8,2,128]{2,0,1:T(8,128)S(1)} %get-tuple-element.1075, f32[]{:T(128)} %constant.151.clone.1), window={size=1x1x128 pad=0_0x0_0x0_127}, to_apply=%region_23.24 | reduce-window | flops 260096 | bytes 16388 | tf_op jit(solution)/shard_map/transpose(jvp(vmap(jit(cumsum))))/reduce_window_sum | solution.py:45
  157.2 15.7 %all-to-all-start.3 = ((f32[2,8,128]{2,0,1:T(2,128)}), f32[2,8,128]{2,0,1:T(2,128)S(1)}, u32[]{:S(2)}, u32[]{:S(2)}) async-start(f32[2,8,128]{2,0,1:T(2,128)} %copy.451), calls=%async_computation.4 | async-start | bytes 16384 | tf_op jit(solution)/shard_map/all_to_all | solution.py:141
  173.0 2.1 copy.423
  175.1 4.3 %all-to-all-done.3 = f32[2,8,128]{2,0,1:T(2,128)S(1)} async-done(((f32[2,8,128]{2,0,1:T(2,128)}), f32[2,8,128]{2,0,1:T(2,128)S(1)}, u32[]{:S(2)}, u32[]{:S(2)}) %all-to-all-start.3) | async-done | bytes 8224 | tf_op jit(solution)/shard_map/all_to_all | solution.py:141
  179.4 3.6 %all-to-all-start.2 = ((bf16[2,1024,256]{2,0,1:T(2,128)(2,1)}), bf16[2,1024,256]{2,0,1:T(2,128)(2,1)S(1)}, u32[]{:S(2)}, u32[]{:S(2)}) async-start(bf16[2,1024,256]{2,0,1:T(2,128)(2,1)} %copy.423), calls=%async_computation.2 | async-start | bytes 2097152 | tf_op jit(solution)/shard_map/all_to_all | solution.py:140
  184.7 36.1 %all-to-all-done.2 = bf16[2,1024,256]{2,0,1:T(2,128)(2,1)S(1)} async-done(((bf16[2,1024,256]{2,0,1:T(2,128)(2,1)}), bf16[2,1024,256]{2,0,1:T(2,128)(2,1)S(1)}, u32[]{:S(2)}, u32[]{:S(2)}) %all-to-all-start.2) | async-done | bytes 1048608 | tf_op jit(solution)/shard_map/all_to_all | solution.py:140
  224.5 28.5 %reduce-scatter.5.cloned.1.call-done = f32[128,512]{1,0:T(8,128)} async-done(((f32[1024,512]{1,0:T(8,128)}), f32[128,512]{1,0:T(8,128)}) %reduce-scatter.5.cloned.1.call-update) | async-done | bytes 262160 | tf_op jit(solution)/shard_map/reduce_scatter | solution.py:323
  (266 shorter events, 59.5 us)
Async XLA Ops:
  7.2 16.4 %all-to-all-start.1 = ((f32[8,2,128]{2,1,0:T(2,128)}), f32[8,2,128]{2,1,0:T(2,128)S(1)}, u32[]{:S(2)}, u32[]{:S(2)}) async-start(f32[8,2,128]{2,1,0:T(2,128)} %bitcast.327), calls=%async_computation.1 | async-start | bytes 16384 | tf_op jit(solution)/shard_map/all_to_all | solution.py:121
  14.5 64.9 %all-gather.2.cloned.1.call-start = ((), (), s32[]{:S(2)}) async-start(), calls=%async_computation.6 | async-start | bytes 1769472 | tf_op jit(solution)/shard_map/all_gather | solution.py:204
  18.9 86.8 %copy-start.33 = (pred[8]{0:T(512)(128)(4,1)}, pred[8]{0:T(512)(128)(4,1)S(1)}, u32[]{:S(2)}) copy-start(pred[8]{0:T(512)(128)(4,1)S(1)} %iota_compare_fusion.7) | copy-start | bytes 28
  19.0 86.8 %copy-start.35 = (pred[8]{0:T(512)(128)(4,1)}, pred[8]{0:T(512)(128)(4,1)S(1)}, u32[]{:S(2)}) copy-start(pred[8]{0:T(512)(128)(4,1)S(1)} %get-tuple-element.1101) | copy-start | bytes 28
  19.0 14.4 %copy-start.51 = (pred[8]{0:T(512)(128)(4,1)}, pred[8]{0:T(512)(128)(4,1)S(1)}, u32[]{:S(2)}) copy-start(pred[8]{0:T(512)(128)(4,1)S(1)} %get-tuple-element.1098) | copy-start | bytes 28
  19.0 86.8 %copy-start.31 = (pred[8]{0:T(512)(128)(4,1)}, pred[8]{0:T(512)(128)(4,1)S(1)}, u32[]{:S(2)}) copy-start(pred[8]{0:T(512)(128)(4,1)S(1)} %get-tuple-element.1099) | copy-start | bytes 28
  19.0 14.4 %copy-start.52 = (pred[8]{0:T(512)(128)(4,1)}, pred[8]{0:T(512)(128)(4,1)S(1)}, u32[]{:S(2)}) copy-start(pred[8]{0:T(512)(128)(4,1)S(1)} %get-tuple-element.1097) | copy-start | bytes 28
  19.0 86.7 %copy-start.37 = (f32[8]{0:T(128)}, f32[8]{0:T(128)S(1)}, u32[]{:S(2)}) copy-start(f32[8]{0:T(128)S(1)} %get-tuple-element.1096) | copy-start | bytes 100
  19.1 86.7 %copy-start.39 = (f32[8]{0:T(128)}, f32[8]{0:T(128)S(1)}, u32[]{:S(2)}) copy-start(f32[8]{0:T(128)S(1)} %get-tuple-element.1095) | copy-start | bytes 100
  19.1 86.7 %copy-start.41 = (f32[8]{0:T(128)}, f32[8]{0:T(128)S(1)}, u32[]{:S(2)}) copy-start(f32[8]{0:T(128)S(1)} %get-tuple-element.1093) | copy-start | bytes 100
  19.1 14.4 %copy-start.53 = (f32[8]{0:T(128)}, f32[8]{0:T(128)S(1)}, u32[]{:S(2)}) copy-start(f32[8]{0:T(128)S(1)} %get-tuple-element.1091) | copy-start | bytes 100
  21.5 8.2 %copy-start.25 = (bf16[128,1024]{1,0:T(8,128)(2,1)S(1)}, bf16[128,1024]{1,0:T(8,128)(2,1)}, u32[]{:S(2)}) copy-start(bf16[128,1024]{1,0:T(8,128)(2,1)} %param.33) | copy-start | bytes 786436
  21.5 8.4 %copy-start.26 = (bf16[128,1024]{1,0:T(8,128)(2,1)S(1)}, bf16[128,1024]{1,0:T(8,128)(2,1)}, u32[]{:S(2)}) copy-start(bf16[128,1024]{1,0:T(8,128)(2,1)} %param.29) | copy-start | bytes 786436
  23.6 6.8 %copy-start.54 = (f32[16]{0:T(128)S(1)}, f32[16]{0:T(128)}, u32[]{:S(2)}) copy-start(f32[16]{0:T(128)} %param.27) | copy-start | bytes 196
  23.6 37.5 %all-to-all-start = ((bf16[2,128,2048]{1,0,2:T(2,128)(2,1)}), bf16[2,128,2048]{1,0,2:T(2,128)(2,1)S(1)}, u32[]{:S(2)}, u32[]{:S(2)}) async-start(bf16[2,128,2048]{1,0,2:T(2,128)(2,1)} %copy.401), calls=%async_computation | async-start | bytes 2097152 | tf_op jit(solution)/shard_map/all_to_all | solution.py:118
  29.6 191.4 %reduce-scatter.3.cloned.1.call-start = ((), (), s32[]{:S(2)}) async-start(), calls=%async_computation.7 | async-start | bytes 1179648 | tf_op jit(solution)/shard_map/reduce_scatter | solution.py:329
  33.4 28.7 %copy-start.45 = (f32[2]{0:T(128)}, f32[2]{0:T(128)S(1)}, u32[]{:S(2)}) copy-start(f32[2]{0:T(128)S(1)} %get-tuple-element.971) | copy-start | bytes 28
  62.2 44.4 %copy-start.3 = (bf16[1,8,128,256]{2,3,1,0:T(8,128)(2,1)}, bf16[1,8,128,256]{2,3,1,0:T(8,128)(2,1)S(1)}, u32[]{:S(2)}) copy-start(bf16[1,8,128,256]{2,3,1,0:T(8,128)(2,1)S(1)} %get-tuple-element.1069) | copy-start | bytes 1572868
  105.5 147.4 %reduce-scatter.5.cloned.1.call-start = ((), (), s32[]{:S(2)}) async-start(), calls=%async_computation.8 | async-start | bytes 2359296 | tf_op jit(solution)/shard_map/reduce_scatter | solution.py:323
  139.6 5.6 %copy-start.34 = (pred[8]{0:T(512)(128)(4,1)S(1)}, pred[8]{0:T(512)(128)(4,1)}, u32[]{:S(2)}) copy-start(pred[8]{0:T(512)(128)(4,1)} %copy-done.33) | copy-start | bytes 28
  139.6 5.5 %copy-start.36 = (pred[8]{0:T(512)(128)(4,1)S(1)}, pred[8]{0:T(512)(128)(4,1)}, u32[]{:S(2)}) copy-start(pred[8]{0:T(512)(128)(4,1)} %copy-done.35) | copy-start | bytes 28
  139.6 5.5 %copy-start.38 = (f32[8]{0:T(128)S(1)}, f32[8]{0:T(128)}, u32[]{:S(2)}) copy-start(f32[8]{0:T(128)} %copy-done.37) | copy-start | bytes 100
  139.6 5.5 %copy-start.40 = (f32[8]{0:T(128)S(1)}, f32[8]{0:T(128)}, u32[]{:S(2)}) copy-start(f32[8]{0:T(128)} %copy-done.39) | copy-start | bytes 100
  139.6 5.5 %copy-start.42 = (f32[8]{0:T(128)S(1)}, f32[8]{0:T(128)}, u32[]{:S(2)}) copy-start(f32[8]{0:T(128)} %copy-done.41) | copy-start | bytes 100
  139.6 7.6 %copy-start.44 = (f32[8]{0:T(128)S(1)}, f32[8]{0:T(128)}, u32[]{:S(2)}) copy-start(f32[8]{0:T(128)} %copy-done.43) | copy-start | bytes 100
  139.6 7.8 %copy-start.4 = (bf16[1,8,128,256]{2,3,1,0:T(8,128)(2,1)S(1)}, bf16[1,8,128,256]{2,3,1,0:T(8,128)(2,1)}, u32[]{:S(2)}) copy-start(bf16[1,8,128,256]{2,3,1,0:T(8,128)(2,1)} %copy-done.3) | copy-start | bytes 1572868
  139.6 7.8 %copy-start.9 = (bf16[1024,128]{1,0:T(8,128)(2,1)S(1)}, bf16[1024,128]{1,0:T(8,128)(2,1)}, u32[]{:S(2)}) copy-start(bf16[1024,128]{1,0:T(8,128)(2,1)} %copy-done.7) | copy-start | bytes 786436
  148.2 24.7 %copy-start.20 = (bf16[1,1024,256]{1,2,0:T(8,128)(2,1)S(1)}, bf16[1,1024,256]{1,2,0:T(8,128)(2,1)}, u32[]{:S(2)}) copy-start(bf16[1,1024,256]{1,2,0:T(8,128)(2,1)} %convert_element_type.197) | copy-start | bytes 1572868
  157.2 22.2 %all-to-all-start.3 = ((f32[2,8,128]{2,0,1:T(2,128)}), f32[2,8,128]{2,0,1:T(2,128)S(1)}, u32[]{:S(2)}, u32[]{:S(2)}) async-start(f32[2,8,128]{2,0,1:T(2,128)} %copy.451), calls=%async_computation.4 | async-start | bytes 16384 | tf_op jit(solution)/shard_map/all_to_all | solution.py:141
  173.0 10.0 %copy-start.22 = (bf16[128,2,4,128]{0,3,2,1:T(8,128)(2,1)S(1)}, bf16[128,2,4,128]{0,3,2,1:T(8,128)(2,1)}, u32[]{:S(2)}) copy-start(bf16[128,2,4,128]{0,3,2,1:T(8,128)(2,1)} %get-tuple-element.1044) | copy-start | bytes 786436
  179.4 41.4 %all-to-all-start.2 = ((bf16[2,1024,256]{2,0,1:T(2,128)(2,1)}), bf16[2,1024,256]{2,0,1:T(2,128)(2,1)S(1)}, u32[]{:S(2)}, u32[]{:S(2)}) async-start(bf16[2,1024,256]{2,0,1:T(2,128)(2,1)} %copy.423), calls=%async_computation.2 | async-start | bytes 2097152 | tf_op jit(solution)/shard_map/all_to_all | solution.py:140
  221.0 2.8 %collective-permute-start = (f32[128,256]{1,0:T(8,128)}, f32[128,256]{1,0:T(8,128)S(1)}, u32[]{:S(2)}, u32[]{:S(2)}) collective-permute-start(f32[128,256]{1,0:T(8,128)} %reduce-scatter.3.cloned.1.call-done), channel_id=1, source_target_pairs={{0,1},{1,0},{2,3},{3,2},{4,5},{5,4},{6,7},{7,6},{8,9},{9,8},{10,11... | collective-permute-start | bytes 393224 | tf_op jit(solution)/shard_map/ppermute | solution.py:331
  (32 other events, 86.8 us)
Sparse Core Ops, SparseCore 0:
  19.1 60.3 all-gather.1
  105.6 62.3 reduce-scatter.2
  171.6 81.2 reduce-scatter.4

commit v4 on v3

--- a/solution.py
+++ b/solution.py
@@ -138,8 +138,10 @@
         ]
     )
     back = lax.all_to_all(back, "seq", split_axis=1, concat_axis=2, tiled=True)
-    grad_decay = lax.all_to_all(grad_decay, "seq", split_axis=1, concat_axis=0, tiled=True)
-    return back[0], back[1], jnp.concatenate([grad_b, grad_c], axis=1), grad_decay
+    decay_cols = lax.dynamic_update_slice_in_dim(
+        jnp.zeros((total, heads_here), jnp.float32), grad_decay.T, place * own, 1
+    )
+    return back[0], back[1], jnp.concatenate([grad_b, grad_c, decay_cols], axis=1)
 
 
 def mamba_by_stretch(
@@ -206,7 +208,7 @@
     if by_heads:
         b_all = gathered[:, 2 * key_width : 2 * key_width + state_width]
         c_all = gathered[:, 2 * key_width + state_width :]
-        mixer_out, x_grad, bc_part, grad_decay = mamba_by_heads(
+        mixer_out, x_grad, bc_part = mamba_by_heads(
             x_input, b_all, c_all, decay_log, skip_gain, doc_lengths, mixer_cot
         )
     else:
@@ -327,6 +329,8 @@
     value_gradient_total = kv_total[:, groups * HEAD_SIZE :]
     if by_heads:
         bc_sum = lax.psum_scatter(bc_part, "seq", scatter_dimension=0, tiled=True)
+        grad_decay = bc_sum[:, 2 * state_width :].T
+        bc_sum = bc_sum[:, : 2 * state_width]
         if lax.axis_size("head") == 2:
             bc_sum = bc_sum + lax.ppermute(bc_sum, "head", [(0, 1), (1, 0)])
         else:

time: 264 us -> 260 us (0.985)
  starting transfers between devices: 33.1 us -> 25.7 us
  local copies, waits for them, and re-layouts: 44 us -> 47.5 us
    reduce_scatter x1, waiting for transfers between devices: 28.5 us -> 51.7 us  [on_device(): lax.psum_scatter(jnp.concatenate([term_key, term_value], axis=1), 'seq',...]
    all_gather x1, waiting for transfers between devices: 17.2 us -> 0.01 us  [on_device(): lax.all_gather(jnp.concatenate(pieces, axis=1), 'seq', axis=0, tiled=True)]
    all_to_all x1 -> x0, starting transfers between devices: 15.7 us -> none  [mamba_by_heads(): lax.all_to_all(grad_decay, 'seq', split_axis=1, concat_axis=0, tiled=True)]
    all_to_all x1, waiting for transfers between devices: 36.1 us -> 26 us  [mamba_by_heads(): back = lax.all_to_all(back, 'seq', split_axis=1, concat_axis=2, tiled=True)]
    all_to_all x1, starting transfers between devices: 3.56 us -> 13.6 us  [mamba_by_heads(): back = lax.all_to_all(back, 'seq', split_axis=1, concat_axis=2, tiled=True)]
    all_to_all x1, waiting for transfers between devices: 27.5 us -> 36.9 us  [mamba_by_heads(): lax.all_to_all(jnp.stack([x_input, mixer_cot]), 'seq', split_axis=2, conc...]
    all_to_all x1 -> x0, waiting for transfers between devices: 4.34 us -> none  [mamba_by_heads(): lax.all_to_all(grad_decay, 'seq', split_axis=1, concat_axis=0, tiled=True)]
    reshape x0 -> x2, local copies, waits for them, and re-layouts: none -> 3.13 us  [the longest x1 2.11 us: mixer_whole(): c_blocks = c_float.reshape(count, width, -1)]
  transfers between devices with their start and end apart: 8 -> 7, of which waited for: 5 -> 4; matrix products, arithmetic and copies ran while one was open for 26% -> 20% of each run, Pallas kernels for 0% -> 0%
where the time goes in v4:
time: 260 us; the launch traced here: 258 us
  waiting for transfers between devices  116 us (45%)
  local copies, waits for them, and re-layouts  47.5 us (18%)
  matrix products  29.7 us (11%)
  starting transfers between devices  25.7 us (10%)
  other arithmetic  24.4 us (9%)
  between operations  14.5 us (6%)
    reduce_scatter x1, waiting for transfers between devices, on_device(): lax.psum_scatter(jnp.concatenate([term_key, term_value], axis=1), 'seq',...  51.7 us
    all_to_all x1, waiting for transfers between devices, mamba_by_heads(): lax.all_to_all(jnp.stack([x_input, mixer_cot]), 'seq', split_axis=2, conc...  36.9 us
    all_to_all x1, waiting for transfers between devices, mamba_by_heads(): back = lax.all_to_all(back, 'seq', split_axis=1, concat_axis=2, tiled=True)  26 us
    all_to_all x1, starting transfers between devices, mamba_by_heads(): back = lax.all_to_all(back, 'seq', split_axis=1, concat_axis=2, tiled=True)  13.6 us
    unnamed x76, local copies, waits for them, and re-layouts  11.4 us
    all_to_all x1, starting transfers between devices, mamba_by_heads(): lax.all_to_all(decay_log, 'seq', split_axis=0, concat_axis=1, tiled=True)  7.32 us
    dot_general x3, matrix products, mixer_whole(): state_in = jnp.einsum('kjh,jhnp->khnp', reach, summary, precision=precise)  6.37 us
    dot_general x3, matrix products, mixer_stretch(): inner = jnp.einsum('hts,shp->thp', kernel, inputs, precision=precise)  5.77 us
  transfers between devices with their start and end apart: 7, of which 4 were waited for; matrix products, arithmetic and copies ran while one was open for 20% of the time, Pallas kernels for 0%

profile of v4, /device:TPU:0, one launch (start us, length us, event | category | flops | bytes accessed | tf_op | source)
XLA Modules:
  0.0 258.3 jit_solution(11701591860280696445)
XLA Ops:
  11.6 7.3 %all-to-all-start.1 = ((f32[8,2,128]{2,1,0:T(2,128)}), f32[8,2,128]{2,1,0:T(2,128)S(1)}, u32[]{:S(2)}, u32[]{:S(2)}) async-start(f32[8,2,128]{2,1,0:T(2,128)} %bitcast.334), calls=%async_computation.1 | async-start | bytes 16384 | tf_op jit(solution)/shard_map/all_to_all | solution.py:121
  22.1 2.0 copy.420
  25.5 4.6 %all-to-all-start = ((bf16[2,128,2048]{1,0,2:T(2,128)(2,1)}), bf16[2,128,2048]{1,0,2:T(2,128)(2,1)S(1)}, u32[]{:S(2)}, u32[]{:S(2)}) async-start(bf16[2,128,2048]{1,0,2:T(2,128)(2,1)} %copy.420), calls=%async_computation | async-start | bytes 2097152 | tf_op jit(solution)/shard_map/all_to_all | solution.py:118
  32.6 36.9 %all-to-all-done = bf16[2,128,2048]{1,0,2:T(2,128)(2,1)S(1)} async-done(((bf16[2,128,2048]{1,0,2:T(2,128)(2,1)}), bf16[2,128,2048]{1,0,2:T(2,128)(2,1)S(1)}, u32[]{:S(2)}, u32[]{:S(2)}) %all-to-all-start) | async-done | bytes 1048608 | tf_op jit(solution)/shard_map/all_to_all | solution.py:118
  74.0 1.6 convolution_bitcast_fusion.2
  75.6 1.6 copy.438
  81.2 2.6 %convolution_bitcast_fusion.3 = f32[8,2,128,128]{3,0,2,1:T(8,128)} fusion(f32[8,2,128,128]{3,2,1,0:T(8,128)S(1)} %fusion.32, f32[8,8,2]{1,0,2:T(8,128)S(1)} %stack.13), kind=kOutput, calls=%fused_computation.65 | convolution fusion | flops 25165824 | bytes 2097664 | tf_op jit(solution)/shard_map/jvp(kjh,jhnp->khnp)/dot_general | solution.py:102
  83.8 2.8 %convolution_bitcast_fusion.6 = f32[8,8,2]{1,0,2:T(8,128)S(1)} fusion(f32[2,128,128,8]{2,3,1,0:T(8,128)S(1)} %copy.438, f32[8,2,128,128]{3,2,1,0:T(8,128)S(1)} %fusion.32), kind=kOutput, calls=%fused_computation.78 | convolution fusion | flops 25165824 | bytes 2097664 | tf_op jit(solution)/shard_map/transpose(jvp(kjh,jhnp->khnp))/dot_general | solution.py:102
  90.9 1.6 copy.436
  92.5 2.1 fusion.48
  95.7 2.1 copy.471
  101.6 1.7 fusion.49
  104.2 2.5 reduce_window_sum.46
  106.7 2.5 reduce_window_sum.47
  109.2 2.2 pad_maximum_fusion.1
  113.5 1.7 while.51
  113.5 1.6 conditional.9
  116.1 3.3 %while.52 = (s32[]{:T(128)}, f32[128,2,4,128]{0,3,2,1:T(8,128)}, s32[]{:T(128)}, bf16[1024,256]{0,1:T(8,128)(2,1)S(1)}, s32[4]{0:T(128)S(1)}, /*index=5*/s32[128...) while((s32[]{:T(128)}, f32[128,2,4,128]{0,3,2,1:T(8,128)}, ...), condition=%wide.region_17.18_spmd.clone, body=%wide.region_12.17_spmd.clone.sunk | while | flops 271390848 | bytes 3031893 | solution.py:281
  116.1 3.3 %conditional.10 = (f32[128,2,4,128]{0,3,2,1:T(8,128)}) conditional(s32[]{:T(128)} %convert_element_type.251, f32[128,2,4,128]{0,3,2,1:T(8,128)} %get-tuple-element.1387, (s32[]{:T(128)}, bf16[1024,256]{0,1:T(8,128)(2,1)S(1)}, s32[]{:T(128)}, s32[4]{0:T(128)S(1)}, s32[128]{0:T(128)S(1)}, /*index=5*/bf16[1024,256]{0,1:T(8,128)(2,1)S(1)}, ...), branch_computations={%region_13.13_spmd, %region_14.16_spmd} | conditional | flops 271390848 | bytes 3031158 | solution.py:247
  116.6 2.7 %fusion.13 = f32[128,2,4,128]{0,3,2,1:T(8,128)} fusion(f32[128,2,4,128]{0,3,2,1:T(8,128)} %get-tuple-element.621, bf16[512,2,128,1]{0,2,3,1:T(8,128)(2,1)S(1)} %bitcast.303, bf16[512,2,128,1]{0,2,3,1:T(8,128)(2,1)S(1)} %bitcast.302, bf16[128,2,4,128]{3,0,2,1:T(8,128)(2,1)S(1)} %get-tuple-element.628, f32[2,4,128]{2,1,0:T(4,128)S(1)} %get-tuple-element.629, ...), kind=kOutput, calls=%fused_computation.19 | convolution fusion | flops 271187968 | bytes 1904640 | tf_op jit(solution)/shard_map/while/body/eval_jaxpr/cond/branch_1_fun/grtk,kgd->tgrd/dot_general | solution.py:277
  119.4 1.8 fusion.62
  123.5 4.9 %while.53 = (s32[]{:T(128)}, f32[128,2,4,128]{0,3,2,1:T(8,128)S(1)}, f32[1024,256]{0,1:T(8,128)}, f32[1024,256]{0,1:T(8,128)}, s32[]{:T(128)}, /*index=5*/bf16[1...) while((s32[]{:T(128)}, ...), condition=%wide.region_37.38_spmd.clone, body=%wide.region_32.37_spmd.clone.sunk | while | flops 675616896 | bytes 33444924 | solution.py:319
  123.5 4.8 %conditional.11 = ((f32[128,2,4,128]{0,3,2,1:T(8,128)S(1)}, f32[1024,256]{0,1:T(8,128)}, f32[1024,256]{0,1:T(8,128)})) conditional(s32[]{:T(128)} %convert_element_type.252, (f32[128,2,4,128]{0,3,2,1:T(8,128)S(1)}, f32[1024,256]{0,1:T(8,128)}, f32[1024,256]{0,1:T(8,128)}) %tuple.201, (s32[]{:T(128)}, bf16[1024,256]{0,1:T(8,128)(2,1)S(1)}, ...), branch_computations={%region_33.33_spmd, %region_34.36_spmd} | conditional | flops 675616896 | bytes 33444102 | solution.py:247
  128.4 2.6 %copy.474 = f32[1024,256]{1,0:T(8,128)} copy(f32[1024,256]{0,1:T(8,128)} %get-tuple-element.691) | data formatting | bytes 2097152 | tf_op jit(solution)/shard_map/while | solution.py:319
  132.3 3.2 %pad_maximum_fusion = f32[1024,512]{1,0:T(8,128)} fusion(f32[1024,256]{1,0:T(8,128)} %copy.475, f32[1024,256]{1,0:T(8,128)} %copy.474), kind=kLoop, calls=%fused_computation.53 | loop fusion | flops 524288 | bytes 4194304 | tf_op jit(solution)/shard_map/concatenate | solution.py:326
  136.7 2.8 %fusion.43 = bf16[8,128,2,128]{1,3,2,0:T(8,128)(2,1)S(1)} fusion(bf16[8,128,2,128]{1,3,2,0:T(8,128)(2,1)S(1)} %bitcast.307, f32[8,128,2,128]{1,3,2,0:T(8,128)} %bitcast.318, f32[2]{0:T(128)S(1)} %dynamic_slice.18, f32[8,128,2]{1,2,0:T(2,128)S(1)} %copy.431, f32[8,128,128]{2,1,0:T(8,128)S(1)} %copy-done.23, f32[8,2,128]{2,1,0:T(2,128)S(1)} %copy.423, ...), kind=kOutput, calls=%fused_computation.71 | convolution fusion | flops 405012480 | bytes 2768904 | tf_op jit(solution)/shard_map/jvp(vmap(hts,shp->thp))/dot_general | solution.py:67
  140.9 2.1 fusion.40
  143.0 2.3 fusion.44
  146.0 2.0 copy.442
  148.0 13.6 %all-to-all-start.2 = ((bf16[2,1024,256]{2,0,1:T(2,128)(2,1)}), bf16[2,1024,256]{2,0,1:T(2,128)(2,1)S(1)}, u32[]{:S(2)}, u32[]{:S(2)}) async-start(bf16[2,1024,256]{2,0,1:T(2,128)(2,1)} %copy.442), calls=%async_computation.2 | async-start | bytes 2097152 | tf_op jit(solution)/shard_map/all_to_all | solution.py:140
  163.4 26.0 %all-to-all-done.2 = bf16[2,1024,256]{2,0,1:T(2,128)(2,1)S(1)} async-done(((bf16[2,1024,256]{2,0,1:T(2,128)(2,1)}), bf16[2,1024,256]{2,0,1:T(2,128)(2,1)S(1)}, u32[]{:S(2)}, u32[]{:S(2)}) %all-to-all-start.2) | async-done | bytes 1048608 | tf_op jit(solution)/shard_map/all_to_all | solution.py:140
  197.0 51.7 %reduce-scatter.5.cloned.1.call-done = f32[128,512]{1,0:T(8,128)} async-done(((f32[1024,512]{1,0:T(8,128)}), f32[128,512]{1,0:T(8,128)}) %reduce-scatter.5.cloned.1.call-update) | async-done | bytes 262160 | tf_op jit(solution)/shard_map/reduce_scatter | solution.py:325
  (230 shorter events, 58.6 us)
Async XLA Ops:
  7.2 63.4 %all-gather.2.cloned.1.call-start = ((), (), s32[]{:S(2)}) async-start(), calls=%async_computation.5 | async-start | bytes 1769472 | tf_op jit(solution)/shard_map/all_gather | solution.py:206
  11.6 13.8 %all-to-all-start.1 = ((f32[8,2,128]{2,1,0:T(2,128)}), f32[8,2,128]{2,1,0:T(2,128)S(1)}, u32[]{:S(2)}, u32[]{:S(2)}) async-start(f32[8,2,128]{2,1,0:T(2,128)} %bitcast.334), calls=%async_computation.1 | async-start | bytes 16384 | tf_op jit(solution)/shard_map/all_to_all | solution.py:121
  18.9 12.8 %copy-start.29 = (pred[8]{0:T(512)(128)(4,1)}, pred[8]{0:T(512)(128)(4,1)S(1)}, u32[]{:S(2)}) copy-start(pred[8]{0:T(512)(128)(4,1)S(1)} %get-tuple-element.1115) | copy-start | bytes 28
  19.0 12.8 %copy-start.30 = (pred[8]{0:T(512)(128)(4,1)}, pred[8]{0:T(512)(128)(4,1)S(1)}, u32[]{:S(2)}) copy-start(pred[8]{0:T(512)(128)(4,1)S(1)} %get-tuple-element.1116) | copy-start | bytes 28
  19.0 12.8 %copy-start.31 = (f32[8]{0:T(128)}, f32[8]{0:T(128)S(1)}, u32[]{:S(2)}) copy-start(f32[8]{0:T(128)S(1)} %get-tuple-element.1109) | copy-start | bytes 100
  25.5 44.1 %all-to-all-start = ((bf16[2,128,2048]{1,0,2:T(2,128)(2,1)}), bf16[2,128,2048]{1,0,2:T(2,128)(2,1)S(1)}, u32[]{:S(2)}, u32[]{:S(2)}) async-start(bf16[2,128,2048]{1,0,2:T(2,128)(2,1)} %copy.420), calls=%async_computation | async-start | bytes 2097152 | tf_op jit(solution)/shard_map/all_to_all | solution.py:118
  30.1 162.2 %reduce-scatter.3.cloned.1.call-start = ((), (), s32[]{:S(2)}) async-start(), calls=%async_computation.6 | async-start | bytes 1253376 | tf_op jit(solution)/shard_map/reduce_scatter | solution.py:331
  30.7 57.3 %copy-start.26 = (pred[8,128,128]{2,1,0:T(8,128)(4,1)}, pred[8,128,128]{2,1,0:T(8,128)(4,1)S(1)}, u32[]{:S(2)}) copy-start(pred[8,128,128]{2,1,0:T(8,128)(4,1)S(1)} %compare_and_fusion.3) | copy-start | bytes 393220
  70.6 2.6 %copy-start = (bf16[1,8,128,256]{2,3,1,0:T(8,128)(2,1)}, bf16[1,8,128,256]{2,3,1,0:T(8,128)(2,1)S(1)}, u32[]{:S(2)}) copy-start(bf16[1,8,128,256]{2,3,1,0:T(8,128)(2,1)S(1)} %get-tuple-element.1087) | copy-start | bytes 1572868
  73.0 6.9 %copy-start.5 = (f32[8,128,128]{2,1,0:T(8,128)}, f32[8,128,128]{2,1,0:T(8,128)S(1)}, u32[]{:S(2)}) copy-start(f32[8,128,128]{2,1,0:T(8,128)S(1)} %convert.7) | copy-start | bytes 1572868
  86.6 1.5 copy-start.1
  86.6 1.5 copy-start.8
  88.0 1.8 copy-start.22
  88.0 1.2 copy-start.18
  92.4 2.1 copy-start.16
  92.5 5.4 %copy-start.28 = (f32[8,2]{0,1:T(2,128)S(1)}, f32[8,2]{0,1:T(2,128)}, u32[]{:S(2)}) copy-start(f32[8,2]{0,1:T(2,128)} %get-tuple-element.1064) | copy-start | bytes 196
  95.7 13.5 %copy-start.17 = (f32[1024,128]{0,1:T(8,128)S(1)}, f32[1024,128]{0,1:T(8,128)}, u32[]{:S(2)}) copy-start(f32[1024,128]{0,1:T(8,128)} %copy.470) | copy-start | bytes 1572868
  103.3 8.2 %copy-start.24 = (bf16[128,1024]{1,0:T(8,128)(2,1)S(1)}, bf16[128,1024]{1,0:T(8,128)(2,1)}, u32[]{:S(2)}) copy-start(bf16[128,1024]{1,0:T(8,128)(2,1)} %param.29) | copy-start | bytes 786436
  109.2 2.7 %copy-start.25 = (bf16[128,1024]{1,0:T(8,128)(2,1)S(1)}, bf16[128,1024]{1,0:T(8,128)(2,1)}, u32[]{:S(2)}) copy-start(bf16[128,1024]{1,0:T(8,128)(2,1)} %param.33) | copy-start | bytes 786436
  109.2 2.9 %copy-start.33 = (s32[4,1]{0,1:T(1,128)S(1)}, s32[4,1]{0,1:T(1,128)}, u32[]{:S(2)}) copy-start(s32[4,1]{0,1:T(1,128)} %copy-done.32) | copy-start | bytes 52
  111.4 2.0 copy-start.34
  111.5 137.2 %reduce-scatter.5.cloned.1.call-start = ((), (), s32[]{:S(2)}) async-start(), calls=%async_computation.7 | async-start | bytes 2359296 | tf_op jit(solution)/shard_map/reduce_scatter | solution.py:325
  125.3 1.5 copy-start.12
  127.0 1.4 copy-start.13
  128.4 2.6 %copy-start.14 = (f32[1024,256]{0,1:T(8,128)S(1)}, f32[1024,256]{0,1:T(8,128)}, u32[]{:S(2)}) copy-start(f32[1024,256]{0,1:T(8,128)} %get-tuple-element.692) | copy-start | bytes 3145732
  135.5 1.2 copy-start.27
  136.7 4.1 %copy-start.2 = (bf16[1,8,128,256]{2,3,1,0:T(8,128)(2,1)S(1)}, bf16[1,8,128,256]{2,3,1,0:T(8,128)(2,1)}, u32[]{:S(2)}) copy-start(bf16[1,8,128,256]{2,3,1,0:T(8,128)(2,1)} %copy-done) | copy-start | bytes 1572868
  139.8 3.1 %copy-start.6 = (f32[8,128,128]{2,1,0:T(8,128)S(1)}, f32[8,128,128]{2,1,0:T(8,128)}, u32[]{:S(2)}) copy-start(f32[8,128,128]{2,1,0:T(8,128)} %copy-done.5) | copy-start | bytes 1572868
  143.0 2.9 %copy-start.19 = (bf16[1,1024,256]{1,2,0:T(8,128)(2,1)S(1)}, bf16[1,1024,256]{1,2,0:T(8,128)(2,1)}, u32[]{:S(2)}) copy-start(bf16[1,1024,256]{1,2,0:T(8,128)(2,1)} %convert_element_type.194) | copy-start | bytes 1572868
  148.0 14.5 %copy-start.21 = (bf16[128,2,4,128]{0,3,2,1:T(8,128)(2,1)S(1)}, bf16[128,2,4,128]{0,3,2,1:T(8,128)(2,1)}, u32[]{:S(2)}) copy-start(bf16[128,2,4,128]{0,3,2,1:T(8,128)(2,1)} %get-tuple-element.1062) | copy-start | bytes 786436
  148.0 41.4 %all-to-all-start.2 = ((bf16[2,1024,256]{2,0,1:T(2,128)(2,1)}), bf16[2,1024,256]{2,0,1:T(2,128)(2,1)S(1)}, u32[]{:S(2)}, u32[]{:S(2)}) async-start(bf16[2,1024,256]{2,0,1:T(2,128)(2,1)} %copy.442), calls=%async_computation.2 | async-start | bytes 2097152 | tf_op jit(solution)/shard_map/all_to_all | solution.py:140
  193.2 1.4 collective-permute-start
  (11 other events, 10.7 us)
Sparse Core Ops, SparseCore 0:
  11.7 58.8 all-gather.1
  111.6 61.5 reduce-scatter.2
  176.7 71.9 reduce-scatter.4

commit v5 on v4

--- a/solution.py
+++ b/solution.py
@@ -322,9 +322,16 @@
         lambda number, carried: visit(number, carried, full_step),
         (query_zero, term_zero, term_zero),
     )
-    kv_total = lax.psum_scatter(
-        jnp.concatenate([term_key, term_value], axis=1), "seq", scatter_dimension=0, tiled=True
-    )
+    seq_count = lax.axis_size("seq")
+    kv_terms = jnp.concatenate([term_key, term_value], axis=1).astype(jnp.bfloat16)
+    kv_terms = lax.all_to_all(
+        kv_terms.reshape(seq_count, tokens, 2 * groups * HEAD_SIZE),
+        "seq",
+        split_axis=0,
+        concat_axis=0,
+        tiled=True,
+    )
+    kv_total = jnp.sum(kv_terms.astype(jnp.float32), axis=0)
     key_gradient_total = kv_total[:, : groups * HEAD_SIZE]
     value_gradient_total = kv_total[:, groups * HEAD_SIZE :]
     if by_heads:

time: 260 us -> 254 us (0.977)
  waiting for transfers between devices: 116 us -> 101 us
  starting transfers between devices: 25.7 us -> 34.3 us
  matrix products: 29.7 us -> 36.4 us
  local copies, waits for them, and re-layouts: 47.5 us -> 42.5 us
    reduce_scatter x1 -> x0, waiting for transfers between devices: 51.7 us -> none  [on_device(): lax.psum_scatter(jnp.concatenate([term_key, term_value], axis=1), 'seq',...]
    reduce_scatter x1, waiting for transfers between devices: 0.01 us -> 29.1 us  [on_device(): bc_sum = lax.psum_scatter(bc_part, 'seq', scatter_dimension=0, tiled=True)]
    all_gather x1, waiting for transfers between devices: 0.01 us -> 17.1 us  [on_device(): lax.all_gather(jnp.concatenate(pieces, axis=1), 'seq', axis=0, tiled=True)]
    all_to_all x0 -> x1, starting transfers between devices: none -> 14.8 us  [on_device(): lax.all_to_all(kv_terms.reshape(seq_count, tokens, 2 * groups * HEAD_SIZE...]
    all_to_all x1, waiting for transfers between devices: 36.9 us -> 26.3 us  [mamba_by_heads(): lax.all_to_all(jnp.stack([x_input, mixer_cot]), 'seq', split_axis=2, conc...]
    all_to_all x1, starting transfers between devices: 13.6 us -> 5.95 us  [mamba_by_heads(): back = lax.all_to_all(back, 'seq', split_axis=1, concat_axis=2, tiled=True)]
    dot_general x3, matrix products: 4.38 us -> 7.45 us  [local_state(): jnp.einsum('hs,sn,shp->hnp', weights, b_float, inputs, precision=precise)]
    unnamed x76 -> x126, local copies, waits for them, and re-layouts: 11.4 us -> 10.5 us
  transfers between devices with their start and end apart: 7 -> 7, of which waited for: 4 -> 4; matrix products, arithmetic and copies ran while one was open for 20% -> 23% of each run, Pallas kernels for 0% -> 0%
where the time goes in v5:
time: 254 us; the launch traced here: 253 us
  waiting for transfers between devices  101 us (40%)
  local copies, waits for them, and re-layouts  42.5 us (17%)
  matrix products  36.4 us (14%)
  starting transfers between devices  34.3 us (14%)
  other arithmetic  23.2 us (9%)
  between operations  15 us (6%)
    reduce_scatter x1, waiting for transfers between devices, on_device(): bc_sum = lax.psum_scatter(bc_part, 'seq', scatter_dimension=0, tiled=True)  29.1 us
    all_to_all x1, waiting for transfers between devices, mamba_by_heads(): back = lax.all_to_all(back, 'seq', split_axis=1, concat_axis=2, tiled=True)  28.6 us
    all_to_all x1, waiting for transfers between devices, mamba_by_heads(): lax.all_to_all(jnp.stack([x_input, mixer_cot]), 'seq', split_axis=2, conc...  26.3 us
    all_gather x1, waiting for transfers between devices, on_device(): lax.all_gather(jnp.concatenate(pieces, axis=1), 'seq', axis=0, tiled=True)  17.1 us
    all_to_all x1, starting transfers between devices, on_device(): lax.all_to_all(kv_terms.reshape(seq_count, tokens, 2 * groups * HEAD_SIZE...  14.8 us
    unnamed x126, local copies, waits for them, and re-layouts  10.5 us
    dot_general x3, matrix products, mixer_stretch(): inner = jnp.einsum('hts,shp->thp', kernel, inputs, precision=precise)  7.59 us
    dot_general x3, matrix products, local_state(): jnp.einsum('hs,sn,shp->hnp', weights, b_float, inputs, precision=precise)  7.45 us
  transfers between devices with their start and end apart: 7, of which 4 were waited for; matrix products, arithmetic and copies ran while one was open for 23% of the time, Pallas kernels for 0%

profile of v5, /device:TPU:0, one launch (start us, length us, event | category | flops | bytes accessed | tf_op | source)
XLA Modules:
  0.0 252.9 jit_solution(6440184320089199667)
XLA Ops:
  7.2 7.3 %all-to-all-start.1 = ((f32[8,2,128]{2,1,0:T(2,128)}), f32[8,2,128]{2,1,0:T(2,128)S(1)}, u32[]{:S(2)}, u32[]{:S(2)}) async-start(f32[8,2,128]{2,1,0:T(2,128)} %bitcast.338), calls=%async_computation.1 | async-start | bytes 16384 | tf_op jit(solution)/shard_map/all_to_all | solution.py:121
  21.9 2.0 copy.417
  23.9 6.1 %all-to-all-start = ((bf16[2,128,2048]{1,0,2:T(2,128)(2,1)}), bf16[2,128,2048]{1,0,2:T(2,128)(2,1)S(1)}, u32[]{:S(2)}, u32[]{:S(2)}) async-start(bf16[2,128,2048]{1,0,2:T(2,128)(2,1)} %copy.417), calls=%async_computation | async-start | bytes 2097152 | tf_op jit(solution)/shard_map/all_to_all | solution.py:118
  34.8 26.3 %all-to-all-done = bf16[2,128,2048]{1,0,2:T(2,128)(2,1)S(1)} async-done(((bf16[2,128,2048]{1,0,2:T(2,128)(2,1)}), bf16[2,128,2048]{1,0,2:T(2,128)(2,1)S(1)}, u32[]{:S(2)}, u32[]{:S(2)}) %all-to-all-start) | async-done | bytes 1048608 | tf_op jit(solution)/shard_map/all_to_all | solution.py:118
  62.2 17.1 %all-gather.2.cloned.1.call-done = bf16[1024,768]{0,1:T(8,128)(2,1)} async-done(((bf16[128,768]{0,1:T(8,128)(2,1)}), bf16[1024,768]{0,1:T(8,128)(2,1)}) %all-gather.2.cloned.1.call-update) | async-done | bytes 1572880 | tf_op jit(solution)/shard_map/all_gather | solution.py:206
  86.2 1.7 fusion.51
  90.0 2.8 %convolution_bitcast_fusion.6 = f32[8,8,2]{1,0,2:T(8,128)S(1)} fusion(f32[2,128,128,8]{2,3,1,0:T(8,128)S(1)} %copy.435, f32[8,2,128,128]{3,2,1,0:T(8,128)S(1)} %fusion.32), kind=kOutput, calls=%fused_computation.78 | convolution fusion | flops 25165824 | bytes 2097664 | tf_op jit(solution)/shard_map/transpose(jvp(kjh,jhnp->khnp))/dot_general | solution.py:102
  92.8 2.6 %convolution_bitcast_fusion.3 = f32[8,2,128,128]{3,0,2,1:T(8,128)} fusion(f32[8,2,128,128]{3,2,1,0:T(8,128)S(1)} %fusion.32, f32[8,8,2]{1,0,2:T(8,128)S(1)} %stack.13), kind=kOutput, calls=%fused_computation.65 | convolution fusion | flops 25165824 | bytes 2097664 | tf_op jit(solution)/shard_map/jvp(kjh,jhnp->khnp)/dot_general | solution.py:102
  95.5 2.4 while.51
  95.5 2.3 conditional.9
  99.3 4.0 %while.52 = (s32[]{:T(128)}, f32[128,2,4,128]{0,3,2,1:T(8,128)}, s32[]{:T(128)}, bf16[1024,256]{0,1:T(8,128)(2,1)S(1)}, s32[4]{0:T(128)}, /*index=5*/s32[128]{0:...) while((s32[]{:T(128)}, f32[128,2,4,128]{0,3,2,1:T(8,128)}, ...), condition=%wide.region_17.18_spmd.clone, body=%wide.region_12.17_spmd.clone.sunk | while | flops 271390848 | bytes 3031901 | solution.py:281
  99.3 4.0 %conditional.10 = (f32[128,2,4,128]{0,3,2,1:T(8,128)}) conditional(s32[]{:T(128)} %convert_element_type.258, f32[128,2,4,128]{0,3,2,1:T(8,128)} %get-tuple-element.1387, (s32[]{:T(128)}, bf16[1024,256]{0,1:T(8,128)(2,1)S(1)}, s32[]{:T(128)}, s32[4]{0:T(128)}, s32[128]{0:T(128)S(1)}, /*index=5*/bf16[1024,256]{0,1:T(8,128)(2,1)S(1)}, ...), branch_computations={%region_13.13_spmd, %region_14.16_spmd} | conditional | flops 271390848 | bytes 3031158 | solution.py:247
  100.5 2.8 %fusion.13 = f32[128,2,4,128]{0,3,2,1:T(8,128)} fusion(f32[128,2,4,128]{0,3,2,1:T(8,128)} %get-tuple-element.621, bf16[512,2,128,1]{0,2,3,1:T(8,128)(2,1)S(1)} %bitcast.305, bf16[512,2,128,1]{0,2,3,1:T(8,128)(2,1)S(1)} %bitcast.304, bf16[128,2,4,128]{3,0,2,1:T(8,128)(2,1)S(1)} %get-tuple-element.628, f32[2,4,128]{2,1,0:T(4,128)} %get-tuple-element.629, ...), kind=kOutput, calls=%fused_computation.19 | convolution fusion | flops 271187968 | bytes 1904640 | tf_op jit(solution)/shard_map/while/body/eval_jaxpr/cond/branch_1_fun/grtk,kgd->tgrd/dot_general | solution.py:277
  103.3 1.8 fusion.62
  106.9 5.9 %while.53 = (s32[]{:T(128)}, f32[128,2,4,128]{0,3,2,1:T(8,128)S(1)}, bf16[1024,256]{0,1:T(8,128)(2,1)}, bf16[1024,256]{0,1:T(8,128)(2,1)}, s32[]{:T(128)}, /*ind...) while((s32[]{:T(128)}, ...), condition=%wide.region_37.38_spmd.clone, body=%wide.region_32.37_spmd.clone.sunk | while | flops 675616896 | bytes 23483460 | solution.py:319
  106.9 5.8 %conditional.11 = ((f32[128,2,4,128]{0,3,2,1:T(8,128)S(1)}, bf16[1024,256]{0,1:T(8,128)(2,1)}, bf16[1024,256]{0,1:T(8,128)(2,1)})) conditional(s32[]{:T(128)} %convert_element_type.259, (f32[128,2,4,128]{0,3,2,1:T(8,128)S(1)}, bf16[1024,256]{0,1:T(8,128)(2,1)}, bf16[1024,256]{0,1:T(8,128)(2,1)}) %tuple.201, (s32[]{:T(128)}, ...), branch_computations={%region_33.33_spmd, %region_34.36_spmd} | conditional | flops 675616896 | bytes 23482630 | solution.py:247
  114.1 2.1 fusion.96
  117.4 2.4 copy.473
  119.8 14.8 %all-to-all-start.3 = ((bf16[8,128,512]{1,2,0:T(8,128)(2,1)}), bf16[8,128,512]{1,2,0:T(8,128)(2,1)}, u32[]{:S(2)}, u32[]{:S(2)}) async-start(bf16[8,128,512]{1,2,0:T(8,128)(2,1)} %copy.473), calls=%async_computation.4 | async-start | bytes 2097152 | tf_op jit(solution)/shard_map/all_to_all | solution.py:327
  134.7 2.7 %fusion.61 = (f32[8,2,128]{2,1,0:T(2,128)S(1)}, f32[8,2,128]{2,1,0:T(2,128)S(1)}, f32[8,128,128]{2,1,0:T(8,128)}) fusion(f32[8,128,128]{2,1,0:T(8,128)S(1)} %copy-done.24, f32[8,2,128]{2,1,0:T(2,128)S(1)} %copy-done.30, pred[8,128,128]{2,1,0:T(8,128)(4,1)} %compare_and_fusion.3, bf16[8,2,128,128]{3,2,1,0:T(8,128)(2,1)S(1)} %bitcast.291, ...), kind=kOutput, calls=%fused_computation.98 | convolution fusion | flops 69332992 | bytes 2252800 | tf_op jit(solution)/shard_map/transpose(jvp(vmap(hts,shp->thp)))/dot_general | solution.py:67
  137.5 2.0 fusion.40
  139.6 4.4 %fusion.44 = bf16[8,128,2,128]{1,3,2,0:T(8,128)(2,1)} fusion(f32[8,128,2,128]{1,3,2,0:T(8,128)} %fusion.40, f32[8,2,128,128]{3,0,2,1:T(8,128)S(1)} %convolution_bitcast_fusion.1, f32[8,128,2]{1,2,0:T(2,128)S(1)} %copy.429, f32[8,128,128]{2,1,0:T(8,128)S(1)} %copy-done.7), kind=kOutput, calls=%fused_computation.72 | convolution fusion | flops 403439616 | bytes 3153920 | tf_op jit(solution)/shard_map/transpose(jvp(vmap(hs,sn,shp->hnp)))/dot_general | solution.py:53
  145.1 1.6 convolution_add_fusion.1
  153.1 1.7 fusion.49
  154.9 2.9 %fusion.43 = bf16[8,128,2,128]{1,3,2,0:T(8,128)(2,1)S(1)} fusion(bf16[8,128,2,128]{1,3,2,0:T(8,128)(2,1)S(1)} %bitcast.309, f32[8,128,2,128]{1,3,2,0:T(8,128)} %bitcast.322, f32[2]{0:T(128)S(1)} %copy-done.59, f32[8,128,2]{1,2,0:T(2,128)S(1)} %copy.428, f32[8,128,128]{2,1,0:T(8,128)} %fusion.96, f32[8,2,128]{2,1,0:T(2,128)S(1)} %copy-done.30, ...), kind=kOutput, calls=%fused_computation.71 | convolution fusion | flops 405012480 | bytes 2768904 | tf_op jit(solution)/shard_map/jvp(vmap(hts,shp->thp))/dot_general | solution.py:67
  159.2 1.9 fusion.48
  161.8 2.7 %reduce_window_sum.47 = f32[8,2,128]{2,0,1:T(8,128)S(1)} reduce-window(f32[8,2,128]{2,0,1:T(8,128)S(1)} %get-tuple-element.1092, f32[]{:T(128)} %constant.152.clone.1), window={size=1x1x128 pad=0_0x0_0x0_127}, to_apply=%region_30.31 | reduce-window | flops 260096 | bytes 16388 | tf_op jit(solution)/shard_map/transpose(jvp(jit(cumsum)))/reduce_window_sum | solution.py:91
  164.5 2.5 reduce_window_sum.46
  168.2 2.1 copy.439
  170.3 5.9 %all-to-all-start.2 = ((bf16[2,1024,256]{2,0,1:T(2,128)(2,1)}), bf16[2,1024,256]{2,0,1:T(2,128)(2,1)S(1)}, u32[]{:S(2)}, u32[]{:S(2)}) async-start(bf16[2,1024,256]{2,0,1:T(2,128)(2,1)} %copy.439), calls=%async_computation.2 | async-start | bytes 2097152 | tf_op jit(solution)/shard_map/all_to_all | solution.py:140
  180.9 28.6 %all-to-all-done.2 = bf16[2,1024,256]{2,0,1:T(2,128)(2,1)S(1)} async-done(((bf16[2,1024,256]{2,0,1:T(2,128)(2,1)}), bf16[2,1024,256]{2,0,1:T(2,128)(2,1)S(1)}, u32[]{:S(2)}, u32[]{:S(2)}) %all-to-all-start.2) | async-done | bytes 1048608 | tf_op jit(solution)/shard_map/all_to_all | solution.py:140
  212.3 29.1 %reduce-scatter.2.cloned.1.call-done = f32[128,272]{0,1:T(8,128)} async-done(((f32[1024,272]{0,1:T(8,128)}), f32[128,272]{0,1:T(8,128)}) %reduce-scatter.2.cloned.1.call-update) | async-done | bytes 139280 | tf_op jit(solution)/shard_map/reduce_scatter | solution.py:338
  (281 shorter events, 59.8 us)
Async XLA Ops:
  7.2 16.8 %all-to-all-start.1 = ((f32[8,2,128]{2,1,0:T(2,128)}), f32[8,2,128]{2,1,0:T(2,128)S(1)}, u32[]{:S(2)}, u32[]{:S(2)}) async-start(f32[8,2,128]{2,1,0:T(2,128)} %bitcast.338), calls=%async_computation.1 | async-start | bytes 16384 | tf_op jit(solution)/shard_map/all_to_all | solution.py:121
  14.5 64.7 %all-gather.2.cloned.1.call-start = ((), (), s32[]{:S(2)}) async-start(), calls=%async_computation.5 | async-start | bytes 1769472 | tf_op jit(solution)/shard_map/all_gather | solution.py:206
  18.9 15.1 %copy-start.33 = (pred[8]{0:T(512)(128)(4,1)}, pred[8]{0:T(512)(128)(4,1)S(1)}, u32[]{:S(2)}) copy-start(pred[8]{0:T(512)(128)(4,1)S(1)} %get-tuple-element.1119) | copy-start | bytes 28
  19.0 14.9 %copy-start.51 = (pred[8]{0:T(512)(128)(4,1)}, pred[8]{0:T(512)(128)(4,1)S(1)}, u32[]{:S(2)}) copy-start(pred[8]{0:T(512)(128)(4,1)S(1)} %get-tuple-element.1116) | copy-start | bytes 28
  19.0 15.1 %copy-start.31 = (pred[8]{0:T(512)(128)(4,1)}, pred[8]{0:T(512)(128)(4,1)S(1)}, u32[]{:S(2)}) copy-start(pred[8]{0:T(512)(128)(4,1)S(1)} %get-tuple-element.1117) | copy-start | bytes 28
  19.0 14.9 %copy-start.53 = (pred[8]{0:T(512)(128)(4,1)}, pred[8]{0:T(512)(128)(4,1)S(1)}, u32[]{:S(2)}) copy-start(pred[8]{0:T(512)(128)(4,1)S(1)} %get-tuple-element.1115) | copy-start | bytes 28
  19.0 15.1 %copy-start.37 = (f32[8]{0:T(128)}, f32[8]{0:T(128)S(1)}, u32[]{:S(2)}) copy-start(f32[8]{0:T(128)S(1)} %get-tuple-element.1114) | copy-start | bytes 100
  19.0 15.1 %copy-start.39 = (f32[8]{0:T(128)}, f32[8]{0:T(128)S(1)}, u32[]{:S(2)}) copy-start(f32[8]{0:T(128)S(1)} %get-tuple-element.1113) | copy-start | bytes 100
  19.1 15.1 %copy-start.41 = (f32[8]{0:T(128)}, f32[8]{0:T(128)S(1)}, u32[]{:S(2)}) copy-start(f32[8]{0:T(128)S(1)} %get-tuple-element.1111) | copy-start | bytes 100
  19.1 14.9 %copy-start.55 = (f32[8]{0:T(128)}, f32[8]{0:T(128)S(1)}, u32[]{:S(2)}) copy-start(f32[8]{0:T(128)S(1)} %get-tuple-element.1109) | copy-start | bytes 100
  20.4 13.7 %copy-start.43 = (pred[8]{0:T(512)(128)(4,1)}, pred[8]{0:T(512)(128)(4,1)S(1)}, u32[]{:S(2)}) copy-start(pred[8]{0:T(512)(128)(4,1)S(1)} %iota_compare_fusion.7) | copy-start | bytes 28
  20.6 13.0 %copy-start.35 = (f32[8]{0:T(128)}, f32[8]{0:T(128)S(1)}, u32[]{:S(2)}) copy-start(f32[8]{0:T(128)S(1)} %convert_reduce_fusion.5) | copy-start | bytes 100
  21.9 8.2 %copy-start.26 = (bf16[128,1024]{1,0:T(8,128)(2,1)S(1)}, bf16[128,1024]{1,0:T(8,128)(2,1)}, u32[]{:S(2)}) copy-start(bf16[128,1024]{1,0:T(8,128)(2,1)} %param.33) | copy-start | bytes 786436
  21.9 8.4 %copy-start.27 = (bf16[128,1024]{1,0:T(8,128)(2,1)S(1)}, bf16[128,1024]{1,0:T(8,128)(2,1)}, u32[]{:S(2)}) copy-start(bf16[128,1024]{1,0:T(8,128)(2,1)} %param.29) | copy-start | bytes 786436
  23.9 6.7 %copy-start.57 = (f32[16]{0:T(128)S(1)}, f32[16]{0:T(128)}, u32[]{:S(2)}) copy-start(f32[16]{0:T(128)} %param.27) | copy-start | bytes 196
  23.9 37.2 %all-to-all-start = ((bf16[2,128,2048]{1,0,2:T(2,128)(2,1)}), bf16[2,128,2048]{1,0,2:T(2,128)(2,1)S(1)}, u32[]{:S(2)}, u32[]{:S(2)}) async-start(bf16[2,128,2048]{1,0,2:T(2,128)(2,1)} %copy.417), calls=%async_computation | async-start | bytes 2097152 | tf_op jit(solution)/shard_map/all_to_all | solution.py:118
  33.9 28.3 %copy-start.45 = (f32[2]{0:T(128)}, f32[2]{0:T(128)S(1)}, u32[]{:S(2)}) copy-start(f32[2]{0:T(128)S(1)} %get-tuple-element.989) | copy-start | bytes 28
  62.2 21.2 %copy-start = (bf16[1,8,128,256]{2,3,1,0:T(8,128)(2,1)}, bf16[1,8,128,256]{2,3,1,0:T(8,128)(2,1)S(1)}, u32[]{:S(2)}) copy-start(bf16[1,8,128,256]{2,3,1,0:T(8,128)(2,1)S(1)} %get-tuple-element.1087) | copy-start | bytes 1572868
  80.5 8.1 %copy-start.6 = (f32[8,128,128]{2,1,0:T(8,128)}, f32[8,128,128]{2,1,0:T(8,128)S(1)}, u32[]{:S(2)}) copy-start(f32[8,128,128]{2,1,0:T(8,128)S(1)} %convert.15) | copy-start | bytes 1572868
  106.9 7.2 %copy-start.3 = (bf16[1024,128]{1,0:T(8,128)(2,1)S(1)}, bf16[1024,128]{1,0:T(8,128)(2,1)}, u32[]{:S(2)}) copy-start(bf16[1024,128]{1,0:T(8,128)(2,1)} %copy-done.2) | copy-start | bytes 786436
  117.4 17.3 %copy-start.1 = (bf16[1,8,128,256]{2,3,1,0:T(8,128)(2,1)S(1)}, bf16[1,8,128,256]{2,3,1,0:T(8,128)(2,1)}, u32[]{:S(2)}) copy-start(bf16[1,8,128,256]{2,3,1,0:T(8,128)(2,1)} %copy-done) | copy-start | bytes 1572868
  117.4 17.3 %copy-start.9 = (bf16[1,8,128,256]{2,3,1,0:T(8,128)(2,1)S(1)}, bf16[1,8,128,256]{2,3,1,0:T(8,128)(2,1)}, u32[]{:S(2)}) copy-start(bf16[1,8,128,256]{2,3,1,0:T(8,128)(2,1)} %get-tuple-element.1086) | copy-start | bytes 1572868
  117.4 17.3 %copy-start.24 = (f32[8,128,128]{2,1,0:T(8,128)S(1)}, f32[8,128,128]{2,1,0:T(8,128)}, u32[]{:S(2)}) copy-start(f32[8,128,128]{2,1,0:T(8,128)} %fusion.96) | copy-start | bytes 1572868
  117.4 17.3 %copy-start.30 = (f32[8,2,128]{2,1,0:T(2,128)S(1)}, f32[8,2,128]{2,1,0:T(2,128)}, u32[]{:S(2)}) copy-start(f32[8,2,128]{2,1,0:T(2,128)} %copy.420) | copy-start | bytes 24580
  119.8 50.5 %all-to-all-start.3 = ((bf16[8,128,512]{1,2,0:T(8,128)(2,1)}), bf16[8,128,512]{1,2,0:T(8,128)(2,1)}, u32[]{:S(2)}, u32[]{:S(2)}) async-start(bf16[8,128,512]{1,2,0:T(8,128)(2,1)} %copy.473), calls=%async_computation.4 | async-start | bytes 2097152 | tf_op jit(solution)/shard_map/all_to_all | solution.py:327
  134.6 106.7 %reduce-scatter.2.cloned.1.call-start = ((), (), s32[]{:S(2)}) async-start(), calls=%async_computation.6 | async-start | bytes 1253376 | tf_op jit(solution)/shard_map/reduce_scatter | solution.py:338
  159.2 7.8 %copy-start.13 = (f32[1024,128]{0,1:T(8,128)S(1)}, f32[1024,128]{0,1:T(8,128)}, u32[]{:S(2)}) copy-start(f32[1024,128]{0,1:T(8,128)} %copy.467) | copy-start | bytes 1572868
  161.4 6.7 %copy-start.19 = (bf16[1,1024,256]{1,2,0:T(8,128)(2,1)S(1)}, bf16[1,1024,256]{1,2,0:T(8,128)(2,1)}, u32[]{:S(2)}) copy-start(bf16[1,1024,256]{1,2,0:T(8,128)(2,1)} %convert_element_type.202) | copy-start | bytes 1572868
  161.5 6.7 %copy-start.20 = (bf16[1,1024,256]{1,2,0:T(8,128)(2,1)S(1)}, bf16[1,1024,256]{1,2,0:T(8,128)(2,1)}, u32[]{:S(2)}) copy-start(bf16[1,1024,256]{1,2,0:T(8,128)(2,1)} %convert_element_type.199) | copy-start | bytes 1572868
  168.2 8.0 %copy-start.23 = (bf16[128,2,4,128]{0,3,2,1:T(8,128)(2,1)S(1)}, bf16[128,2,4,128]{0,3,2,1:T(8,128)(2,1)}, u32[]{:S(2)}) copy-start(bf16[128,2,4,128]{0,3,2,1:T(8,128)(2,1)} %get-tuple-element.1062) | copy-start | bytes 786436
  170.3 39.2 %all-to-all-start.2 = ((bf16[2,1024,256]{2,0,1:T(2,128)(2,1)}), bf16[2,1024,256]{2,0,1:T(2,128)(2,1)S(1)}, u32[]{:S(2)}, u32[]{:S(2)}) async-start(bf16[2,1024,256]{2,0,1:T(2,128)(2,1)} %copy.439), calls=%async_computation.2 | async-start | bytes 2097152 | tf_op jit(solution)/shard_map/all_to_all | solution.py:140
  242.3 1.4 collective-permute-start
  (35 other events, 109.4 us)
Sparse Core Ops, SparseCore 0:
  19.1 60.1 all-gather.1
  168.2 73.0 reduce-scatter.1

commit v6 on v5

--- a/solution.py
+++ b/solution.py
@@ -203,7 +203,17 @@
     key_width = attention_key_rows.shape[1]
     state_width = b_rows.shape[1]
     pieces = [attention_key_rows, values] + ([b_rows, c_rows] if by_heads else [])
-    gathered = lax.all_gather(jnp.concatenate(pieces, axis=1), "seq", axis=0, tiled=True)
+    joined = jnp.concatenate(pieces, axis=1)
+    if by_heads:
+        gathered = lax.all_to_all(
+            jnp.broadcast_to(joined[None], (lax.axis_size("seq"),) + joined.shape),
+            "seq",
+            split_axis=0,
+            concat_axis=0,
+            tiled=True,
+        ).reshape(total_len, joined.shape[1])
+    else:
+        gathered = lax.all_gather(joined, "seq", axis=0, tiled=True)
     key_all, value_all = gathered[:, :key_width], gathered[:, key_width : 2 * key_width]
     if by_heads:
         b_all = gathered[:, 2 * key_width : 2 * key_width + state_width]
@@ -335,7 +345,14 @@
     key_gradient_total = kv_total[:, : groups * HEAD_SIZE]
     value_gradient_total = kv_total[:, groups * HEAD_SIZE :]
     if by_heads:
-        bc_sum = lax.psum_scatter(bc_part, "seq", scatter_dimension=0, tiled=True)
+        bc_sum = lax.all_to_all(
+            bc_part.reshape(seq_count, tokens, bc_part.shape[1]),
+            "seq",
+            split_axis=0,
+            concat_axis=0,
+            tiled=True,
+        )
+        bc_sum = jnp.sum(bc_sum, axis=0)
         grad_decay = bc_sum[:, 2 * state_width :].T
         bc_sum = bc_sum[:, : 2 * state_width]
         if lax.axis_size("head") == 2:

time: 254 us -> 238 us (0.937)
  between operations: 15 us -> 1.64 us
  waiting for transfers between devices: 101 us -> 93.2 us
  matrix products: 36.4 us -> 30.3 us
  local copies, waits for them, and re-layouts: 42.5 us -> 47.6 us
  starting transfers between devices: 34.3 us -> 39.2 us
    all_to_all x0 -> x2, waiting for transfers between devices: none -> 48.6 us  [the longest x1 30.1 us: on_device(): lax.all_to_all(jnp.broadcast_to(joined[None], (lax.axis_size('seq'),) + j...]
    reduce_scatter x1 -> x0, waiting for transfers between devices: 29.1 us -> none  [on_device(): bc_sum = lax.psum_scatter(bc_part, 'seq', scatter_dimension=0, tiled=True)]
    all_gather x1 -> x0, waiting for transfers between devices: 17.1 us -> none  [on_device(): lax.all_gather(jnp.concatenate(pieces, axis=1), 'seq', axis=0, tiled=True)]
    all_to_all x1, waiting for transfers between devices: 28.6 us -> 14.8 us  [mamba_by_heads(): back = lax.all_to_all(back, 'seq', split_axis=1, concat_axis=2, tiled=True)]
    all_to_all x0 -> x2, starting transfers between devices: none -> 7.98 us  [the longest x1 4.42 us: on_device(): lax.all_to_all(jnp.broadcast_to(joined[None], (lax.axis_size('seq'),) + j...]
    all_to_all x1, waiting for transfers between devices: 0.01 us -> 3.17 us  [mamba_by_heads(): lax.all_to_all(decay_log, 'seq', split_axis=0, concat_axis=1, tiled=True)]
    all_to_all x1, waiting for transfers between devices: 26.3 us -> 23.3 us  [mamba_by_heads(): lax.all_to_all(jnp.stack([x_input, mixer_cot]), 'seq', split_axis=2, conc...]
    all_to_all x1, waiting for transfers between devices: 0.01 us -> 2.66 us  [on_device(): lax.all_to_all(kv_terms.reshape(seq_count, tokens, 2 * groups * HEAD_SIZE...]
  transfers between devices with their start and end apart: 7 -> 7, of which waited for: 4 -> 7; matrix products, arithmetic and copies ran while one was open for 23% -> 22% of each run, Pallas kernels for 0% -> 0%
where the time goes in v6:
time: 238 us; the launch traced here: 237 us
  waiting for transfers between devices  93.2 us (39%)
  local copies, waits for them, and re-layouts  47.6 us (20%)
  starting transfers between devices  39.2 us (16%)
  matrix products  30.3 us (13%)
  other arithmetic  24.4 us (10%)
    all_to_all x1, waiting for transfers between devices, on_device(): lax.all_to_all(jnp.broadcast_to(joined[None], (lax.axis_size('seq'),) + j...  30.1 us
    all_to_all x1, waiting for transfers between devices, mamba_by_heads(): lax.all_to_all(jnp.stack([x_input, mixer_cot]), 'seq', split_axis=2, conc...  23.3 us
    all_to_all x1, waiting for transfers between devices, on_device(): lax.all_to_all(bc_part.reshape(seq_count, tokens, bc_part.shape[1]), 'seq...  18.4 us
    all_to_all x1, starting transfers between devices, on_device(): lax.all_to_all(kv_terms.reshape(seq_count, tokens, 2 * groups * HEAD_SIZE...  15.8 us
    all_to_all x1, waiting for transfers between devices, mamba_by_heads(): back = lax.all_to_all(back, 'seq', split_axis=1, concat_axis=2, tiled=True)  14.8 us
    unnamed x120, local copies, waits for them, and re-layouts  8.58 us
    all_to_all x1, starting transfers between devices, mamba_by_heads(): lax.all_to_all(decay_log, 'seq', split_axis=0, concat_axis=1, tiled=True)  7.32 us
    dot_general x3, matrix products, mixer_whole(): state_in = jnp.einsum('kjh,jhnp->khnp', reach, summary, precision=precise)  6.46 us
  transfers between devices with their start and end apart: 7, of which 7 were waited for; matrix products, arithmetic and copies ran while one was open for 22% of the time, Pallas kernels for 0%

profile of v6, /device:TPU:0, one launch (start us, length us, event | category | flops | bytes accessed | tf_op | source)
XLA Modules:
  0.0 236.7 jit_solution(6434027770669730573)
XLA Ops:
  0.6 7.3 %all-to-all-start.1 = ((f32[8,2,128]{2,1,0:T(2,128)}), f32[8,2,128]{2,1,0:T(2,128)S(1)}, u32[]{:S(2)}, u32[]{:S(2)}) async-start(f32[8,2,128]{2,1,0:T(2,128)} %bitcast.342), calls=%async_computation.1 | async-start | bytes 16384 | tf_op jit(solution)/shard_map/all_to_all | solution.py:121
  9.3 2.0 copy.405
  11.3 3.2 %all-to-all-done.1 = f32[8,2,128]{2,1,0:T(2,128)S(1)} async-done(((f32[8,2,128]{2,1,0:T(2,128)}), f32[8,2,128]{2,1,0:T(2,128)S(1)}, u32[]{:S(2)}, u32[]{:S(2)}) %all-to-all-start.1) | async-done | bytes 8224 | tf_op jit(solution)/shard_map/all_to_all | solution.py:121
  14.5 3.6 %all-to-all-start = ((bf16[2,128,2048]{1,0,2:T(2,128)(2,1)}), bf16[2,128,2048]{1,0,2:T(2,128)(2,1)S(1)}, u32[]{:S(2)}, u32[]{:S(2)}) async-start(bf16[2,128,2048]{1,0,2:T(2,128)(2,1)} %copy.405), calls=%async_computation | async-start | bytes 2097152 | tf_op jit(solution)/shard_map/all_to_all | solution.py:118
  19.5 23.3 %all-to-all-done = bf16[2,128,2048]{1,0,2:T(2,128)(2,1)S(1)} async-done(((bf16[2,128,2048]{1,0,2:T(2,128)(2,1)}), bf16[2,128,2048]{1,0,2:T(2,128)(2,1)S(1)}, u32[]{:S(2)}, u32[]{:S(2)}) %all-to-all-start) | async-done | bytes 1048608 | tf_op jit(solution)/shard_map/all_to_all | solution.py:118
  44.1 4.4 %all-to-all-start.2 = ((bf16[8,128,768]{1,2,0:T(8,128)(2,1)}), bf16[8,128,768]{1,2,0:T(8,128)(2,1)}, u32[]{:S(2)}, u32[]{:S(2)}) async-start(bf16[8,128,768]{1,2,0:T(8,128)(2,1)} %broadcast_in_dim.254), calls=%async_computation.2 | async-start | bytes 3145728 | tf_op jit(solution)/shard_map/all_to_all | solution.py:208
  54.9 30.1 %all-to-all-done.2 = bf16[8,128,768]{1,2,0:T(8,128)(2,1)} async-done(((bf16[8,128,768]{1,2,0:T(8,128)(2,1)}), bf16[8,128,768]{1,2,0:T(8,128)(2,1)}, u32[]{:S(2)}, u32[]{:S(2)}) %all-to-all-start.2) | async-done | bytes 1572896 | tf_op jit(solution)/shard_map/all_to_all | solution.py:208
  85.0 2.6 %copy.411 = bf16[8,128,768]{2,1,0:T(8,128)(2,1)} copy(bf16[8,128,768]{1,2,0:T(8,128)(2,1)} %all-to-all-done.2) | data formatting | bytes 3145728 | tf_op jit(solution)/shard_map/all_to_all | solution.py:208
  88.7 2.5 %fusion.88 = (bf16[1024,256]{1,0:T(8,128)(2,1)}, bf16[1024,256]{1,0:T(8,128)(2,1)}) fusion(bf16[1024,768]{1,0:T(8,128)(2,1)} %bitcast.311), kind=kLoop, calls=%fused_computation.201 | loop fusion | bytes 2097152 | tf_op jit(solution)/shard_map/slice | solution.py:217
  100.4 2.8 %convolution_bitcast_fusion.6 = f32[8,8,2]{1,0,2:T(8,128)S(1)} fusion(f32[2,128,128,8]{2,3,1,0:T(8,128)S(1)} %copy.419, f32[8,2,128,128]{3,2,1,0:T(8,128)S(1)} %fusion.32), kind=kOutput, calls=%fused_computation.78 | convolution fusion | flops 25165824 | bytes 2097664 | tf_op jit(solution)/shard_map/transpose(jvp(kjh,jhnp->khnp))/dot_general | solution.py:102
  103.2 2.7 %convolution_bitcast_fusion.3 = f32[8,2,128,128]{3,0,2,1:T(8,128)} fusion(f32[8,2,128,128]{3,2,1,0:T(8,128)S(1)} %fusion.32, f32[8,8,2]{1,0,2:T(8,128)S(1)} %stack.13), kind=kOutput, calls=%fused_computation.65 | convolution fusion | flops 25165824 | bytes 2097664 | tf_op jit(solution)/shard_map/jvp(kjh,jhnp->khnp)/dot_general | solution.py:102
  106.1 2.5 %while.51 = (s32[]{:T(128)}, f32[2,4,128]{2,1,0:T(4,128)S(1)}, f32[2,4,128]{2,1,0:T(4,128)S(1)}, s32[]{:T(128)}, s32[4]{0:T(128)}, /*index=5*/s32[128]{0:T(128)S...) while((s32[]{:T(128)}, f32[2,4,128]{2,1,0:T(4,128)S(1)}, ...), condition=%wide.region_11.12_spmd.clone, body=%wide.region_4.11_spmd.clone.sunk | while | flops 138616976 | bytes 5505901 | solution.py:274
  106.1 2.4 conditional.9
  112.4 4.0 %while.52 = (s32[]{:T(128)}, f32[128,2,4,128]{0,3,2,1:T(8,128)}, s32[]{:T(128)}, bf16[1024,256]{0,1:T(8,128)(2,1)S(1)}, s32[4]{0:T(128)}, /*index=5*/s32[128]{0:...) while((s32[]{:T(128)}, f32[128,2,4,128]{0,3,2,1:T(8,128)}, ...), condition=%wide.region_17.18_spmd.clone, body=%wide.region_12.17_spmd.clone.sunk | while | flops 271390848 | bytes 3031901 | solution.py:291
  112.4 4.0 %conditional.10 = (f32[128,2,4,128]{0,3,2,1:T(8,128)}) conditional(s32[]{:T(128)} %convert_element_type.258, f32[128,2,4,128]{0,3,2,1:T(8,128)} %get-tuple-element.1415, (s32[]{:T(128)}, bf16[1024,256]{0,1:T(8,128)(2,1)S(1)}, s32[]{:T(128)}, s32[4]{0:T(128)}, s32[128]{0:T(128)S(1)}, /*index=5*/bf16[1024,256]{0,1:T(8,128)(2,1)S(1)}, ...), branch_computations={%region_13.13_spmd, %region_14.16_spmd} | conditional | flops 271390848 | bytes 3031158 | solution.py:257
  113.6 2.8 %fusion.13 = f32[128,2,4,128]{0,3,2,1:T(8,128)} fusion(f32[128,2,4,128]{0,3,2,1:T(8,128)} %get-tuple-element.621, bf16[512,2,128,1]{0,2,3,1:T(8,128)(2,1)S(1)} %bitcast.309, bf16[512,2,128,1]{0,2,3,1:T(8,128)(2,1)S(1)} %bitcast.308, bf16[128,2,4,128]{3,0,2,1:T(8,128)(2,1)S(1)} %get-tuple-element.628, f32[2,4,128]{2,1,0:T(4,128)} %get-tuple-element.629, ...), kind=kOutput, calls=%fused_computation.19 | convolution fusion | flops 271187968 | bytes 1904640 | tf_op jit(solution)/shard_map/while/body/eval_jaxpr/cond/branch_1_fun/grtk,kgd->tgrd/dot_general | solution.py:287
  119.3 5.9 %while.53 = (s32[]{:T(128)}, f32[128,2,4,128]{0,3,2,1:T(8,128)S(1)}, bf16[1024,256]{0,1:T(8,128)(2,1)}, bf16[1024,256]{0,1:T(8,128)(2,1)}, s32[]{:T(128)}, /*ind...) while((s32[]{:T(128)}, ...), condition=%wide.region_37.38_spmd.clone, body=%wide.region_32.37_spmd.clone.sunk | while | flops 675616896 | bytes 23483460 | solution.py:329
  119.4 5.9 %conditional.11 = ((f32[128,2,4,128]{0,3,2,1:T(8,128)S(1)}, bf16[1024,256]{0,1:T(8,128)(2,1)}, bf16[1024,256]{0,1:T(8,128)(2,1)})) conditional(s32[]{:T(128)} %convert_element_type.259, (f32[128,2,4,128]{0,3,2,1:T(8,128)S(1)}, bf16[1024,256]{0,1:T(8,128)(2,1)}, bf16[1024,256]{0,1:T(8,128)(2,1)}) %tuple.203, (s32[]{:T(128)}, ...), branch_computations={%region_33.33_spmd, %region_34.36_spmd} | conditional | flops 675616896 | bytes 23482630 | solution.py:257
  128.8 2.4 %copy.462 = bf16[8,128,512]{1,2,0:T(8,128)(2,1)} copy(bf16[8,128,512]{2,1,0:T(8,128)(2,1)} %pad_maximum_fusion.3) | data formatting | bytes 2097152 | tf_op jit(solution)/shard_map/concatenate | solution.py:336
  131.2 15.8 %all-to-all-start.5 = ((bf16[8,128,512]{1,2,0:T(8,128)(2,1)}), bf16[8,128,512]{1,2,0:T(8,128)(2,1)}, u32[]{:S(2)}, u32[]{:S(2)}) async-start(bf16[8,128,512]{1,2,0:T(8,128)(2,1)} %copy.462), calls=%async_computation.5 | async-start | bytes 2097152 | tf_op jit(solution)/shard_map/all_to_all | solution.py:337
  149.0 2.3 fusion.44
  159.6 2.1 convert_element_type.199
  161.7 2.3 pad_maximum_fusion.2
  164.0 3.7 %copy.423 = bf16[2,1024,256]{2,0,1:T(2,128)(2,1)} copy(bf16[2,1024,256]{1,2,0:T(8,128)(2,1)} %pad_maximum_fusion.2) | data formatting | bytes 2097152 | tf_op jit(solution)/shard_map/stack | solution.py:134
  167.6 2.8 %fusion.61 = (f32[8,2,128]{2,1,0:T(2,128)S(1)}, f32[8,2,128]{2,1,0:T(2,128)S(1)}, f32[8,128,128]{2,1,0:T(8,128)}) fusion(f32[8,128,128]{2,1,0:T(8,128)} %fusion.96, f32[8,2,128]{2,1,0:T(2,128)S(1)} %copy-done.28, pred[8,128,128]{2,1,0:T(8,128)(4,1)S(1)} %copy-done.23, bf16[8,2,128,128]{3,2,1,0:T(8,128)(2,1)S(1)} %bitcast.298, ...), kind=kOutput, calls=%fused_computation.98 | convolution fusion | flops 69332992 | bytes 2252800 | tf_op jit(solution)/shard_map/transpose(jvp(vmap(hts,shp->thp)))/dot_general | solution.py:67
  170.4 2.7 %all-to-all-done.5 = bf16[8,128,512]{1,2,0:T(8,128)(2,1)} async-done(((bf16[8,128,512]{1,2,0:T(8,128)(2,1)}), bf16[8,128,512]{1,2,0:T(8,128)(2,1)}, u32[]{:S(2)}, u32[]{:S(2)}) %all-to-all-start.5) | async-done | bytes 1048608 | tf_op jit(solution)/shard_map/all_to_all | solution.py:337
  173.1 4.5 %all-to-all-start.3 = ((bf16[2,1024,256]{2,0,1:T(2,128)(2,1)}), bf16[2,1024,256]{2,0,1:T(2,128)(2,1)}, u32[]{:S(2)}, u32[]{:S(2)}) async-start(bf16[2,1024,256]{2,0,1:T(2,128)(2,1)} %copy.423), calls=%async_computation.3 | async-start | bytes 2097152 | tf_op jit(solution)/shard_map/all_to_all | solution.py:140
  177.6 2.5 %reduce_window_sum.47 = f32[8,2,128]{2,0,1:T(8,128)S(1)} reduce-window(f32[8,2,128]{2,0,1:T(8,128)S(1)} %get-tuple-element.1120, f32[]{:T(128)} %constant.152.clone.1), window={size=1x1x128 pad=0_0x0_0x0_127}, to_apply=%region_30.31 | reduce-window | flops 260096 | bytes 16388 | tf_op jit(solution)/shard_map/transpose(jvp(jit(cumsum)))/reduce_window_sum | solution.py:91
  180.1 2.5 %reduce_window_sum.46 = f32[8,2,128]{2,0,1:T(8,128)S(1)} reduce-window(f32[8,2,128]{2,0,1:T(8,128)S(1)} %get-tuple-element.1121, f32[]{:T(128)} %constant.152.clone.1), window={size=1x1x128 pad=0_0x0_0x0_127}, to_apply=%region_22.23 | reduce-window | flops 260096 | bytes 16388 | tf_op jit(solution)/shard_map/transpose(jvp(vmap(jit(cumsum))))/reduce_window_sum | solution.py:45
  188.2 14.8 %all-to-all-done.3 = bf16[2,1024,256]{2,0,1:T(2,128)(2,1)} async-done(((bf16[2,1024,256]{2,0,1:T(2,128)(2,1)}), bf16[2,1024,256]{2,0,1:T(2,128)(2,1)}, u32[]{:S(2)}, u32[]{:S(2)}) %all-to-all-start.3) | async-done | bytes 1048608 | tf_op jit(solution)/shard_map/all_to_all | solution.py:140
  203.0 3.6 %all-to-all-start.4 = ((f32[8,128,272]{1,2,0:T(8,128)}), f32[8,128,272]{1,2,0:T(8,128)S(1)}, u32[]{:S(2)}, u32[]{:S(2)}) async-start(f32[8,128,272]{1,2,0:T(8,128)} %pad_maximum_fusion), calls=%async_computation.4 | async-start | bytes 2228224 | tf_op jit(solution)/shard_map/all_to_all | solution.py:348
  215.3 18.4 %all-to-all-done.4 = f32[8,128,272]{1,2,0:T(8,128)S(1)} async-done(((f32[8,128,272]{1,2,0:T(8,128)}), f32[8,128,272]{1,2,0:T(8,128)S(1)}, u32[]{:S(2)}, u32[]{:S(2)}) %all-to-all-start.4) | async-done | bytes 1114144 | tf_op jit(solution)/shard_map/all_to_all | solution.py:348
  (273 shorter events, 67.3 us)
Async XLA Ops:
  0.6 13.8 %all-to-all-start.1 = ((f32[8,2,128]{2,1,0:T(2,128)}), f32[8,2,128]{2,1,0:T(2,128)S(1)}, u32[]{:S(2)}, u32[]{:S(2)}) async-start(f32[8,2,128]{2,1,0:T(2,128)} %bitcast.342), calls=%async_computation.1 | async-start | bytes 16384 | tf_op jit(solution)/shard_map/all_to_all | solution.py:121
  9.3 8.8 %copy-start.24 = (bf16[128,256]{1,0:T(8,128)(2,1)S(1)}, bf16[128,256]{1,0:T(8,128)(2,1)}, u32[]{:S(2)}) copy-start(bf16[128,256]{1,0:T(8,128)(2,1)} %param.31) | copy-start | bytes 196612
  9.3 8.8 %copy-start.25 = (bf16[128,256]{1,0:T(8,128)(2,1)S(1)}, bf16[128,256]{1,0:T(8,128)(2,1)}, u32[]{:S(2)}) copy-start(bf16[128,256]{1,0:T(8,128)(2,1)} %param.30) | copy-start | bytes 196612
  9.3 8.8 %copy-start.26 = (bf16[128,128]{1,0:T(8,128)(2,1)S(1)}, bf16[128,128]{1,0:T(8,128)(2,1)}, u32[]{:S(2)}) copy-start(bf16[128,128]{1,0:T(8,128)(2,1)} %param.25) | copy-start | bytes 98308
  9.3 8.8 %copy-start.27 = (bf16[128,128]{1,0:T(8,128)(2,1)S(1)}, bf16[128,128]{1,0:T(8,128)(2,1)}, u32[]{:S(2)}) copy-start(bf16[128,128]{1,0:T(8,128)(2,1)} %param.24) | copy-start | bytes 98308
  14.5 28.3 %all-to-all-start = ((bf16[2,128,2048]{1,0,2:T(2,128)(2,1)}), bf16[2,128,2048]{1,0,2:T(2,128)(2,1)S(1)}, u32[]{:S(2)}, u32[]{:S(2)}) async-start(bf16[2,128,2048]{1,0,2:T(2,128)(2,1)} %copy.405), calls=%async_computation | async-start | bytes 2097152 | tf_op jit(solution)/shard_map/all_to_all | solution.py:118
  19.1 33.9 %copy-start.31 = (pred[8]{0:T(512)(128)(4,1)}, pred[8]{0:T(512)(128)(4,1)S(1)}, u32[]{:S(2)}) copy-start(pred[8]{0:T(512)(128)(4,1)S(1)} %iota_compare_fusion.7) | copy-start | bytes 28
  19.1 33.9 %copy-start.33 = (pred[8]{0:T(512)(128)(4,1)}, pred[8]{0:T(512)(128)(4,1)S(1)}, u32[]{:S(2)}) copy-start(pred[8]{0:T(512)(128)(4,1)S(1)} %get-tuple-element.1147) | copy-start | bytes 28
  19.2 33.7 %copy-start.49 = (pred[8]{0:T(512)(128)(4,1)}, pred[8]{0:T(512)(128)(4,1)S(1)}, u32[]{:S(2)}) copy-start(pred[8]{0:T(512)(128)(4,1)S(1)} %get-tuple-element.1144) | copy-start | bytes 28
  19.2 33.9 %copy-start.29 = (pred[8]{0:T(512)(128)(4,1)}, pred[8]{0:T(512)(128)(4,1)S(1)}, u32[]{:S(2)}) copy-start(pred[8]{0:T(512)(128)(4,1)S(1)} %get-tuple-element.1145) | copy-start | bytes 28
  19.5 29.2 %copy-start.21 = (bf16[128,1024]{1,0:T(8,128)(2,1)S(1)}, bf16[128,1024]{1,0:T(8,128)(2,1)}, u32[]{:S(2)}) copy-start(bf16[128,1024]{1,0:T(8,128)(2,1)} %param.33) | copy-start | bytes 786436
  44.1 4.7 %copy-start.22 = (bf16[128,1024]{1,0:T(8,128)(2,1)S(1)}, bf16[128,1024]{1,0:T(8,128)(2,1)}, u32[]{:S(2)}) copy-start(bf16[128,1024]{1,0:T(8,128)(2,1)} %param.29) | copy-start | bytes 786436
  44.1 5.1 %copy-start.55 = (f32[16]{0:T(128)S(1)}, f32[16]{0:T(128)}, u32[]{:S(2)}) copy-start(f32[16]{0:T(128)} %param.27) | copy-start | bytes 196
  44.1 40.9 %all-to-all-start.2 = ((bf16[8,128,768]{1,2,0:T(8,128)(2,1)}), bf16[8,128,768]{1,2,0:T(8,128)(2,1)}, u32[]{:S(2)}, u32[]{:S(2)}) async-start(bf16[8,128,768]{1,2,0:T(8,128)(2,1)} %broadcast_in_dim.254), calls=%async_computation.2 | async-start | bytes 3145728 | tf_op jit(solution)/shard_map/all_to_all | solution.py:208
  49.8 5.0 %copy-start.37 = (f32[8]{0:T(128)}, f32[8]{0:T(128)S(1)}, u32[]{:S(2)}) copy-start(f32[8]{0:T(128)S(1)} %get-tuple-element.1142) | copy-start | bytes 100
  49.8 5.0 %copy-start.51 = (pred[8]{0:T(512)(128)(4,1)}, pred[8]{0:T(512)(128)(4,1)S(1)}, u32[]{:S(2)}) copy-start(pred[8]{0:T(512)(128)(4,1)S(1)} %get-tuple-element.1143) | copy-start | bytes 28
  49.8 5.0 %copy-start.39 = (f32[8]{0:T(128)}, f32[8]{0:T(128)S(1)}, u32[]{:S(2)}) copy-start(f32[8]{0:T(128)S(1)} %get-tuple-element.1141) | copy-start | bytes 100
  49.8 5.0 %copy-start.41 = (f32[8]{0:T(128)}, f32[8]{0:T(128)S(1)}, u32[]{:S(2)}) copy-start(f32[8]{0:T(128)S(1)} %get-tuple-element.1139) | copy-start | bytes 100
  49.9 5.0 %copy-start.53 = (f32[8]{0:T(128)}, f32[8]{0:T(128)S(1)}, u32[]{:S(2)}) copy-start(f32[8]{0:T(128)S(1)} %get-tuple-element.1137) | copy-start | bytes 100
  50.2 4.6 %copy-start.35 = (f32[8]{0:T(128)}, f32[8]{0:T(128)S(1)}, u32[]{:S(2)}) copy-start(f32[8]{0:T(128)S(1)} %convert_reduce_fusion.5) | copy-start | bytes 100
  54.9 37.3 %copy-start = (bf16[1,8,128,256]{2,3,1,0:T(8,128)(2,1)}, bf16[1,8,128,256]{2,3,1,0:T(8,128)(2,1)S(1)}, u32[]{:S(2)}) copy-start(bf16[1,8,128,256]{2,3,1,0:T(8,128)(2,1)S(1)} %get-tuple-element.1115) | copy-start | bytes 1572868
  91.2 7.9 %copy-start.8 = (f32[8,128,128]{2,1,0:T(8,128)}, f32[8,128,128]{2,1,0:T(8,128)S(1)}, u32[]{:S(2)}) copy-start(f32[8,128,128]{2,1,0:T(8,128)S(1)} %convert.15) | copy-start | bytes 1572868
  128.8 18.2 %copy-start.1 = (bf16[1,8,128,256]{2,3,1,0:T(8,128)(2,1)S(1)}, bf16[1,8,128,256]{2,3,1,0:T(8,128)(2,1)}, u32[]{:S(2)}) copy-start(bf16[1,8,128,256]{2,3,1,0:T(8,128)(2,1)} %copy-done) | copy-start | bytes 1572868
  128.8 18.2 %copy-start.19 = (f32[8,128,128]{2,1,0:T(8,128)S(1)}, f32[8,128,128]{2,1,0:T(8,128)}, u32[]{:S(2)}) copy-start(f32[8,128,128]{2,1,0:T(8,128)} %fusion.96) | copy-start | bytes 1572868
  128.8 18.2 %copy-start.28 = (f32[8,2,128]{2,1,0:T(2,128)S(1)}, f32[8,2,128]{2,1,0:T(2,128)}, u32[]{:S(2)}) copy-start(f32[8,2,128]{2,1,0:T(2,128)} %copy.408) | copy-start | bytes 24580
  128.8 18.2 %copy-start.56 = (f32[2]{0:T(128)S(1)}, f32[2]{0:T(128)}, u32[]{:S(2)}) copy-start(f32[2]{0:T(128)} %dynamic_slice.18) | copy-start | bytes 28
  131.2 17.8 %copy-start.9 = (f32[8,128,128]{2,1,0:T(8,128)S(1)}, f32[8,128,128]{2,1,0:T(8,128)}, u32[]{:S(2)}) copy-start(f32[8,128,128]{2,1,0:T(8,128)} %copy-done.8) | copy-start | bytes 1572868
  131.2 41.9 %all-to-all-start.5 = ((bf16[8,128,512]{1,2,0:T(8,128)(2,1)}), bf16[8,128,512]{1,2,0:T(8,128)(2,1)}, u32[]{:S(2)}, u32[]{:S(2)}) async-start(bf16[8,128,512]{1,2,0:T(8,128)(2,1)} %copy.462), calls=%async_computation.5 | async-start | bytes 2097152 | tf_op jit(solution)/shard_map/all_to_all | solution.py:337
  173.1 29.9 %all-to-all-start.3 = ((bf16[2,1024,256]{2,0,1:T(2,128)(2,1)}), bf16[2,1024,256]{2,0,1:T(2,128)(2,1)}, u32[]{:S(2)}, u32[]{:S(2)}) async-start(bf16[2,1024,256]{2,0,1:T(2,128)(2,1)} %copy.423), calls=%async_computation.3 | async-start | bytes 2097152 | tf_op jit(solution)/shard_map/all_to_all | solution.py:140
  177.5 8.4 %copy-start.12 = (f32[8,128,128]{2,1,0:T(8,128)S(1)}, f32[8,128,128]{2,1,0:T(8,128)}, u32[]{:S(2)}) copy-start(f32[8,128,128]{2,1,0:T(8,128)} %get-tuple-element.1008) | copy-start | bytes 1572868
  203.0 30.7 %all-to-all-start.4 = ((f32[8,128,272]{1,2,0:T(8,128)}), f32[8,128,272]{1,2,0:T(8,128)S(1)}, u32[]{:S(2)}, u32[]{:S(2)}) async-start(f32[8,128,272]{1,2,0:T(8,128)} %pad_maximum_fusion), calls=%async_computation.4 | async-start | bytes 2228224 | tf_op jit(solution)/shard_map/all_to_all | solution.py:348
  233.8 1.4 collective-permute-start
  (33 other events, 90.9 us)

commit v7 on v4

--- a/solution.py
+++ b/solution.py
@@ -108,21 +108,17 @@
     return outputs.reshape(count * width, heads, P_SIZE)
 
 
-def mamba_by_heads(x_input, b_all, c_all, decay_log, skip_gain, doc_lengths, mixer_cot):
+def mamba_by_heads(x_all, cot_all, b_all, c_all, decay_log, skip_gain, doc_lengths):
     seq_count = lax.axis_size("seq")
     place = lax.axis_index("seq")
-    tokens = x_input.shape[0]
     heads_here = skip_gain.shape[0]
     own = heads_here // seq_count
-    total = tokens * seq_count
-    pair = lax.all_to_all(
-        jnp.stack([x_input, mixer_cot]), "seq", split_axis=2, concat_axis=1, tiled=True
-    )
+    total = x_all.shape[0]
     decay = lax.all_to_all(decay_log, "seq", split_axis=0, concat_axis=1, tiled=True)
     gains = lax.dynamic_slice_in_dim(skip_gain, place * own, own)
     segment = doc_index(jnp.arange(total, dtype=jnp.int32), doc_lengths)
-    inputs = pair[0].astype(jnp.float32).reshape(total, own, P_SIZE)
-    cot = pair[1].astype(jnp.float32).reshape(total, own, P_SIZE)
+    inputs = x_all.astype(jnp.float32).reshape(total, own, P_SIZE)
+    cot = cot_all.astype(jnp.float32).reshape(total, own, P_SIZE)
 
     def whole_of(i, brow, crow, d):
         return mixer_whole(i, brow, crow, d, gains, segment)
@@ -131,17 +127,14 @@
         whole_of, inputs, b_all.astype(jnp.float32), c_all.astype(jnp.float32), decay
     )
     grad_x, grad_b, grad_c, grad_decay = pull(cot)
-    back = jnp.stack(
-        [
-            mixed.reshape(total, own * P_SIZE).astype(jnp.bfloat16),
-            grad_x.reshape(total, own * P_SIZE).astype(jnp.bfloat16),
-        ]
-    )
-    back = lax.all_to_all(back, "seq", split_axis=1, concat_axis=2, tiled=True)
     decay_cols = lax.dynamic_update_slice_in_dim(
         jnp.zeros((total, heads_here), jnp.float32), grad_decay.T, place * own, 1
     )
-    return back[0], back[1], jnp.concatenate([grad_b, grad_c, decay_cols], axis=1)
+    return (
+        mixed.reshape(total, own * P_SIZE).astype(jnp.bfloat16),
+        grad_x.reshape(total, own * P_SIZE).astype(jnp.bfloat16),
+        jnp.concatenate([grad_b, grad_c, decay_cols], axis=1),
+    )
 
 
 def mamba_by_stretch(
@@ -203,13 +196,34 @@
     key_width = attention_key_rows.shape[1]
     state_width = b_rows.shape[1]
     pieces = [attention_key_rows, values] + ([b_rows, c_rows] if by_heads else [])
-    gathered = lax.all_gather(jnp.concatenate(pieces, axis=1), "seq", axis=0, tiled=True)
+    joined = jnp.concatenate(pieces, axis=1)
+    seq_count = lax.axis_size("seq")
+    if by_heads:
+        own_width = heads_here // seq_count * P_SIZE
+
+        def by_owner(a):
+            return a.reshape(tokens, seq_count, own_width).transpose(1, 0, 2)
+
+        sent = jnp.concatenate(
+            [
+                by_owner(x_input),
+                by_owner(mixer_cot),
+                jnp.broadcast_to(joined[None], (seq_count,) + joined.shape),
+            ],
+            axis=2,
+        )
+        got = lax.all_to_all(sent, "seq", split_axis=0, concat_axis=0, tiled=True)
+        x_all = got[:, :, :own_width].reshape(total_len, own_width)
+        cot_all = got[:, :, own_width : 2 * own_width].reshape(total_len, own_width)
+        gathered = got[:, :, 2 * own_width :].reshape(total_len, joined.shape[1])
+    else:
+        gathered = lax.all_gather(joined, "seq", axis=0, tiled=True)
     key_all, value_all = gathered[:, :key_width], gathered[:, key_width : 2 * key_width]
     if by_heads:
         b_all = gathered[:, 2 * key_width : 2 * key_width + state_width]
         c_all = gathered[:, 2 * key_width + state_width :]
-        mixer_out, x_grad, bc_part = mamba_by_heads(
-            x_input, b_all, c_all, decay_log, skip_gain, doc_lengths, mixer_cot
+        mixed_own, x_grad_own, bc_part = mamba_by_heads(
+            x_all, cot_all, b_all, c_all, decay_log, skip_gain, doc_lengths
         )
     else:
         mixer_out, x_grad, grad_b, grad_c, grad_decay = mamba_by_stretch(
@@ -322,13 +336,27 @@
         lambda number, carried: visit(number, carried, full_step),
         (query_zero, term_zero, term_zero),
     )
-    kv_total = lax.psum_scatter(
-        jnp.concatenate([term_key, term_value], axis=1), "seq", scatter_dimension=0, tiled=True
-    )
-    key_gradient_total = kv_total[:, : groups * HEAD_SIZE]
-    value_gradient_total = kv_total[:, groups * HEAD_SIZE :]
+    kv_terms = jnp.concatenate([term_key, term_value], axis=1).astype(jnp.bfloat16)
+    kv_width = kv_terms.shape[1]
     if by_heads:
-        bc_sum = lax.psum_scatter(bc_part, "seq", scatter_dimension=0, tiled=True)
+        sent = jnp.concatenate(
+            [
+                mixed_own.reshape(seq_count, tokens, own_width),
+                x_grad_own.reshape(seq_count, tokens, own_width),
+                kv_terms.reshape(seq_count, tokens, kv_width),
+                bc_part.astype(jnp.bfloat16).reshape(seq_count, tokens, bc_part.shape[1]),
+            ],
+            axis=2,
+        )
+        got = lax.all_to_all(sent, "seq", split_axis=0, concat_axis=0, tiled=True)
+
+        def from_owners(a):
+            return a.transpose(1, 0, 2).reshape(tokens, seq_count * own_width)
+
+        mixer_out = from_owners(got[:, :, :own_width])
+        x_grad = from_owners(got[:, :, own_width : 2 * own_width])
+        kv_total = jnp.sum(got[:, :, 2 * own_width : 2 * own_width + kv_width].astype(jnp.float32), axis=0)
+        bc_sum = jnp.sum(got[:, :, 2 * own_width + kv_width :].astype(jnp.float32), axis=0)
         grad_decay = bc_sum[:, 2 * state_width :].T
         bc_sum = bc_sum[:, : 2 * state_width]
         if lax.axis_size("head") == 2:
@@ -336,6 +364,17 @@
         else:
             bc_sum = lax.psum(bc_sum, "head")
         grad_b, grad_c = bc_sum[:, :state_width], bc_sum[:, state_width:]
+    else:
+        kv_terms = lax.all_to_all(
+            kv_terms.reshape(seq_count, tokens, kv_width),
+            "seq",
+            split_axis=0,
+            concat_axis=0,
+            tiled=True,
+        )
+        kv_total = jnp.sum(kv_terms.astype(jnp.float32), axis=0)
+    key_gradient_total = kv_total[:, : groups * HEAD_SIZE]
+    value_gradient_total = kv_total[:, groups * HEAD_SIZE :]
     attn_out = attention_table.reshape(tokens, groups * heads_per_group * HEAD_SIZE)
     q_grad = (
         (grad_query * logit_scale)

time: 260 us -> 243 us (0.935)
  between operations: 14.5 us -> 1.55 us
  local copies, waits for them, and re-layouts: 47.5 us -> 35.4 us
  matrix products: 29.7 us -> 38.4 us
  waiting for transfers between devices: 116 us -> 113 us
  starting transfers between devices: 25.7 us -> 28.5 us
    reduce_scatter x2 -> x0, waiting for transfers between devices: 51.7 us -> none  [the longest x1 51.7 us: on_device(): lax.psum_scatter(jnp.concatenate([term_key, term_value], axis=1), 'seq',...]
    all_to_all x2, waiting for transfers between devices: 63 us -> 111 us  [on_device(): got = lax.all_to_all(sent, 'seq', split_axis=0, concat_axis=0, tiled=True)]
    another operation x5 -> x3, local copies, waits for them, and re-layouts: 4.91 us -> 0.87 us  [the longest x1 2.04 us: mamba_by_heads(): jnp.stack([mixed.reshape(total, own * P_SIZE).astype(jnp.bfloat16), grad_...]
    while x2 -> x0, local copies, waits for them, and re-layouts: 3.96 us -> none  [on_device(): lax.fori_loop(0, blocks, lambda number, carried: visit(number, carried, f...]
    concatenate x3 -> x2, other arithmetic: 6.06 us -> 2.63 us  [the longest x1 1.7 us: on_device(): jnp.concatenate([by_owner(x_input), by_owner(mixer_cot), jnp.broadcast_to...]
    dot_general x3, matrix products: 4.38 us -> 7.36 us  [local_state(): jnp.einsum('hs,sn,shp->hnp', weights, b_float, inputs, precision=precise)]
    all_to_all x2, starting transfers between devices: 18.2 us -> 21 us  [on_device(): got = lax.all_to_all(sent, 'seq', split_axis=0, concat_axis=0, tiled=True)]
    reshape x2 -> x5, local copies, waits for them, and re-layouts: 3.13 us -> 5.23 us  [the longest x2 2.02 us: from_owners(): return a.transpose(1, 0, 2).reshape(tokens, seq_count * own_width)]
  transfers between devices with their start and end apart: 7 -> 4, of which waited for: 4 -> 3; matrix products, arithmetic and copies ran while one was open for 20% -> 7% of each run, Pallas kernels for 0% -> 0%
where the time goes in v7:
time: 243 us; the launch traced here: 242 us
  waiting for transfers between devices  113 us (47%)
  matrix products  38.4 us (16%)
  local copies, waits for them, and re-layouts  35.4 us (15%)
  starting transfers between devices  28.5 us (12%)
  other arithmetic  24.8 us (10%)
    all_to_all x2, waiting for transfers between devices, on_device(): got = lax.all_to_all(sent, 'seq', split_axis=0, concat_axis=0, tiled=True)  111 us
    all_to_all x2, starting transfers between devices, on_device(): got = lax.all_to_all(sent, 'seq', split_axis=0, concat_axis=0, tiled=True)  21 us
    unnamed x120, local copies, waits for them, and re-layouts  10.5 us
    dot_general x3, matrix products, mixer_whole(): state_in = jnp.einsum('kjh,jhnp->khnp', reach, summary, precision=precise)  7.69 us
    dot_general x3, matrix products, mixer_stretch(): inner = jnp.einsum('hts,shp->thp', kernel, inputs, precision=precise)  7.55 us
    all_to_all x1, starting transfers between devices, mamba_by_heads(): lax.all_to_all(decay_log, 'seq', split_axis=0, concat_axis=1, tiled=True)  7.45 us
    dot_general x3, matrix products, local_state(): jnp.einsum('hs,sn,shp->hnp', weights, b_float, inputs, precision=precise)  7.36 us
  transfers between devices with their start and end apart: 4, of which 3 were waited for; matrix products, arithmetic and copies ran while one was open for 7% of the time, Pallas kernels for 0%

profile of v7, /device:TPU:0, one launch (start us, length us, event | category | flops | bytes accessed | tf_op | source)
XLA Modules:
  0.0 242.1 jit_solution(11162361103191794006)
XLA Ops:
  0.7 7.5 %all-to-all-start.1 = ((f32[8,2,128]{2,1,0:T(2,128)}), f32[8,2,128]{2,1,0:T(2,128)S(1)}, u32[]{:S(2)}, u32[]{:S(2)}) async-start(f32[8,2,128]{2,1,0:T(2,128)} %bitcast.350), calls=%async_computation.1 | async-start | bytes 16384 | tf_op jit(solution)/shard_map/all_to_all | solution.py:117
  11.0 1.7 pad_maximum_fusion
  12.7 1.9 all-to-all-done.1
  14.6 4.4 %all-to-all-start = ((bf16[8,128,1280]{1,2,0:T(8,128)(2,1)}), bf16[8,128,1280]{1,2,0:T(8,128)(2,1)}, u32[]{:S(2)}, u32[]{:S(2)}) async-start(bf16[8,128,1280]{1,2,0:T(8,128)(2,1)} %pad_maximum_fusion), calls=%async_computation | async-start | bytes 5242880 | tf_op jit(solution)/shard_map/all_to_all | solution.py:215
  25.3 52.6 %all-to-all-done = bf16[8,128,1280]{1,2,0:T(8,128)(2,1)} async-done(((bf16[8,128,1280]{1,2,0:T(8,128)(2,1)}), bf16[8,128,1280]{1,2,0:T(8,128)(2,1)}, u32[]{:S(2)}, u32[]{:S(2)}) %all-to-all-start) | async-done | bytes 2621472 | tf_op jit(solution)/shard_map/all_to_all | solution.py:215
  81.9 2.2 fusion.93
  85.8 2.5 %copy.346 = f32[2,128,128,8]{2,3,1,0:T(8,128)} copy(f32[2,128,128,8]{1,2,0,3:T(8,128)} %convolution_bitcast_fusion.2) | data formatting | bytes 2097152 | tf_op jit(solution)/shard_map/transpose(jvp(kjh,jhnp->khnp))/transpose;transpose(jvp(vmap(tn,hnp->thp)))/transpose | solution.py:102
  88.3 2.3 convolution_bitcast_fusion.1
  90.7 1.8 fusion.55
  94.5 2.8 %convolution_bitcast_fusion.6 = f32[8,8,2]{1,0,2:T(8,128)S(1)} fusion(f32[2,128,128,8]{2,3,1,0:T(8,128)S(1)} %copy-done, f32[8,2,128,128]{3,2,1,0:T(8,128)S(1)} %fusion.32), kind=kOutput, calls=%fused_computation.85 | convolution fusion | flops 25165824 | bytes 2097664 | tf_op jit(solution)/shard_map/transpose(jvp(kjh,jhnp->khnp))/dot_general | solution.py:102
  97.2 2.6 %convolution_bitcast_fusion.3 = f32[8,2,128,128]{3,0,2,1:T(8,128)} fusion(f32[8,2,128,128]{3,2,1,0:T(8,128)S(1)} %fusion.32, f32[8,8,2]{1,0,2:T(8,128)S(1)} %stack.2), kind=kOutput, calls=%fused_computation.68 | convolution fusion | flops 25165824 | bytes 2097664 | tf_op jit(solution)/shard_map/jvp(kjh,jhnp->khnp)/dot_general | solution.py:102
  99.8 2.3 while.51
  99.8 2.3 conditional.9
  103.6 4.7 %while.52 = (s32[]{:T(128)}, f32[128,2,4,128]{0,3,2,1:T(8,128)}, s32[]{:T(128)}, bf16[1024,256]{0,1:T(8,128)(2,1)S(1)}, s32[4]{0:T(128)}, /*index=5*/s32[128]{0:...) while((s32[]{:T(128)}, f32[128,2,4,128]{0,3,2,1:T(8,128)}, ...), condition=%wide.region_17.18_spmd.clone, body=%wide.region_12.17_spmd.clone.sunk | while | flops 271390848 | bytes 3031901 | solution.py:295
  103.6 4.7 %conditional.10 = (f32[128,2,4,128]{0,3,2,1:T(8,128)}) conditional(s32[]{:T(128)} %convert_element_type.253, f32[128,2,4,128]{0,3,2,1:T(8,128)} %get-tuple-element.1359, (s32[]{:T(128)}, bf16[1024,256]{0,1:T(8,128)(2,1)S(1)}, s32[]{:T(128)}, s32[4]{0:T(128)}, s32[128]{0:T(128)S(1)}, /*index=5*/bf16[1024,256]{0,1:T(8,128)(2,1)S(1)}, ...), branch_computations={%region_13.13_spmd, %region_14.16_spmd} | conditional | flops 271390848 | bytes 3031158 | solution.py:261
  105.5 2.8 %fusion.13 = f32[128,2,4,128]{0,3,2,1:T(8,128)} fusion(f32[128,2,4,128]{0,3,2,1:T(8,128)} %get-tuple-element.621, bf16[512,2,128,1]{0,2,3,1:T(8,128)(2,1)} %bitcast.317, bf16[512,2,128,1]{0,2,3,1:T(8,128)(2,1)S(1)} %bitcast.316, bf16[128,2,4,128]{3,0,2,1:T(8,128)(2,1)S(1)} %get-tuple-element.628, f32[2,4,128]{2,1,0:T(4,128)} %get-tuple-element.629, ...), kind=kOutput, calls=%fused_computation.19 | convolution fusion | flops 271187968 | bytes 1904640 | tf_op jit(solution)/shard_map/while/body/eval_jaxpr/cond/branch_1_fun/grtk,kgd->tgrd/dot_general | solution.py:291
  108.4 1.8 fusion.66
  112.0 5.9 %while.53 = (s32[]{:T(128)}, f32[128,2,4,128]{0,3,2,1:T(8,128)S(1)}, bf16[1024,256]{0,1:T(8,128)(2,1)}, bf16[1024,256]{0,1:T(8,128)(2,1)}, s32[]{:T(128)}, /*ind...) while((s32[]{:T(128)}, ...), condition=%wide.region_23.24_spmd.clone, body=%wide.region_18.23_spmd.clone.sunk | while | flops 675616896 | bytes 23483460 | solution.py:333
  112.1 5.9 %conditional.11 = ((f32[128,2,4,128]{0,3,2,1:T(8,128)S(1)}, bf16[1024,256]{0,1:T(8,128)(2,1)}, bf16[1024,256]{0,1:T(8,128)(2,1)})) conditional(s32[]{:T(128)} %convert_element_type.254, (f32[128,2,4,128]{0,3,2,1:T(8,128)S(1)}, bf16[1024,256]{0,1:T(8,128)(2,1)}, bf16[1024,256]{0,1:T(8,128)(2,1)}) %tuple.198, (s32[]{:T(128)}, ...), branch_computations={%region_19.19_spmd, %region_20.22_spmd} | conditional | flops 675616896 | bytes 23482630 | solution.py:261
  119.3 3.2 %fusion.65 = (f32[8,2,128]{2,1,0:T(2,128)S(1)}, f32[8,2,128]{2,1,0:T(2,128)S(1)}, f32[8,128,128]{2,1,0:T(8,128)}) fusion(f32[8,128,128]{2,1,0:T(8,128)S(1)} %fusion.99, f32[8,2,128]{2,1,0:T(2,128)S(1)} %copy-done.28, pred[8,128,128]{2,1,0:T(8,128)(4,1)} %compare_and_fusion.3, bf16[8,2,128,128]{3,2,1,0:T(8,128)(2,1)} %bitcast.319, ...), kind=kOutput, calls=%fused_computation.101 | convolution fusion | flops 69332992 | bytes 2252800 | tf_op jit(solution)/shard_map/transpose(jvp(vmap(hts,shp->thp)))/dot_general | solution.py:67
  122.5 2.1 fusion.40
  124.6 4.3 %fusion.44 = bf16[8,128,2,128]{1,3,2,0:T(8,128)(2,1)} fusion(f32[8,128,2,128]{1,3,2,0:T(8,128)} %fusion.40, f32[8,2,128,128]{3,0,2,1:T(8,128)S(1)} %convolution_bitcast_fusion.1, f32[8,128,2]{1,2,0:T(2,128)S(1)} %copy.341, f32[8,128,128]{2,1,0:T(8,128)S(1)} %copy-done.7), kind=kOutput, calls=%fused_computation.75 | convolution fusion | flops 403439616 | bytes 3153920 | tf_op jit(solution)/shard_map/transpose(jvp(vmap(hs,sn,shp->hnp)))/dot_general | solution.py:53
  128.9 2.2 fusion.54
  132.8 2.7 %fusion.48 = f32[8,128,128]{1,2,0:T(8,128)} fusion(f32[8,2,128,128]{2,3,1,0:T(8,128)S(1)} %copy.345, bf16[8,128,2,128]{1,3,2,0:T(8,128)(2,1)S(1)} %bitcast.322, f32[8,128,2]{1,2,0:T(2,128)S(1)} %copy.340), kind=kOutput, calls=%fused_computation.77 | convolution fusion | flops 403177472 | bytes 2105344 | tf_op jit(solution)/shard_map/transpose(jvp(vmap(tn,hnp->thp)))/dot_general | solution.py:69
  135.5 1.8 fusion.53
  137.5 2.3 fusion.43
  141.1 2.0 constant_dynamic-update-slice_fusion.3
  143.2 2.5 %reduce_window_sum.47 = f32[8,2,128]{2,0,1:T(8,128)S(1)} reduce-window(f32[8,2,128]{2,0,1:T(8,128)S(1)} %get-tuple-element.1064, f32[]{:T(128)} %constant.152.clone.1), window={size=1x1x128 pad=0_0x0_0x0_127}, to_apply=%region_36.37 | reduce-window | flops 260096 | bytes 16388 | tf_op jit(solution)/shard_map/transpose(jvp(jit(cumsum)))/reduce_window_sum | solution.py:91
  145.7 2.7 %reduce_window_sum.46 = f32[8,2,128]{2,0,1:T(8,128)S(1)} reduce-window(f32[8,2,128]{2,0,1:T(8,128)S(1)} %get-tuple-element.1065, f32[]{:T(128)} %constant.152.clone.1), window={size=1x1x128 pad=0_0x0_0x0_127}, to_apply=%region_28.29 | reduce-window | flops 260096 | bytes 16388 | tf_op jit(solution)/shard_map/transpose(jvp(vmap(jit(cumsum))))/reduce_window_sum | solution.py:45
  149.3 2.0 bitcast_dynamic-update-slice_fusion.1
  155.5 16.6 %all-to-all-start.2 = ((bf16[8,128,1296]{1,2,0:T(8,128)(2,1)}), bf16[8,128,1296]{1,2,0:T(8,128)(2,1)}, u32[]{:S(2)}, u32[]{:S(2)}) async-start(bf16[8,128,1296]{1,2,0:T(8,128)(2,1)} %bitcast_dynamic-update-slice_fusion.2), calls=%async_computation.2 | async-start | bytes 5308416 | tf_op jit(solution)/shard_map/all_to_all | solution.py:351
  173.9 58.7 %all-to-all-done.2 = bf16[8,128,1296]{1,2,0:T(8,128)(2,1)} async-done(((bf16[8,128,1296]{1,2,0:T(8,128)(2,1)}), bf16[8,128,1296]{1,2,0:T(8,128)(2,1)}, u32[]{:S(2)}, u32[]{:S(2)}) %all-to-all-start.2) | async-done | bytes 2654240 | tf_op jit(solution)/shard_map/all_to_all | solution.py:351
  (257 shorter events, 50.5 us)
Async XLA Ops:
  0.6 9.9 %copy-start.21 = (bf16[128,2048]{1,0:T(8,128)(2,1)S(1)}, bf16[128,2048]{1,0:T(8,128)(2,1)}, u32[]{:S(2)}) copy-start(bf16[128,2048]{1,0:T(8,128)(2,1)} %param.32) | copy-start | bytes 1572868
  0.7 14.0 %all-to-all-start.1 = ((f32[8,2,128]{2,1,0:T(2,128)}), f32[8,2,128]{2,1,0:T(2,128)S(1)}, u32[]{:S(2)}, u32[]{:S(2)}) async-start(f32[8,2,128]{2,1,0:T(2,128)} %bitcast.350), calls=%async_computation.1 | async-start | bytes 16384 | tf_op jit(solution)/shard_map/all_to_all | solution.py:117
  12.7 7.1 %copy-start.24 = (bf16[128,1024]{1,0:T(8,128)(2,1)S(1)}, bf16[128,1024]{1,0:T(8,128)(2,1)}, u32[]{:S(2)}) copy-start(bf16[128,1024]{1,0:T(8,128)(2,1)} %param.33) | copy-start | bytes 786436
  12.7 7.3 %copy-start.25 = (bf16[128,1024]{1,0:T(8,128)(2,1)S(1)}, bf16[128,1024]{1,0:T(8,128)(2,1)}, u32[]{:S(2)}) copy-start(bf16[128,1024]{1,0:T(8,128)(2,1)} %param.29) | copy-start | bytes 786436
  12.7 7.7 %copy-start.55 = (f32[16]{0:T(128)S(1)}, f32[16]{0:T(128)}, u32[]{:S(2)}) copy-start(f32[16]{0:T(128)} %param.27) | copy-start | bytes 196
  14.6 63.3 %all-to-all-start = ((bf16[8,128,1280]{1,2,0:T(8,128)(2,1)}), bf16[8,128,1280]{1,2,0:T(8,128)(2,1)}, u32[]{:S(2)}, u32[]{:S(2)}) async-start(bf16[8,128,1280]{1,2,0:T(8,128)(2,1)} %pad_maximum_fusion), calls=%async_computation | async-start | bytes 5242880 | tf_op jit(solution)/shard_map/all_to_all | solution.py:215
  21.0 58.6 %copy-start.31 = (pred[8]{0:T(512)(128)(4,1)}, pred[8]{0:T(512)(128)(4,1)S(1)}, u32[]{:S(2)}) copy-start(pred[8]{0:T(512)(128)(4,1)S(1)} %iota_compare_fusion.7) | copy-start | bytes 28
  21.4 58.2 %copy-start.35 = (pred[8]{0:T(512)(128)(4,1)}, pred[8]{0:T(512)(128)(4,1)S(1)}, u32[]{:S(2)}) copy-start(pred[8]{0:T(512)(128)(4,1)S(1)} %get-tuple-element.1091) | copy-start | bytes 28
  21.4 58.2 %copy-start.29 = (pred[8]{0:T(512)(128)(4,1)}, pred[8]{0:T(512)(128)(4,1)S(1)}, u32[]{:S(2)}) copy-start(pred[8]{0:T(512)(128)(4,1)S(1)} %get-tuple-element.1089) | copy-start | bytes 28
  21.4 58.2 %copy-start.49 = (pred[8]{0:T(512)(128)(4,1)}, pred[8]{0:T(512)(128)(4,1)S(1)}, u32[]{:S(2)}) copy-start(pred[8]{0:T(512)(128)(4,1)S(1)} %get-tuple-element.1088) | copy-start | bytes 28
  21.4 58.2 %copy-start.37 = (f32[8]{0:T(128)}, f32[8]{0:T(128)S(1)}, u32[]{:S(2)}) copy-start(f32[8]{0:T(128)S(1)} %get-tuple-element.1086) | copy-start | bytes 100
  21.4 58.2 %copy-start.51 = (pred[8]{0:T(512)(128)(4,1)}, pred[8]{0:T(512)(128)(4,1)S(1)}, u32[]{:S(2)}) copy-start(pred[8]{0:T(512)(128)(4,1)S(1)} %get-tuple-element.1087) | copy-start | bytes 28
  21.5 58.2 %copy-start.39 = (f32[8]{0:T(128)}, f32[8]{0:T(128)S(1)}, u32[]{:S(2)}) copy-start(f32[8]{0:T(128)S(1)} %get-tuple-element.1085) | copy-start | bytes 100
  21.5 58.2 %copy-start.41 = (f32[8]{0:T(128)}, f32[8]{0:T(128)S(1)}, u32[]{:S(2)}) copy-start(f32[8]{0:T(128)S(1)} %get-tuple-element.1083) | copy-start | bytes 100
  21.5 58.2 %copy-start.53 = (f32[8]{0:T(128)}, f32[8]{0:T(128)S(1)}, u32[]{:S(2)}) copy-start(f32[8]{0:T(128)S(1)} %get-tuple-element.1081) | copy-start | bytes 100
  21.9 57.8 %copy-start.33 = (f32[8]{0:T(128)}, f32[8]{0:T(128)S(1)}, u32[]{:S(2)}) copy-start(f32[8]{0:T(128)S(1)} %convert_reduce_fusion.6) | copy-start | bytes 100
  24.5 55.1 %copy-start.43 = (f32[2]{0:T(128)}, f32[2]{0:T(128)S(1)}, u32[]{:S(2)}) copy-start(f32[2]{0:T(128)S(1)} %get-tuple-element.961) | copy-start | bytes 28
  112.0 7.2 %copy-start.28 = (f32[8,2,128]{2,1,0:T(2,128)S(1)}, f32[8,2,128]{2,1,0:T(2,128)}, u32[]{:S(2)}) copy-start(f32[8,2,128]{2,1,0:T(2,128)} %copy.335) | copy-start | bytes 24580
  119.2 5.3 %copy-start.22 = (f32[8,128,128]{2,1,0:T(8,128)}, f32[8,128,128]{2,1,0:T(8,128)S(1)}, u32[]{:S(2)}) copy-start(f32[8,128,128]{2,1,0:T(8,128)S(1)} %fusion.99) | copy-start | bytes 1572868
  131.2 4.3 %copy-start.2 = (bf16[1024,128]{1,0:T(8,128)(2,1)S(1)}, bf16[1024,128]{1,0:T(8,128)(2,1)}, u32[]{:S(2)}) copy-start(bf16[1024,128]{1,0:T(8,128)(2,1)} %copy-done.1) | copy-start | bytes 786436
  132.8 4.6 %copy-start.9 = (bf16[8,128,256]{1,2,0:T(8,128)(2,1)S(1)}, bf16[8,128,256]{1,2,0:T(8,128)(2,1)}, u32[]{:S(2)}) copy-start(bf16[8,128,256]{1,2,0:T(8,128)(2,1)} %get-tuple-element.1055) | copy-start | bytes 1572868
  132.8 4.6 %copy-start.23 = (f32[8,128,128]{2,1,0:T(8,128)S(1)}, f32[8,128,128]{2,1,0:T(8,128)}, u32[]{:S(2)}) copy-start(f32[8,128,128]{2,1,0:T(8,128)} %copy-done.22) | copy-start | bytes 1572868
  132.8 4.6 %copy-start.27 = (pred[8,128,128]{2,1,0:T(8,128)(4,1)S(1)}, pred[8,128,128]{2,1,0:T(8,128)(4,1)}, u32[]{:S(2)}) copy-start(pred[8,128,128]{2,1,0:T(8,128)(4,1)} %compare_and_fusion.3) | copy-start | bytes 393220
  132.8 4.6 %copy-start.57 = (f32[2]{0:T(128)S(1)}, f32[2]{0:T(128)}, u32[]{:S(2)}) copy-start(f32[2]{0:T(128)} %dynamic_slice.18) | copy-start | bytes 28
  137.5 11.0 %copy-start.18 = (bf16[8,128,2,128]{1,3,2,0:T(8,128)(2,1)S(1)}, bf16[8,128,2,128]{1,3,2,0:T(8,128)(2,1)}, u32[]{:S(2)}) copy-start(bf16[8,128,2,128]{1,3,2,0:T(8,128)(2,1)} %fusion.44) | copy-start | bytes 1572868
  139.8 11.6 %copy-start.15 = (bf16[1024,256]{0,1:T(8,128)(2,1)S(1)}, bf16[1024,256]{0,1:T(8,128)(2,1)}, u32[]{:S(2)}) copy-start(bf16[1024,256]{0,1:T(8,128)(2,1)} %get-tuple-element.691) | copy-start | bytes 1572868
  141.1 11.2 %copy-start.10 = (f32[8,128,128]{2,1,0:T(8,128)S(1)}, f32[8,128,128]{2,1,0:T(8,128)}, u32[]{:S(2)}) copy-start(f32[8,128,128]{2,1,0:T(8,128)} %get-tuple-element.952) | copy-start | bytes 1572868
  141.1 11.2 %copy-start.11 = (f32[8,128,128]{1,2,0:T(8,128)S(1)}, f32[8,128,128]{1,2,0:T(8,128)}, u32[]{:S(2)}) copy-start(f32[8,128,128]{1,2,0:T(8,128)} %fusion.54) | copy-start | bytes 1572868
  149.3 4.1 %copy-start.12 = (f32[8,128,128]{1,2,0:T(8,128)S(1)}, f32[8,128,128]{1,2,0:T(8,128)}, u32[]{:S(2)}) copy-start(f32[8,128,128]{1,2,0:T(8,128)} %fusion.48) | copy-start | bytes 1572868
  155.5 16.6 %copy-start.20 = (bf16[128,2,4,128]{0,3,2,1:T(8,128)(2,1)S(1)}, bf16[128,2,4,128]{0,3,2,1:T(8,128)(2,1)}, u32[]{:S(2)}) copy-start(bf16[128,2,4,128]{0,3,2,1:T(8,128)(2,1)} %get-tuple-element.1039) | copy-start | bytes 786436
  155.5 77.1 %all-to-all-start.2 = ((bf16[8,128,1296]{1,2,0:T(8,128)(2,1)}), bf16[8,128,1296]{1,2,0:T(8,128)(2,1)}, u32[]{:S(2)}, u32[]{:S(2)}) async-start(bf16[8,128,1296]{1,2,0:T(8,128)(2,1)} %bitcast_dynamic-update-slice_fusion.2), calls=%async_computation.2 | async-start | bytes 5308416 | tf_op jit(solution)/shard_map/all_to_all | solution.py:351
  235.2 5.5 %collective-permute-start = (f32[128,256]{0,1:T(8,128)S(1)}, f32[128,256]{0,1:T(8,128)S(1)}, u32[]{:S(2)}, u32[]{:S(2)}) collective-permute-start(f32[128,256]{0,1:T(8,128)S(1)} %slice.119), channel_id=1, source_target_pairs={{0,1},{1,0},{2,3},{3,2},{4,5},{5,4},{6,7},{7,6},{8,9},{9,8},{10,11... | collective-permute-start | bytes 393224 | tf_op jit(solution)/shard_map/ppermute | solution.py:363
  (30 other events, 76.8 us)

commit v8 on v7

--- a/solution.py
+++ b/solution.py
@@ -195,8 +195,6 @@
     by_heads = heads_here % lax.axis_size("seq") == 0
     key_width = attention_key_rows.shape[1]
     state_width = b_rows.shape[1]
-    pieces = [attention_key_rows, values] + ([b_rows, c_rows] if by_heads else [])
-    joined = jnp.concatenate(pieces, axis=1)
     seq_count = lax.axis_size("seq")
     if by_heads:
         own_width = heads_here // seq_count * P_SIZE
@@ -204,24 +202,26 @@
         def by_owner(a):
             return a.reshape(tokens, seq_count, own_width).transpose(1, 0, 2)
 
+        def spread(a):
+            return jnp.broadcast_to(a[None], (seq_count,) + a.shape)
+
         sent = jnp.concatenate(
-            [
-                by_owner(x_input),
-                by_owner(mixer_cot),
-                jnp.broadcast_to(joined[None], (seq_count,) + joined.shape),
-            ],
-            axis=2,
+            [by_owner(x_input), by_owner(mixer_cot), spread(b_rows), spread(c_rows)], axis=2
         )
         got = lax.all_to_all(sent, "seq", split_axis=0, concat_axis=0, tiled=True)
         x_all = got[:, :, :own_width].reshape(total_len, own_width)
         cot_all = got[:, :, own_width : 2 * own_width].reshape(total_len, own_width)
-        gathered = got[:, :, 2 * own_width :].reshape(total_len, joined.shape[1])
+        b_all = got[:, :, 2 * own_width : 2 * own_width + state_width].reshape(total_len, -1)
+        c_all = got[:, :, 2 * own_width + state_width :].reshape(total_len, -1)
+        kv_sent = spread(jnp.concatenate([attention_key_rows, values], axis=1))
+        gathered = lax.all_to_all(kv_sent, "seq", split_axis=0, concat_axis=0, tiled=True)
+        gathered = gathered.reshape(total_len, 2 * key_width)
     else:
-        gathered = lax.all_gather(joined, "seq", axis=0, tiled=True)
+        gathered = lax.all_gather(
+            jnp.concatenate([attention_key_rows, values], axis=1), "seq", axis=0, tiled=True
+        )
     key_all, value_all = gathered[:, :key_width], gathered[:, key_width : 2 * key_width]
     if by_heads:
-        b_all = gathered[:, 2 * key_width : 2 * key_width + state_width]
-        c_all = gathered[:, 2 * key_width + state_width :]
         mixed_own, x_grad_own, bc_part = mamba_by_heads(
             x_all, cot_all, b_all, c_all, decay_log, skip_gain, doc_lengths
         )
@@ -343,20 +343,26 @@
             [
                 mixed_own.reshape(seq_count, tokens, own_width),
                 x_grad_own.reshape(seq_count, tokens, own_width),
-                kv_terms.reshape(seq_count, tokens, kv_width),
                 bc_part.astype(jnp.bfloat16).reshape(seq_count, tokens, bc_part.shape[1]),
             ],
             axis=2,
         )
         got = lax.all_to_all(sent, "seq", split_axis=0, concat_axis=0, tiled=True)
+        kv_got = lax.all_to_all(
+            kv_terms.reshape(seq_count, tokens, kv_width),
+            "seq",
+            split_axis=0,
+            concat_axis=0,
+            tiled=True,
+        )
 
         def from_owners(a):
             return a.transpose(1, 0, 2).reshape(tokens, seq_count * own_width)
 
         mixer_out = from_owners(got[:, :, :own_width])
         x_grad = from_owners(got[:, :, own_width : 2 * own_width])
-        kv_total = jnp.sum(got[:, :, 2 * own_width : 2 * own_width + kv_width].astype(jnp.float32), axis=0)
-        bc_sum = jnp.sum(got[:, :, 2 * own_width + kv_width :].astype(jnp.float32), axis=0)
+        kv_total = jnp.sum(kv_got.astype(jnp.float32), axis=0)
+        bc_sum = jnp.sum(got[:, :, 2 * own_width :].astype(jnp.float32), axis=0)
         grad_decay = bc_sum[:, 2 * state_width :].T
         bc_sum = bc_sum[:, : 2 * state_width]
         if lax.axis_size("head") == 2:

time: 243 us -> 189 us (0.78)
  waiting for transfers between devices: 113 us -> 66.5 us
  matrix products: 38.4 us -> 34.7 us
  other arithmetic: 24.8 us -> 22.2 us
    all_to_all x2, waiting for transfers between devices: 111 us -> 43.8 us  [on_device(): got = lax.all_to_all(sent, 'seq', split_axis=0, concat_axis=0, tiled=True)]
    all_to_all x0 -> x2, waiting for transfers between devices: none -> 17.2 us  [the longest x1 17.2 us: on_device(): lax.all_to_all(kv_sent, 'seq', split_axis=0, concat_axis=0, tiled=True)]
    all_to_all x2, starting transfers between devices: 21 us -> 10.4 us  [on_device(): got = lax.all_to_all(sent, 'seq', split_axis=0, concat_axis=0, tiled=True)]
    all_to_all x0 -> x2, starting transfers between devices: none -> 8.74 us  [the longest x1 5.05 us: on_device(): lax.all_to_all(kv_terms.reshape(seq_count, tokens, kv_width), 'seq', spli...]
    all_to_all x1, waiting for transfers between devices: 1.9 us -> 5.5 us  [mamba_by_heads(): lax.all_to_all(decay_log, 'seq', split_axis=0, concat_axis=1, tiled=True)]
    unnamed x120 -> x142, local copies, waits for them, and re-layouts: 10.5 us -> 11.6 us
  transfers between devices with their start and end apart: 4 -> 6, of which waited for: 3 -> 4; matrix products, arithmetic and copies ran while one was open for 7% -> 47% of each run, Pallas kernels for 0% -> 0%
where the time goes in v8:
time: 189 us; the launch traced here: 188 us
  waiting for transfers between devices  66.5 us (35%)
  local copies, waits for them, and re-layouts  35.4 us (19%)
  matrix products  34.7 us (18%)
  starting transfers between devices  26.7 us (14%)
  other arithmetic  22.2 us (12%)
    all_to_all x2, waiting for transfers between devices, on_device(): got = lax.all_to_all(sent, 'seq', split_axis=0, concat_axis=0, tiled=True)  43.8 us
    all_to_all x1, waiting for transfers between devices, on_device(): lax.all_to_all(kv_sent, 'seq', split_axis=0, concat_axis=0, tiled=True)  17.2 us
    unnamed x142, local copies, waits for them, and re-layouts  11.6 us
    all_to_all x2, starting transfers between devices, on_device(): got = lax.all_to_all(sent, 'seq', split_axis=0, concat_axis=0, tiled=True)  10.4 us
    all_to_all x1, starting transfers between devices, mamba_by_heads(): lax.all_to_all(decay_log, 'seq', split_axis=0, concat_axis=1, tiled=True)  7.45 us
    dot_general x3, matrix products, mixer_whole(): state_in = jnp.einsum('kjh,jhnp->khnp', reach, summary, precision=precise)  6.41 us
    dot_general x3, matrix products, local_state(): jnp.einsum('hs,sn,shp->hnp', weights, b_float, inputs, precision=precise)  6.4 us
    dot_general x3, matrix products, mixer_stretch(): inner = jnp.einsum('hts,shp->thp', kernel, inputs, precision=precise)  6.15 us
  transfers between devices with their start and end apart: 6, of which 4 were waited for; matrix products, arithmetic and copies ran while one was open for 47% of the time, Pallas kernels for 0%

profile of v8, /device:TPU:0, one launch (start us, length us, event | category | flops | bytes accessed | tf_op | source)
XLA Modules:
  0.0 187.8 jit_solution(15656294747974018082)
XLA Ops:
  0.7 7.5 %all-to-all-start.1 = ((f32[8,2,128]{2,1,0:T(2,128)}), f32[8,2,128]{2,1,0:T(2,128)S(1)}, u32[]{:S(2)}, u32[]{:S(2)}) async-start(f32[8,2,128]{2,1,0:T(2,128)} %bitcast.324), calls=%async_computation.1 | async-start | bytes 16384 | tf_op jit(solution)/shard_map/all_to_all | solution.py:117
  9.1 5.5 %all-to-all-done.1 = f32[8,2,128]{2,1,0:T(2,128)S(1)} async-done(((f32[8,2,128]{2,1,0:T(2,128)}), f32[8,2,128]{2,1,0:T(2,128)S(1)}, u32[]{:S(2)}, u32[]{:S(2)}) %all-to-all-start.1) | async-done | bytes 8224 | tf_op jit(solution)/shard_map/all_to_all | solution.py:117
  15.7 3.7 %all-to-all-start.3 = ((bf16[8,128,512]{1,2,0:T(8,128)(2,1)}), bf16[8,128,512]{1,2,0:T(8,128)(2,1)S(1)}, u32[]{:S(2)}, u32[]{:S(2)}) async-start(bf16[8,128,512]{1,2,0:T(8,128)(2,1)} %broadcast_in_dim.296), calls=%async_computation.3 | async-start | bytes 2097152 | tf_op jit(solution)/shard_map/all_to_all | solution.py:217
  24.6 2.3 %pad_maximum_fusion = bf16[8,128,768]{2,1,0:T(8,128)(2,1)} fusion(bf16[8,128,128]{2,1,0:T(8,128)(2,1)S(1)} %broadcast_in_dim.265, bf16[8,128,128]{2,1,0:T(8,128)(2,1)S(1)} %broadcast_in_dim.264, bf16[8,128,256]{2,1,0:T(8,128)(2,1)} %bitcast.300, bf16[8,128,256]{2,1,0:T(8,128)(2,1)S(1)} %bitcast.299), kind=kLoop, calls=%fused_computation.54 | loop fusion | flops 6291456 | bytes 3145728 | tf_op jit(solution)/shard_map/concatenate | solution.py:208
  27.0 17.2 %all-to-all-done.3 = bf16[8,128,512]{1,2,0:T(8,128)(2,1)S(1)} async-done(((bf16[8,128,512]{1,2,0:T(8,128)(2,1)}), bf16[8,128,512]{1,2,0:T(8,128)(2,1)S(1)}, u32[]{:S(2)}, u32[]{:S(2)}) %all-to-all-start.3) | async-done | bytes 1048608 | tf_op jit(solution)/shard_map/all_to_all | solution.py:217
  44.2 4.3 %all-to-all-start = ((bf16[8,128,768]{2,1,0:T(8,128)(2,1)}), bf16[8,128,768]{2,1,0:T(8,128)(2,1)}, u32[]{:S(2)}, u32[]{:S(2)}) async-start(bf16[8,128,768]{2,1,0:T(8,128)(2,1)} %pad_maximum_fusion), calls=%async_computation | async-start | bytes 3145728 | tf_op jit(solution)/shard_map/all_to_all | solution.py:211
  56.9 2.4 %while.51 = (s32[]{:T(128)}, f32[2,4,128]{2,1,0:T(4,128)S(1)}, f32[2,4,128]{2,1,0:T(4,128)S(1)}, s32[]{:T(128)}, s32[4]{0:T(128)S(1)}, /*index=5*/s32[128]{0:T(1...) while((s32[]{:T(128)}, f32[2,4,128]{2,1,0:T(4,128)S(1)}, ...), condition=%wide.region_24.25_spmd.clone, body=%wide.region_17.24_spmd.clone.sunk | while | flops 138616976 | bytes 5505893 | solution.py:278
  57.0 2.3 %conditional.9 = ((f32[2,4,128]{2,1,0:T(4,128)S(1)}, f32[2,4,128]{2,1,0:T(4,128)S(1)})) conditional(s32[]{:T(128)} %convert_element_type.252, (f32[2,4,128]{2,1,0:T(4,128)S(1)}, f32[2,4,128]{2,1,0:T(4,128)S(1)}) %tuple.197, (s32[]{:T(128)}, s32[]{:T(128)}, s32[4]{0:T(128)S(1)}, s32[128]{0:T(128)}, bf16[1024,256]{0,1:T(8,128)(2,1)S(1)}, ...), branch_computations={%region_18.18_spmd, %region_19.23_spmd} | conditional | flops 138616976 | bytes 5505158 | solution.py:261
  59.4 2.3 %while.52 = (s32[]{:T(128)}, f32[128,2,4,128]{0,3,2,1:T(8,128)S(1)}, s32[]{:T(128)}, bf16[1024,256]{0,1:T(8,128)(2,1)S(1)}, s32[4]{0:T(128)S(1)}, /*index=5*/s32...) while((s32[]{:T(128)}, ...), condition=%wide.region_30.31_spmd.clone, body=%wide.region_25.30_spmd.clone.sunk | while | flops 271390848 | bytes 3031893 | solution.py:295
  59.4 2.2 %conditional.10 = (f32[128,2,4,128]{0,3,2,1:T(8,128)S(1)}) conditional(s32[]{:T(128)} %convert_element_type.253, f32[128,2,4,128]{0,3,2,1:T(8,128)S(1)} %get-tuple-element.1413, (s32[]{:T(128)}, bf16[1024,256]{0,1:T(8,128)(2,1)S(1)}, s32[]{:T(128)}, s32[4]{0:T(128)S(1)}, s32[128]{0:T(128)}, /*index=5*/bf16[1024,256]{0,1:T(8,128)(2,1)S(1)}, ...), branch_computations={%region_26.26_spmd, %region_27.29_spmd} | conditional | flops 271390848 | bytes 3031158 | solution.py:261
  62.7 8.1 %while.53 = (s32[]{:T(128)}, f32[128,2,4,128]{0,3,2,1:T(8,128)S(1)}, bf16[1024,256]{0,1:T(8,128)(2,1)S(1)}, bf16[1024,256]{0,1:T(8,128)(2,1)S(1)}, s32[]{:T(128)...) while((s32[]{:T(128)}, ...), condition=%wide.region_37.38_spmd.clone, body=%wide.region_32.37_spmd.clone.sunk | while | flops 675616896 | bytes 15094733 | solution.py:333
  63.3 6.9 %conditional.11 = ((f32[128,2,4,128]{0,3,2,1:T(8,128)S(1)}, bf16[1024,256]{0,1:T(8,128)(2,1)S(1)}, bf16[1024,256]{0,1:T(8,128)(2,1)S(1)})) conditional(s32[]{:T(128)} %convert_element_type.254, (f32[128,2,4,128]{0,3,2,1:T(8,128)S(1)}, bf16[1024,256]{0,1:T(8,128)(2,1)S(1)}, bf16[1024,256]{0,1:T(8,128)(2,1)S(1)}) %tuple.202, (s32[]{:T(128)}, ...), branch_computations={%region_33.33_spmd, %region_34.36_spmd} | conditional | flops 675616896 | bytes 15093910 | solution.py:261
  72.6 12.3 %all-to-all-done = bf16[8,128,768]{2,1,0:T(8,128)(2,1)} async-done(((bf16[8,128,768]{2,1,0:T(8,128)(2,1)}), bf16[8,128,768]{2,1,0:T(8,128)(2,1)}, u32[]{:S(2)}, u32[]{:S(2)}) %all-to-all-start) | async-done | bytes 1572896 | tf_op jit(solution)/shard_map/all_to_all | solution.py:211
  84.9 5.1 %all-to-all-start.4 = ((bf16[8,128,512]{1,2,0:T(8,128)(2,1)}), bf16[8,128,512]{1,2,0:T(8,128)(2,1)}, u32[]{:S(2)}, u32[]{:S(2)}) async-start(bf16[8,128,512]{1,2,0:T(8,128)(2,1)} %copy.470), calls=%async_computation.4 | async-start | bytes 2097152 | tf_op jit(solution)/shard_map/all_to_all | solution.py:351
  89.9 2.1 %fusion.102 = (bf16[8,128,256]{2,1,0:T(8,128)(2,1)S(1)}, bf16[8,128,256]{2,1,0:T(8,128)(2,1)}) fusion(bf16[8,128,768]{2,1,0:T(8,128)(2,1)} %all-to-all-done), kind=kLoop, calls=%fused_computation.217 | loop fusion | bytes 2097152 | tf_op jit(solution)/shard_map/slice | solution.py:213
  94.3 2.0 %copy.543 = bf16[8,128,256]{1,2,0:T(8,128)(2,1)} copy(bf16[8,128,256]{2,1,0:T(8,128)(2,1)} %get-tuple-element.1111) | data formatting | bytes 1048576 | tf_op jit(solution)/shard_map/jvp()/reshape;reshape | solution.py:85
  100.4 1.8 fusion.55
  103.8 2.8 %convolution_bitcast_fusion.6 = f32[8,8,2]{1,0,2:T(8,128)S(1)} fusion(f32[2,128,128,8]{2,3,1,0:T(8,128)S(1)} %copy.428, f32[8,2,128,128]{3,2,1,0:T(8,128)S(1)} %fusion.32), kind=kOutput, calls=%fused_computation.83 | convolution fusion | flops 25165824 | bytes 2097664 | tf_op jit(solution)/shard_map/transpose(jvp(kjh,jhnp->khnp))/dot_general | solution.py:102
  106.6 2.6 %convolution_bitcast_fusion.3 = f32[8,2,128,128]{3,0,2,1:T(8,128)} fusion(f32[8,2,128,128]{3,2,1,0:T(8,128)S(1)} %fusion.32, f32[8,8,2]{1,0,2:T(8,128)S(1)} %copy-done.13), kind=kOutput, calls=%fused_computation.66 | convolution fusion | flops 25165824 | bytes 2097664 | tf_op jit(solution)/shard_map/jvp(kjh,jhnp->khnp)/dot_general | solution.py:102
  113.7 2.8 %fusion.65 = (f32[8,2,128]{2,1,0:T(2,128)S(1)}, f32[8,2,128]{2,1,0:T(2,128)S(1)}, f32[8,128,128]{2,1,0:T(8,128)}) fusion(f32[8,128,128]{2,1,0:T(8,128)S(1)} %fusion.85, f32[8,2,128]{2,1,0:T(2,128)S(1)} %copy-done.31, pred[8,128,128]{2,1,0:T(8,128)(4,1)S(1)} %compare_and_fusion.3, bf16[8,2,128,128]{3,2,1,0:T(8,128)(2,1)S(1)} %bitcast.286, ...), kind=kOutput, calls=%fused_computation.100 | convolution fusion | flops 69332992 | bytes 2252800 | tf_op jit(solution)/shard_map/transpose(jvp(vmap(hts,shp->thp)))/dot_general | solution.py:67
  117.5 3.3 %fusion.44 = bf16[8,128,2,128]{1,3,2,0:T(8,128)(2,1)} fusion(f32[8,128,2,128]{1,3,2,0:T(8,128)S(1)} %fusion.40, f32[8,2,128,128]{3,0,2,1:T(8,128)S(1)} %convolution_bitcast_fusion.1, f32[8,128,2]{1,2,0:T(2,128)S(1)} %copy.420, f32[8,128,128]{2,1,0:T(8,128)S(1)} %copy-done.2), kind=kOutput, calls=%fused_computation.73 | convolution fusion | flops 403439616 | bytes 3153920 | tf_op jit(solution)/shard_map/transpose(jvp(vmap(hs,sn,shp->hnp)))/dot_general | solution.py:53
  120.9 1.7 fusion.53
  122.6 2.3 %fusion.43 = bf16[8,128,2,128]{1,3,2,0:T(8,128)(2,1)} fusion(bf16[8,128,2,128]{1,3,2,0:T(8,128)(2,1)S(1)} %bitcast.295, f32[8,128,2,128]{1,3,2,0:T(8,128)S(1)} %bitcast.309, f32[2]{0:T(128)S(1)} %copy-done.63, f32[8,128,2]{1,2,0:T(2,128)S(1)} %copy-done.12, f32[8,128,128]{2,1,0:T(8,128)S(1)} %fusion.85, f32[8,2,128]{2,1,0:T(2,128)S(1)} %copy-done.31, ...), kind=kOutput, calls=%fused_computation.72 | convolution fusion | flops 405012480 | bytes 2768904 | tf_op jit(solution)/shard_map/jvp(vmap(hts,shp->thp))/dot_general | solution.py:67
  125.0 2.5 %reduce_window_sum.46 = f32[8,2,128]{2,0,1:T(8,128)S(1)} reduce-window(f32[8,2,128]{2,0,1:T(8,128)S(1)} %get-tuple-element.1119, f32[]{:T(128)} %constant.152.clone.1), window={size=1x1x128 pad=0_0x0_0x0_127}, to_apply=%region_7.8 | reduce-window | flops 260096 | bytes 16388 | tf_op jit(solution)/shard_map/transpose(jvp(vmap(jit(cumsum))))/reduce_window_sum | solution.py:45
  127.5 2.5 %reduce_window_sum.47 = f32[8,2,128]{2,0,1:T(8,128)S(1)} reduce-window(f32[8,2,128]{2,0,1:T(8,128)S(1)} %get-tuple-element.1118, f32[]{:T(128)} %constant.152.clone.1), window={size=1x1x128 pad=0_0x0_0x0_127}, to_apply=%region_15.16 | reduce-window | flops 260096 | bytes 16388 | tf_op jit(solution)/shard_map/transpose(jvp(jit(cumsum)))/reduce_window_sum | solution.py:91
  130.0 2.0 %constant_dynamic-update-slice_fusion.3 = bf16[8,128,784]{1,2,0:T(8,128)(2,1)} fusion(bf16[8,128,256]{1,2,0:T(8,128)(2,1)} %bitcast.312), kind=kLoop, calls=%fused_computation.141 | loop fusion | bytes 1048576
  131.9 1.9 %constant_dynamic-update-slice_fusion.2 = bf16[8,128,784]{1,2,0:T(8,128)(2,1)} fusion(bf16[8,128,784]{1,2,0:T(8,128)(2,1)} %constant_dynamic-update-slice_fusion.3, bf16[8,128,256]{1,2,0:T(8,128)(2,1)} %bitcast.301), kind=kLoop, calls=%fused_computation.140 | loop fusion | bytes 1048576
  134.0 1.9 fusion.48
  135.9 2.1 %fusion.50 = bf16[8,128,784]{1,2,0:T(8,128)(2,1)} fusion(bf16[8,128,784]{1,2,0:T(8,128)(2,1)} %constant_dynamic-update-slice_fusion.2, f32[8,128,128]{1,2,0:T(8,128)S(1)} %fusion.54, f32[8,128,128]{2,1,0:T(8,128)S(1)} %copy-done.6, bf16[8,128,768]{2,1,0:T(8,128)(2,1)} %all-to-all-done), kind=kOutput, calls=%fused_computation.79 | convolution fusion | flops 201588736 | bytes 1572864 | tf_op jit(solution)/shard_map/transpose(jvp(vmap()))/dot_general | solution.py:66
  138.0 2.4 %fusion.52 = bf16[8,128,784]{1,2,0:T(8,128)(2,1)} fusion(bf16[8,128,784]{1,2,0:T(8,128)(2,1)} %fusion.50, f32[8,128,128]{1,2,0:T(8,128)S(1)} %fusion.48, f32[8,128,128]{2,1,0:T(8,128)S(1)} %copy-done.6, bf16[8,128,768]{2,1,0:T(8,128)(2,1)} %all-to-all-done), kind=kOutput, calls=%fused_computation.81 | convolution fusion | flops 201588736 | bytes 1572864 | tf_op jit(solution)/shard_map/transpose(jvp(vmap()))/dot_general | solution.py:66
  141.0 6.1 %all-to-all-start.2 = ((bf16[8,128,784]{1,2,0:T(8,128)(2,1)}), bf16[8,128,784]{1,2,0:T(8,128)(2,1)S(1)}, u32[]{:S(2)}, u32[]{:S(2)}) async-start(bf16[8,128,784]{1,2,0:T(8,128)(2,1)} %bitcast_dynamic-update-slice_fusion), calls=%async_computation.2 | async-start | bytes 3211264 | tf_op jit(solution)/shard_map/all_to_all | solution.py:350
  151.9 31.5 %all-to-all-done.2 = bf16[8,128,784]{1,2,0:T(8,128)(2,1)S(1)} async-done(((bf16[8,128,784]{1,2,0:T(8,128)(2,1)}), bf16[8,128,784]{1,2,0:T(8,128)(2,1)S(1)}, u32[]{:S(2)}, u32[]{:S(2)}) %all-to-all-start.2) | async-done | bytes 1605664 | tf_op jit(solution)/shard_map/all_to_all | solution.py:350
  (280 shorter events, 53.4 us)
Async XLA Ops:
  0.6 18.8 %copy-start.60 = (s32[4]{0:T(128)S(1)}, s32[4]{0:T(128)}, u32[]{:S(2)}) copy-start(s32[4]{0:T(128)} %param.28) | copy-start | bytes 52
  0.7 19.0 %copy-start.10 = (bf16[128,1024]{1,0:T(8,128)(2,1)S(1)}, bf16[128,1024]{1,0:T(8,128)(2,1)}, u32[]{:S(2)}) copy-start(bf16[128,1024]{1,0:T(8,128)(2,1)} %param.29) | copy-start | bytes 786436
  0.7 14.0 %all-to-all-start.1 = ((f32[8,2,128]{2,1,0:T(2,128)}), f32[8,2,128]{2,1,0:T(2,128)S(1)}, u32[]{:S(2)}, u32[]{:S(2)}) async-start(f32[8,2,128]{2,1,0:T(2,128)} %bitcast.324), calls=%async_computation.1 | async-start | bytes 16384 | tf_op jit(solution)/shard_map/all_to_all | solution.py:117
  9.1 10.9 %copy-start.11 = (bf16[128,1024]{1,0:T(8,128)(2,1)S(1)}, bf16[128,1024]{1,0:T(8,128)(2,1)}, u32[]{:S(2)}) copy-start(bf16[128,1024]{1,0:T(8,128)(2,1)} %param.33) | copy-start | bytes 786436
  15.7 28.4 %all-to-all-start.3 = ((bf16[8,128,512]{1,2,0:T(8,128)(2,1)}), bf16[8,128,512]{1,2,0:T(8,128)(2,1)S(1)}, u32[]{:S(2)}, u32[]{:S(2)}) async-start(bf16[8,128,512]{1,2,0:T(8,128)(2,1)} %broadcast_in_dim.296), calls=%async_computation.3 | async-start | bytes 2097152 | tf_op jit(solution)/shard_map/all_to_all | solution.py:217
  23.7 29.4 %copy-start.38 = (pred[8]{0:T(512)(128)(4,1)}, pred[8]{0:T(512)(128)(4,1)S(1)}, u32[]{:S(2)}) copy-start(pred[8]{0:T(512)(128)(4,1)S(1)} %iota_compare_fusion.7) | copy-start | bytes 28
  23.7 28.6 %copy-start.53 = (pred[8]{0:T(512)(128)(4,1)}, pred[8]{0:T(512)(128)(4,1)S(1)}, u32[]{:S(2)}) copy-start(pred[8]{0:T(512)(128)(4,1)S(1)} %get-tuple-element.1141) | copy-start | bytes 28
  23.7 29.4 %copy-start.40 = (f32[8]{0:T(128)}, f32[8]{0:T(128)S(1)}, u32[]{:S(2)}) copy-start(f32[8]{0:T(128)S(1)} %get-tuple-element.1140) | copy-start | bytes 100
  23.8 29.3 %copy-start.21 = (pred[8]{0:T(512)(128)(4,1)}, pred[8]{0:T(512)(128)(4,1)S(1)}, u32[]{:S(2)}) copy-start(pred[8]{0:T(512)(128)(4,1)S(1)} %get-tuple-element.1144) | copy-start | bytes 28
  23.8 29.3 %copy-start.42 = (pred[8]{0:T(512)(128)(4,1)}, pred[8]{0:T(512)(128)(4,1)S(1)}, u32[]{:S(2)}) copy-start(pred[8]{0:T(512)(128)(4,1)S(1)} %get-tuple-element.1145) | copy-start | bytes 28
  23.8 29.3 %copy-start.44 = (f32[8]{0:T(128)}, f32[8]{0:T(128)S(1)}, u32[]{:S(2)}) copy-start(f32[8]{0:T(128)S(1)} %get-tuple-element.1137) | copy-start | bytes 100
  23.8 29.3 %copy-start.46 = (f32[8]{0:T(128)}, f32[8]{0:T(128)S(1)}, u32[]{:S(2)}) copy-start(f32[8]{0:T(128)S(1)} %get-tuple-element.1139) | copy-start | bytes 100
  23.8 28.5 %copy-start.55 = (pred[8]{0:T(512)(128)(4,1)}, pred[8]{0:T(512)(128)(4,1)S(1)}, u32[]{:S(2)}) copy-start(pred[8]{0:T(512)(128)(4,1)S(1)} %get-tuple-element.1142) | copy-start | bytes 28
  23.8 29.3 %copy-start.34 = (pred[8]{0:T(512)(128)(4,1)}, pred[8]{0:T(512)(128)(4,1)S(1)}, u32[]{:S(2)}) copy-start(pred[8]{0:T(512)(128)(4,1)S(1)} %get-tuple-element.1143) | copy-start | bytes 28
  23.9 28.5 %copy-start.57 = (f32[8]{0:T(128)}, f32[8]{0:T(128)S(1)}, u32[]{:S(2)}) copy-start(f32[8]{0:T(128)S(1)} %get-tuple-element.1135) | copy-start | bytes 100
  24.5 27.5 %copy-start.36 = (f32[8]{0:T(128)}, f32[8]{0:T(128)S(1)}, u32[]{:S(2)}) copy-start(f32[8]{0:T(128)S(1)} %convert_reduce_fusion.6) | copy-start | bytes 100
  44.2 40.7 %all-to-all-start = ((bf16[8,128,768]{2,1,0:T(8,128)(2,1)}), bf16[8,128,768]{2,1,0:T(8,128)(2,1)}, u32[]{:S(2)}, u32[]{:S(2)}) async-start(bf16[8,128,768]{2,1,0:T(8,128)(2,1)} %pad_maximum_fusion), calls=%async_computation | async-start | bytes 3145728 | tf_op jit(solution)/shard_map/all_to_all | solution.py:211
  49.8 6.6 %copy-start.15 = (f32[8,128]{1,0:T(8,128)}, f32[8,128]{1,0:T(8,128)S(1)}, u32[]{:S(2)}) copy-start(f32[8,128]{1,0:T(8,128)S(1)} %get-tuple-element.1126) | copy-start | bytes 12292
  84.9 56.2 %all-to-all-start.4 = ((bf16[8,128,512]{1,2,0:T(8,128)(2,1)}), bf16[8,128,512]{1,2,0:T(8,128)(2,1)}, u32[]{:S(2)}, u32[]{:S(2)}) async-start(bf16[8,128,512]{1,2,0:T(8,128)(2,1)} %copy.470), calls=%async_computation.4 | async-start | bytes 2097152 | tf_op jit(solution)/shard_map/all_to_all | solution.py:351
  103.7 5.9 %copy-start.26 = (f32[2]{0:T(128)S(1)}, f32[2]{0:T(128)}, u32[]{:S(2)}) copy-start(f32[2]{0:T(128)} %copy-done.25) | copy-start | bytes 28
  103.7 5.9 %copy-start.28 = (f32[2]{0:T(128)S(1)}, f32[2]{0:T(128)}, u32[]{:S(2)}) copy-start(f32[2]{0:T(128)} %copy-done.27) | copy-start | bytes 28
  103.7 5.9 %copy-start.30 = (f32[2]{0:T(128)S(1)}, f32[2]{0:T(128)}, u32[]{:S(2)}) copy-start(f32[2]{0:T(128)} %copy-done.29) | copy-start | bytes 28
  103.8 5.9 %copy-start.39 = (pred[8]{0:T(512)(128)(4,1)S(1)}, pred[8]{0:T(512)(128)(4,1)}, u32[]{:S(2)}) copy-start(pred[8]{0:T(512)(128)(4,1)} %copy-done.38) | copy-start | bytes 28
  103.8 5.9 %copy-start.41 = (f32[8]{0:T(128)S(1)}, f32[8]{0:T(128)}, u32[]{:S(2)}) copy-start(f32[8]{0:T(128)} %copy-done.40) | copy-start | bytes 100
  103.8 5.9 %copy-start.43 = (pred[8]{0:T(512)(128)(4,1)S(1)}, pred[8]{0:T(512)(128)(4,1)}, u32[]{:S(2)}) copy-start(pred[8]{0:T(512)(128)(4,1)} %copy-done.42) | copy-start | bytes 28
  103.8 5.9 %copy-start.45 = (f32[8]{0:T(128)S(1)}, f32[8]{0:T(128)}, u32[]{:S(2)}) copy-start(f32[8]{0:T(128)} %copy-done.44) | copy-start | bytes 100
  103.8 5.9 %copy-start.47 = (f32[8]{0:T(128)S(1)}, f32[8]{0:T(128)}, u32[]{:S(2)}) copy-start(f32[8]{0:T(128)} %copy-done.46) | copy-start | bytes 100
  103.8 6.7 %copy-start.37 = (f32[8]{0:T(128)S(1)}, f32[8]{0:T(128)}, u32[]{:S(2)}) copy-start(f32[8]{0:T(128)} %copy-done.36) | copy-start | bytes 100
  122.6 11.3 %copy-start.5 = (f32[8,2,128,128]{3,2,1,0:T(8,128)S(1)}, f32[8,2,128,128]{3,2,1,0:T(8,128)}, u32[]{:S(2)}) copy-start(f32[8,2,128,128]{3,2,1,0:T(8,128)} %get-tuple-element.1131) | copy-start | bytes 3145732
  141.0 7.1 %copy-start.8 = (bf16[128,2,4,128]{0,3,2,1:T(8,128)(2,1)S(1)}, bf16[128,2,4,128]{0,3,2,1:T(8,128)(2,1)}, u32[]{:S(2)}) copy-start(bf16[128,2,4,128]{0,3,2,1:T(8,128)(2,1)} %get-tuple-element.1090) | copy-start | bytes 786436
  141.0 42.3 %all-to-all-start.2 = ((bf16[8,128,784]{1,2,0:T(8,128)(2,1)}), bf16[8,128,784]{1,2,0:T(8,128)(2,1)S(1)}, u32[]{:S(2)}, u32[]{:S(2)}) async-start(bf16[8,128,784]{1,2,0:T(8,128)(2,1)} %bitcast_dynamic-update-slice_fusion), calls=%async_computation.2 | async-start | bytes 3211264 | tf_op jit(solution)/shard_map/all_to_all | solution.py:350
  183.5 2.8 %collective-permute-start = (f32[128,256]{0,1:T(8,128)S(1)}, f32[128,256]{0,1:T(8,128)S(1)}, u32[]{:S(2)}, u32[]{:S(2)}) collective-permute-start(f32[128,256]{0,1:T(8,128)S(1)} %slice.110), channel_id=1, source_target_pairs={{0,1},{1,0},{2,3},{3,2},{4,5},{5,4},{6,7},{7,6},{8,9},{9,8},{10,11... | collective-permute-start | bytes 393224 | tf_op jit(solution)/shard_map/ppermute | solution.py:369
  (38 other events, 136.7 us)

commit v9 on v8

--- a/solution.py
+++ b/solution.py
@@ -10,7 +10,7 @@
 TOK_SPAN = 128
 
 
-precise = lax.Precision.HIGHEST
+precise = lax.Precision.HIGH
 big_negative = -1e30
 
 

time: 189 us -> 184 us (0.974)
  matrix products: 34.7 us -> 28.8 us
    dot_general x3, matrix products: 6.41 us -> 4.27 us  [mixer_whole(): state_in = jnp.einsum('kjh,jhnp->khnp', reach, summary, precision=precise)]
  transfers between devices with their start and end apart: 6 -> 6, of which waited for: 4 -> 4; matrix products, arithmetic and copies ran while one was open for 47% -> 45% of each run, Pallas kernels for 0% -> 0%
where the time goes in v9:
time: 184 us; the launch traced here: 183 us
  waiting for transfers between devices  66.5 us (36%)
  local copies, waits for them, and re-layouts  36 us (20%)
  matrix products  28.8 us (16%)
  starting transfers between devices  26.7 us (15%)
  other arithmetic  22.4 us (12%)
  between operations  1.85 us (1%)
    all_to_all x2, waiting for transfers between devices, on_device(): got = lax.all_to_all(sent, 'seq', split_axis=0, concat_axis=0, tiled=True)  43.8 us
    all_to_all x1, waiting for transfers between devices, on_device(): lax.all_to_all(kv_sent, 'seq', split_axis=0, concat_axis=0, tiled=True)  17.2 us
    unnamed x142, local copies, waits for them, and re-layouts  12.2 us
    all_to_all x2, starting transfers between devices, on_device(): got = lax.all_to_all(sent, 'seq', split_axis=0, concat_axis=0, tiled=True)  10.4 us
    all_to_all x1, starting transfers between devices, mamba_by_heads(): lax.all_to_all(decay_log, 'seq', split_axis=0, concat_axis=1, tiled=True)  7.45 us
    dot_general x3, matrix products, mixer_stretch(): jnp.dot(c_float, b_float.T, precision=precise)[None]  5.56 us
    all_to_all x1, waiting for transfers between devices, mamba_by_heads(): lax.all_to_all(decay_log, 'seq', split_axis=0, concat_axis=1, tiled=True)  5.5 us
    dot_general x3, matrix products, mixer_stretch(): inner = jnp.einsum('hts,shp->thp', kernel, inputs, precision=precise)  5.47 us
  transfers between devices with their start and end apart: 6, of which 4 were waited for; matrix products, arithmetic and copies ran while one was open for 45% of the time, Pallas kernels for 0%

profile of v9, /device:TPU:0, one launch (start us, length us, event | category | flops | bytes accessed | tf_op | source)
XLA Modules:
  0.0 182.7 jit_solution(7335341683551277846)
XLA Ops:
  0.7 7.5 %all-to-all-start.1 = ((f32[8,2,128]{2,1,0:T(2,128)}), f32[8,2,128]{2,1,0:T(2,128)S(1)}, u32[]{:S(2)}, u32[]{:S(2)}) async-start(f32[8,2,128]{2,1,0:T(2,128)} %bitcast.324), calls=%async_computation.1 | async-start | bytes 16384 | tf_op jit(solution)/shard_map/all_to_all | solution.py:117
  9.1 5.5 %all-to-all-done.1 = f32[8,2,128]{2,1,0:T(2,128)S(1)} async-done(((f32[8,2,128]{2,1,0:T(2,128)}), f32[8,2,128]{2,1,0:T(2,128)S(1)}, u32[]{:S(2)}, u32[]{:S(2)}) %all-to-all-start.1) | async-done | bytes 8224 | tf_op jit(solution)/shard_map/all_to_all | solution.py:117
  15.7 3.7 %all-to-all-start.3 = ((bf16[8,128,512]{1,2,0:T(8,128)(2,1)}), bf16[8,128,512]{1,2,0:T(8,128)(2,1)S(1)}, u32[]{:S(2)}, u32[]{:S(2)}) async-start(bf16[8,128,512]{1,2,0:T(8,128)(2,1)} %broadcast_in_dim.296), calls=%async_computation.3 | async-start | bytes 2097152 | tf_op jit(solution)/shard_map/all_to_all | solution.py:217
  24.6 2.3 %pad_maximum_fusion = bf16[8,128,768]{2,1,0:T(8,128)(2,1)} fusion(bf16[8,128,128]{2,1,0:T(8,128)(2,1)S(1)} %broadcast_in_dim.265, bf16[8,128,128]{2,1,0:T(8,128)(2,1)S(1)} %broadcast_in_dim.264, bf16[8,128,256]{2,1,0:T(8,128)(2,1)} %bitcast.300, bf16[8,128,256]{2,1,0:T(8,128)(2,1)S(1)} %bitcast.299), kind=kLoop, calls=%fused_computation.54 | loop fusion | flops 6291456 | bytes 3145728 | tf_op jit(solution)/shard_map/concatenate | solution.py:208
  27.0 17.2 %all-to-all-done.3 = bf16[8,128,512]{1,2,0:T(8,128)(2,1)S(1)} async-done(((bf16[8,128,512]{1,2,0:T(8,128)(2,1)}), bf16[8,128,512]{1,2,0:T(8,128)(2,1)S(1)}, u32[]{:S(2)}, u32[]{:S(2)}) %all-to-all-start.3) | async-done | bytes 1048608 | tf_op jit(solution)/shard_map/all_to_all | solution.py:217
  44.2 4.3 %all-to-all-start = ((bf16[8,128,768]{2,1,0:T(8,128)(2,1)}), bf16[8,128,768]{2,1,0:T(8,128)(2,1)}, u32[]{:S(2)}, u32[]{:S(2)}) async-start(bf16[8,128,768]{2,1,0:T(8,128)(2,1)} %pad_maximum_fusion), calls=%async_computation | async-start | bytes 3145728 | tf_op jit(solution)/shard_map/all_to_all | solution.py:211
  56.9 2.4 %while.51 = (s32[]{:T(128)}, f32[2,4,128]{2,1,0:T(4,128)S(1)}, f32[2,4,128]{2,1,0:T(4,128)S(1)}, s32[]{:T(128)}, s32[4]{0:T(128)S(1)}, /*index=5*/s32[128]{0:T(1...) while((s32[]{:T(128)}, f32[2,4,128]{2,1,0:T(4,128)S(1)}, ...), condition=%wide.region_24.25_spmd.clone, body=%wide.region_17.24_spmd.clone.sunk | while | flops 138616976 | bytes 5505893 | solution.py:278
  57.0 2.3 %conditional.9 = ((f32[2,4,128]{2,1,0:T(4,128)S(1)}, f32[2,4,128]{2,1,0:T(4,128)S(1)})) conditional(s32[]{:T(128)} %convert_element_type.252, (f32[2,4,128]{2,1,0:T(4,128)S(1)}, f32[2,4,128]{2,1,0:T(4,128)S(1)}) %tuple.197, (s32[]{:T(128)}, s32[]{:T(128)}, s32[4]{0:T(128)S(1)}, s32[128]{0:T(128)}, bf16[1024,256]{0,1:T(8,128)(2,1)S(1)}, ...), branch_computations={%region_18.18_spmd, %region_19.23_spmd} | conditional | flops 138616976 | bytes 5505158 | solution.py:261
  59.4 2.3 %while.52 = (s32[]{:T(128)}, f32[128,2,4,128]{0,3,2,1:T(8,128)S(1)}, s32[]{:T(128)}, bf16[1024,256]{0,1:T(8,128)(2,1)S(1)}, s32[4]{0:T(128)S(1)}, /*index=5*/s32...) while((s32[]{:T(128)}, ...), condition=%wide.region_30.31_spmd.clone, body=%wide.region_25.30_spmd.clone.sunk | while | flops 271390848 | bytes 3031893 | solution.py:295
  59.4 2.2 %conditional.10 = (f32[128,2,4,128]{0,3,2,1:T(8,128)S(1)}) conditional(s32[]{:T(128)} %convert_element_type.253, f32[128,2,4,128]{0,3,2,1:T(8,128)S(1)} %get-tuple-element.1413, (s32[]{:T(128)}, bf16[1024,256]{0,1:T(8,128)(2,1)S(1)}, s32[]{:T(128)}, s32[4]{0:T(128)S(1)}, s32[128]{0:T(128)}, /*index=5*/bf16[1024,256]{0,1:T(8,128)(2,1)S(1)}, ...), branch_computations={%region_26.26_spmd, %region_27.29_spmd} | conditional | flops 271390848 | bytes 3031158 | solution.py:261
  62.7 8.1 %while.53 = (s32[]{:T(128)}, f32[128,2,4,128]{0,3,2,1:T(8,128)S(1)}, bf16[1024,256]{0,1:T(8,128)(2,1)S(1)}, bf16[1024,256]{0,1:T(8,128)(2,1)S(1)}, s32[]{:T(128)...) while((s32[]{:T(128)}, ...), condition=%wide.region_37.38_spmd.clone, body=%wide.region_32.37_spmd.clone.sunk | while | flops 675616896 | bytes 15094733 | solution.py:333
  63.3 6.9 %conditional.11 = ((f32[128,2,4,128]{0,3,2,1:T(8,128)S(1)}, bf16[1024,256]{0,1:T(8,128)(2,1)S(1)}, bf16[1024,256]{0,1:T(8,128)(2,1)S(1)})) conditional(s32[]{:T(128)} %convert_element_type.254, (f32[128,2,4,128]{0,3,2,1:T(8,128)S(1)}, bf16[1024,256]{0,1:T(8,128)(2,1)S(1)}, bf16[1024,256]{0,1:T(8,128)(2,1)S(1)}) %tuple.202, (s32[]{:T(128)}, ...), branch_computations={%region_33.33_spmd, %region_34.36_spmd} | conditional | flops 675616896 | bytes 15093910 | solution.py:261
  72.6 12.3 %all-to-all-done = bf16[8,128,768]{2,1,0:T(8,128)(2,1)} async-done(((bf16[8,128,768]{2,1,0:T(8,128)(2,1)}), bf16[8,128,768]{2,1,0:T(8,128)(2,1)}, u32[]{:S(2)}, u32[]{:S(2)}) %all-to-all-start) | async-done | bytes 1572896 | tf_op jit(solution)/shard_map/all_to_all | solution.py:211
  84.9 5.1 %all-to-all-start.4 = ((bf16[8,128,512]{1,2,0:T(8,128)(2,1)}), bf16[8,128,512]{1,2,0:T(8,128)(2,1)}, u32[]{:S(2)}, u32[]{:S(2)}) async-start(bf16[8,128,512]{1,2,0:T(8,128)(2,1)} %copy.470), calls=%async_computation.4 | async-start | bytes 2097152 | tf_op jit(solution)/shard_map/all_to_all | solution.py:351
  89.9 2.1 %fusion.102 = (bf16[8,128,256]{2,1,0:T(8,128)(2,1)S(1)}, bf16[8,128,256]{2,1,0:T(8,128)(2,1)}) fusion(bf16[8,128,768]{2,1,0:T(8,128)(2,1)} %all-to-all-done), kind=kLoop, calls=%fused_computation.217 | loop fusion | bytes 2097152 | tf_op jit(solution)/shard_map/slice | solution.py:213
  94.1 2.0 %copy.543 = bf16[8,128,256]{1,2,0:T(8,128)(2,1)} copy(bf16[8,128,256]{2,1,0:T(8,128)(2,1)} %get-tuple-element.1111) | data formatting | bytes 1048576 | tf_op jit(solution)/shard_map/jvp()/reshape;reshape | solution.py:85
  100.2 1.6 fusion.55
  103.2 1.6 convolution_bitcast_fusion.6
  104.8 2.1 %convolution_bitcast_fusion.3 = f32[8,2,128,128]{3,0,2,1:T(8,128)} fusion(f32[8,2,128,128]{3,2,1,0:T(8,128)S(1)} %fusion.32, f32[8,8,2]{1,0,2:T(8,128)S(1)} %copy-done.13), kind=kOutput, calls=%fused_computation.66 | convolution fusion | flops 12582912 | bytes 2097664 | tf_op jit(solution)/shard_map/jvp(kjh,jhnp->khnp)/dot_general | solution.py:102
  108.3 1.6 copy.424
  111.3 2.8 %fusion.65 = (f32[8,2,128]{2,1,0:T(2,128)S(1)}, f32[8,2,128]{2,1,0:T(2,128)S(1)}, f32[8,128,128]{2,1,0:T(8,128)}) fusion(f32[8,128,128]{2,1,0:T(8,128)S(1)} %fusion.85, f32[8,2,128]{2,1,0:T(2,128)S(1)} %copy-done.31, pred[8,128,128]{2,1,0:T(8,128)(4,1)S(1)} %compare_and_fusion.3, bf16[8,2,128,128]{3,2,1,0:T(8,128)(2,1)S(1)} %bitcast.286, ...), kind=kOutput, calls=%fused_computation.100 | convolution fusion | flops 69332992 | bytes 2252800 | tf_op jit(solution)/shard_map/transpose(jvp(vmap(hts,shp->thp)))/dot_general | solution.py:67
  115.1 2.1 %fusion.44 = bf16[8,128,2,128]{1,3,2,0:T(8,128)(2,1)} fusion(f32[8,128,2,128]{1,3,2,0:T(8,128)S(1)} %fusion.40, f32[8,2,128,128]{3,0,2,1:T(8,128)S(1)} %convolution_bitcast_fusion.1, f32[8,128,2]{1,2,0:T(2,128)S(1)} %copy.420, f32[8,128,128]{2,1,0:T(8,128)S(1)} %copy-done.2), kind=kOutput, calls=%fused_computation.73 | convolution fusion | flops 202113024 | bytes 3153920 | tf_op jit(solution)/shard_map/transpose(jvp(vmap(hs,sn,shp->hnp)))/dot_general | solution.py:53
  117.3 1.6 fusion.53
  118.8 1.9 %fusion.43 = bf16[8,128,2,128]{1,3,2,0:T(8,128)(2,1)} fusion(bf16[8,128,2,128]{1,3,2,0:T(8,128)(2,1)S(1)} %bitcast.295, f32[8,128,2,128]{1,3,2,0:T(8,128)S(1)} %bitcast.309, f32[2]{0:T(128)S(1)} %copy-done.63, f32[8,128,2]{1,2,0:T(2,128)S(1)} %copy-done.12, f32[8,128,128]{2,1,0:T(8,128)S(1)} %fusion.85, f32[8,2,128]{2,1,0:T(2,128)S(1)} %copy-done.31, ...), kind=kOutput, calls=%fused_computation.72 | convolution fusion | flops 203685888 | bytes 2768904 | tf_op jit(solution)/shard_map/jvp(vmap(hts,shp->thp))/dot_general | solution.py:67
  120.8 2.7 %reduce_window_sum.46 = f32[8,2,128]{2,0,1:T(8,128)S(1)} reduce-window(f32[8,2,128]{2,0,1:T(8,128)S(1)} %get-tuple-element.1119, f32[]{:T(128)} %constant.152.clone.1), window={size=1x1x128 pad=0_0x0_0x0_127}, to_apply=%region_7.8 | reduce-window | flops 260096 | bytes 16388 | tf_op jit(solution)/shard_map/transpose(jvp(vmap(jit(cumsum))))/reduce_window_sum | solution.py:45
  123.5 2.5 %reduce_window_sum.47 = f32[8,2,128]{2,0,1:T(8,128)S(1)} reduce-window(f32[8,2,128]{2,0,1:T(8,128)S(1)} %get-tuple-element.1118, f32[]{:T(128)} %constant.152.clone.1), window={size=1x1x128 pad=0_0x0_0x0_127}, to_apply=%region_15.16 | reduce-window | flops 260096 | bytes 16388 | tf_op jit(solution)/shard_map/transpose(jvp(jit(cumsum)))/reduce_window_sum | solution.py:91
  126.0 2.0 %constant_dynamic-update-slice_fusion.3 = bf16[8,128,784]{1,2,0:T(8,128)(2,1)} fusion(bf16[8,128,256]{1,2,0:T(8,128)(2,1)} %bitcast.312), kind=kLoop, calls=%fused_computation.141 | loop fusion | bytes 1048576
  128.0 1.9 %constant_dynamic-update-slice_fusion.2 = bf16[8,128,784]{1,2,0:T(8,128)(2,1)} fusion(bf16[8,128,784]{1,2,0:T(8,128)(2,1)} %constant_dynamic-update-slice_fusion.3, bf16[8,128,256]{1,2,0:T(8,128)(2,1)} %bitcast.301), kind=kLoop, calls=%fused_computation.140 | loop fusion | bytes 1048576
  131.1 2.0 %fusion.50 = bf16[8,128,784]{1,2,0:T(8,128)(2,1)} fusion(bf16[8,128,784]{1,2,0:T(8,128)(2,1)} %constant_dynamic-update-slice_fusion.2, f32[8,128,128]{1,2,0:T(8,128)S(1)} %fusion.54, f32[8,128,128]{2,1,0:T(8,128)S(1)} %copy-done.6, bf16[8,128,768]{2,1,0:T(8,128)(2,1)} %all-to-all-done), kind=kOutput, calls=%fused_computation.79 | convolution fusion | flops 100925440 | bytes 1572864 | tf_op jit(solution)/shard_map/transpose(jvp(vmap()))/dot_general | solution.py:66
  133.1 2.2 %fusion.52 = bf16[8,128,784]{1,2,0:T(8,128)(2,1)} fusion(bf16[8,128,784]{1,2,0:T(8,128)(2,1)} %fusion.50, f32[8,128,128]{1,2,0:T(8,128)S(1)} %fusion.48, f32[8,128,128]{2,1,0:T(8,128)S(1)} %copy-done.6, bf16[8,128,768]{2,1,0:T(8,128)(2,1)} %all-to-all-done), kind=kOutput, calls=%fused_computation.81 | convolution fusion | flops 100925440 | bytes 1572864 | tf_op jit(solution)/shard_map/transpose(jvp(vmap()))/dot_general | solution.py:66
  136.0 6.1 %all-to-all-start.2 = ((bf16[8,128,784]{1,2,0:T(8,128)(2,1)}), bf16[8,128,784]{1,2,0:T(8,128)(2,1)S(1)}, u32[]{:S(2)}, u32[]{:S(2)}) async-start(bf16[8,128,784]{1,2,0:T(8,128)(2,1)} %bitcast_dynamic-update-slice_fusion), calls=%async_computation.2 | async-start | bytes 3211264 | tf_op jit(solution)/shard_map/all_to_all | solution.py:350
  146.8 31.5 %all-to-all-done.2 = bf16[8,128,784]{1,2,0:T(8,128)(2,1)S(1)} async-done(((bf16[8,128,784]{1,2,0:T(8,128)(2,1)}), bf16[8,128,784]{1,2,0:T(8,128)(2,1)S(1)}, u32[]{:S(2)}, u32[]{:S(2)}) %all-to-all-start.2) | async-done | bytes 1605664 | tf_op jit(solution)/shard_map/all_to_all | solution.py:350
  (280 shorter events, 52.4 us)
Async XLA Ops:
  0.6 18.8 %copy-start.60 = (s32[4]{0:T(128)S(1)}, s32[4]{0:T(128)}, u32[]{:S(2)}) copy-start(s32[4]{0:T(128)} %param.28) | copy-start | bytes 52
  0.7 19.0 %copy-start.10 = (bf16[128,1024]{1,0:T(8,128)(2,1)S(1)}, bf16[128,1024]{1,0:T(8,128)(2,1)}, u32[]{:S(2)}) copy-start(bf16[128,1024]{1,0:T(8,128)(2,1)} %param.29) | copy-start | bytes 786436
  0.7 14.0 %all-to-all-start.1 = ((f32[8,2,128]{2,1,0:T(2,128)}), f32[8,2,128]{2,1,0:T(2,128)S(1)}, u32[]{:S(2)}, u32[]{:S(2)}) async-start(f32[8,2,128]{2,1,0:T(2,128)} %bitcast.324), calls=%async_computation.1 | async-start | bytes 16384 | tf_op jit(solution)/shard_map/all_to_all | solution.py:117
  9.1 10.9 %copy-start.11 = (bf16[128,1024]{1,0:T(8,128)(2,1)S(1)}, bf16[128,1024]{1,0:T(8,128)(2,1)}, u32[]{:S(2)}) copy-start(bf16[128,1024]{1,0:T(8,128)(2,1)} %param.33) | copy-start | bytes 786436
  15.7 4.4 %copy-start.9 = (bf16[128,2048]{1,0:T(8,128)(2,1)S(1)}, bf16[128,2048]{1,0:T(8,128)(2,1)}, u32[]{:S(2)}) copy-start(bf16[128,2048]{1,0:T(8,128)(2,1)} %param.23) | copy-start | bytes 1572868
  15.7 28.4 %all-to-all-start.3 = ((bf16[8,128,512]{1,2,0:T(8,128)(2,1)}), bf16[8,128,512]{1,2,0:T(8,128)(2,1)S(1)}, u32[]{:S(2)}, u32[]{:S(2)}) async-start(bf16[8,128,512]{1,2,0:T(8,128)(2,1)} %broadcast_in_dim.296), calls=%async_computation.3 | async-start | bytes 2097152 | tf_op jit(solution)/shard_map/all_to_all | solution.py:217
  20.2 4.3 %copy-start.17 = (bf16[128,128]{1,0:T(8,128)(2,1)S(1)}, bf16[128,128]{1,0:T(8,128)(2,1)}, u32[]{:S(2)}) copy-start(bf16[128,128]{1,0:T(8,128)(2,1)} %param.24) | copy-start | bytes 98308
  20.2 4.4 %copy-start.18 = (bf16[128,128]{1,0:T(8,128)(2,1)S(1)}, bf16[128,128]{1,0:T(8,128)(2,1)}, u32[]{:S(2)}) copy-start(bf16[128,128]{1,0:T(8,128)(2,1)} %param.25) | copy-start | bytes 98308
  23.7 29.4 %copy-start.38 = (pred[8]{0:T(512)(128)(4,1)}, pred[8]{0:T(512)(128)(4,1)S(1)}, u32[]{:S(2)}) copy-start(pred[8]{0:T(512)(128)(4,1)S(1)} %iota_compare_fusion.7) | copy-start | bytes 28
  23.7 28.6 %copy-start.53 = (pred[8]{0:T(512)(128)(4,1)}, pred[8]{0:T(512)(128)(4,1)S(1)}, u32[]{:S(2)}) copy-start(pred[8]{0:T(512)(128)(4,1)S(1)} %get-tuple-element.1141) | copy-start | bytes 28
  23.7 29.4 %copy-start.40 = (f32[8]{0:T(128)}, f32[8]{0:T(128)S(1)}, u32[]{:S(2)}) copy-start(f32[8]{0:T(128)S(1)} %get-tuple-element.1140) | copy-start | bytes 100
  23.8 29.3 %copy-start.21 = (pred[8]{0:T(512)(128)(4,1)}, pred[8]{0:T(512)(128)(4,1)S(1)}, u32[]{:S(2)}) copy-start(pred[8]{0:T(512)(128)(4,1)S(1)} %get-tuple-element.1144) | copy-start | bytes 28
  23.8 29.3 %copy-start.42 = (pred[8]{0:T(512)(128)(4,1)}, pred[8]{0:T(512)(128)(4,1)S(1)}, u32[]{:S(2)}) copy-start(pred[8]{0:T(512)(128)(4,1)S(1)} %get-tuple-element.1145) | copy-start | bytes 28
  23.8 29.3 %copy-start.44 = (f32[8]{0:T(128)}, f32[8]{0:T(128)S(1)}, u32[]{:S(2)}) copy-start(f32[8]{0:T(128)S(1)} %get-tuple-element.1137) | copy-start | bytes 100
  23.8 29.3 %copy-start.46 = (f32[8]{0:T(128)}, f32[8]{0:T(128)S(1)}, u32[]{:S(2)}) copy-start(f32[8]{0:T(128)S(1)} %get-tuple-element.1139) | copy-start | bytes 100
  23.8 28.5 %copy-start.55 = (pred[8]{0:T(512)(128)(4,1)}, pred[8]{0:T(512)(128)(4,1)S(1)}, u32[]{:S(2)}) copy-start(pred[8]{0:T(512)(128)(4,1)S(1)} %get-tuple-element.1142) | copy-start | bytes 28
  23.8 29.3 %copy-start.34 = (pred[8]{0:T(512)(128)(4,1)}, pred[8]{0:T(512)(128)(4,1)S(1)}, u32[]{:S(2)}) copy-start(pred[8]{0:T(512)(128)(4,1)S(1)} %get-tuple-element.1143) | copy-start | bytes 28
  23.9 28.5 %copy-start.57 = (f32[8]{0:T(128)}, f32[8]{0:T(128)S(1)}, u32[]{:S(2)}) copy-start(f32[8]{0:T(128)S(1)} %get-tuple-element.1135) | copy-start | bytes 100
  24.5 27.5 %copy-start.36 = (f32[8]{0:T(128)}, f32[8]{0:T(128)S(1)}, u32[]{:S(2)}) copy-start(f32[8]{0:T(128)S(1)} %convert_reduce_fusion.6) | copy-start | bytes 100
  44.2 40.7 %all-to-all-start = ((bf16[8,128,768]{2,1,0:T(8,128)(2,1)}), bf16[8,128,768]{2,1,0:T(8,128)(2,1)}, u32[]{:S(2)}, u32[]{:S(2)}) async-start(bf16[8,128,768]{2,1,0:T(8,128)(2,1)} %pad_maximum_fusion), calls=%async_computation | async-start | bytes 3145728 | tf_op jit(solution)/shard_map/all_to_all | solution.py:211
  49.8 6.6 %copy-start.15 = (f32[8,128]{1,0:T(8,128)}, f32[8,128]{1,0:T(8,128)S(1)}, u32[]{:S(2)}) copy-start(f32[8,128]{1,0:T(8,128)S(1)} %get-tuple-element.1126) | copy-start | bytes 12292
  52.0 4.4 %copy-start.19 = (f32[8,2]{0,1:T(2,128)}, f32[8,2]{0,1:T(2,128)S(1)}, u32[]{:S(2)}) copy-start(f32[8,2]{0,1:T(2,128)S(1)} %slice_reduce_fusion) | copy-start | bytes 196
  84.9 51.1 %all-to-all-start.4 = ((bf16[8,128,512]{1,2,0:T(8,128)(2,1)}), bf16[8,128,512]{1,2,0:T(8,128)(2,1)}, u32[]{:S(2)}, u32[]{:S(2)}) async-start(bf16[8,128,512]{1,2,0:T(8,128)(2,1)} %copy.470), calls=%async_computation.4 | async-start | bytes 2097152 | tf_op jit(solution)/shard_map/all_to_all | solution.py:351
  93.7 5.3 %copy-start.13 = (f32[8,8,2]{1,0,2:T(8,128)S(1)}, f32[8,8,2]{1,0,2:T(8,128)}, u32[]{:S(2)}) copy-start(f32[8,8,2]{1,0,2:T(8,128)} %stack.2) | copy-start | bytes 1540
  103.1 4.2 %copy-start.26 = (f32[2]{0:T(128)S(1)}, f32[2]{0:T(128)}, u32[]{:S(2)}) copy-start(f32[2]{0:T(128)} %copy-done.25) | copy-start | bytes 28
  103.1 4.1 %copy-start.28 = (f32[2]{0:T(128)S(1)}, f32[2]{0:T(128)}, u32[]{:S(2)}) copy-start(f32[2]{0:T(128)} %copy-done.27) | copy-start | bytes 28
  103.2 4.9 %copy-start.37 = (f32[8]{0:T(128)S(1)}, f32[8]{0:T(128)}, u32[]{:S(2)}) copy-start(f32[8]{0:T(128)} %copy-done.36) | copy-start | bytes 100
  106.8 4.4 %copy-start.31 = (f32[8,2,128]{2,1,0:T(2,128)S(1)}, f32[8,2,128]{2,1,0:T(2,128)}, u32[]{:S(2)}) copy-start(f32[8,2,128]{2,1,0:T(2,128)} %copy.416) | copy-start | bytes 24580
  118.8 11.1 %copy-start.5 = (f32[8,2,128,128]{3,2,1,0:T(8,128)S(1)}, f32[8,2,128,128]{3,2,1,0:T(8,128)}, u32[]{:S(2)}) copy-start(f32[8,2,128,128]{3,2,1,0:T(8,128)} %get-tuple-element.1131) | copy-start | bytes 3145732
  135.9 7.1 %copy-start.8 = (bf16[128,2,4,128]{0,3,2,1:T(8,128)(2,1)S(1)}, bf16[128,2,4,128]{0,3,2,1:T(8,128)(2,1)}, u32[]{:S(2)}) copy-start(bf16[128,2,4,128]{0,3,2,1:T(8,128)(2,1)} %get-tuple-element.1090) | copy-start | bytes 786436
  136.0 42.3 %all-to-all-start.2 = ((bf16[8,128,784]{1,2,0:T(8,128)(2,1)}), bf16[8,128,784]{1,2,0:T(8,128)(2,1)S(1)}, u32[]{:S(2)}, u32[]{:S(2)}) async-start(bf16[8,128,784]{1,2,0:T(8,128)(2,1)} %bitcast_dynamic-update-slice_fusion), calls=%async_computation.2 | async-start | bytes 3211264 | tf_op jit(solution)/shard_map/all_to_all | solution.py:350
  178.4 2.8 %collective-permute-start = (f32[128,256]{0,1:T(8,128)S(1)}, f32[128,256]{0,1:T(8,128)S(1)}, u32[]{:S(2)}, u32[]{:S(2)}) collective-permute-start(f32[128,256]{0,1:T(8,128)S(1)} %slice.110), channel_id=1, source_target_pairs={{0,1},{1,0},{2,3},{3,2},{4,5},{5,4},{6,7},{7,6},{8,9},{9,8},{10,11... | collective-permute-start | bytes 393224 | tf_op jit(solution)/shard_map/ppermute | solution.py:369
  (38 other events, 116.2 us)

commit v10 on v9

--- a/solution.py
+++ b/solution.py
@@ -108,13 +108,12 @@
     return outputs.reshape(count * width, heads, P_SIZE)
 
 
-def mamba_by_heads(x_all, cot_all, b_all, c_all, decay_log, skip_gain, doc_lengths):
+def mamba_by_heads(x_all, cot_all, b_all, c_all, decay, skip_gain, doc_lengths):
     seq_count = lax.axis_size("seq")
     place = lax.axis_index("seq")
     heads_here = skip_gain.shape[0]
     own = heads_here // seq_count
     total = x_all.shape[0]
-    decay = lax.all_to_all(decay_log, "seq", split_axis=0, concat_axis=1, tiled=True)
     gains = lax.dynamic_slice_in_dim(skip_gain, place * own, own)
     segment = doc_index(jnp.arange(total, dtype=jnp.int32), doc_lengths)
     inputs = x_all.astype(jnp.float32).reshape(total, own, P_SIZE)
@@ -205,14 +204,35 @@
         def spread(a):
             return jnp.broadcast_to(a[None], (seq_count,) + a.shape)
 
+        decay_parts = []
+        rest = decay_log
+        for scale in (2.0**8, 2.0**16, 2.0**24, 2.0**32):
+            part = jnp.round(rest * scale) / scale
+            rest = rest - part
+            decay_parts.append(part)
+        decay_sent = jnp.concatenate(decay_parts, axis=0).astype(jnp.bfloat16)
+        decay_sent = decay_sent.reshape(len(decay_parts), seq_count, heads_here // seq_count, tokens)
+        decay_sent = decay_sent.transpose(1, 3, 0, 2).reshape(seq_count, tokens, -1)
         sent = jnp.concatenate(
-            [by_owner(x_input), by_owner(mixer_cot), spread(b_rows), spread(c_rows)], axis=2
+            [
+                by_owner(x_input),
+                by_owner(mixer_cot),
+                spread(b_rows),
+                spread(c_rows),
+                decay_sent,
+            ],
+            axis=2,
         )
         got = lax.all_to_all(sent, "seq", split_axis=0, concat_axis=0, tiled=True)
         x_all = got[:, :, :own_width].reshape(total_len, own_width)
         cot_all = got[:, :, own_width : 2 * own_width].reshape(total_len, own_width)
         b_all = got[:, :, 2 * own_width : 2 * own_width + state_width].reshape(total_len, -1)
-        c_all = got[:, :, 2 * own_width + state_width :].reshape(total_len, -1)
+        c_all = got[:, :, 2 * own_width + state_width : 2 * own_width + 2 * state_width]
+        c_all = c_all.reshape(total_len, -1)
+        decay_got = got[:, :, 2 * own_width + 2 * state_width :].astype(jnp.float32)
+        decay_got = decay_got.reshape(total_len, 4, heads_here // seq_count)
+        decay_own = ((decay_got[:, 0] + decay_got[:, 1]) + decay_got[:, 2]) + decay_got[:, 3]
+        decay_own = decay_own.T
         kv_sent = spread(jnp.concatenate([attention_key_rows, values], axis=1))
         gathered = lax.all_to_all(kv_sent, "seq", split_axis=0, concat_axis=0, tiled=True)
         gathered = gathered.reshape(total_len, 2 * key_width)
@@ -223,7 +243,7 @@
     key_all, value_all = gathered[:, :key_width], gathered[:, key_width : 2 * key_width]
     if by_heads:
         mixed_own, x_grad_own, bc_part = mamba_by_heads(
-            x_all, cot_all, b_all, c_all, decay_log, skip_gain, doc_lengths
+            x_all, cot_all, b_all, c_all, decay_own, skip_gain, doc_lengths
         )
     else:
         mixer_out, x_grad, grad_b, grad_c, grad_decay = mamba_by_stretch(

time: 184 us -> 198 us (1.076)
  local copies, waits for them, and re-layouts: 36 us -> 45.9 us
  other arithmetic: 22.4 us -> 30.6 us
  starting transfers between devices: 26.7 us -> 21.9 us
  matrix products: 28.8 us -> 31.7 us
    all_to_all x1 -> x0, starting transfers between devices: 7.45 us -> none  [mamba_by_heads(): lax.all_to_all(decay_log, 'seq', split_axis=0, concat_axis=1, tiled=True)]
    reshape x6, local copies, waits for them, and re-layouts: 0.55 us -> 7.71 us  [mixer_whole(): row * factor[k - 1][None, :]]
    all_to_all x1 -> x0, waiting for transfers between devices: 5.5 us -> none  [mamba_by_heads(): lax.all_to_all(decay_log, 'seq', split_axis=0, concat_axis=1, tiled=True)]
    unnamed x142 -> x107, local copies, waits for them, and re-layouts: 12.2 us -> 16 us
    all_to_all x1, starting transfers between devices: 3.69 us -> 7.44 us  [on_device(): lax.all_to_all(kv_sent, 'seq', split_axis=0, concat_axis=0, tiled=True)]
    reduce_sum x2, other arithmetic: 0.44 us -> 3.02 us  [mixer_whole(): row * factor[k - 1][None, :]]
    concatenate x1, other arithmetic: 2.33 us -> 0.01 us  [on_device(): decay_sent = jnp.concatenate(decay_parts, axis=0).astype(jnp.bfloat16)]
    dot_general x3, matrix products: 4.77 us -> 7.02 us  [local_state(): jnp.einsum('hs,sn,shp->hnp', weights, b_float, inputs, precision=precise)]
  transfers between devices with their start and end apart: 6 -> 5, of which waited for: 4 -> 4; matrix products, arithmetic and copies ran while one was open for 45% -> 51% of each run, Pallas kernels for 0% -> 0%
where the time goes in v10:
time: 198 us; the launch traced here: 197 us
  waiting for transfers between devices  64.9 us (33%)
  local copies, waits for them, and re-layouts  45.9 us (23%)
  matrix products  31.7 us (16%)
  other arithmetic  30.6 us (15%)
  starting transfers between devices  21.9 us (11%)
    all_to_all x2, waiting for transfers between devices, on_device(): got = lax.all_to_all(sent, 'seq', split_axis=0, concat_axis=0, tiled=True)  45.8 us
    all_to_all x1, waiting for transfers between devices, on_device(): lax.all_to_all(kv_sent, 'seq', split_axis=0, concat_axis=0, tiled=True)  18.4 us
    unnamed x107, local copies, waits for them, and re-layouts  16 us
    all_to_all x2, starting transfers between devices, on_device(): got = lax.all_to_all(sent, 'seq', split_axis=0, concat_axis=0, tiled=True)  10 us
    reshape x6, local copies, waits for them, and re-layouts, mixer_whole(): row * factor[k - 1][None, :]  7.71 us
    all_to_all x1, starting transfers between devices, on_device(): lax.all_to_all(kv_sent, 'seq', split_axis=0, concat_axis=0, tiled=True)  7.44 us
    dot_general x3, matrix products, local_state(): jnp.einsum('hs,sn,shp->hnp', weights, b_float, inputs, precision=precise)  7.02 us
    dot_general x3, matrix products, mixer_stretch(): jnp.dot(c_float, b_float.T, precision=precise)[None]  5.46 us
  transfers between devices with their start and end apart: 5, of which 4 were waited for; matrix products, arithmetic and copies ran while one was open for 51% of the time, Pallas kernels for 0%

profile of v10, /device:TPU:0, one launch (start us, length us, event | category | flops | bytes accessed | tf_op | source)
XLA Modules:
  0.0 196.9 jit_solution(17137876440587640739)
XLA Ops:
  2.9 7.4 %all-to-all-start.2 = ((bf16[8,128,512]{1,2,0:T(8,128)(2,1)}), bf16[8,128,512]{1,2,0:T(8,128)(2,1)S(1)}, u32[]{:S(2)}, u32[]{:S(2)}) async-start(bf16[8,128,512]{1,2,0:T(8,128)(2,1)} %broadcast_in_dim.296), calls=%async_computation.2 | async-start | bytes 2097152 | tf_op jit(solution)/shard_map/all_to_all | solution.py:237
  17.7 18.4 %all-to-all-done.2 = bf16[8,128,512]{1,2,0:T(8,128)(2,1)S(1)} async-done(((bf16[8,128,512]{1,2,0:T(8,128)(2,1)}), bf16[8,128,512]{1,2,0:T(8,128)(2,1)S(1)}, u32[]{:S(2)}, u32[]{:S(2)}) %all-to-all-start.2) | async-done | bytes 1048608 | tf_op jit(solution)/shard_map/all_to_all | solution.py:237
  36.1 4.3 %all-to-all-start = ((bf16[8,128,776]{1,2,0:T(8,128)(2,1)}), bf16[8,128,776]{1,2,0:T(8,128)(2,1)}, u32[]{:S(2)}, u32[]{:S(2)}) async-start(bf16[8,128,776]{1,2,0:T(8,128)(2,1)} %constant_dynamic-update-slice_fusion.2), calls=%async_computation | async-start | bytes 3178496 | tf_op jit(solution)/shard_map/all_to_all | solution.py:226
  48.9 2.4 %while.51 = (s32[]{:T(128)}, f32[2,4,128]{2,1,0:T(4,128)S(1)}, f32[2,4,128]{2,1,0:T(4,128)S(1)}, s32[]{:T(128)}, s32[4]{0:T(128)}, /*index=5*/s32[128]{0:T(128)S...) while((s32[]{:T(128)}, f32[2,4,128]{2,1,0:T(4,128)S(1)}, ...), condition=%wide.region_24.25_spmd.clone, body=%wide.region_17.24_spmd.clone.sunk | while | flops 138616976 | bytes 5505901 | solution.py:298
  48.9 2.3 %conditional.9 = ((f32[2,4,128]{2,1,0:T(4,128)S(1)}, f32[2,4,128]{2,1,0:T(4,128)S(1)})) conditional(s32[]{:T(128)} %convert_element_type.259, (f32[2,4,128]{2,1,0:T(4,128)S(1)}, f32[2,4,128]{2,1,0:T(4,128)S(1)}) %tuple.200, (s32[]{:T(128)}, s32[]{:T(128)}, s32[4]{0:T(128)}, s32[128]{0:T(128)S(1)}, bf16[1024,256]{0,1:T(8,128)(2,1)S(1)}, ...), branch_computations={%region_18.18_spmd, %region_19.23_spmd} | conditional | flops 138616976 | bytes 5505158 | solution.py:281
  51.3 2.3 %while.52 = (s32[]{:T(128)}, f32[128,2,4,128]{0,3,2,1:T(8,128)S(1)}, s32[]{:T(128)}, bf16[1024,256]{0,1:T(8,128)(2,1)S(1)}, s32[4]{0:T(128)}, /*index=5*/s32[128...) while((s32[]{:T(128)}, ...), condition=%wide.region_30.31_spmd.clone, body=%wide.region_25.30_spmd.clone.sunk | while | flops 271390848 | bytes 3031901 | solution.py:315
  51.3 2.2 %conditional.10 = (f32[128,2,4,128]{0,3,2,1:T(8,128)S(1)}) conditional(s32[]{:T(128)} %convert_element_type.260, f32[128,2,4,128]{0,3,2,1:T(8,128)S(1)} %get-tuple-element.1417, (s32[]{:T(128)}, bf16[1024,256]{0,1:T(8,128)(2,1)S(1)}, s32[]{:T(128)}, s32[4]{0:T(128)}, s32[128]{0:T(128)S(1)}, /*index=5*/bf16[1024,256]{0,1:T(8,128)(2,1)S(1)}, ...), branch_computations={%region_26.26_spmd, %region_27.29_spmd} | conditional | flops 271390848 | bytes 3031158 | solution.py:281
  54.3 7.6 %while.53 = (s32[]{:T(128)}, f32[128,2,4,128]{0,3,2,1:T(8,128)S(1)}, bf16[1024,256]{0,1:T(8,128)(2,1)S(1)}, bf16[1024,256]{0,1:T(8,128)(2,1)S(1)}, s32[]{:T(128)...) while((s32[]{:T(128)}, ...), condition=%wide.region_37.38_spmd.clone, body=%wide.region_32.37_spmd.clone.sunk | while | flops 675616896 | bytes 15094741 | solution.py:353
  54.9 6.3 %conditional.11 = ((f32[128,2,4,128]{0,3,2,1:T(8,128)S(1)}, bf16[1024,256]{0,1:T(8,128)(2,1)S(1)}, bf16[1024,256]{0,1:T(8,128)(2,1)S(1)})) conditional(s32[]{:T(128)} %convert_element_type.261, (f32[128,2,4,128]{0,3,2,1:T(8,128)S(1)}, bf16[1024,256]{0,1:T(8,128)(2,1)S(1)}, bf16[1024,256]{0,1:T(8,128)(2,1)S(1)}) %tuple.205, (s32[]{:T(128)}, ...), branch_computations={%region_33.33_spmd, %region_34.36_spmd} | conditional | flops 675616896 | bytes 15093910 | solution.py:281
  58.0 1.4 fusion.26
  63.7 13.6 %all-to-all-done = bf16[8,128,776]{1,2,0:T(8,128)(2,1)} async-done(((bf16[8,128,776]{1,2,0:T(8,128)(2,1)}), bf16[8,128,776]{1,2,0:T(8,128)(2,1)}, u32[]{:S(2)}, u32[]{:S(2)}) %all-to-all-start) | async-done | bytes 1589280 | tf_op jit(solution)/shard_map/all_to_all | solution.py:226
  77.3 4.4 %all-to-all-start.3 = ((bf16[8,128,512]{1,2,0:T(8,128)(2,1)}), bf16[8,128,512]{1,2,0:T(8,128)(2,1)}, u32[]{:S(2)}, u32[]{:S(2)}) async-start(bf16[8,128,512]{1,2,0:T(8,128)(2,1)} %copy.476), calls=%async_computation.3 | async-start | bytes 2097152 | tf_op jit(solution)/shard_map/all_to_all | solution.py:371
  87.7 2.1 %fusion.108 = (bf16[8,128,256]{1,2,0:T(8,128)(2,1)S(1)}, bf16[8,128,256]{1,2,0:T(8,128)(2,1)}) fusion(bf16[8,128,776]{1,2,0:T(8,128)(2,1)} %all-to-all-done), kind=kLoop, calls=%fused_computation.236 | loop fusion | bytes 2097152 | tf_op jit(solution)/shard_map/slice | solution.py:228
  95.5 2.6 %fusion.55 = (f32[8,128,2]{1,2,0:T(2,128)S(1)}, f32[8,2,128,128]{3,2,1,0:T(8,128)}) fusion(f32[8,128,128]{1,2,0:T(8,128)S(1)} %copy-done.6, bf16[8,128,2,128]{1,3,2,0:T(8,128)(2,1)} %bitcast.309, f32[8,2,128,128]{3,0,2,1:T(8,128)S(1)} %convolution_bitcast_fusion.1), kind=kOutput, calls=%fused_computation.88 | convolution fusion | flops 201848832 | bytes 3153920 | tf_op jit(solution)/shard_map/transpose(jvp(vmap(hs,sn,shp->hnp)))/dot_general | solution.py:53
  99.9 2.3 %convolution_bitcast_fusion.6 = f32[8,8,2]{1,0,2:T(8,128)} fusion(f32[2,128,128,8]{2,3,1,0:T(8,128)S(1)} %copy.434, f32[8,2,128,128]{3,2,1,0:T(8,128)S(1)} %fusion.32), kind=kOutput, calls=%fused_computation.82 | convolution fusion | flops 12582912 | bytes 2097664 | tf_op jit(solution)/shard_map/transpose(jvp(kjh,jhnp->khnp))/dot_general | solution.py:102
  102.3 2.1 %convolution_bitcast_fusion.3 = f32[8,2,128,128]{3,0,2,1:T(8,128)} fusion(f32[8,2,128,128]{3,2,1,0:T(8,128)S(1)} %fusion.32, f32[8,8,2]{1,0,2:T(8,128)S(1)} %copy-done.17), kind=kOutput, calls=%fused_computation.65 | convolution fusion | flops 12582912 | bytes 2097664 | tf_op jit(solution)/shard_map/jvp(kjh,jhnp->khnp)/dot_general | solution.py:102
  105.7 1.7 fusion.65
  107.4 1.8 fusion.40
  110.5 3.4 %fusion.44 = bf16[8,128,2,128]{1,3,2,0:T(8,128)(2,1)} fusion(f32[8,128,2,128]{1,3,2,0:T(8,128)} %fusion.40, f32[8,2,128,128]{3,0,2,1:T(8,128)S(1)} %convolution_bitcast_fusion.1, f32[8,128,2]{1,2,0:T(2,128)S(1)} %copy.429, f32[8,128,128]{2,1,0:T(8,128)S(1)} %copy-done.1), kind=kOutput, calls=%fused_computation.72 | convolution fusion | flops 202113024 | bytes 3153920 | tf_op jit(solution)/shard_map/transpose(jvp(vmap(hs,sn,shp->hnp)))/dot_general | solution.py:53
  114.4 1.6 copy.433
  116.1 1.5 multiply_reduce_fusion.6
  118.3 1.5 multiply_reduce_fusion.4
  130.2 1.7 fusion.53
  132.0 1.9 fusion.43
  134.0 2.7 %reduce_window_sum.47 = f32[8,2,128]{2,0,1:T(8,128)S(1)} reduce-window(f32[8,2,128]{2,0,1:T(8,128)S(1)} %get-tuple-element.1118, f32[]{:T(128)} %constant.168.clone.1), window={size=1x1x128 pad=0_0x0_0x0_127}, to_apply=%region_15.16 | reduce-window | flops 260096 | bytes 16388 | tf_op jit(solution)/shard_map/transpose(jvp(jit(cumsum)))/reduce_window_sum | solution.py:91
  136.8 2.5 %reduce_window_sum.46 = f32[8,2,128]{2,0,1:T(8,128)S(1)} reduce-window(f32[8,2,128]{2,0,1:T(8,128)S(1)} %get-tuple-element.1119, f32[]{:T(128)} %constant.168.clone.1), window={size=1x1x128 pad=0_0x0_0x0_127}, to_apply=%region_7.8 | reduce-window | flops 260096 | bytes 16388 | tf_op jit(solution)/shard_map/transpose(jvp(vmap(jit(cumsum))))/reduce_window_sum | solution.py:45
  139.3 1.9 constant_dynamic-update-slice_fusion.6
  141.2 2.0 %constant_dynamic-update-slice_fusion.5 = bf16[8,128,784]{1,2,0:T(8,128)(2,1)} fusion(bf16[8,128,784]{1,2,0:T(8,128)(2,1)} %constant_dynamic-update-slice_fusion.6, bf16[8,128,256]{1,2,0:T(8,128)(2,1)} %bitcast.316), kind=kLoop, calls=%fused_computation.139 | loop fusion | bytes 1048576
  144.4 2.0 %fusion.50 = bf16[8,128,784]{1,2,0:T(8,128)(2,1)} fusion(bf16[8,128,784]{1,2,0:T(8,128)(2,1)} %constant_dynamic-update-slice_fusion.5, f32[8,128,128]{1,2,0:T(8,128)S(1)} %fusion.54, f32[8,128,128]{2,1,0:T(8,128)S(1)} %copy-done.5, bf16[8,128,776]{1,2,0:T(8,128)(2,1)} %all-to-all-done), kind=kOutput, calls=%fused_computation.78 | convolution fusion | flops 100925440 | bytes 1572864 | tf_op jit(solution)/shard_map/transpose(jvp(vmap()))/dot_general | solution.py:66
  146.4 2.2 %fusion.52 = bf16[8,128,784]{1,2,0:T(8,128)(2,1)} fusion(bf16[8,128,784]{1,2,0:T(8,128)(2,1)} %fusion.50, f32[8,128,128]{1,2,0:T(8,128)S(1)} %fusion.48, f32[8,128,128]{2,1,0:T(8,128)S(1)} %copy-done.5, bf16[8,128,776]{1,2,0:T(8,128)(2,1)} %all-to-all-done), kind=kOutput, calls=%fused_computation.80 | convolution fusion | flops 100925440 | bytes 1572864 | tf_op jit(solution)/shard_map/transpose(jvp(vmap()))/dot_general | solution.py:66
  149.2 5.7 %all-to-all-start.1 = ((bf16[8,128,784]{1,2,0:T(8,128)(2,1)}), bf16[8,128,784]{1,2,0:T(8,128)(2,1)S(1)}, u32[]{:S(2)}, u32[]{:S(2)}) async-start(bf16[8,128,784]{1,2,0:T(8,128)(2,1)} %bitcast_dynamic-update-slice_fusion), calls=%async_computation.1 | async-start | bytes 3211264 | tf_op jit(solution)/shard_map/all_to_all | solution.py:370
  159.6 32.2 %all-to-all-done.1 = bf16[8,128,784]{1,2,0:T(8,128)(2,1)S(1)} async-done(((bf16[8,128,784]{1,2,0:T(8,128)(2,1)}), bf16[8,128,784]{1,2,0:T(8,128)(2,1)S(1)}, u32[]{:S(2)}, u32[]{:S(2)}) %all-to-all-start.1) | async-done | bytes 1605664 | tf_op jit(solution)/shard_map/all_to_all | solution.py:370
  (243 shorter events, 70.1 us)
Async XLA Ops:
  0.6 10.5 %copy-start.32 = (f32[16,128]{1,0:T(8,128)S(1)}, f32[16,128]{1,0:T(8,128)}, u32[]{:S(2)}) copy-start(f32[16,128]{1,0:T(8,128)} %param.26) | copy-start | bytes 24580
  0.7 10.6 %copy-start.24 = (bf16[128,128]{1,0:T(8,128)(2,1)S(1)}, bf16[128,128]{1,0:T(8,128)(2,1)}, u32[]{:S(2)}) copy-start(bf16[128,128]{1,0:T(8,128)(2,1)} %param.24) | copy-start | bytes 98308
  0.7 10.7 %copy-start.25 = (bf16[128,128]{1,0:T(8,128)(2,1)S(1)}, bf16[128,128]{1,0:T(8,128)(2,1)}, u32[]{:S(2)}) copy-start(bf16[128,128]{1,0:T(8,128)(2,1)} %param.25) | copy-start | bytes 98308
  0.7 10.8 %copy-start.11 = (bf16[128,1024]{1,0:T(8,128)(2,1)S(1)}, bf16[128,1024]{1,0:T(8,128)(2,1)}, u32[]{:S(2)}) copy-start(bf16[128,1024]{1,0:T(8,128)(2,1)} %param.33) | copy-start | bytes 786436
  1.6 10.0 %copy-start.12 = (bf16[128,1024]{1,0:T(8,128)(2,1)S(1)}, bf16[128,1024]{1,0:T(8,128)(2,1)}, u32[]{:S(2)}) copy-start(bf16[128,1024]{1,0:T(8,128)(2,1)} %param.29) | copy-start | bytes 786436
  2.9 9.1 %copy-start.7 = (bf16[128,2048]{1,0:T(8,128)(2,1)S(1)}, bf16[128,2048]{1,0:T(8,128)(2,1)}, u32[]{:S(2)}) copy-start(bf16[128,2048]{1,0:T(8,128)(2,1)} %param.23) | copy-start | bytes 1572868
  2.9 9.4 %copy-start.8 = (bf16[128,2048]{1,0:T(8,128)(2,1)S(1)}, bf16[128,2048]{1,0:T(8,128)(2,1)}, u32[]{:S(2)}) copy-start(bf16[128,2048]{1,0:T(8,128)(2,1)} %param.32) | copy-start | bytes 1572868
  2.9 33.2 %all-to-all-start.2 = ((bf16[8,128,512]{1,2,0:T(8,128)(2,1)}), bf16[8,128,512]{1,2,0:T(8,128)(2,1)S(1)}, u32[]{:S(2)}, u32[]{:S(2)}) async-start(bf16[8,128,512]{1,2,0:T(8,128)(2,1)} %broadcast_in_dim.296), calls=%async_computation.2 | async-start | bytes 2097152 | tf_op jit(solution)/shard_map/all_to_all | solution.py:237
  10.3 2.3 %copy-start.39 = (f32[16]{0:T(128)S(1)}, f32[16]{0:T(128)}, u32[]{:S(2)}) copy-start(f32[16]{0:T(128)} %param.27) | copy-start | bytes 196
  36.1 41.2 %all-to-all-start = ((bf16[8,128,776]{1,2,0:T(8,128)(2,1)}), bf16[8,128,776]{1,2,0:T(8,128)(2,1)}, u32[]{:S(2)}, u32[]{:S(2)}) async-start(bf16[8,128,776]{1,2,0:T(8,128)(2,1)} %constant_dynamic-update-slice_fusion.2), calls=%async_computation | async-start | bytes 3178496 | tf_op jit(solution)/shard_map/all_to_all | solution.py:226
  45.8 41.9 %copy-start.22 = (f32[8,128]{1,0:T(8,128)}, f32[8,128]{1,0:T(8,128)S(1)}, u32[]{:S(2)}) copy-start(f32[8,128]{1,0:T(8,128)S(1)} %get-tuple-element.1130) | copy-start | bytes 12292
  63.7 23.2 %copy-start.37 = (f32[8]{0:T(128)S(1)}, f32[8]{0:T(128)}, u32[]{:S(2)}) copy-start(f32[8]{0:T(128)} %convert_reduce_fusion.6) | copy-start | bytes 100
  77.3 71.9 %all-to-all-start.3 = ((bf16[8,128,512]{1,2,0:T(8,128)(2,1)}), bf16[8,128,512]{1,2,0:T(8,128)(2,1)}, u32[]{:S(2)}, u32[]{:S(2)}) async-start(bf16[8,128,512]{1,2,0:T(8,128)(2,1)} %copy.476), calls=%async_computation.3 | async-start | bytes 2097152 | tf_op jit(solution)/shard_map/all_to_all | solution.py:371
  83.3 6.5 %copy-start.28 = (f32[8,2]{0,1:T(2,128)}, f32[8,2]{0,1:T(2,128)S(1)}, u32[]{:S(2)}) copy-start(f32[8,2]{0,1:T(2,128)S(1)} %slice_reduce_fusion) | copy-start | bytes 196
  87.7 3.9 %copy-start.13 = (f32[8,128,2]{1,2,0:T(2,128)}, f32[8,128,2]{1,2,0:T(2,128)S(1)}, u32[]{:S(2)}) copy-start(f32[8,128,2]{1,2,0:T(2,128)S(1)} %copy.428) | copy-start | bytes 24580
  94.5 3.7 %copy-start.16 = (f32[8,8,2]{1,0,2:T(8,128)}, f32[8,8,2]{1,0,2:T(8,128)S(1)}, u32[]{:S(2)}) copy-start(f32[8,8,2]{1,0,2:T(8,128)S(1)} %stack.2) | copy-start | bytes 1540
  95.1 3.0 %copy-start.20 = (f32[8,128]{1,0:T(8,128)S(1)}, f32[8,128]{1,0:T(8,128)}, u32[]{:S(2)}) copy-start(f32[8,128]{1,0:T(8,128)} %get-tuple-element.1131) | copy-start | bytes 12292
  95.2 3.0 %copy-start.29 = (f32[8,2]{0,1:T(2,128)S(1)}, f32[8,2]{0,1:T(2,128)}, u32[]{:S(2)}) copy-start(f32[8,2]{0,1:T(2,128)} %copy-done.28) | copy-start | bytes 196
  95.2 3.7 %copy-start = (f32[8,128,128]{2,1,0:T(8,128)S(1)}, f32[8,128,128]{2,1,0:T(8,128)}, u32[]{:S(2)}) copy-start(f32[8,128,128]{2,1,0:T(8,128)} %convert.42) | copy-start | bytes 1572868
  95.2 3.7 %copy-start.2 = (bf16[8,128,256]{1,2,0:T(8,128)(2,1)S(1)}, bf16[8,128,256]{1,2,0:T(8,128)(2,1)}, u32[]{:S(2)}) copy-start(bf16[8,128,256]{1,2,0:T(8,128)(2,1)} %get-tuple-element.1111) | copy-start | bytes 1572868
  98.9 3.4 %copy-start.17 = (f32[8,8,2]{1,0,2:T(8,128)S(1)}, f32[8,8,2]{1,0,2:T(8,128)}, u32[]{:S(2)}) copy-start(f32[8,8,2]{1,0,2:T(8,128)} %copy-done.16) | copy-start | bytes 1540
  102.3 3.4 %copy-start.33 = (f32[8,2,128]{2,1,0:T(2,128)S(1)}, f32[8,2,128]{2,1,0:T(2,128)}, u32[]{:S(2)}) copy-start(f32[8,2,128]{2,1,0:T(2,128)} %copy.424) | copy-start | bytes 24580
  105.7 3.5 %copy-start.9 = (f32[8,128,128]{2,1,0:T(8,128)}, f32[8,128,128]{2,1,0:T(8,128)S(1)}, u32[]{:S(2)}) copy-start(f32[8,128,128]{2,1,0:T(8,128)S(1)} %fusion.87) | copy-start | bytes 1572868
  107.4 3.0 %copy-start.1 = (f32[8,128,128]{2,1,0:T(8,128)S(1)}, f32[8,128,128]{2,1,0:T(8,128)}, u32[]{:S(2)}) copy-start(f32[8,128,128]{2,1,0:T(8,128)} %convert.42) | copy-start | bytes 1572868
  109.2 4.6 %copy-start.31 = (f32[8,8,2]{1,0,2:T(8,128)S(1)}, f32[8,8,2]{1,0,2:T(8,128)}, u32[]{:S(2)}) copy-start(f32[8,8,2]{1,0,2:T(8,128)} %convolution_bitcast_fusion.6) | copy-start | bytes 1540
  114.4 17.6 %copy-start.3 = (bf16[8,128,256]{1,2,0:T(8,128)(2,1)S(1)}, bf16[8,128,256]{1,2,0:T(8,128)(2,1)}, u32[]{:S(2)}) copy-start(bf16[8,128,256]{1,2,0:T(8,128)(2,1)} %get-tuple-element.1111) | copy-start | bytes 1572868
  114.4 17.6 %copy-start.10 = (f32[8,128,128]{2,1,0:T(8,128)S(1)}, f32[8,128,128]{2,1,0:T(8,128)}, u32[]{:S(2)}) copy-start(f32[8,128,128]{2,1,0:T(8,128)} %copy-done.9) | copy-start | bytes 1572868
  131.9 2.0 %copy-start.19 = (f32[8,128,2]{1,2,0:T(2,128)S(1)}, f32[8,128,2]{1,2,0:T(2,128)}, u32[]{:S(2)}) copy-start(f32[8,128,2]{1,2,0:T(2,128)} %copy-done.18) | copy-start | bytes 24580
  133.9 9.3 %copy-start.4 = (f32[8,2,128,128]{3,2,1,0:T(8,128)S(1)}, f32[8,2,128,128]{3,2,1,0:T(8,128)}, u32[]{:S(2)}) copy-start(f32[8,2,128,128]{3,2,1,0:T(8,128)} %get-tuple-element.1135) | copy-start | bytes 3145732
  133.9 9.4 %copy-start.15 = (f32[8,128,2]{1,2,0:T(2,128)S(1)}, f32[8,128,2]{1,2,0:T(2,128)}, u32[]{:S(2)}) copy-start(f32[8,128,2]{1,2,0:T(2,128)} %copy-done.13) | copy-start | bytes 24580
  149.2 42.6 %all-to-all-start.1 = ((bf16[8,128,784]{1,2,0:T(8,128)(2,1)}), bf16[8,128,784]{1,2,0:T(8,128)(2,1)S(1)}, u32[]{:S(2)}, u32[]{:S(2)}) async-start(bf16[8,128,784]{1,2,0:T(8,128)(2,1)} %bitcast_dynamic-update-slice_fusion), calls=%async_computation.1 | async-start | bytes 3211264 | tf_op jit(solution)/shard_map/all_to_all | solution.py:370
  194.0 1.4 collective-permute-start
  (15 other events, 24.6 us)

commit v11 on v9

--- a/solution.py
+++ b/solution.py
@@ -339,30 +339,35 @@
     kv_terms = jnp.concatenate([term_key, term_value], axis=1).astype(jnp.bfloat16)
     kv_width = kv_terms.shape[1]
     if by_heads:
+        kv_got = lax.all_to_all(
+            jnp.concatenate(
+                [
+                    kv_terms.reshape(seq_count, tokens, kv_width),
+                    mixed_own.reshape(seq_count, tokens, own_width),
+                ],
+                axis=2,
+            ),
+            "seq",
+            split_axis=0,
+            concat_axis=0,
+            tiled=True,
+        )
         sent = jnp.concatenate(
             [
-                mixed_own.reshape(seq_count, tokens, own_width),
                 x_grad_own.reshape(seq_count, tokens, own_width),
                 bc_part.astype(jnp.bfloat16).reshape(seq_count, tokens, bc_part.shape[1]),
             ],
             axis=2,
         )
         got = lax.all_to_all(sent, "seq", split_axis=0, concat_axis=0, tiled=True)
-        kv_got = lax.all_to_all(
-            kv_terms.reshape(seq_count, tokens, kv_width),
-            "seq",
-            split_axis=0,
-            concat_axis=0,
-            tiled=True,
-        )
 
         def from_owners(a):
             return a.transpose(1, 0, 2).reshape(tokens, seq_count * own_width)
 
-        mixer_out = from_owners(got[:, :, :own_width])
-        x_grad = from_owners(got[:, :, own_width : 2 * own_width])
-        kv_total = jnp.sum(kv_got.astype(jnp.float32), axis=0)
-        bc_sum = jnp.sum(got[:, :, 2 * own_width :].astype(jnp.float32), axis=0)
+        mixer_out = from_owners(kv_got[:, :, kv_width:])
+        x_grad = from_owners(got[:, :, :own_width])
+        kv_total = jnp.sum(kv_got[:, :, :kv_width].astype(jnp.float32), axis=0)
+        bc_sum = jnp.sum(got[:, :, own_width:].astype(jnp.float32), axis=0)
         grad_decay = bc_sum[:, 2 * state_width :].T
         bc_sum = bc_sum[:, : 2 * state_width]
         if lax.axis_size("head") == 2:

time: 184 us -> 183 us (level)
  starting transfers between devices: 26.7 us -> 34.3 us
  other arithmetic: 22.4 us -> 18.5 us
  local copies, waits for them, and re-layouts: 36 us -> 32.8 us
    all_to_all x1, waiting for transfers between devices: 0.01 us -> 28.2 us  [on_device(): lax.all_to_all(jnp.concatenate([kv_terms.reshape(seq_count, tokens, kv_wi...]
    all_to_all x1, waiting for transfers between devices: 17.2 us -> 0.01 us  [on_device(): lax.all_to_all(kv_sent, 'seq', split_axis=0, concat_axis=0, tiled=True)]
    all_to_all x1, starting transfers between devices: 5.05 us -> 12.4 us  [on_device(): lax.all_to_all(jnp.concatenate([kv_terms.reshape(seq_count, tokens, kv_wi...]
    all_to_all x2, waiting for transfers between devices: 43.8 us -> 36.7 us  [on_device(): got = lax.all_to_all(sent, 'seq', split_axis=0, concat_axis=0, tiled=True)]
    all_to_all x1, waiting for transfers between devices: 5.5 us -> 1.89 us  [mamba_by_heads(): lax.all_to_all(decay_log, 'seq', split_axis=0, concat_axis=1, tiled=True)]
    unnamed x142 -> x60, local copies, waits for them, and re-layouts: 12.2 us -> 8.6 us
    dot_general x3, matrix products: 5.56 us -> 2.22 us  [mixer_stretch(): jnp.dot(c_float, b_float.T, precision=precise)[None]]
    concatenate x1 -> x2, other arithmetic: 0.08 us -> 2.31 us  [the longest x1 1.26 us: on_device(): jnp.concatenate([kv_terms.reshape(seq_count, tokens, kv_width), mixed_own...]
  transfers between devices with their start and end apart: 6 -> 6, of which waited for: 4 -> 4; matrix products, arithmetic and copies ran while one was open for 45% -> 41% of each run, Pallas kernels for 0% -> 0%
where the time goes in v11:
time: 183 us
  waiting for transfers between devices  66.9 us (37%)
  starting transfers between devices  34.3 us (19%)
  local copies, waits for them, and re-layouts  32.8 us (18%)
  matrix products  28.5 us (16%)
  other arithmetic  18.5 us (10%)
    all_to_all x2, waiting for transfers between devices, on_device(): got = lax.all_to_all(sent, 'seq', split_axis=0, concat_axis=0, tiled=True)  36.7 us
    all_to_all x1, waiting for transfers between devices, on_device(): lax.all_to_all(jnp.concatenate([kv_terms.reshape(seq_count, tokens, kv_wi...  28.2 us
    all_to_all x1, starting transfers between devices, on_device(): lax.all_to_all(jnp.concatenate([kv_terms.reshape(seq_count, tokens, kv_wi...  12.4 us
    all_to_all x2, starting transfers between devices, on_device(): got = lax.all_to_all(sent, 'seq', split_axis=0, concat_axis=0, tiled=True)  9.99 us
    unnamed x60, local copies, waits for them, and re-layouts  8.6 us
    all_to_all x1, starting transfers between devices, mamba_by_heads(): lax.all_to_all(decay_log, 'seq', split_axis=0, concat_axis=1, tiled=True)  7.45 us
    dot_general x3, matrix products, mixer_stretch(): inner = jnp.einsum('hts,shp->thp', kernel, inputs, precision=precise)  5.8 us
    dot_general x3, matrix products, mixer_whole(): state_in = jnp.einsum('kjh,jhnp->khnp', reach, summary, precision=precise)  5.6 us
  transfers between devices with their start and end apart: 6, of which 4 were waited for; matrix products, arithmetic and copies ran while one was open for 41% of the time, Pallas kernels for 0%

profile of v11, /device:TPU:0, one launch (start us, length us, event | category | flops | bytes accessed | tf_op | source)
XLA Modules:
  0.0 182.5 jit_solution(3402926295652188302)
XLA Ops:
  0.7 7.5 %all-to-all-start.2 = ((f32[8,2,128]{2,1,0:T(2,128)}), f32[8,2,128]{2,1,0:T(2,128)S(1)}, u32[]{:S(2)}, u32[]{:S(2)}) async-start(f32[8,2,128]{2,1,0:T(2,128)} %bitcast.334), calls=%async_computation.2 | async-start | bytes 16384 | tf_op jit(solution)/shard_map/all_to_all | solution.py:117
  12.7 1.9 %all-to-all-done.2 = f32[8,2,128]{2,1,0:T(2,128)S(1)} async-done(((f32[8,2,128]{2,1,0:T(2,128)}), f32[8,2,128]{2,1,0:T(2,128)S(1)}, u32[]{:S(2)}, u32[]{:S(2)}) %all-to-all-start.2) | async-done | bytes 8224 | tf_op jit(solution)/shard_map/all_to_all | solution.py:117
  14.6 4.1 %all-to-all-start.1 = ((bf16[8,128,768]{2,1,0:T(8,128)(2,1)}), bf16[8,128,768]{2,1,0:T(8,128)(2,1)S(1)}, u32[]{:S(2)}, u32[]{:S(2)}) async-start(bf16[8,128,768]{2,1,0:T(8,128)(2,1)} %pad_maximum_fusion), calls=%async_computation.1 | async-start | bytes 3145728 | tf_op jit(solution)/shard_map/all_to_all | solution.py:211
  21.1 34.1 %all-to-all-done.1 = bf16[8,128,768]{2,1,0:T(8,128)(2,1)S(1)} async-done(((bf16[8,128,768]{2,1,0:T(8,128)(2,1)}), bf16[8,128,768]{2,1,0:T(8,128)(2,1)S(1)}, u32[]{:S(2)}, u32[]{:S(2)}) %all-to-all-start.1) | async-done | bytes 1572896 | tf_op jit(solution)/shard_map/all_to_all | solution.py:211
  56.3 4.4 %all-to-all-start = ((bf16[8,128,512]{1,2,0:T(8,128)(2,1)}), bf16[8,128,512]{1,2,0:T(8,128)(2,1)}, u32[]{:S(2)}, u32[]{:S(2)}) async-start(bf16[8,128,512]{1,2,0:T(8,128)(2,1)} %broadcast_in_dim.265), calls=%async_computation | async-start | bytes 2097152 | tf_op jit(solution)/shard_map/all_to_all | solution.py:217
  63.7 2.0 %copy.547 = bf16[8,128,256]{1,2,0:T(8,128)(2,1)} copy(bf16[8,128,256]{2,1,0:T(8,128)(2,1)} %get-tuple-element.1109) | data formatting | bytes 1048576 | tf_op jit(solution)/shard_map/jvp()/reshape;reshape | solution.py:85
  67.6 1.9 %convolution_bitcast_fusion.1 = f32[8,2,128,128]{3,0,2,1:T(8,128)S(1)} fusion(f32[2,128,128,8]{2,3,1,0:T(8,128)} %copy.450, f32[8,8,2]{1,0,2:T(8,128)S(1)} %stack.2), kind=kOutput, calls=%fused_computation.65 | convolution fusion | flops 12582912 | bytes 2097664 | tf_op jit(solution)/shard_map/transpose(jvp(kjh,jhnp->khnp))/dot_general | solution.py:102
  69.5 1.6 fusion.53
  72.4 2.1 %convolution_bitcast_fusion.3 = f32[8,2,128,128]{3,0,2,1:T(8,128)} fusion(f32[8,2,128,128]{3,2,1,0:T(8,128)S(1)} %fusion.32, f32[8,8,2]{1,0,2:T(8,128)S(1)} %stack.2), kind=kOutput, calls=%fused_computation.67 | convolution fusion | flops 12582912 | bytes 2097664 | tf_op jit(solution)/shard_map/jvp(kjh,jhnp->khnp)/dot_general | solution.py:102
  74.5 1.6 convolution_bitcast_fusion.6
  76.1 2.6 %copy.442 = f32[8,2,128,128]{2,3,1,0:T(8,128)} copy(f32[8,2,128,128]{3,0,2,1:T(8,128)} %convolution_bitcast_fusion.3) | data formatting | bytes 2097152 | tf_op jit(solution)/shard_map/jvp(kjh,jhnp->khnp)/transpose | solution.py:102
  78.6 3.1 %fusion.48 = f32[8,128,128]{1,2,0:T(8,128)} fusion(f32[8,2,128,128]{2,3,1,0:T(8,128)} %copy.442, bf16[8,128,2,128]{1,3,2,0:T(8,128)(2,1)S(1)} %bitcast.298, f32[8,128,2]{1,2,0:T(2,128)S(1)} %copy.437), kind=kOutput, calls=%fused_computation.76 | convolution fusion | flops 201850880 | bytes 2105344 | tf_op jit(solution)/shard_map/transpose(jvp(vmap(tn,hnp->thp)))/dot_general | solution.py:69
  83.4 3.0 %fusion.63 = (f32[8,2,128]{2,1,0:T(2,128)S(1)}, f32[8,2,128]{2,1,0:T(2,128)S(1)}, f32[8,128,128]{2,1,0:T(8,128)}) fusion(f32[8,128,128]{2,1,0:T(8,128)S(1)} %fusion.83, f32[8,2,128]{2,1,0:T(2,128)S(1)} %copy.434, pred[8,128,128]{2,1,0:T(8,128)(4,1)S(1)} %compare_and_fusion.3, bf16[8,2,128,128]{3,2,1,0:T(8,128)(2,1)S(1)} %bitcast.299, ...), kind=kOutput, calls=%fused_computation.99 | convolution fusion | flops 69332992 | bytes 2252800 | tf_op jit(solution)/shard_map/transpose(jvp(vmap(hts,shp->thp)))/dot_general | solution.py:67
  86.4 1.5 fusion.51
  88.0 2.5 %reduce_window_sum.46 = f32[8,2,128]{2,0,1:T(8,128)S(1)} reduce-window(f32[8,2,128]{2,0,1:T(8,128)S(1)} %get-tuple-element.1117, f32[]{:T(128)} %constant.152.clone.1), window={size=1x1x128 pad=0_0x0_0x0_127}, to_apply=%region_28.29 | reduce-window | flops 260096 | bytes 16388 | tf_op jit(solution)/shard_map/transpose(jvp(vmap(jit(cumsum))))/reduce_window_sum | solution.py:45
  90.5 2.7 %reduce_window_sum.47 = f32[8,2,128]{2,0,1:T(8,128)S(1)} reduce-window(f32[8,2,128]{2,0,1:T(8,128)S(1)} %get-tuple-element.1116, f32[]{:T(128)} %constant.152.clone.1), window={size=1x1x128 pad=0_0x0_0x0_127}, to_apply=%region_36.37 | reduce-window | flops 260096 | bytes 16388 | tf_op jit(solution)/shard_map/transpose(jvp(jit(cumsum)))/reduce_window_sum | solution.py:91
  100.0 5.9 %all-to-all-start.4 = ((bf16[8,128,528]{1,2,0:T(8,128)(2,1)}), bf16[8,128,528]{1,2,0:T(8,128)(2,1)S(1)}, u32[]{:S(2)}, u32[]{:S(2)}) async-start(bf16[8,128,528]{1,2,0:T(8,128)(2,1)} %pad_maximum_fusion.2), calls=%async_computation.4 | async-start | bytes 2162688 | tf_op jit(solution)/shard_map/all_to_all | solution.py:362
  106.5 1.5 copy.419
  110.4 1.7 while.51
  110.4 1.6 conditional.9
  113.0 3.3 %while.52 = (s32[]{:T(128)}, f32[128,2,4,128]{0,3,2,1:T(8,128)}, s32[]{:T(128)}, bf16[1024,256]{0,1:T(8,128)(2,1)S(1)}, s32[4]{0:T(128)S(1)}, /*index=5*/s32[128...) while((s32[]{:T(128)}, f32[128,2,4,128]{0,3,2,1:T(8,128)}, ...), condition=%wide.region_15.16_spmd.clone, body=%wide.region_10.15_spmd.clone.sunk | while | flops 271390848 | bytes 3031893 | solution.py:295
  113.0 3.3 %conditional.10 = (f32[128,2,4,128]{0,3,2,1:T(8,128)}) conditional(s32[]{:T(128)} %convert_element_type.253, f32[128,2,4,128]{0,3,2,1:T(8,128)} %get-tuple-element.1413, (s32[]{:T(128)}, bf16[1024,256]{0,1:T(8,128)(2,1)S(1)}, s32[]{:T(128)}, s32[4]{0:T(128)S(1)}, s32[128]{0:T(128)S(1)}, /*index=5*/bf16[1024,256]{0,1:T(8,128)(2,1)S(1)}, ...), branch_computations={%region_11.11_spmd, %region_12.14_spmd} | conditional | flops 271390848 | bytes 3031158 | solution.py:261
  113.5 2.8 %fusion.13 = f32[128,2,4,128]{0,3,2,1:T(8,128)} fusion(f32[128,2,4,128]{0,3,2,1:T(8,128)} %get-tuple-element.621, bf16[512,2,128,1]{0,2,3,1:T(8,128)(2,1)S(1)} %bitcast.303, bf16[512,2,128,1]{0,2,3,1:T(8,128)(2,1)S(1)} %bitcast.302, bf16[128,2,4,128]{3,0,2,1:T(8,128)(2,1)S(1)} %get-tuple-element.628, f32[2,4,128]{2,1,0:T(4,128)S(1)} %get-tuple-element.629, ...), kind=kOutput, calls=%fused_computation.19 | convolution fusion | flops 271187968 | bytes 1904640 | tf_op jit(solution)/shard_map/while/body/eval_jaxpr/cond/branch_1_fun/grtk,kgd->tgrd/dot_general | solution.py:291
  116.3 1.8 fusion.64
  119.9 4.1 %while.53 = (s32[]{:T(128)}, f32[128,2,4,128]{0,3,2,1:T(8,128)S(1)}, bf16[1024,256]{0,1:T(8,128)(2,1)}, bf16[1024,256]{0,1:T(8,128)(2,1)}, s32[]{:T(128)}, /*ind...) while((s32[]{:T(128)}, ...), condition=%wide.region_21.22_spmd.clone, body=%wide.region_16.21_spmd.clone.sunk | while | flops 675616896 | bytes 23483452 | solution.py:333
  119.9 4.1 %conditional.11 = ((f32[128,2,4,128]{0,3,2,1:T(8,128)S(1)}, bf16[1024,256]{0,1:T(8,128)(2,1)}, bf16[1024,256]{0,1:T(8,128)(2,1)})) conditional(s32[]{:T(128)} %convert_element_type.254, (f32[128,2,4,128]{0,3,2,1:T(8,128)S(1)}, bf16[1024,256]{0,1:T(8,128)(2,1)}, bf16[1024,256]{0,1:T(8,128)(2,1)}) %tuple.202, (s32[]{:T(128)}, ...), branch_computations={%region_17.17_spmd, %region_18.20_spmd} | conditional | flops 675616896 | bytes 23482630 | solution.py:261
  124.0 1.6 copy_bitcast_fusion
  125.8 2.0 %fusion.43 = bf16[8,128,2,128]{1,3,2,0:T(8,128)(2,1)S(1)} fusion(bf16[8,128,2,128]{1,3,2,0:T(8,128)(2,1)S(1)} %bitcast.307, f32[8,128,2,128]{1,3,2,0:T(8,128)S(1)} %bitcast.319, f32[2]{0:T(128)S(1)} %dynamic_slice.18, f32[8,128,2]{1,2,0:T(2,128)S(1)} %copy.437, f32[8,128,128]{2,1,0:T(8,128)S(1)} %copy-done.18, f32[8,2,128]{2,1,0:T(2,128)S(1)} %copy.434, ...), kind=kOutput, calls=%fused_computation.73 | convolution fusion | flops 203685888 | bytes 2768904 | tf_op jit(solution)/shard_map/jvp(vmap(hts,shp->thp))/dot_general | solution.py:67
  129.0 2.6 %all-to-all-done.4 = bf16[8,128,528]{1,2,0:T(8,128)(2,1)S(1)} async-done(((bf16[8,128,528]{1,2,0:T(8,128)(2,1)}), bf16[8,128,528]{1,2,0:T(8,128)(2,1)S(1)}, u32[]{:S(2)}, u32[]{:S(2)}) %all-to-all-start.4) | async-done | bytes 1081376 | tf_op jit(solution)/shard_map/all_to_all | solution.py:362
  131.6 12.4 %all-to-all-start.3 = ((bf16[8,128,768]{1,2,0:T(8,128)(2,1)}), bf16[8,128,768]{1,2,0:T(8,128)(2,1)S(1)}, u32[]{:S(2)}, u32[]{:S(2)}) async-start(bf16[8,128,768]{1,2,0:T(8,128)(2,1)} %pad_maximum_fusion.1), calls=%async_computation.3 | async-start | bytes 3145728 | tf_op jit(solution)/shard_map/all_to_all | solution.py:342
  144.9 1.8 copy.535
  151.6 28.2 %all-to-all-done.3 = bf16[8,128,768]{1,2,0:T(8,128)(2,1)S(1)} async-done(((bf16[8,128,768]{1,2,0:T(8,128)(2,1)}), bf16[8,128,768]{1,2,0:T(8,128)(2,1)S(1)}, u32[]{:S(2)}, u32[]{:S(2)}) %all-to-all-start.3) | async-done | bytes 1572896 | tf_op jit(solution)/shard_map/all_to_all | solution.py:342
  (206 shorter events, 43.7 us)
Async XLA Ops:
  0.6 10.1 %copy-start.15 = (bf16[128,2048]{1,0:T(8,128)(2,1)S(1)}, bf16[128,2048]{1,0:T(8,128)(2,1)}, u32[]{:S(2)}) copy-start(bf16[128,2048]{1,0:T(8,128)(2,1)} %param.32) | copy-start | bytes 1572868
  0.7 14.0 %all-to-all-start.2 = ((f32[8,2,128]{2,1,0:T(2,128)}), f32[8,2,128]{2,1,0:T(2,128)S(1)}, u32[]{:S(2)}, u32[]{:S(2)}) async-start(f32[8,2,128]{2,1,0:T(2,128)} %bitcast.334), calls=%async_computation.2 | async-start | bytes 16384 | tf_op jit(solution)/shard_map/all_to_all | solution.py:117
  9.2 2.1 %copy-start.24 = (bf16[128,128]{1,0:T(8,128)(2,1)S(1)}, bf16[128,128]{1,0:T(8,128)(2,1)}, u32[]{:S(2)}) copy-start(bf16[128,128]{1,0:T(8,128)(2,1)} %param.24) | copy-start | bytes 98308
  9.2 2.2 %copy-start.25 = (bf16[128,128]{1,0:T(8,128)(2,1)S(1)}, bf16[128,128]{1,0:T(8,128)(2,1)}, u32[]{:S(2)}) copy-start(bf16[128,128]{1,0:T(8,128)(2,1)} %param.25) | copy-start | bytes 98308
  11.3 1.4 copy-start.22
  11.3 1.4 copy-start.23
  12.7 6.2 %copy-start.26 = (f32[16]{0:T(128)S(1)}, f32[16]{0:T(128)}, u32[]{:S(2)}) copy-start(f32[16]{0:T(128)} %param.27) | copy-start | bytes 196
  14.6 40.6 %all-to-all-start.1 = ((bf16[8,128,768]{2,1,0:T(8,128)(2,1)}), bf16[8,128,768]{2,1,0:T(8,128)(2,1)S(1)}, u32[]{:S(2)}, u32[]{:S(2)}) async-start(bf16[8,128,768]{2,1,0:T(8,128)(2,1)} %pad_maximum_fusion), calls=%async_computation.1 | async-start | bytes 3145728 | tf_op jit(solution)/shard_map/all_to_all | solution.py:211
  19.8 76.9 %copy-start.21 = (pred[8,128,128]{2,1,0:T(8,128)(4,1)}, pred[8,128,128]{2,1,0:T(8,128)(4,1)S(1)}, u32[]{:S(2)}) copy-start(pred[8,128,128]{2,1,0:T(8,128)(4,1)S(1)} %compare_and_fusion.3) | copy-start | bytes 393220
  56.3 43.7 %all-to-all-start = ((bf16[8,128,512]{1,2,0:T(8,128)(2,1)}), bf16[8,128,512]{1,2,0:T(8,128)(2,1)}, u32[]{:S(2)}, u32[]{:S(2)}) async-start(bf16[8,128,512]{1,2,0:T(8,128)(2,1)} %broadcast_in_dim.265), calls=%async_computation | async-start | bytes 2097152 | tf_op jit(solution)/shard_map/all_to_all | solution.py:217
  67.6 2.0 %copy-start.5 = (bf16[8,128,256]{1,2,0:T(8,128)(2,1)S(1)}, bf16[8,128,256]{1,2,0:T(8,128)(2,1)}, u32[]{:S(2)}) copy-start(bf16[8,128,256]{1,2,0:T(8,128)(2,1)} %copy.547) | copy-start | bytes 1572868
  67.6 2.0 %copy-start.13 = (f32[8,128,128]{1,2,0:T(8,128)S(1)}, f32[8,128,128]{1,2,0:T(8,128)}, u32[]{:S(2)}) copy-start(f32[8,128,128]{1,2,0:T(8,128)} %copy.544) | copy-start | bytes 1572868
  69.5 1.8 %copy-start.3 = (f32[8,128,128]{2,1,0:T(8,128)S(1)}, f32[8,128,128]{2,1,0:T(8,128)}, u32[]{:S(2)}) copy-start(f32[8,128,128]{2,1,0:T(8,128)} %copy-done.2) | copy-start | bytes 1572868
  71.3 3.1 %copy-start = (f32[2,128,128,8]{2,3,1,0:T(8,128)S(1)}, f32[2,128,128,8]{2,3,1,0:T(8,128)}, u32[]{:S(2)}) copy-start(f32[2,128,128,8]{2,3,1,0:T(8,128)} %copy.450) | copy-start | bytes 3145732
  83.4 4.6 %copy-start.16 = (f32[8,128,128]{2,1,0:T(8,128)}, f32[8,128,128]{2,1,0:T(8,128)S(1)}, u32[]{:S(2)}) copy-start(f32[8,128,128]{2,1,0:T(8,128)S(1)} %fusion.83) | copy-start | bytes 1572868
  83.4 3.0 %copy-start.1 = (f32[8,2,128,128]{2,3,1,0:T(8,128)S(1)}, f32[8,2,128,128]{2,3,1,0:T(8,128)}, u32[]{:S(2)}) copy-start(f32[8,2,128,128]{2,3,1,0:T(8,128)} %copy.442) | copy-start | bytes 3145732
  93.2 3.0 %copy-start.7 = (f32[8,128,128]{2,1,0:T(8,128)S(1)}, f32[8,128,128]{2,1,0:T(8,128)}, u32[]{:S(2)}) copy-start(f32[8,128,128]{2,1,0:T(8,128)} %get-tuple-element.1008) | copy-start | bytes 1572868
  93.2 3.0 %copy-start.8 = (f32[8,128,128]{1,2,0:T(8,128)S(1)}, f32[8,128,128]{1,2,0:T(8,128)}, u32[]{:S(2)}) copy-start(f32[8,128,128]{1,2,0:T(8,128)} %fusion.48) | copy-start | bytes 1572868
  93.2 3.5 %copy-start.17 = (f32[8,128,128]{2,1,0:T(8,128)S(1)}, f32[8,128,128]{2,1,0:T(8,128)}, u32[]{:S(2)}) copy-start(f32[8,128,128]{2,1,0:T(8,128)} %copy-done.16) | copy-start | bytes 1572868
  96.2 1.4 copy-start.4
  98.9 6.9 %copy-start.19 = (bf16[128,1024]{1,0:T(8,128)(2,1)S(1)}, bf16[128,1024]{1,0:T(8,128)(2,1)}, u32[]{:S(2)}) copy-start(bf16[128,1024]{1,0:T(8,128)(2,1)} %param.29) | copy-start | bytes 786436
  100.0 6.2 %copy-start.20 = (bf16[128,1024]{1,0:T(8,128)(2,1)S(1)}, bf16[128,1024]{1,0:T(8,128)(2,1)}, u32[]{:S(2)}) copy-start(bf16[128,1024]{1,0:T(8,128)(2,1)} %param.33) | copy-start | bytes 786436
  100.0 31.7 %all-to-all-start.4 = ((bf16[8,128,528]{1,2,0:T(8,128)(2,1)}), bf16[8,128,528]{1,2,0:T(8,128)(2,1)S(1)}, u32[]{:S(2)}, u32[]{:S(2)}) async-start(bf16[8,128,528]{1,2,0:T(8,128)(2,1)} %pad_maximum_fusion.2), calls=%async_computation.4 | async-start | bytes 2162688 | tf_op jit(solution)/shard_map/all_to_all | solution.py:362
  108.0 2.4 %copy-start.27 = (s32[4]{0:T(128)S(1)}, s32[4]{0:T(128)}, u32[]{:S(2)}) copy-start(s32[4]{0:T(128)} %param.28) | copy-start | bytes 52
  121.7 1.0 copy-start.9
  121.7 1.2 copy-start.11
  123.0 1.0 copy-start.12
  124.0 1.6 copy-start.6
  124.0 1.7 copy-start.14
  124.0 1.8 copy-start.18
  131.6 48.2 %all-to-all-start.3 = ((bf16[8,128,768]{1,2,0:T(8,128)(2,1)}), bf16[8,128,768]{1,2,0:T(8,128)(2,1)S(1)}, u32[]{:S(2)}, u32[]{:S(2)}) async-start(bf16[8,128,768]{1,2,0:T(8,128)(2,1)} %pad_maximum_fusion.1), calls=%async_computation.3 | async-start | bytes 3145728 | tf_op jit(solution)/shard_map/all_to_all | solution.py:342
  147.5 1.7 collective-permute-start
  (2 other events, 1.6 us)

commit v12 on v11

--- a/solution.py
+++ b/solution.py
@@ -232,7 +232,7 @@
     logit_scale = 1.0 / math.sqrt(HEAD_SIZE)
     groups = attention_key_rows.shape[1] // HEAD_SIZE
     heads_per_group = queries.shape[1] // HEAD_SIZE // groups
-    key_span = min(512, total_len)
+    key_span = total_len
     blocks = total_len // key_span
     last_pos = offset + tokens - 1
     query_grid = queries.reshape(tokens, groups, heads_per_group, HEAD_SIZE)

time: 183 us -> 193 us (1.055)
  matrix products: 28.5 us -> 38.7 us
  starting transfers between devices: 34.3 us -> 28.9 us
  other arithmetic: 18.5 us -> 22.4 us
  waiting for transfers between devices: 66.9 us -> 64.3 us
  local copies, waits for them, and re-layouts: 32.8 us -> 35.4 us
    all_to_all x1, starting transfers between devices: 12.4 us -> 6.02 us  [on_device(): lax.all_to_all(jnp.concatenate([kv_terms.reshape(seq_count, tokens, kv_wi...]
    another operation x3 -> x17, local copies, waits for them, and re-layouts: 0.9 us -> 5.98 us
    dot_general x1, matrix products: 0.49 us -> 3.92 us  [grad_terms(): jnp.einsum('tgrd,kgd->grtk', cotangent_table, value_blk, preferred_elemen...]
    cond x9 -> x21, local copies, waits for them, and re-layouts: 0.87 us -> 3.88 us
    all_to_all x2, waiting for transfers between devices: 36.7 us -> 34.2 us  [on_device(): got = lax.all_to_all(sent, 'seq', split_axis=0, concat_axis=0, tiled=True)]
    dot_general x2, matrix products: 1.26 us -> 3.36 us  [block_view(): jnp.einsum('tgrd,kgd->grtk', query_grid, key_blk, preferred_element_type=...]
    unnamed x1 -> x3, other arithmetic: 0.01 us -> 1.95 us
  transfers between devices with their start and end apart: 6 -> 6, of which waited for: 4 -> 3; matrix products, arithmetic and copies ran while one was open for 41% -> 47% of each run, Pallas kernels for 0% -> 0%
where the time goes in v12:
time: 193 us; the launch traced here: 191 us
  waiting for transfers between devices  64.3 us (33%)
  matrix products  38.7 us (20%)
  local copies, waits for them, and re-layouts  35.4 us (18%)
  starting transfers between devices  28.9 us (15%)
  other arithmetic  22.4 us (12%)
    all_to_all x2, waiting for transfers between devices, on_device(): got = lax.all_to_all(sent, 'seq', split_axis=0, concat_axis=0, tiled=True)  34.2 us
    all_to_all x1, waiting for transfers between devices, on_device(): lax.all_to_all(jnp.concatenate([kv_terms.reshape(seq_count, tokens, kv_wi...  29.2 us
    all_to_all x2, starting transfers between devices, on_device(): got = lax.all_to_all(sent, 'seq', split_axis=0, concat_axis=0, tiled=True)  11 us
    unnamed x60, local copies, waits for them, and re-layouts  8.81 us
    all_to_all x1, starting transfers between devices, mamba_by_heads(): lax.all_to_all(decay_log, 'seq', split_axis=0, concat_axis=1, tiled=True)  7.45 us
    dot_general x3, matrix products, mixer_stretch(): inner = jnp.einsum('hts,shp->thp', kernel, inputs, precision=precise)  6.46 us
    all_to_all x1, starting transfers between devices, on_device(): lax.all_to_all(jnp.concatenate([kv_terms.reshape(seq_count, tokens, kv_wi...  6.02 us
    another operation x17, local copies, waits for them, and re-layouts  5.98 us
  transfers between devices with their start and end apart: 6, of which 3 were waited for; matrix products, arithmetic and copies ran while one was open for 47% of the time, Pallas kernels for 0%

profile of v12, /device:TPU:0, one launch (start us, length us, event | category | flops | bytes accessed | tf_op | source)
XLA Modules:
  0.0 191.4 jit_solution(8708285777838231408)
XLA Ops:
  0.7 7.5 %all-to-all-start.2 = ((f32[8,2,128]{2,1,0:T(2,128)}), f32[8,2,128]{2,1,0:T(2,128)S(1)}, u32[]{:S(2)}, u32[]{:S(2)}) async-start(f32[8,2,128]{2,1,0:T(2,128)} %bitcast.321), calls=%async_computation.2 | async-start | bytes 16384 | tf_op jit(solution)/shard_map/all_to_all | solution.py:117
  14.6 5.1 %all-to-all-start.1 = ((bf16[8,128,768]{2,1,0:T(8,128)(2,1)}), bf16[8,128,768]{2,1,0:T(8,128)(2,1)S(1)}, u32[]{:S(2)}, u32[]{:S(2)}) async-start(bf16[8,128,768]{2,1,0:T(8,128)(2,1)} %pad_maximum_fusion), calls=%async_computation.1 | async-start | bytes 3145728 | tf_op jit(solution)/shard_map/all_to_all | solution.py:211
  22.0 34.2 %all-to-all-done.1 = bf16[8,128,768]{2,1,0:T(8,128)(2,1)S(1)} async-done(((bf16[8,128,768]{2,1,0:T(8,128)(2,1)}), bf16[8,128,768]{2,1,0:T(8,128)(2,1)S(1)}, u32[]{:S(2)}, u32[]{:S(2)}) %all-to-all-start.1) | async-done | bytes 1572896 | tf_op jit(solution)/shard_map/all_to_all | solution.py:211
  57.3 4.4 %all-to-all-start = ((bf16[8,128,512]{2,1,0:T(8,128)(2,1)}), bf16[8,128,512]{2,1,0:T(8,128)(2,1)}, u32[]{:S(2)}, u32[]{:S(2)}) async-start(bf16[8,128,512]{2,1,0:T(8,128)(2,1)} %broadcast_in_dim.268), calls=%async_computation | async-start | bytes 2097152 | tf_op jit(solution)/shard_map/all_to_all | solution.py:217
  63.3 1.3 copy.312
  64.7 2.0 %copy.419 = bf16[8,128,256]{1,2,0:T(8,128)(2,1)} copy(bf16[8,128,256]{2,1,0:T(8,128)(2,1)} %get-tuple-element.468) | data formatting | bytes 1048576 | tf_op jit(solution)/shard_map/jvp()/reshape;reshape | solution.py:85
  68.5 1.9 %convolution_bitcast_fusion.2 = f32[8,2,128,128]{3,0,2,1:T(8,128)S(1)} fusion(f32[2,128,128,8]{2,3,1,0:T(8,128)} %copy.312, f32[8,8,2]{1,0,2:T(8,128)S(1)} %stack.2), kind=kOutput, calls=%fused_computation.68 | convolution fusion | flops 12582912 | bytes 2097664 | tf_op jit(solution)/shard_map/transpose(jvp(kjh,jhnp->khnp))/dot_general | solution.py:102
  70.5 2.9 %fusion.69 = (f32[8,128,2]{1,2,0:T(2,128)S(1)}, f32[8,2,128,128]{3,2,1,0:T(8,128)}) fusion(f32[8,128,128]{1,2,0:T(8,128)} %copy.416, bf16[8,128,2,128]{1,3,2,0:T(8,128)(2,1)} %bitcast.284, f32[8,2,128,128]{3,0,2,1:T(8,128)S(1)} %convolution_bitcast_fusion.2), kind=kOutput, calls=%fused_computation.91 | convolution fusion | flops 201848832 | bytes 3153920 | tf_op jit(solution)/shard_map/transpose(jvp(vmap(hs,sn,shp->hnp)))/dot_general | solution.py:53
  74.6 2.1 %convolution_bitcast_fusion.4 = f32[8,2,128,128]{3,0,2,1:T(8,128)} fusion(f32[8,2,128,128]{3,2,1,0:T(8,128)S(1)} %fusion.48, f32[8,8,2]{1,0,2:T(8,128)S(1)} %stack.2), kind=kOutput, calls=%fused_computation.70 | convolution fusion | flops 12582912 | bytes 2097664 | tf_op jit(solution)/shard_map/jvp(kjh,jhnp->khnp)/dot_general | solution.py:102
  76.7 1.6 convolution_bitcast_fusion.7
  78.3 2.6 %copy.306 = f32[8,2,128,128]{2,3,1,0:T(8,128)} copy(f32[8,2,128,128]{3,0,2,1:T(8,128)} %convolution_bitcast_fusion.4) | data formatting | bytes 2097152 | tf_op jit(solution)/shard_map/jvp(kjh,jhnp->khnp)/transpose | solution.py:102
  80.8 3.1 %fusion.64 = f32[8,128,128]{1,2,0:T(8,128)} fusion(f32[8,2,128,128]{2,3,1,0:T(8,128)} %copy.306, bf16[8,128,2,128]{1,3,2,0:T(8,128)(2,1)S(1)} %bitcast.278, f32[8,128,2]{1,2,0:T(2,128)S(1)} %copy.301), kind=kOutput, calls=%fused_computation.79 | convolution fusion | flops 201850880 | bytes 2105344 | tf_op jit(solution)/shard_map/transpose(jvp(vmap(tn,hnp->thp)))/dot_general | solution.py:69
  85.6 2.9 %fusion.79 = (f32[8,2,128]{2,1,0:T(2,128)S(1)}, f32[8,2,128]{2,1,0:T(2,128)S(1)}, f32[8,128,128]{2,1,0:T(8,128)}) fusion(f32[8,128,128]{2,1,0:T(8,128)S(1)} %fusion.98, f32[8,2,128]{2,1,0:T(2,128)S(1)} %copy.298, pred[8,128,128]{2,1,0:T(8,128)(4,1)S(1)} %compare_and_fusion, bf16[8,2,128,128]{3,2,1,0:T(8,128)(2,1)S(1)} %bitcast.279, ...), kind=kOutput, calls=%fused_computation.102 | convolution fusion | flops 69332992 | bytes 2252800 | tf_op jit(solution)/shard_map/transpose(jvp(vmap(hts,shp->thp)))/dot_general | solution.py:67
  88.5 1.5 fusion.67
  90.1 2.5 %reduce_window_sum.46 = f32[8,2,128]{2,0,1:T(8,128)S(1)} reduce-window(f32[8,2,128]{2,0,1:T(8,128)S(1)} %get-tuple-element.476, f32[]{:T(128)} %constant.126.clone.1), window={size=1x1x128 pad=0_0x0_0x0_127}, to_apply=%region_22.23 | reduce-window | flops 260096 | bytes 16388 | tf_op jit(solution)/shard_map/transpose(jvp(vmap(jit(cumsum))))/reduce_window_sum | solution.py:45
  92.6 2.7 %reduce_window_sum.47 = f32[8,2,128]{2,0,1:T(8,128)S(1)} reduce-window(f32[8,2,128]{2,0,1:T(8,128)S(1)} %get-tuple-element.475, f32[]{:T(128)} %constant.126.clone.1), window={size=1x1x128 pad=0_0x0_0x0_127}, to_apply=%region_30.31 | reduce-window | flops 260096 | bytes 16388 | tf_op jit(solution)/shard_map/transpose(jvp(jit(cumsum)))/reduce_window_sum | solution.py:91
  95.4 1.5 fusion.68
  96.9 1.4 fusion.65
  99.8 1.3 fusion.60
  102.2 5.9 %all-to-all-start.4 = ((bf16[8,128,528]{1,2,0:T(8,128)(2,1)}), bf16[8,128,528]{1,2,0:T(8,128)(2,1)}, u32[]{:S(2)}, u32[]{:S(2)}) async-start(bf16[8,128,528]{1,2,0:T(8,128)(2,1)} %pad_maximum_fusion.2), calls=%async_computation.4 | async-start | bytes 2162688 | tf_op jit(solution)/shard_map/all_to_all | solution.py:362
  110.7 2.4 %conditional.8 = ((f32[2,4,128]{2,1,0:T(4,128)S(1)}, f32[2,4,128]{2,1,0:T(4,128)S(1)})) conditional(s32[]{:T(128)} %convert_element_type.181, (f32[2,4,128]{2,1,0:T(4,128)S(1)}, f32[2,4,128]{2,1,0:T(4,128)S(1)}) %tuple.71, (s32[128]{0:T(128)S(1)}, s32[4]{0:T(128)S(1)}, s32[128]{0:T(128)S(1)}, bf16[1024,256]{1,0:T(8,128)(2,1)S(1)}, ...), branch_computations={%region_2.3_spmd, %region_3.8_spmd} | conditional | flops 277230592 | bytes 10679372 | solution.py:261
  113.7 8.3 %conditional.9 = (bf16[128,2,4,128]{0,3,2,1:T(8,128)(2,1)}, bf16[128,1024]{1,0:T(8,128)(2,1)S(1)}) conditional(s32[]{:T(128)} %convert_element_type.181, (f32[128,2,4,128]{3,0,2,1:T(8,128)S(1)}) %tuple.105, (s32[128]{0:T(128)S(1)}, s32[4]{0:T(128)S(1)}, s32[128]{0:T(128)S(1)}, bf16[1024,256]{1,0:T(8,128)(2,1)S(1)}, ...), branch_computations={%region_8.9_spmd, %region_9.12_spmd} | conditional | flops 542780416 | bytes 6063440
  117.6 3.3 %fusion.10 = bf16[128,2,4,128]{0,3,2,1:T(8,128)(2,1)} fusion(f32[128,2,4,128]{0,3,2,1:T(8,128)} %copy.290, bf16[1024,2,128,1]{0,2,3,1:T(8,128)(2,1)} %bitcast.307, bf16[128,2,4,128]{0,3,2,1:T(8,128)(2,1)S(1)} %get-tuple-element.404, f32[2,4,128]{2,1,0:T(4,128)S(1)} %copy-done.28, pred[128,1024]{0,1:T(8,128)(4,1)S(1)} %fusion.13, ...), kind=kOutput, calls=%fused_computation.17 | convolution fusion | flops 542375936 | bytes 2232320 | tf_op jit(solution)/shard_map/while/body/eval_jaxpr/cond/branch_1_fun/grtk,kgd->tgrd/dot_general | solution.py:291
  123.1 18.6 %conditional.10 = (f32[128,2,4,128]{3,0,2,1:T(8,128)S(1)}, bf16[8,128,256]{1,2,0:T(8,128)(2,1)}, bf16[8,128,256]{1,2,0:T(8,128)(2,1)}) conditional(s32[]{:T(128)} %convert_element_type.181, f32[128,2,4,128]{3,0,2,1:T(8,128)S(1)} %broadcast.1390, (s32[128]{0:T(128)}, s32[4]{0:T(128)}, s32[128]{0:T(128)}, bf16[1024,256]{1,0:T(8,128)(2,1)S(1)}, ...), branch_computations={%region_12.13_spmd, %region_13.16_spmd} | conditional | flops 1356081152 | bytes 52868464 | solution.py:261
  124.0 2.6 %fusion.41 = f32[2,1024,128,4]{2,1,3,0:T(8,128)} fusion(bf16[128,2,4,128]{0,3,2,1:T(8,128)(2,1)S(1)} %get-tuple-element.412, bf16[1024,2,128,1]{2,1,0,3:T(2,128)(2,1)S(1)} %bitcast.282), kind=kOutput, calls=%fused_computation.49 | convolution fusion | flops 268435456 | bytes 4980736 | tf_op jit(solution)/shard_map/while/body/eval_jaxpr/cond/branch_1_fun/tgrd,kgd->grtk/dot_general | solution.py:254
  128.7 3.9 %fusion.18 = bf16[2,4,128,1024]{2,3,1,0:T(8,128)(2,1)S(1)} fusion(f32[2,1024,128,4]{2,1,3,0:T(8,128)} %fusion.41, bf16[128,2,4,128]{0,3,2,1:T(8,128)(2,1)} %copy-done.10, f32[2,4,128]{2,1,0:T(4,128)S(1)} %multiply_reduce_fusion, f32[2,4,128]{2,1,0:T(4,128)} %get-tuple-element.242, pred[128,1024]{0,1:T(8,128)(4,1)} %fusion.39, ...), kind=kOutput, calls=%fused_computation.28 | convolution fusion | flops 275775488 | bytes 7217152 | tf_op jit(solution)/shard_map/while/body/eval_jaxpr/cond/branch_1_fun/tgrd,kgd->grtk/dot_general | solution.py:307
  132.7 1.5 fusion.36
  134.1 2.1 %copy.282 = bf16[1024,2,128]{0,2,1:T(8,128)(2,1)} copy(bf16[1024,2,128]{2,0,1:T(8,128)(2,1)} %fusion.36) | data formatting | bytes 1048576 | tf_op jit(solution)/shard_map/convert.7
  141.7 2.7 %fusion.59 = bf16[8,128,2,128]{1,3,2,0:T(8,128)(2,1)S(1)} fusion(bf16[8,128,2,128]{1,3,2,0:T(8,128)(2,1)} %bitcast.286, f32[8,128,2,128]{1,3,2,0:T(8,128)} %bitcast.305, f32[2]{0:T(128)} %copy-done.37, f32[8,128,2]{1,2,0:T(2,128)S(1)} %copy.301, f32[8,128,128]{2,1,0:T(8,128)} %copy-done.12, f32[8,2,128]{2,1,0:T(2,128)S(1)} %copy.298, ...), kind=kOutput, calls=%fused_computation.76 | convolution fusion | flops 203685888 | bytes 2768904 | tf_op jit(solution)/shard_map/jvp(vmap(hts,shp->thp))/dot_general | solution.py:67
  144.4 2.5 %pad_maximum_fusion.1 = bf16[8,128,768]{1,2,0:T(8,128)(2,1)} fusion(bf16[8,128,256]{1,2,0:T(8,128)(2,1)S(1)} %bitcast.309, bf16[8,128,256]{1,2,0:T(8,128)(2,1)} %get-tuple-element.432, bf16[8,128,256]{1,2,0:T(8,128)(2,1)} %get-tuple-element.431), kind=kLoop, calls=%fused_computation.58 | loop fusion | flops 4718592 | bytes 3145728 | tf_op jit(solution)/shard_map/concatenate | solution.py:343
  146.9 6.0 %all-to-all-start.3 = ((bf16[8,128,768]{1,2,0:T(8,128)(2,1)}), bf16[8,128,768]{1,2,0:T(8,128)(2,1)S(1)}, u32[]{:S(2)}, u32[]{:S(2)}) async-start(bf16[8,128,768]{1,2,0:T(8,128)(2,1)} %pad_maximum_fusion.1), calls=%async_computation.3 | async-start | bytes 3145728 | tf_op jit(solution)/shard_map/all_to_all | solution.py:342
  159.5 29.2 %all-to-all-done.3 = bf16[8,128,768]{1,2,0:T(8,128)(2,1)S(1)} async-done(((bf16[8,128,768]{1,2,0:T(8,128)(2,1)}), bf16[8,128,768]{1,2,0:T(8,128)(2,1)S(1)}, u32[]{:S(2)}, u32[]{:S(2)}) %all-to-all-start.3) | async-done | bytes 1572896 | tf_op jit(solution)/shard_map/all_to_all | solution.py:342
  (209 shorter events, 47.6 us)
Async XLA Ops:
  0.6 11.7 %copy-start.20 = (bf16[128,128]{1,0:T(8,128)(2,1)S(1)}, bf16[128,128]{1,0:T(8,128)(2,1)}, u32[]{:S(2)}) copy-start(bf16[128,128]{1,0:T(8,128)(2,1)} %param.18) | copy-start | bytes 98308
  0.7 11.7 %copy-start.21 = (bf16[128,128]{1,0:T(8,128)(2,1)S(1)}, bf16[128,128]{1,0:T(8,128)(2,1)}, u32[]{:S(2)}) copy-start(bf16[128,128]{1,0:T(8,128)(2,1)} %param.19) | copy-start | bytes 98308
  0.7 14.0 %all-to-all-start.2 = ((f32[8,2,128]{2,1,0:T(2,128)}), f32[8,2,128]{2,1,0:T(2,128)S(1)}, u32[]{:S(2)}, u32[]{:S(2)}) async-start(f32[8,2,128]{2,1,0:T(2,128)} %bitcast.321), calls=%async_computation.2 | async-start | bytes 16384 | tf_op jit(solution)/shard_map/all_to_all | solution.py:117
  8.9 4.8 %copy-start.30 = (s32[4,1]{0,1:T(1,128)}, s32[4,1]{0,1:T(1,128)S(1)}, u32[]{:S(2)}) copy-start(s32[4,1]{0,1:T(1,128)S(1)} %reduce-window.32) | copy-start | bytes 52
  12.4 7.4 %copy-start.32 = (f32[16]{0:T(128)S(1)}, f32[16]{0:T(128)}, u32[]{:S(2)}) copy-start(f32[16]{0:T(128)} %param.21) | copy-start | bytes 196
  12.4 7.9 %copy-start.18 = (bf16[128,256]{1,0:T(8,128)(2,1)S(1)}, bf16[128,256]{1,0:T(8,128)(2,1)}, u32[]{:S(2)}) copy-start(bf16[128,256]{1,0:T(8,128)(2,1)} %param.25) | copy-start | bytes 196612
  12.4 7.9 %copy-start.19 = (bf16[128,256]{1,0:T(8,128)(2,1)S(1)}, bf16[128,256]{1,0:T(8,128)(2,1)}, u32[]{:S(2)}) copy-start(bf16[128,256]{1,0:T(8,128)(2,1)} %param.24) | copy-start | bytes 196612
  14.6 41.6 %all-to-all-start.1 = ((bf16[8,128,768]{2,1,0:T(8,128)(2,1)}), bf16[8,128,768]{2,1,0:T(8,128)(2,1)S(1)}, u32[]{:S(2)}, u32[]{:S(2)}) async-start(bf16[8,128,768]{2,1,0:T(8,128)(2,1)} %pad_maximum_fusion), calls=%async_computation.1 | async-start | bytes 3145728 | tf_op jit(solution)/shard_map/all_to_all | solution.py:211
  19.9 79.0 %copy-start.37 = (f32[2]{0:T(128)}, f32[2]{0:T(128)S(1)}, u32[]{:S(2)}) copy-start(f32[2]{0:T(128)S(1)} %dynamic_slice.3) | copy-start | bytes 28
  57.3 44.9 %all-to-all-start = ((bf16[8,128,512]{2,1,0:T(8,128)(2,1)}), bf16[8,128,512]{2,1,0:T(8,128)(2,1)}, u32[]{:S(2)}, u32[]{:S(2)}) async-start(bf16[8,128,512]{2,1,0:T(8,128)(2,1)} %broadcast_in_dim.268), calls=%async_computation | async-start | bytes 2097152 | tf_op jit(solution)/shard_map/all_to_all | solution.py:217
  68.5 5.0 %copy-start.3 = (f32[8,128,128]{2,1,0:T(8,128)S(1)}, f32[8,128,128]{2,1,0:T(8,128)}, u32[]{:S(2)}) copy-start(f32[8,128,128]{2,1,0:T(8,128)} %copy-done.2) | copy-start | bytes 1572868
  68.5 5.1 %copy-start.5 = (bf16[8,128,256]{1,2,0:T(8,128)(2,1)S(1)}, bf16[8,128,256]{1,2,0:T(8,128)(2,1)}, u32[]{:S(2)}) copy-start(bf16[8,128,256]{1,2,0:T(8,128)(2,1)} %copy.419) | copy-start | bytes 1572868
  70.5 6.2 %copy-start = (f32[2,128,128,8]{2,3,1,0:T(8,128)S(1)}, f32[2,128,128,8]{2,3,1,0:T(8,128)}, u32[]{:S(2)}) copy-start(f32[2,128,128,8]{2,3,1,0:T(8,128)} %copy.312) | copy-start | bytes 3145732
  85.2 3.3 %copy-start.1 = (f32[8,2,128,128]{2,3,1,0:T(8,128)S(1)}, f32[8,2,128,128]{2,3,1,0:T(8,128)}, u32[]{:S(2)}) copy-start(f32[8,2,128,128]{2,3,1,0:T(8,128)} %copy.306) | copy-start | bytes 3145732
  85.6 4.5 %copy-start.12 = (f32[8,128,128]{2,1,0:T(8,128)}, f32[8,128,128]{2,1,0:T(8,128)S(1)}, u32[]{:S(2)}) copy-start(f32[8,128,128]{2,1,0:T(8,128)S(1)} %fusion.98) | copy-start | bytes 1572868
  95.3 3.0 %copy-start.7 = (f32[8,128,128]{2,1,0:T(8,128)S(1)}, f32[8,128,128]{2,1,0:T(8,128)}, u32[]{:S(2)}) copy-start(f32[8,128,128]{2,1,0:T(8,128)} %get-tuple-element.439) | copy-start | bytes 1572868
  95.3 3.6 %copy-start.13 = (f32[8,128,128]{2,1,0:T(8,128)S(1)}, f32[8,128,128]{2,1,0:T(8,128)}, u32[]{:S(2)}) copy-start(f32[8,128,128]{2,1,0:T(8,128)} %copy-done.12) | copy-start | bytes 1572868
  99.7 8.3 %copy-start.14 = (bf16[128,1024]{1,0:T(8,128)(2,1)S(1)}, bf16[128,1024]{1,0:T(8,128)(2,1)}, u32[]{:S(2)}) copy-start(bf16[128,1024]{1,0:T(8,128)(2,1)} %param.23) | copy-start | bytes 786436
  101.1 7.2 %copy-start.15 = (bf16[128,1024]{1,0:T(8,128)(2,1)S(1)}, bf16[128,1024]{1,0:T(8,128)(2,1)}, u32[]{:S(2)}) copy-start(bf16[128,1024]{1,0:T(8,128)(2,1)} %param.27) | copy-start | bytes 786436
  101.1 8.2 %copy-start.31 = (s32[4,1]{0,1:T(1,128)S(1)}, s32[4,1]{0,1:T(1,128)}, u32[]{:S(2)}) copy-start(s32[4,1]{0,1:T(1,128)} %copy-done.30) | copy-start | bytes 52
  102.2 8.5 %copy-start.33 = (s32[4]{0:T(128)S(1)}, s32[4]{0:T(128)}, u32[]{:S(2)}) copy-start(s32[4]{0:T(128)} %param.22) | copy-start | bytes 52
  102.2 44.7 %all-to-all-start.4 = ((bf16[8,128,528]{1,2,0:T(8,128)(2,1)}), bf16[8,128,528]{1,2,0:T(8,128)(2,1)}, u32[]{:S(2)}, u32[]{:S(2)}) async-start(bf16[8,128,528]{1,2,0:T(8,128)(2,1)} %pad_maximum_fusion.2), calls=%async_computation.4 | async-start | bytes 2162688 | tf_op jit(solution)/shard_map/all_to_all | solution.py:362
  109.3 4.4 %copy-start.22 = (s32[128]{0:T(128)}, s32[128]{0:T(128)S(1)}, u32[]{:S(2)}) copy-start(s32[128]{0:T(128)S(1)} %iota_add_fusion) | copy-start | bytes 1540
  109.4 4.3 %copy-start.25 = (s32[128]{0:T(128)}, s32[128]{0:T(128)S(1)}, u32[]{:S(2)}) copy-start(s32[128]{0:T(128)S(1)} %convert_reduce_fusion.7) | copy-start | bytes 1540
  113.7 9.4 %copy-start.8 = (f32[2,4,128,128]{2,3,1,0:T(8,128)S(1)}, f32[2,4,128,128]{2,3,1,0:T(8,128)}, u32[]{:S(2)}) copy-start(f32[2,4,128,128]{2,3,1,0:T(8,128)} %convert.41) | copy-start | bytes 1572868
  114.3 3.3 %copy-start.28 = (f32[2,4,128]{2,1,0:T(4,128)S(1)}, f32[2,4,128]{2,1,0:T(4,128)}, u32[]{:S(2)}) copy-start(f32[2,4,128]{2,1,0:T(4,128)} %get-tuple-element.234) | copy-start | bytes 12292 | tf_op jit(solution)/shard_map/conditional
  136.2 3.1 %copy-start.6 = (f32[2,1024,128,4]{2,1,3,0:T(8,128)S(1)}, f32[2,1024,128,4]{2,1,3,0:T(8,128)}, u32[]{:S(2)}) copy-start(f32[2,1024,128,4]{2,1,3,0:T(8,128)} %fusion.41) | copy-start | bytes 12582916 | tf_op jit(solution)/shard_map/while/body/eval_jaxpr/cond
  136.2 3.2 %copy-start.11 = (bf16[128,2,4,128]{0,3,2,1:T(8,128)(2,1)S(1)}, bf16[128,2,4,128]{0,3,2,1:T(8,128)(2,1)}, u32[]{:S(2)}) copy-start(bf16[128,2,4,128]{0,3,2,1:T(8,128)(2,1)} %copy-done.10) | copy-start | bytes 786436 | tf_op jit(solution)/shard_map/while/body/eval_jaxpr/cond
  136.2 3.2 %copy-start.17 = (pred[128,1024]{0,1:T(8,128)(4,1)S(1)}, pred[128,1024]{0,1:T(8,128)(4,1)}, u32[]{:S(2)}) copy-start(pred[128,1024]{0,1:T(8,128)(4,1)} %fusion.39) | copy-start | bytes 393220 | tf_op jit(solution)/shard_map/while/body/eval_jaxpr/cond
  136.2 3.2 %copy-start.29 = (f32[2,4,128]{2,1,0:T(4,128)S(1)}, f32[2,4,128]{2,1,0:T(4,128)}, u32[]{:S(2)}) copy-start(f32[2,4,128]{2,1,0:T(4,128)} %get-tuple-element.242) | copy-start | bytes 12292 | tf_op jit(solution)/shard_map/while/body/eval_jaxpr/cond
  146.9 41.8 %all-to-all-start.3 = ((bf16[8,128,768]{1,2,0:T(8,128)(2,1)}), bf16[8,128,768]{1,2,0:T(8,128)(2,1)S(1)}, u32[]{:S(2)}, u32[]{:S(2)}) async-start(bf16[8,128,768]{1,2,0:T(8,128)(2,1)} %pad_maximum_fusion.1), calls=%async_computation.3 | async-start | bytes 3145728 | tf_op jit(solution)/shard_map/all_to_all | solution.py:342
  155.2 2.8 %collective-permute-start = (f32[128,256]{0,1:T(8,128)S(1)}, f32[128,256]{0,1:T(8,128)S(1)}, u32[]{:S(2)}, u32[]{:S(2)}) collective-permute-start(f32[128,256]{0,1:T(8,128)S(1)} %slice.114), channel_id=1, source_target_pairs={{0,1},{1,0},{2,3},{3,2},{4,5},{5,4},{6,7},{7,6},{8,9},{9,8},{10,11... | collective-permute-start | bytes 393224 | tf_op jit(solution)/shard_map/ppermute | solution.py:374
  (12 other events, 24.6 us)

commit v13 on v12

--- a/solution.py
+++ b/solution.py
@@ -232,7 +232,7 @@
     logit_scale = 1.0 / math.sqrt(HEAD_SIZE)
     groups = attention_key_rows.shape[1] // HEAD_SIZE
     heads_per_group = queries.shape[1] // HEAD_SIZE // groups
-    key_span = total_len
+    key_span = min(256, total_len)
     blocks = total_len // key_span
     last_pos = offset + tokens - 1
     query_grid = queries.reshape(tokens, groups, heads_per_group, HEAD_SIZE)

time: 193 us -> 193 us (level)
  starting transfers between devices: 28.9 us -> 44.6 us
  matrix products: 38.7 us -> 25.2 us
  other arithmetic: 22.4 us -> 17.7 us
  waiting for transfers between devices: 64.3 us -> 67.6 us
    all_to_all x1, starting transfers between devices: 6.02 us -> 22.8 us  [on_device(): lax.all_to_all(jnp.concatenate([kv_terms.reshape(seq_count, tokens, kv_wi...]
    another operation x17 -> x3, local copies, waits for them, and re-layouts: 5.98 us -> 0.9 us
    all_to_all x2, waiting for transfers between devices: 34.2 us -> 38.1 us  [on_device(): got = lax.all_to_all(sent, 'seq', split_axis=0, concat_axis=0, tiled=True)]
    cond x21 -> x1, local copies, waits for them, and re-layouts: 3.88 us -> 0.01 us
    dot_general x1, matrix products: 3.92 us -> 0.35 us  [grad_terms(): jnp.einsum('tgrd,kgd->grtk', cotangent_table, value_blk, preferred_elemen...]
    dot_general x2, matrix products: 3.36 us -> 0.81 us  [block_view(): jnp.einsum('tgrd,kgd->grtk', query_grid, key_blk, preferred_element_type=...]
    unnamed x3 -> x1, other arithmetic: 1.95 us -> 0.01 us
    unnamed x60 -> x58, local copies, waits for them, and re-layouts: 8.81 us -> 9.98 us
  transfers between devices with their start and end apart: 6 -> 6, of which waited for: 3 -> 4; matrix products, arithmetic and copies ran while one was open for 47% -> 38% of each run, Pallas kernels for 0% -> 0%
where the time goes in v13:
time: 193 us; the launch traced here: 192 us
  waiting for transfers between devices  67.6 us (35%)
  starting transfers between devices  44.6 us (23%)
  local copies, waits for them, and re-layouts  35.1 us (18%)
  matrix products  25.2 us (13%)
  other arithmetic  17.7 us (9%)
    all_to_all x2, waiting for transfers between devices, on_device(): got = lax.all_to_all(sent, 'seq', split_axis=0, concat_axis=0, tiled=True)  38.1 us
    all_to_all x1, waiting for transfers between devices, on_device(): lax.all_to_all(jnp.concatenate([kv_terms.reshape(seq_count, tokens, kv_wi...  27.6 us
    all_to_all x1, starting transfers between devices, on_device(): lax.all_to_all(jnp.concatenate([kv_terms.reshape(seq_count, tokens, kv_wi...  22.8 us
    unnamed x58, local copies, waits for them, and re-layouts  9.98 us
    all_to_all x2, starting transfers between devices, on_device(): got = lax.all_to_all(sent, 'seq', split_axis=0, concat_axis=0, tiled=True)  9.98 us
    all_to_all x1, starting transfers between devices, mamba_by_heads(): lax.all_to_all(decay_log, 'seq', split_axis=0, concat_axis=1, tiled=True)  7.45 us
    dot_general x3, matrix products, mixer_whole(): state_in = jnp.einsum('kjh,jhnp->khnp', reach, summary, precision=precise)  5.6 us
    dot_general x3, matrix products, mixer_stretch(): inner = jnp.einsum('hts,shp->thp', kernel, inputs, precision=precise)  4.9 us
  transfers between devices with their start and end apart: 6, of which 4 were waited for; matrix products, arithmetic and copies ran while one was open for 38% of the time, Pallas kernels for 0%

profile of v13, /device:TPU:0, one launch (start us, length us, event | category | flops | bytes accessed | tf_op | source)
XLA Modules:
  0.0 192.2 jit_solution(6080409193359502882)
XLA Ops:
  0.7 7.5 %all-to-all-start.2 = ((f32[8,2,128]{2,1,0:T(2,128)}), f32[8,2,128]{2,1,0:T(2,128)S(1)}, u32[]{:S(2)}, u32[]{:S(2)}) async-start(f32[8,2,128]{2,1,0:T(2,128)} %bitcast.336), calls=%async_computation.2 | async-start | bytes 16384 | tf_op jit(solution)/shard_map/all_to_all | solution.py:117
  12.7 1.9 all-to-all-done.2
  14.6 4.1 %all-to-all-start.1 = ((bf16[8,128,768]{2,1,0:T(8,128)(2,1)}), bf16[8,128,768]{2,1,0:T(8,128)(2,1)S(1)}, u32[]{:S(2)}, u32[]{:S(2)}) async-start(bf16[8,128,768]{2,1,0:T(8,128)(2,1)} %pad_maximum_fusion), calls=%async_computation.1 | async-start | bytes 3145728 | tf_op jit(solution)/shard_map/all_to_all | solution.py:211
  21.1 34.1 %all-to-all-done.1 = bf16[8,128,768]{2,1,0:T(8,128)(2,1)S(1)} async-done(((bf16[8,128,768]{2,1,0:T(8,128)(2,1)}), bf16[8,128,768]{2,1,0:T(8,128)(2,1)S(1)}, u32[]{:S(2)}, u32[]{:S(2)}) %all-to-all-start.1) | async-done | bytes 1572896 | tf_op jit(solution)/shard_map/all_to_all | solution.py:211
  56.3 4.4 %all-to-all-start = ((bf16[8,128,512]{1,2,0:T(8,128)(2,1)}), bf16[8,128,512]{1,2,0:T(8,128)(2,1)}, u32[]{:S(2)}, u32[]{:S(2)}) async-start(bf16[8,128,512]{1,2,0:T(8,128)(2,1)} %broadcast_in_dim.265), calls=%async_computation | async-start | bytes 2097152 | tf_op jit(solution)/shard_map/all_to_all | solution.py:217
  62.4 1.3 copy.450
  63.7 2.0 %copy.547 = bf16[8,128,256]{1,2,0:T(8,128)(2,1)} copy(bf16[8,128,256]{2,1,0:T(8,128)(2,1)} %get-tuple-element.1109) | data formatting | bytes 1048576 | tf_op jit(solution)/shard_map/jvp()/reshape;reshape | solution.py:85
  67.6 1.9 %convolution_bitcast_fusion.3 = f32[8,2,128,128]{3,0,2,1:T(8,128)S(1)} fusion(f32[2,128,128,8]{2,3,1,0:T(8,128)} %copy.450, f32[8,8,2]{1,0,2:T(8,128)S(1)} %stack.2), kind=kOutput, calls=%fused_computation.70 | convolution fusion | flops 12582912 | bytes 2097664 | tf_op jit(solution)/shard_map/transpose(jvp(kjh,jhnp->khnp))/dot_general | solution.py:102
  69.5 1.6 fusion.57
  72.4 2.1 %convolution_bitcast_fusion.5 = f32[8,2,128,128]{3,0,2,1:T(8,128)} fusion(f32[8,2,128,128]{3,2,1,0:T(8,128)S(1)} %fusion.36, f32[8,8,2]{1,0,2:T(8,128)S(1)} %stack.2), kind=kOutput, calls=%fused_computation.72 | convolution fusion | flops 12582912 | bytes 2097664 | tf_op jit(solution)/shard_map/jvp(kjh,jhnp->khnp)/dot_general | solution.py:102
  74.5 1.6 convolution_bitcast_fusion.8
  76.1 2.6 %copy.442 = f32[8,2,128,128]{2,3,1,0:T(8,128)} copy(f32[8,2,128,128]{3,0,2,1:T(8,128)} %convolution_bitcast_fusion.5) | data formatting | bytes 2097152 | tf_op jit(solution)/shard_map/jvp(kjh,jhnp->khnp)/transpose | solution.py:102
  78.6 3.1 %fusion.52 = f32[8,128,128]{1,2,0:T(8,128)} fusion(f32[8,2,128,128]{2,3,1,0:T(8,128)} %copy.442, bf16[8,128,2,128]{1,3,2,0:T(8,128)(2,1)S(1)} %bitcast.300, f32[8,128,2]{1,2,0:T(2,128)S(1)} %copy.437), kind=kOutput, calls=%fused_computation.81 | convolution fusion | flops 201850880 | bytes 2105344 | tf_op jit(solution)/shard_map/transpose(jvp(vmap(tn,hnp->thp)))/dot_general | solution.py:69
  83.4 3.0 %fusion.67 = (f32[8,2,128]{2,1,0:T(2,128)S(1)}, f32[8,2,128]{2,1,0:T(2,128)S(1)}, f32[8,128,128]{2,1,0:T(8,128)}) fusion(f32[8,128,128]{2,1,0:T(8,128)S(1)} %fusion.87, f32[8,2,128]{2,1,0:T(2,128)S(1)} %copy.434, pred[8,128,128]{2,1,0:T(8,128)(4,1)S(1)} %compare_and_fusion.3, bf16[8,2,128,128]{3,2,1,0:T(8,128)(2,1)S(1)} %bitcast.301, ...), kind=kOutput, calls=%fused_computation.104 | convolution fusion | flops 69332992 | bytes 2252800 | tf_op jit(solution)/shard_map/transpose(jvp(vmap(hts,shp->thp)))/dot_general | solution.py:67
  86.4 1.5 fusion.55
  88.0 2.5 %reduce_window_sum.46 = f32[8,2,128]{2,0,1:T(8,128)S(1)} reduce-window(f32[8,2,128]{2,0,1:T(8,128)S(1)} %get-tuple-element.1117, f32[]{:T(128)} %constant.152.clone.1), window={size=1x1x128 pad=0_0x0_0x0_127}, to_apply=%region_28.29 | reduce-window | flops 260096 | bytes 16388 | tf_op jit(solution)/shard_map/transpose(jvp(vmap(jit(cumsum))))/reduce_window_sum | solution.py:45
  90.5 2.7 %reduce_window_sum.47 = f32[8,2,128]{2,0,1:T(8,128)S(1)} reduce-window(f32[8,2,128]{2,0,1:T(8,128)S(1)} %get-tuple-element.1116, f32[]{:T(128)} %constant.152.clone.1), window={size=1x1x128 pad=0_0x0_0x0_127}, to_apply=%region_36.37 | reduce-window | flops 260096 | bytes 16388 | tf_op jit(solution)/shard_map/transpose(jvp(jit(cumsum)))/reduce_window_sum | solution.py:91
  93.2 1.4 fusion.56
  99.2 5.9 %all-to-all-start.4 = ((bf16[8,128,528]{1,2,0:T(8,128)(2,1)}), bf16[8,128,528]{1,2,0:T(8,128)(2,1)S(1)}, u32[]{:S(2)}, u32[]{:S(2)}) async-start(bf16[8,128,528]{1,2,0:T(8,128)(2,1)} %pad_maximum_fusion.2), calls=%async_computation.4 | async-start | bytes 2162688 | tf_op jit(solution)/shard_map/all_to_all | solution.py:362
  105.7 1.5 copy.419
  113.0 3.0 %while.52 = (s32[]{:T(128)}, f32[128,2,4,128]{0,3,2,1:T(8,128)}, s32[]{:T(128)}, bf16[1024,256]{0,1:T(8,128)(2,1)S(1)}, s32[4]{0:T(128)S(1)}, /*index=5*/s32[128...) while((s32[]{:T(128)}, f32[128,2,4,128]{0,3,2,1:T(8,128)}, ...), condition=%wide.region_15.16_spmd.clone, body=%wide.region_10.15_spmd.clone.sunk | while | flops 135761040 | bytes 2174805 | solution.py:295
  113.0 2.9 %conditional.10 = (f32[128,2,4,128]{0,3,2,1:T(8,128)}) conditional(s32[]{:T(128)} %convert_element_type.251, f32[128,2,4,128]{0,3,2,1:T(8,128)} %get-tuple-element.1413, (s32[]{:T(128)}, bf16[1024,256]{0,1:T(8,128)(2,1)S(1)}, s32[]{:T(128)}, s32[4]{0:T(128)S(1)}, s32[128]{0:T(128)S(1)}, /*index=5*/bf16[1024,256]{0,1:T(8,128)(2,1)S(1)}, ...), branch_computations={%region_11.11_spmd, %region_12.14_spmd} | conditional | flops 135761040 | bytes 2174070 | solution.py:261
  113.5 2.5 %fusion.14 = f32[128,2,4,128]{0,3,2,1:T(8,128)} fusion(f32[128,2,4,128]{0,3,2,1:T(8,128)} %get-tuple-element.621, bf16[256,2,128,1]{0,2,3,1:T(8,128)(2,1)S(1)} %bitcast.310, bf16[256,2,128,1]{0,2,3,1:T(8,128)(2,1)S(1)} %bitcast.309, bf16[128,2,4,128]{3,0,2,1:T(8,128)(2,1)S(1)} %get-tuple-element.628, f32[2,4,128]{2,1,0:T(4,128)S(1)} %get-tuple-element.629, ...), kind=kOutput, calls=%fused_computation.21 | convolution fusion | flops 135659520 | bytes 1609728 | tf_op jit(solution)/shard_map/while/body/eval_jaxpr/cond/branch_1_fun/grtk,kgd->tgrd/dot_general | solution.py:291
  116.0 1.8 fusion.68
  119.6 3.1 %while.53 = (s32[]{:T(128)}, f32[128,2,4,128]{0,3,2,1:T(8,128)S(1)}, bf16[1024,256]{0,1:T(8,128)(2,1)}, bf16[1024,256]{0,1:T(8,128)(2,1)}, s32[]{:T(128)}, /*ind...) while((s32[]{:T(128)}, ...), condition=%wide.region_21.22_spmd.clone, body=%wide.region_16.21_spmd.clone.sunk | while | flops 337874048 | bytes 8601549 | solution.py:333
  119.6 2.9 %conditional.11 = ((f32[128,2,4,128]{0,3,2,1:T(8,128)S(1)}, bf16[1024,256]{0,1:T(8,128)(2,1)}, bf16[1024,256]{0,1:T(8,128)(2,1)})) conditional(s32[]{:T(128)} %convert_element_type.252, (f32[128,2,4,128]{0,3,2,1:T(8,128)S(1)}, bf16[1024,256]{0,1:T(8,128)(2,1)}, bf16[1024,256]{0,1:T(8,128)(2,1)}) %tuple.202, (s32[]{:T(128)}, ...), branch_computations={%region_17.17_spmd, %region_18.20_spmd} | conditional | flops 337874048 | bytes 8600726 | solution.py:261
  122.7 1.6 copy_bitcast_fusion
  126.9 4.0 %all-to-all-done.4 = bf16[8,128,528]{1,2,0:T(8,128)(2,1)S(1)} async-done(((bf16[8,128,528]{1,2,0:T(8,128)(2,1)}), bf16[8,128,528]{1,2,0:T(8,128)(2,1)S(1)}, u32[]{:S(2)}, u32[]{:S(2)}) %all-to-all-start.4) | async-done | bytes 1081376 | tf_op jit(solution)/shard_map/all_to_all | solution.py:362
  130.9 22.8 %all-to-all-start.3 = ((bf16[8,128,768]{1,2,0:T(8,128)(2,1)}), bf16[8,128,768]{1,2,0:T(8,128)(2,1)S(1)}, u32[]{:S(2)}, u32[]{:S(2)}) async-start(bf16[8,128,768]{1,2,0:T(8,128)(2,1)} %pad_maximum_fusion.1), calls=%async_computation.3 | async-start | bytes 3145728 | tf_op jit(solution)/shard_map/all_to_all | solution.py:342
  154.4 1.8 copy.541
  156.2 1.8 copy.535
  161.9 27.6 %all-to-all-done.3 = bf16[8,128,768]{1,2,0:T(8,128)(2,1)S(1)} async-done(((bf16[8,128,768]{1,2,0:T(8,128)(2,1)}), bf16[8,128,768]{1,2,0:T(8,128)(2,1)S(1)}, u32[]{:S(2)}, u32[]{:S(2)}) %all-to-all-start.3) | async-done | bytes 1572896 | tf_op jit(solution)/shard_map/all_to_all | solution.py:342
  (208 shorter events, 42.1 us)
Async XLA Ops:
  0.6 10.1 %copy-start.11 = (bf16[128,2048]{1,0:T(8,128)(2,1)S(1)}, bf16[128,2048]{1,0:T(8,128)(2,1)}, u32[]{:S(2)}) copy-start(bf16[128,2048]{1,0:T(8,128)(2,1)} %param.32) | copy-start | bytes 1572868
  0.7 14.0 %all-to-all-start.2 = ((f32[8,2,128]{2,1,0:T(2,128)}), f32[8,2,128]{2,1,0:T(2,128)S(1)}, u32[]{:S(2)}, u32[]{:S(2)}) async-start(f32[8,2,128]{2,1,0:T(2,128)} %bitcast.336), calls=%async_computation.2 | async-start | bytes 16384 | tf_op jit(solution)/shard_map/all_to_all | solution.py:117
  10.5 0.8 copy-start.19
  10.5 0.8 copy-start.20
  11.4 1.3 copy-start.17
  11.4 1.3 copy-start.18
  12.7 6.2 %copy-start.21 = (f32[16]{0:T(128)S(1)}, f32[16]{0:T(128)}, u32[]{:S(2)}) copy-start(f32[16]{0:T(128)} %param.27) | copy-start | bytes 196
  14.6 40.6 %all-to-all-start.1 = ((bf16[8,128,768]{2,1,0:T(8,128)(2,1)}), bf16[8,128,768]{2,1,0:T(8,128)(2,1)S(1)}, u32[]{:S(2)}, u32[]{:S(2)}) async-start(bf16[8,128,768]{2,1,0:T(8,128)(2,1)} %pad_maximum_fusion), calls=%async_computation.1 | async-start | bytes 3145728 | tf_op jit(solution)/shard_map/all_to_all | solution.py:211
  56.3 42.9 %all-to-all-start = ((bf16[8,128,512]{1,2,0:T(8,128)(2,1)}), bf16[8,128,512]{1,2,0:T(8,128)(2,1)}, u32[]{:S(2)}, u32[]{:S(2)}) async-start(bf16[8,128,512]{1,2,0:T(8,128)(2,1)} %broadcast_in_dim.265), calls=%async_computation | async-start | bytes 2097152 | tf_op jit(solution)/shard_map/all_to_all | solution.py:217
  65.8 0.8 copy-start.2
  67.6 1.9 %copy-start.5 = (bf16[8,128,256]{1,2,0:T(8,128)(2,1)S(1)}, bf16[8,128,256]{1,2,0:T(8,128)(2,1)}, u32[]{:S(2)}) copy-start(bf16[8,128,256]{1,2,0:T(8,128)(2,1)} %copy.547) | copy-start | bytes 1572868
  67.6 2.0 %copy-start.9 = (f32[8,128,128]{1,2,0:T(8,128)S(1)}, f32[8,128,128]{1,2,0:T(8,128)}, u32[]{:S(2)}) copy-start(f32[8,128,128]{1,2,0:T(8,128)} %copy.544) | copy-start | bytes 1572868
  69.5 1.8 copy-start.3
  72.4 2.1 %copy-start = (f32[2,128,128,8]{2,3,1,0:T(8,128)S(1)}, f32[2,128,128,8]{2,3,1,0:T(8,128)}, u32[]{:S(2)}) copy-start(f32[2,128,128,8]{2,3,1,0:T(8,128)} %copy.450) | copy-start | bytes 3145732
  83.4 3.1 %copy-start.12 = (f32[8,128,128]{2,1,0:T(8,128)}, f32[8,128,128]{2,1,0:T(8,128)S(1)}, u32[]{:S(2)}) copy-start(f32[8,128,128]{2,1,0:T(8,128)S(1)} %fusion.87) | copy-start | bytes 1572868
  83.4 3.0 %copy-start.1 = (f32[8,2,128,128]{2,3,1,0:T(8,128)S(1)}, f32[8,2,128,128]{2,3,1,0:T(8,128)}, u32[]{:S(2)}) copy-start(f32[8,2,128,128]{2,3,1,0:T(8,128)} %copy.442) | copy-start | bytes 3145732
  93.2 1.5 copy-start.7
  93.2 1.9 copy-start.8
  94.7 1.0 copy-start.13
  95.8 1.0 copy-start.4
  99.2 5.9 %copy-start.15 = (bf16[128,1024]{1,0:T(8,128)(2,1)S(1)}, bf16[128,1024]{1,0:T(8,128)(2,1)}, u32[]{:S(2)}) copy-start(bf16[128,1024]{1,0:T(8,128)(2,1)} %param.29) | copy-start | bytes 786436
  99.2 6.2 %copy-start.16 = (bf16[128,1024]{1,0:T(8,128)(2,1)S(1)}, bf16[128,1024]{1,0:T(8,128)(2,1)}, u32[]{:S(2)}) copy-start(bf16[128,1024]{1,0:T(8,128)(2,1)} %param.33) | copy-start | bytes 786436
  99.2 31.7 %all-to-all-start.4 = ((bf16[8,128,528]{1,2,0:T(8,128)(2,1)}), bf16[8,128,528]{1,2,0:T(8,128)(2,1)S(1)}, u32[]{:S(2)}, u32[]{:S(2)}) async-start(bf16[8,128,528]{1,2,0:T(8,128)(2,1)} %pad_maximum_fusion.2), calls=%async_computation.4 | async-start | bytes 2162688 | tf_op jit(solution)/shard_map/all_to_all | solution.py:362
  108.3 2.5 %copy-start.22 = (s32[4]{0:T(128)S(1)}, s32[4]{0:T(128)}, u32[]{:S(2)}) copy-start(s32[4]{0:T(128)} %param.28) | copy-start | bytes 52
  122.7 1.6 copy-start.6
  122.7 1.7 copy-start.10
  122.7 1.8 copy-start.14
  130.9 58.6 %all-to-all-start.3 = ((bf16[8,128,768]{1,2,0:T(8,128)(2,1)}), bf16[8,128,768]{1,2,0:T(8,128)(2,1)S(1)}, u32[]{:S(2)}, u32[]{:S(2)}) async-start(bf16[8,128,768]{1,2,0:T(8,128)(2,1)} %pad_maximum_fusion.1), calls=%async_computation.3 | async-start | bytes 3145728 | tf_op jit(solution)/shard_map/all_to_all | solution.py:342
  158.7 1.7 collective-permute-start

commit v14 on v11

--- a/solution.py
+++ b/solution.py
@@ -171,6 +171,12 @@
     mixer_out = mixed.reshape(tokens, heads_here * P_SIZE).astype(jnp.bfloat16)
     x_grad = grad_x.reshape(tokens, heads_here * P_SIZE).astype(jnp.bfloat16)
     return (mixer_out, x_grad, grad_b, grad_c, grad_decay)
+
+
+def unrolled(count, step, carried):
+    for number in range(count):
+        carried = step(number, carried)
+    return carried
 
 
 def on_device(
@@ -275,8 +281,7 @@
         return (new_peak, row_total * jnp.exp(row_peak - new_peak) + fresh)
 
     stat_shape = (groups, heads_per_group, tokens)
-    row_peak, row_total = lax.fori_loop(
-        0,
+    row_peak, row_total = unrolled(
         blocks,
         lambda number, carried: visit(number, carried, stats_step),
         (jnp.full(stat_shape, big_negative, jnp.float32), jnp.zeros(stat_shape, jnp.float32)),
@@ -292,8 +297,7 @@
             "grtk,kgd->tgrd", weights, value_blk, preferred_element_type=jnp.float32
         )
 
-    attention_table = lax.fori_loop(
-        0,
+    attention_table = unrolled(
         blocks,
         lambda number, carried: visit(number, carried, output_step),
         jnp.zeros((tokens, groups, heads_per_group, HEAD_SIZE), jnp.float32),
@@ -330,8 +334,7 @@
         return (grad_query, term_key, term_value)
 
     term_zero = jnp.zeros((total_len, groups * HEAD_SIZE), jnp.float32)
-    grad_query, term_key, term_value = lax.fori_loop(
-        0,
+    grad_query, term_key, term_value = unrolled(
         blocks,
         lambda number, carried: visit(number, carried, full_step),
         (query_zero, term_zero, term_zero),

time: 183 us -> 193 us (1.055)
  starting transfers between devices: 34.3 us -> 43.1 us
  other arithmetic: 18.5 us -> 22.1 us
  waiting for transfers between devices: 66.9 us -> 64.2 us
    all_to_all x1, starting transfers between devices: 12.4 us -> 21.2 us  [on_device(): lax.all_to_all(jnp.concatenate([kv_terms.reshape(seq_count, tokens, kv_wi...]
    all_to_all x2, waiting for transfers between devices: 36.7 us -> 34.1 us  [on_device(): got = lax.all_to_all(sent, 'seq', split_axis=0, concat_axis=0, tiled=True)]
    another operation x3 -> x7, local copies, waits for them, and re-layouts: 0.9 us -> 2.94 us
    unnamed x60 -> x73, local copies, waits for them, and re-layouts: 8.6 us -> 9.58 us
  transfers between devices with their start and end apart: 6 -> 6, of which waited for: 4 -> 3; matrix products, arithmetic and copies ran while one was open for 41% -> 41% of each run, Pallas kernels for 0% -> 0%
where the time goes in v14:
time: 193 us; the launch traced here: 192 us
  waiting for transfers between devices  64.2 us (33%)
  starting transfers between devices  43.1 us (22%)
  local copies, waits for them, and re-layouts  32.9 us (17%)
  matrix products  27.8 us (14%)
  other arithmetic  22.1 us (11%)
    all_to_all x2, waiting for transfers between devices, on_device(): got = lax.all_to_all(sent, 'seq', split_axis=0, concat_axis=0, tiled=True)  34.1 us
    all_to_all x1, waiting for transfers between devices, on_device(): lax.all_to_all(jnp.concatenate([kv_terms.reshape(seq_count, tokens, kv_wi...  28.1 us
    all_to_all x1, starting transfers between devices, on_device(): lax.all_to_all(jnp.concatenate([kv_terms.reshape(seq_count, tokens, kv_wi...  21.2 us
    all_to_all x2, starting transfers between devices, on_device(): got = lax.all_to_all(sent, 'seq', split_axis=0, concat_axis=0, tiled=True)  9.85 us
    unnamed x73, local copies, waits for them, and re-layouts  9.58 us
    all_to_all x1, starting transfers between devices, mamba_by_heads(): lax.all_to_all(decay_log, 'seq', split_axis=0, concat_axis=1, tiled=True)  7.45 us
    dot_general x3, matrix products, mixer_whole(): state_in = jnp.einsum('kjh,jhnp->khnp', reach, summary, precision=precise)  5.61 us
    dot_general x3, matrix products, mixer_stretch(): inner = jnp.einsum('hts,shp->thp', kernel, inputs, precision=precise)  4.86 us
  transfers between devices with their start and end apart: 6, of which 3 were waited for; matrix products, arithmetic and copies ran while one was open for 41% of the time, Pallas kernels for 0%

profile of v14, /device:TPU:0, one launch (start us, length us, event | category | flops | bytes accessed | tf_op | source)
XLA Modules:
  0.0 191.9 jit_solution(12302985558947573896)
XLA Ops:
  0.7 7.5 %all-to-all-start.2 = ((f32[8,2,128]{2,1,0:T(2,128)}), f32[8,2,128]{2,1,0:T(2,128)S(1)}, u32[]{:S(2)}, u32[]{:S(2)}) async-start(f32[8,2,128]{2,1,0:T(2,128)} %bitcast.434), calls=%async_computation.2 | async-start | bytes 16384 | tf_op jit(solution)/shard_map/all_to_all | solution.py:117
  9.2 1.3 copy.546
  12.7 1.9 all-to-all-done.2
  14.6 4.1 %all-to-all-start.1 = ((bf16[8,128,768]{2,1,0:T(8,128)(2,1)}), bf16[8,128,768]{2,1,0:T(8,128)(2,1)S(1)}, u32[]{:S(2)}, u32[]{:S(2)}) async-start(bf16[8,128,768]{2,1,0:T(8,128)(2,1)} %pad_maximum_fusion), calls=%async_computation.1 | async-start | bytes 3145728 | tf_op jit(solution)/shard_map/all_to_all | solution.py:217
  21.1 34.1 %all-to-all-done.1 = bf16[8,128,768]{2,1,0:T(8,128)(2,1)S(1)} async-done(((bf16[8,128,768]{2,1,0:T(8,128)(2,1)}), bf16[8,128,768]{2,1,0:T(8,128)(2,1)S(1)}, u32[]{:S(2)}, u32[]{:S(2)}) %all-to-all-start.1) | async-done | bytes 1572896 | tf_op jit(solution)/shard_map/all_to_all | solution.py:217
  56.4 4.4 %all-to-all-start = ((bf16[8,128,512]{1,2,0:T(8,128)(2,1)}), bf16[8,128,512]{1,2,0:T(8,128)(2,1)}, u32[]{:S(2)}, u32[]{:S(2)}) async-start(bf16[8,128,512]{1,2,0:T(8,128)(2,1)} %broadcast_in_dim.341), calls=%async_computation | async-start | bytes 2097152 | tf_op jit(solution)/shard_map/all_to_all | solution.py:223
  62.4 1.3 copy.565
  63.8 2.0 %copy.698 = bf16[8,128,256]{1,2,0:T(8,128)(2,1)} copy(bf16[8,128,256]{2,1,0:T(8,128)(2,1)} %get-tuple-element.568) | data formatting | bytes 1048576 | tf_op jit(solution)/shard_map/jvp()/reshape;reshape | solution.py:85
  67.6 1.9 %convolution_bitcast_fusion.2 = f32[8,2,128,128]{3,0,2,1:T(8,128)S(1)} fusion(f32[2,128,128,8]{2,3,1,0:T(8,128)} %copy.565, f32[8,8,2]{1,0,2:T(8,128)S(1)} %stack.2), kind=kOutput, calls=%fused_computation.96 | convolution fusion | flops 12582912 | bytes 2097664 | tf_op jit(solution)/shard_map/transpose(jvp(kjh,jhnp->khnp))/dot_general | solution.py:102
  69.6 1.6 fusion.72
  72.4 2.1 %convolution_bitcast_fusion.4 = f32[8,2,128,128]{3,0,2,1:T(8,128)} fusion(f32[8,2,128,128]{3,2,1,0:T(8,128)S(1)} %fusion.51, f32[8,8,2]{1,0,2:T(8,128)S(1)} %stack.2), kind=kOutput, calls=%fused_computation.98 | convolution fusion | flops 12582912 | bytes 2097664 | tf_op jit(solution)/shard_map/jvp(kjh,jhnp->khnp)/dot_general | solution.py:102
  74.5 1.6 convolution_bitcast_fusion.7
  76.1 2.6 %copy.559 = f32[8,2,128,128]{2,3,1,0:T(8,128)} copy(f32[8,2,128,128]{3,0,2,1:T(8,128)} %convolution_bitcast_fusion.4) | data formatting | bytes 2097152 | tf_op jit(solution)/shard_map/jvp(kjh,jhnp->khnp)/transpose | solution.py:102
  78.7 3.1 %fusion.67 = f32[8,128,128]{1,2,0:T(8,128)} fusion(f32[8,2,128,128]{2,3,1,0:T(8,128)} %copy.559, bf16[8,128,2,128]{1,3,2,0:T(8,128)(2,1)S(1)} %bitcast.385, f32[8,128,2]{1,2,0:T(2,128)S(1)} %copy.554), kind=kOutput, calls=%fused_computation.107 | convolution fusion | flops 201850880 | bytes 2105344 | tf_op jit(solution)/shard_map/transpose(jvp(vmap(tn,hnp->thp)))/dot_general | solution.py:69
  83.4 3.0 %fusion.82 = (f32[8,2,128]{2,1,0:T(2,128)S(1)}, f32[8,2,128]{2,1,0:T(2,128)S(1)}, f32[8,128,128]{2,1,0:T(8,128)}) fusion(f32[8,128,128]{2,1,0:T(8,128)S(1)} %fusion.102, f32[8,2,128]{2,1,0:T(2,128)S(1)} %copy.551, pred[8,128,128]{2,1,0:T(8,128)(4,1)S(1)} %compare_and_fusion.3, bf16[8,2,128,128]{3,2,1,0:T(8,128)(2,1)S(1)} %bitcast.386, ...), kind=kOutput, calls=%fused_computation.130 | convolution fusion | flops 69332992 | bytes 2252800 | tf_op jit(solution)/shard_map/transpose(jvp(vmap(hts,shp->thp)))/dot_general | solution.py:67
  86.5 1.5 fusion.70
  88.1 2.5 %reduce_window_sum.52 = f32[8,2,128]{2,0,1:T(8,128)S(1)} reduce-window(f32[8,2,128]{2,0,1:T(8,128)S(1)} %get-tuple-element.576, f32[]{:T(128)} %constant.142.clone.1), window={size=1x1x128 pad=0_0x0_0x0_127}, to_apply=%region_36.37 | reduce-window | flops 260096 | bytes 16388 | tf_op jit(solution)/shard_map/transpose(jvp(vmap(jit(cumsum))))/reduce_window_sum | solution.py:45
  90.6 2.7 %reduce_window_sum.53 = f32[8,2,128]{2,0,1:T(8,128)S(1)} reduce-window(f32[8,2,128]{2,0,1:T(8,128)S(1)} %get-tuple-element.575, f32[]{:T(128)} %constant.142.clone.1), window={size=1x1x128 pad=0_0x0_0x0_127}, to_apply=%region_44.45 | reduce-window | flops 260096 | bytes 16388 | tf_op jit(solution)/shard_map/transpose(jvp(jit(cumsum)))/reduce_window_sum | solution.py:91
  93.3 1.5 fusion.71
  94.8 1.4 fusion.68
  97.6 1.3 fusion.63
  100.1 5.7 %all-to-all-start.4 = ((bf16[8,128,528]{1,2,0:T(8,128)(2,1)}), bf16[8,128,528]{1,2,0:T(8,128)(2,1)}, u32[]{:S(2)}, u32[]{:S(2)}) async-start(bf16[8,128,528]{1,2,0:T(8,128)(2,1)} %pad_maximum_fusion.2), calls=%async_computation.4 | async-start | bytes 2162688 | tf_op jit(solution)/shard_map/all_to_all | solution.py:365
  106.3 1.5 copy.527
  107.9 3.0 %conditional.11 = (f32[2,4,128]{2,1,0:T(4,128)}, f32[2,4,128]{2,1,0:T(4,128)S(1)}) conditional(s32[]{:T(128)} %convert_element_type.199, () %tuple.90, (s32[128]{0:T(128)S(1)}, s32[4]{0:T(128)S(1)}, s32[128]{0:T(128)S(1)}, bf16[1024,256]{1,0:T(8,128)(2,1)S(1)}, bf16[128,2,4,128]{0,3,2,1:T(8,128)(2,1)S(1)}) %tuple.228), branch_computations={%region_2.3_spmd, %region_3.8_spmd} | conditional | flops 138617360 | bytes 6526020 | solution.py:267
  111.6 2.0 %conditional.13 = (f32[128,2,4,128]{3,0,2,1:T(8,128)S(1)}) conditional(s32[]{:T(128)} %convert_element_type.199, () %tuple.93, (s32[128]{0:T(128)S(1)}, s32[4]{0:T(128)S(1)}, s32[128]{0:T(128)S(1)}, bf16[1024,256]{1,0:T(8,128)(2,1)S(1)}, bf16[128,2,4,128]{0,3,2,1:T(8,128)(2,1)S(1)}, /*index=5*/f32[2,4,128]{2,1,0:T(4,128)S(1)}, ...), branch_computations={%region_14.15_spmd, %region_15.18_spmd} | conditional | flops 271259136 | bytes 4596796 | solution.py:267
  113.6 2.2 %conditional.14 = (bf16[128,2,4,128]{0,3,2,1:T(8,128)(2,1)}, bf16[128,1024]{1,0:T(8,128)(2,1)S(1)}) conditional(s32[]{:T(128)} %convert_element_type.198, (f32[128,2,4,128]{3,0,2,1:T(8,128)S(1)}) %conditional.13, (s32[128]{0:T(128)S(1)}, s32[4]{0:T(128)S(1)}, s32[128]{0:T(128)S(1)}, bf16[1024,256]{1,0:T(8,128)(2,1)S(1)}, ...), branch_computations={%region_18.19_spmd, %region_19.22_spmd} | conditional | flops 271521792 | bytes 6470780
  116.9 11.1 %conditional.15 = (f32[128,2,4,128]{3,0,2,1:T(8,128)}, bf16[1024,256]{0,1:T(8,128)(2,1)}, bf16[1024,256]{0,1:T(8,128)(2,1)}) conditional(s32[]{:T(128)} %convert_element_type.199, () %tuple.89, (s32[128]{0:T(128)S(1)}, s32[4]{0:T(128)}, s32[128]{0:T(128)}, bf16[1024,256]{1,0:T(8,128)(2,1)S(1)}, bf16[128,2,4,128]{0,3,2,1:T(8,128)(2,1)S(1)}, ...), branch_computations={%region_22.23_spmd, %region_23.26_spmd} | conditional | flops 675485184 | bytes 20329636 | solution.py:267
  119.6 1.8 fusion.37
  125.3 1.3 convolution_bitcast_fusion
  128.0 1.6 copy_bitcast_fusion
  132.1 21.2 %all-to-all-start.3 = ((bf16[8,128,768]{1,2,0:T(8,128)(2,1)}), bf16[8,128,768]{1,2,0:T(8,128)(2,1)S(1)}, u32[]{:S(2)}, u32[]{:S(2)}) async-start(bf16[8,128,768]{1,2,0:T(8,128)(2,1)} %pad_maximum_fusion.1), calls=%async_computation.3 | async-start | bytes 3145728 | tf_op jit(solution)/shard_map/all_to_all | solution.py:345
  161.0 28.1 %all-to-all-done.3 = bf16[8,128,768]{1,2,0:T(8,128)(2,1)S(1)} async-done(((bf16[8,128,768]{1,2,0:T(8,128)(2,1)}), bf16[8,128,768]{1,2,0:T(8,128)(2,1)S(1)}, u32[]{:S(2)}, u32[]{:S(2)}) %all-to-all-start.3) | async-done | bytes 1572896 | tf_op jit(solution)/shard_map/all_to_all | solution.py:345
  (202 shorter events, 45.2 us)
Async XLA Ops:
  0.6 10.1 %copy-start.18 = (bf16[128,2048]{1,0:T(8,128)(2,1)S(1)}, bf16[128,2048]{1,0:T(8,128)(2,1)}, u32[]{:S(2)}) copy-start(bf16[128,2048]{1,0:T(8,128)(2,1)} %param.32) | copy-start | bytes 1572868
  0.7 14.0 %all-to-all-start.2 = ((f32[8,2,128]{2,1,0:T(2,128)}), f32[8,2,128]{2,1,0:T(2,128)S(1)}, u32[]{:S(2)}, u32[]{:S(2)}) async-start(f32[8,2,128]{2,1,0:T(2,128)} %bitcast.434), calls=%async_computation.2 | async-start | bytes 16384 | tf_op jit(solution)/shard_map/all_to_all | solution.py:117
  9.2 2.1 %copy-start.27 = (bf16[128,128]{1,0:T(8,128)(2,1)S(1)}, bf16[128,128]{1,0:T(8,128)(2,1)}, u32[]{:S(2)}) copy-start(bf16[128,128]{1,0:T(8,128)(2,1)} %param.24) | copy-start | bytes 98308
  9.2 2.2 %copy-start.28 = (bf16[128,128]{1,0:T(8,128)(2,1)S(1)}, bf16[128,128]{1,0:T(8,128)(2,1)}, u32[]{:S(2)}) copy-start(bf16[128,128]{1,0:T(8,128)(2,1)} %param.25) | copy-start | bytes 98308
  12.7 6.2 %copy-start.35 = (f32[16]{0:T(128)S(1)}, f32[16]{0:T(128)}, u32[]{:S(2)}) copy-start(f32[16]{0:T(128)} %param.27) | copy-start | bytes 196
  14.6 40.6 %all-to-all-start.1 = ((bf16[8,128,768]{2,1,0:T(8,128)(2,1)}), bf16[8,128,768]{2,1,0:T(8,128)(2,1)S(1)}, u32[]{:S(2)}, u32[]{:S(2)}) async-start(bf16[8,128,768]{2,1,0:T(8,128)(2,1)} %pad_maximum_fusion), calls=%async_computation.1 | async-start | bytes 3145728 | tf_op jit(solution)/shard_map/all_to_all | solution.py:217
  19.0 77.8 %copy-start.37 = (f32[2]{0:T(128)}, f32[2]{0:T(128)S(1)}, u32[]{:S(2)}) copy-start(f32[2]{0:T(128)S(1)} %dynamic_slice.33) | copy-start | bytes 28
  20.4 76.4 %copy-start.30 = (f32[8,2,128]{2,1,0:T(2,128)}, f32[8,2,128]{2,1,0:T(2,128)S(1)}, u32[]{:S(2)}) copy-start(f32[8,2,128]{2,1,0:T(2,128)S(1)} %copy.551) | copy-start | bytes 24580
  56.4 43.7 %all-to-all-start = ((bf16[8,128,512]{1,2,0:T(8,128)(2,1)}), bf16[8,128,512]{1,2,0:T(8,128)(2,1)}, u32[]{:S(2)}, u32[]{:S(2)}) async-start(bf16[8,128,512]{1,2,0:T(8,128)(2,1)} %broadcast_in_dim.341), calls=%async_computation | async-start | bytes 2097152 | tf_op jit(solution)/shard_map/all_to_all | solution.py:223
  67.6 2.0 %copy-start.9 = (bf16[8,128,256]{1,2,0:T(8,128)(2,1)S(1)}, bf16[8,128,256]{1,2,0:T(8,128)(2,1)}, u32[]{:S(2)}) copy-start(bf16[8,128,256]{1,2,0:T(8,128)(2,1)} %copy.698) | copy-start | bytes 1572868
  67.6 2.0 %copy-start.13 = (f32[8,128,128]{1,2,0:T(8,128)S(1)}, f32[8,128,128]{1,2,0:T(8,128)}, u32[]{:S(2)}) copy-start(f32[8,128,128]{1,2,0:T(8,128)} %copy.695) | copy-start | bytes 1572868
  69.6 1.8 copy-start.3
  71.4 3.2 %copy-start = (f32[2,128,128,8]{2,3,1,0:T(8,128)S(1)}, f32[2,128,128,8]{2,3,1,0:T(8,128)}, u32[]{:S(2)}) copy-start(f32[2,128,128,8]{2,3,1,0:T(8,128)} %copy.565) | copy-start | bytes 3145732
  83.4 4.6 %copy-start.19 = (f32[8,128,128]{2,1,0:T(8,128)}, f32[8,128,128]{2,1,0:T(8,128)S(1)}, u32[]{:S(2)}) copy-start(f32[8,128,128]{2,1,0:T(8,128)S(1)} %fusion.102) | copy-start | bytes 1572868
  83.4 3.0 %copy-start.1 = (f32[8,2,128,128]{2,3,1,0:T(8,128)S(1)}, f32[8,2,128,128]{2,3,1,0:T(8,128)}, u32[]{:S(2)}) copy-start(f32[8,2,128,128]{2,3,1,0:T(8,128)} %copy.559) | copy-start | bytes 3145732
  93.2 3.0 %copy-start.11 = (f32[8,128,128]{2,1,0:T(8,128)S(1)}, f32[8,128,128]{2,1,0:T(8,128)}, u32[]{:S(2)}) copy-start(f32[8,128,128]{2,1,0:T(8,128)} %get-tuple-element.535) | copy-start | bytes 1572868
  93.3 3.0 %copy-start.12 = (f32[8,128,128]{1,2,0:T(8,128)S(1)}, f32[8,128,128]{1,2,0:T(8,128)}, u32[]{:S(2)}) copy-start(f32[8,128,128]{1,2,0:T(8,128)} %fusion.67) | copy-start | bytes 1572868
  93.3 3.5 %copy-start.20 = (f32[8,128,128]{2,1,0:T(8,128)S(1)}, f32[8,128,128]{2,1,0:T(8,128)}, u32[]{:S(2)}) copy-start(f32[8,128,128]{2,1,0:T(8,128)} %copy-done.19) | copy-start | bytes 1572868
  99.0 6.8 %copy-start.22 = (bf16[128,1024]{1,0:T(8,128)(2,1)S(1)}, bf16[128,1024]{1,0:T(8,128)(2,1)}, u32[]{:S(2)}) copy-start(bf16[128,1024]{1,0:T(8,128)(2,1)} %param.29) | copy-start | bytes 786436
  99.0 7.0 %copy-start.23 = (bf16[128,1024]{1,0:T(8,128)(2,1)S(1)}, bf16[128,1024]{1,0:T(8,128)(2,1)}, u32[]{:S(2)}) copy-start(bf16[128,1024]{1,0:T(8,128)(2,1)} %param.33) | copy-start | bytes 786436
  100.1 32.1 %all-to-all-start.4 = ((bf16[8,128,528]{1,2,0:T(8,128)(2,1)}), bf16[8,128,528]{1,2,0:T(8,128)(2,1)}, u32[]{:S(2)}, u32[]{:S(2)}) async-start(bf16[8,128,528]{1,2,0:T(8,128)(2,1)} %pad_maximum_fusion.2), calls=%async_computation.4 | async-start | bytes 2162688 | tf_op jit(solution)/shard_map/all_to_all | solution.py:365
  106.0 11.0 %copy-start.5 = (bf16[128,1024]{0,1:T(8,128)(2,1)}, bf16[128,1024]{0,1:T(8,128)(2,1)S(1)}, u32[]{:S(2)}) copy-start(bf16[128,1024]{0,1:T(8,128)(2,1)S(1)} %copy.528) | copy-start | bytes 786436
  106.3 7.3 %copy-start.29 = (s32[128]{0:T(128)}, s32[128]{0:T(128)S(1)}, u32[]{:S(2)}) copy-start(s32[128]{0:T(128)S(1)} %convert_reduce_fusion.10) | copy-start | bytes 1540
  111.6 2.0 %copy-start.32 = (f32[1,8,128]{2,1,0:T(8,128)}, f32[1,8,128]{2,1,0:T(8,128)S(1)}, u32[]{:S(2)}) copy-start(f32[1,8,128]{2,1,0:T(8,128)S(1)} %log_add_fusion) | copy-start | bytes 12292
  116.9 2.7 %copy-start.6 = (bf16[128,2,4,128]{0,3,2,1:T(8,128)(2,1)}, bf16[128,2,4,128]{0,3,2,1:T(8,128)(2,1)S(1)}, u32[]{:S(2)}) copy-start(bf16[128,2,4,128]{0,3,2,1:T(8,128)(2,1)S(1)} %get-tuple-element.174) | copy-start | bytes 786436 | tf_op jit(solution)/shard_map/cond
  128.0 1.6 copy-start.10
  128.0 1.7 copy-start.17
  128.0 1.8 copy-start.21
  128.0 1.8 copy-start.31
  128.0 1.8 copy-start.38
  132.1 57.0 %all-to-all-start.3 = ((bf16[8,128,768]{1,2,0:T(8,128)(2,1)}), bf16[8,128,768]{1,2,0:T(8,128)(2,1)S(1)}, u32[]{:S(2)}, u32[]{:S(2)}) async-start(bf16[8,128,768]{1,2,0:T(8,128)(2,1)} %pad_maximum_fusion.1), calls=%async_computation.3 | async-start | bytes 3145728 | tf_op jit(solution)/shard_map/all_to_all | solution.py:345
  156.7 2.8 %collective-permute-start = (f32[128,256]{0,1:T(8,128)S(1)}, f32[128,256]{0,1:T(8,128)S(1)}, u32[]{:S(2)}, u32[]{:S(2)}) collective-permute-start(f32[128,256]{0,1:T(8,128)S(1)} %slice.114), channel_id=1, source_target_pairs={{0,1},{1,0},{2,3},{3,2},{4,5},{5,4},{6,7},{7,6},{8,9},{9,8},{10,11... | collective-permute-start | bytes 393224 | tf_op jit(solution)/shard_map/ppermute | solution.py:377
  (8 other events, 10.6 us)

commit v15 on v11

--- a/solution.py
+++ b/solution.py
@@ -205,14 +205,24 @@
         def spread(a):
             return jnp.broadcast_to(a[None], (seq_count,) + a.shape)
 
-        sent = jnp.concatenate(
-            [by_owner(x_input), by_owner(mixer_cot), spread(b_rows), spread(c_rows)], axis=2
-        )
+        shared = lax.axis_size("head") == 2
+        if shared:
+            first = lax.axis_index("head") == 0
+            rows_sent = [spread(jnp.where(first, b_rows, c_rows))]
+        else:
+            rows_sent = [spread(b_rows), spread(c_rows)]
+        sent = jnp.concatenate([by_owner(x_input), by_owner(mixer_cot)] + rows_sent, axis=2)
         got = lax.all_to_all(sent, "seq", split_axis=0, concat_axis=0, tiled=True)
         x_all = got[:, :, :own_width].reshape(total_len, own_width)
         cot_all = got[:, :, own_width : 2 * own_width].reshape(total_len, own_width)
-        b_all = got[:, :, 2 * own_width : 2 * own_width + state_width].reshape(total_len, -1)
-        c_all = got[:, :, 2 * own_width + state_width :].reshape(total_len, -1)
+        if shared:
+            mine = got[:, :, 2 * own_width :].reshape(total_len, -1)
+            theirs = lax.ppermute(mine, "head", [(0, 1), (1, 0)])
+            b_all = jnp.where(first, mine, theirs)
+            c_all = jnp.where(first, theirs, mine)
+        else:
+            b_all = got[:, :, 2 * own_width : 2 * own_width + state_width].reshape(total_len, -1)
+            c_all = got[:, :, 2 * own_width + state_width :].reshape(total_len, -1)
         kv_sent = spread(jnp.concatenate([attention_key_rows, values], axis=1))
         gathered = lax.all_to_all(kv_sent, "seq", split_axis=0, concat_axis=0, tiled=True)
         gathered = gathered.reshape(total_len, 2 * key_width)

time: 183 us -> 193 us (1.055)
  other arithmetic: 18.5 us -> 25.8 us
  local copies, waits for them, and re-layouts: 32.8 us -> 38.7 us
  waiting for transfers between devices: 66.9 us -> 61.7 us
    reshape x6, local copies, waits for them, and re-layouts: 0.55 us -> 7.63 us  [mixer_whole(): row * factor[k - 1][None, :]]
    all_to_all x2, waiting for transfers between devices: 36.7 us -> 31.4 us  [on_device(): got = lax.all_to_all(sent, 'seq', split_axis=0, concat_axis=0, tiled=True)]
    another operation x4 -> x3, local copies, waits for them, and re-layouts: 2.94 us -> 0.07 us  [the longest x1 2.04 us: mixer_whole(): inp = inputs.reshape(count, width, heads, P_SIZE)]
    another operation x5, other arithmetic: 1.4 us -> 4.14 us
    all_to_all x1, starting transfers between devices: 12.4 us -> 9.93 us  [on_device(): lax.all_to_all(jnp.concatenate([kv_terms.reshape(seq_count, tokens, kv_wi...]
    unnamed x60 -> x170, local copies, waits for them, and re-layouts: 8.6 us -> 10.6 us
  transfers between devices with their start and end apart: 6 -> 7, of which waited for: 4 -> 5; matrix products, arithmetic and copies ran while one was open for 41% -> 46% of each run, Pallas kernels for 0% -> 0%
where the time goes in v15:
time: 193 us; the launch traced here: 191 us
  waiting for transfers between devices  61.7 us (32%)
  local copies, waits for them, and re-layouts  38.7 us (20%)
  starting transfers between devices  33.7 us (17%)
  matrix products  29 us (15%)
  other arithmetic  25.8 us (13%)
  between operations  1.96 us (1%)
    all_to_all x2, waiting for transfers between devices, on_device(): got = lax.all_to_all(sent, 'seq', split_axis=0, concat_axis=0, tiled=True)  31.4 us
    all_to_all x1, waiting for transfers between devices, on_device(): lax.all_to_all(jnp.concatenate([kv_terms.reshape(seq_count, tokens, kv_wi...  29.5 us
    all_to_all x2, starting transfers between devices, on_device(): got = lax.all_to_all(sent, 'seq', split_axis=0, concat_axis=0, tiled=True)  11.8 us
    unnamed x170, local copies, waits for them, and re-layouts  10.6 us
    all_to_all x1, starting transfers between devices, on_device(): lax.all_to_all(jnp.concatenate([kv_terms.reshape(seq_count, tokens, kv_wi...  9.93 us
    reshape x6, local copies, waits for them, and re-layouts, mixer_whole(): row * factor[k - 1][None, :]  7.63 us
    all_to_all x1, starting transfers between devices, mamba_by_heads(): lax.all_to_all(decay_log, 'seq', split_axis=0, concat_axis=1, tiled=True)  7.45 us
    dot_general x3, matrix products, mixer_whole(): state_in = jnp.einsum('kjh,jhnp->khnp', reach, summary, precision=precise)  5.79 us
  transfers between devices with their start and end apart: 7, of which 5 were waited for; matrix products, arithmetic and copies ran while one was open for 46% of the time, Pallas kernels for 0%

profile of v15, /device:TPU:0, one launch (start us, length us, event | category | flops | bytes accessed | tf_op | source)
XLA Modules:
  0.0 191.2 jit_solution(6945673751792502872)
XLA Ops:
  0.7 7.5 %all-to-all-start.2 = ((f32[8,2,128]{2,1,0:T(2,128)}), f32[8,2,128]{2,1,0:T(2,128)S(1)}, u32[]{:S(2)}, u32[]{:S(2)}) async-start(f32[8,2,128]{2,1,0:T(2,128)} %bitcast.347), calls=%async_computation.2 | async-start | bytes 16384 | tf_op jit(solution)/shard_map/all_to_all | solution.py:117
  14.6 5.9 %all-to-all-start.1 = ((bf16[8,128,640]{1,2,0:T(8,128)(2,1)}), bf16[8,128,640]{1,2,0:T(8,128)(2,1)S(1)}, u32[]{:S(2)}, u32[]{:S(2)}) async-start(bf16[8,128,640]{1,2,0:T(8,128)(2,1)} %pad_maximum_fusion.1), calls=%async_computation.1 | async-start | bytes 2621440 | tf_op jit(solution)/shard_map/all_to_all | solution.py:215
  25.9 25.6 %all-to-all-done.1 = bf16[8,128,640]{1,2,0:T(8,128)(2,1)S(1)} async-done(((bf16[8,128,640]{1,2,0:T(8,128)(2,1)}), bf16[8,128,640]{1,2,0:T(8,128)(2,1)S(1)}, u32[]{:S(2)}, u32[]{:S(2)}) %all-to-all-start.1) | async-done | bytes 1310752 | tf_op jit(solution)/shard_map/all_to_all | solution.py:215
  52.6 4.4 %all-to-all-start = ((bf16[8,128,512]{1,2,0:T(8,128)(2,1)}), bf16[8,128,512]{1,2,0:T(8,128)(2,1)}, u32[]{:S(2)}, u32[]{:S(2)}) async-start(bf16[8,128,512]{1,2,0:T(8,128)(2,1)} %broadcast_in_dim.259), calls=%async_computation | async-start | bytes 2097152 | tf_op jit(solution)/shard_map/all_to_all | solution.py:227
  60.8 1.4 convolution_bitcast_fusion.2
  62.2 1.6 copy.426
  63.9 1.4 convolution_bitcast_fusion.1
  65.4 1.6 fusion.50
  68.8 2.0 %convolution_bitcast_fusion.3 = f32[8,2,128,128]{3,0,2,1:T(8,128)} fusion(f32[8,2,128,128]{3,2,1,0:T(8,128)S(1)} %fusion.32, f32[8,8,2]{1,0,2:T(8,128)S(1)} %copy-done.22), kind=kOutput, calls=%fused_computation.66 | convolution fusion | flops 12582912 | bytes 2097664 | tf_op jit(solution)/shard_map/jvp(kjh,jhnp->khnp)/dot_general | solution.py:102
  70.8 2.3 %convolution_bitcast_fusion.6 = f32[8,8,2]{1,0,2:T(8,128)} fusion(f32[2,128,128,8]{2,3,1,0:T(8,128)S(1)} %copy.426, f32[8,2,128,128]{3,2,1,0:T(8,128)S(1)} %fusion.32), kind=kOutput, calls=%fused_computation.79 | convolution fusion | flops 12582912 | bytes 2097664 | tf_op jit(solution)/shard_map/transpose(jvp(kjh,jhnp->khnp))/dot_general | solution.py:102
  74.3 1.6 copy.421
  76.0 2.9 %fusion.45 = f32[8,128,128]{1,2,0:T(8,128)} fusion(f32[8,2,128,128]{2,3,1,0:T(8,128)S(1)} %copy.421, bf16[8,128,2,128]{1,3,2,0:T(8,128)(2,1)} %bitcast.314, f32[8,128,2]{1,2,0:T(2,128)} %copy-done.21), kind=kOutput, calls=%fused_computation.73 | convolution fusion | flops 201850880 | bytes 2105344 | tf_op jit(solution)/shard_map/transpose(jvp(vmap(tn,hnp->thp)))/dot_general | solution.py:69
  88.3 1.4 multiply_bitcast_fusion.2
  89.7 1.4 copy.449
  92.4 3.1 %fusion.62 = (f32[8,2,128]{2,1,0:T(2,128)S(1)}, f32[8,2,128]{2,1,0:T(2,128)S(1)}, f32[8,128,128]{2,1,0:T(8,128)}) fusion(f32[8,128,128]{2,1,0:T(8,128)} %fusion.94, f32[8,2,128]{2,1,0:T(2,128)} %copy.413, pred[8,128,128]{2,1,0:T(8,128)(4,1)S(1)} %compare_and_fusion.3, bf16[8,2,128,128]{3,2,1,0:T(8,128)(2,1)} %bitcast.315, bf16[8,128,2,128]{1,3,2,0:T(8,128)(2,1)} %bitcast.318), kind=kOutput, calls=%fused_computation.97 | convolution fusion | flops 69332992 | bytes 2252800 | tf_op jit(solution)/shard_map/transpose(jvp(vmap(hts,shp->thp)))/dot_general | solution.py:67
  95.6 1.5 fusion.48
  97.2 2.5 %reduce_window_sum.46 = f32[8,2,128]{2,0,1:T(8,128)S(1)} reduce-window(f32[8,2,128]{2,0,1:T(8,128)S(1)} %get-tuple-element.1119, f32[]{:T(128)} %constant.154.clone.1), window={size=1x1x128 pad=0_0x0_0x0_127}, to_apply=%region_28.29 | reduce-window | flops 260096 | bytes 16388 | tf_op jit(solution)/shard_map/transpose(jvp(vmap(jit(cumsum))))/reduce_window_sum | solution.py:45
  99.7 2.7 %reduce_window_sum.47 = f32[8,2,128]{2,0,1:T(8,128)S(1)} reduce-window(f32[8,2,128]{2,0,1:T(8,128)S(1)} %get-tuple-element.1118, f32[]{:T(128)} %constant.154.clone.1), window={size=1x1x128 pad=0_0x0_0x0_127}, to_apply=%region_36.37 | reduce-window | flops 260096 | bytes 16388 | tf_op jit(solution)/shard_map/transpose(jvp(jit(cumsum)))/reduce_window_sum | solution.py:91
  102.5 1.4 fusion.49
  109.1 5.9 %all-to-all-start.4 = ((bf16[8,128,528]{1,2,0:T(8,128)(2,1)}), bf16[8,128,528]{1,2,0:T(8,128)(2,1)}, u32[]{:S(2)}, u32[]{:S(2)}) async-start(bf16[8,128,528]{1,2,0:T(8,128)(2,1)} %pad_maximum_fusion.2), calls=%async_computation.4 | async-start | bytes 2162688 | tf_op jit(solution)/shard_map/all_to_all | solution.py:372
  115.6 1.5 copy.399
  119.5 2.4 %while.51 = (s32[]{:T(128)}, f32[2,4,128]{2,1,0:T(4,128)S(1)}, f32[2,4,128]{2,1,0:T(4,128)S(1)}, s32[]{:T(128)}, s32[4]{0:T(128)}, /*index=5*/s32[128]{0:T(128)S...) while((s32[]{:T(128)}, f32[2,4,128]{2,1,0:T(4,128)S(1)}, ...), condition=%wide.region_9.10_spmd.clone, body=%wide.region_2.9_spmd.clone.sunk | while | flops 138616976 | bytes 5505893 | solution.py:288
  119.5 2.3 %conditional.9 = ((f32[2,4,128]{2,1,0:T(4,128)S(1)}, f32[2,4,128]{2,1,0:T(4,128)S(1)})) conditional(s32[]{:T(128)} %convert_element_type.252, (f32[2,4,128]{2,1,0:T(4,128)S(1)}, f32[2,4,128]{2,1,0:T(4,128)S(1)}) %tuple.198, (s32[]{:T(128)}, s32[]{:T(128)}, s32[4]{0:T(128)}, s32[128]{0:T(128)S(1)}, bf16[1024,256]{0,1:T(8,128)(2,1)S(1)}, ...), branch_computations={%region_3.3_spmd, %region_4.8_spmd} | conditional | flops 138616976 | bytes 5505158 | solution.py:271
  121.9 2.3 %while.52 = (s32[]{:T(128)}, f32[128,2,4,128]{0,3,2,1:T(8,128)S(1)}, s32[]{:T(128)}, bf16[1024,256]{0,1:T(8,128)(2,1)S(1)}, s32[4]{0:T(128)}, /*index=5*/s32[128...) while((s32[]{:T(128)}, ...), condition=%wide.region_15.16_spmd.clone, body=%wide.region_10.15_spmd.clone.sunk | while | flops 271390848 | bytes 3031893 | solution.py:305
  122.0 2.2 %conditional.10 = (f32[128,2,4,128]{0,3,2,1:T(8,128)S(1)}) conditional(s32[]{:T(128)} %convert_element_type.253, f32[128,2,4,128]{0,3,2,1:T(8,128)S(1)} %get-tuple-element.1415, (s32[]{:T(128)}, bf16[1024,256]{0,1:T(8,128)(2,1)S(1)}, s32[]{:T(128)}, s32[4]{0:T(128)}, s32[128]{0:T(128)S(1)}, /*index=5*/bf16[1024,256]{0,1:T(8,128)(2,1)S(1)}, ...), branch_computations={%region_11.11_spmd, %region_12.14_spmd} | conditional | flops 271390848 | bytes 3031158 | solution.py:271
  125.2 6.2 %while.53 = (s32[]{:T(128)}, f32[128,2,4,128]{0,3,2,1:T(8,128)S(1)}, bf16[1024,256]{0,1:T(8,128)(2,1)S(1)}, bf16[1024,256]{0,1:T(8,128)(2,1)S(1)}, s32[]{:T(128)...) while((s32[]{:T(128)}, ...), condition=%wide.region_21.22_spmd.clone, body=%wide.region_16.21_spmd.clone.sunk | while | flops 675616896 | bytes 15094733 | solution.py:343
  125.7 5.1 %conditional.11 = ((f32[128,2,4,128]{0,3,2,1:T(8,128)S(1)}, bf16[1024,256]{0,1:T(8,128)(2,1)S(1)}, bf16[1024,256]{0,1:T(8,128)(2,1)S(1)})) conditional(s32[]{:T(128)} %convert_element_type.254, (f32[128,2,4,128]{0,3,2,1:T(8,128)S(1)}, bf16[1024,256]{0,1:T(8,128)(2,1)S(1)}, bf16[1024,256]{0,1:T(8,128)(2,1)S(1)}) %tuple.203, (s32[]{:T(128)}, ...), branch_computations={%region_17.17_spmd, %region_18.20_spmd} | conditional | flops 675616896 | bytes 15093910 | solution.py:271
  127.5 1.4 fusion.26
  132.9 1.8 add_convert_fusion
  136.0 5.8 %all-to-all-done.4 = bf16[8,128,528]{1,2,0:T(8,128)(2,1)} async-done(((bf16[8,128,528]{1,2,0:T(8,128)(2,1)}), bf16[8,128,528]{1,2,0:T(8,128)(2,1)}, u32[]{:S(2)}, u32[]{:S(2)}) %all-to-all-start.4) | async-done | bytes 1081376 | tf_op jit(solution)/shard_map/all_to_all | solution.py:372
  141.8 9.9 %all-to-all-start.3 = ((bf16[8,128,768]{1,2,0:T(8,128)(2,1)}), bf16[8,128,768]{1,2,0:T(8,128)(2,1)S(1)}, u32[]{:S(2)}, u32[]{:S(2)}) async-start(bf16[8,128,768]{1,2,0:T(8,128)(2,1)} %pad_maximum_fusion), calls=%async_computation.3 | async-start | bytes 3145728 | tf_op jit(solution)/shard_map/all_to_all | solution.py:352
  159.0 29.5 %all-to-all-done.3 = bf16[8,128,768]{1,2,0:T(8,128)(2,1)S(1)} async-done(((bf16[8,128,768]{1,2,0:T(8,128)(2,1)}), bf16[8,128,768]{1,2,0:T(8,128)(2,1)S(1)}, u32[]{:S(2)}, u32[]{:S(2)}) %all-to-all-start.3) | async-done | bytes 1572896 | tf_op jit(solution)/shard_map/all_to_all | solution.py:352
  (310 shorter events, 60.7 us)
Async XLA Ops:
  0.6 12.6 %copy-start.26 = (bf16[128,256]{1,0:T(8,128)(2,1)S(1)}, bf16[128,256]{1,0:T(8,128)(2,1)}, u32[]{:S(2)}) copy-start(bf16[128,256]{1,0:T(8,128)(2,1)} %param.30) | copy-start | bytes 196612
  0.7 12.6 %copy-start.25 = (bf16[128,256]{1,0:T(8,128)(2,1)S(1)}, bf16[128,256]{1,0:T(8,128)(2,1)}, u32[]{:S(2)}) copy-start(bf16[128,256]{1,0:T(8,128)(2,1)} %param.31) | copy-start | bytes 196612
  0.7 14.0 %all-to-all-start.2 = ((f32[8,2,128]{2,1,0:T(2,128)}), f32[8,2,128]{2,1,0:T(2,128)S(1)}, u32[]{:S(2)}, u32[]{:S(2)}) async-start(f32[8,2,128]{2,1,0:T(2,128)} %bitcast.347), calls=%async_computation.2 | async-start | bytes 16384 | tf_op jit(solution)/shard_map/all_to_all | solution.py:117
  8.1 16.4 %copy-start.68 = (pred[8]{0:T(512)(128)(4,1)}, pred[8]{0:T(512)(128)(4,1)S(1)}, u32[]{:S(2)}) copy-start(pred[8]{0:T(512)(128)(4,1)S(1)} %get-tuple-element.1141) | copy-start | bytes 28
  8.1 17.1 %copy-start.52 = (f32[8]{0:T(128)}, f32[8]{0:T(128)S(1)}, u32[]{:S(2)}) copy-start(f32[8]{0:T(128)S(1)} %get-tuple-element.1140) | copy-start | bytes 100
  8.2 17.1 %copy-start.37 = (pred[8]{0:T(512)(128)(4,1)}, pred[8]{0:T(512)(128)(4,1)S(1)}, u32[]{:S(2)}) copy-start(pred[8]{0:T(512)(128)(4,1)S(1)} %get-tuple-element.1144) | copy-start | bytes 28
  8.2 17.1 %copy-start.54 = (pred[8]{0:T(512)(128)(4,1)}, pred[8]{0:T(512)(128)(4,1)S(1)}, u32[]{:S(2)}) copy-start(pred[8]{0:T(512)(128)(4,1)S(1)} %get-tuple-element.1145) | copy-start | bytes 28
  8.2 17.0 %copy-start.56 = (f32[8]{0:T(128)}, f32[8]{0:T(128)S(1)}, u32[]{:S(2)}) copy-start(f32[8]{0:T(128)S(1)} %get-tuple-element.1137) | copy-start | bytes 100
  14.6 38.0 %copy-start.58 = (pred[8]{0:T(512)(128)(4,1)}, pred[8]{0:T(512)(128)(4,1)S(1)}, u32[]{:S(2)}) copy-start(pred[8]{0:T(512)(128)(4,1)S(1)} %iota_compare_fusion.7) | copy-start | bytes 28
  14.6 36.8 %all-to-all-start.1 = ((bf16[8,128,640]{1,2,0:T(8,128)(2,1)}), bf16[8,128,640]{1,2,0:T(8,128)(2,1)S(1)}, u32[]{:S(2)}, u32[]{:S(2)}) async-start(bf16[8,128,640]{1,2,0:T(8,128)(2,1)} %pad_maximum_fusion.1), calls=%async_computation.1 | async-start | bytes 2621440 | tf_op jit(solution)/shard_map/all_to_all | solution.py:215
  21.4 35.6 %copy-start.61 = (f32[8]{0:T(128)}, f32[8]{0:T(128)S(1)}, u32[]{:S(2)}) copy-start(f32[8]{0:T(128)S(1)} %get-tuple-element.1139) | copy-start | bytes 100
  21.4 35.6 %copy-start.50 = (pred[8]{0:T(512)(128)(4,1)}, pred[8]{0:T(512)(128)(4,1)S(1)}, u32[]{:S(2)}) copy-start(pred[8]{0:T(512)(128)(4,1)S(1)} %get-tuple-element.1143) | copy-start | bytes 28
  21.5 35.6 %copy-start.70 = (pred[8]{0:T(512)(128)(4,1)}, pred[8]{0:T(512)(128)(4,1)S(1)}, u32[]{:S(2)}) copy-start(pred[8]{0:T(512)(128)(4,1)S(1)} %get-tuple-element.1142) | copy-start | bytes 28
  21.5 35.6 %copy-start.72 = (f32[8]{0:T(128)}, f32[8]{0:T(128)S(1)}, u32[]{:S(2)}) copy-start(f32[8]{0:T(128)S(1)} %get-tuple-element.1135) | copy-start | bytes 100
  22.5 34.5 %copy-start.29 = (f32[8,128]{1,0:T(8,128)}, f32[8,128]{1,0:T(8,128)S(1)}, u32[]{:S(2)}) copy-start(f32[8,128]{1,0:T(8,128)S(1)} %get-tuple-element.1126) | copy-start | bytes 12292
  24.0 36.8 %copy-start.21 = (f32[8,128,2]{1,2,0:T(2,128)}, f32[8,128,2]{1,2,0:T(2,128)S(1)}, u32[]{:S(2)}) copy-start(f32[8,128,2]{1,2,0:T(2,128)S(1)} %copy.416) | copy-start | bytes 24580
  24.1 32.9 %copy-start.33 = (f32[8,2]{0,1:T(2,128)}, f32[8,2]{0,1:T(2,128)S(1)}, u32[]{:S(2)}) copy-start(f32[8,2]{0,1:T(2,128)S(1)} %slice_reduce_fusion) | copy-start | bytes 196
  24.4 32.7 %copy-start.39 = (f32[2]{0:T(128)}, f32[2]{0:T(128)S(1)}, u32[]{:S(2)}) copy-start(f32[2]{0:T(128)S(1)} %get-tuple-element.1019) | copy-start | bytes 28
  24.4 32.7 %copy-start.41 = (f32[2]{0:T(128)}, f32[2]{0:T(128)S(1)}, u32[]{:S(2)}) copy-start(f32[2]{0:T(128)S(1)} %get-tuple-element.1020) | copy-start | bytes 28
  24.4 32.7 %copy-start.43 = (f32[2]{0:T(128)}, f32[2]{0:T(128)S(1)}, u32[]{:S(2)}) copy-start(f32[2]{0:T(128)S(1)} %get-tuple-element.1021) | copy-start | bytes 28
  24.4 32.7 %copy-start.45 = (f32[2]{0:T(128)}, f32[2]{0:T(128)S(1)}, u32[]{:S(2)}) copy-start(f32[2]{0:T(128)S(1)} %get-tuple-element.1022) | copy-start | bytes 28
  24.5 32.7 %copy-start.48 = (f32[2]{0:T(128)}, f32[2]{0:T(128)S(1)}, u32[]{:S(2)}) copy-start(f32[2]{0:T(128)S(1)} %get-tuple-element.1018) | copy-start | bytes 28
  24.5 32.7 %copy-start.63 = (f32[2]{0:T(128)}, f32[2]{0:T(128)S(1)}, u32[]{:S(2)}) copy-start(f32[2]{0:T(128)S(1)} %get-tuple-element.1017) | copy-start | bytes 28
  52.6 56.5 %all-to-all-start = ((bf16[8,128,512]{1,2,0:T(8,128)(2,1)}), bf16[8,128,512]{1,2,0:T(8,128)(2,1)}, u32[]{:S(2)}, u32[]{:S(2)}) async-start(bf16[8,128,512]{1,2,0:T(8,128)(2,1)} %broadcast_in_dim.259), calls=%async_computation | async-start | bytes 2097152 | tf_op jit(solution)/shard_map/all_to_all | solution.py:227
  57.3 1.6 collective-permute-start
  97.1 8.2 %copy-start.2 = (bf16[1024,128]{1,0:T(8,128)(2,1)S(1)}, bf16[1024,128]{1,0:T(8,128)(2,1)}, u32[]{:S(2)}) copy-start(bf16[1024,128]{1,0:T(8,128)(2,1)} %copy-done) | copy-start | bytes 786436
  97.1 8.2 %copy-start.13 = (f32[8,128,128]{1,2,0:T(8,128)S(1)}, f32[8,128,128]{1,2,0:T(8,128)}, u32[]{:S(2)}) copy-start(f32[8,128,128]{1,2,0:T(8,128)} %fusion.45) | copy-start | bytes 1572868
  108.0 6.9 %copy-start.19 = (bf16[128,1024]{1,0:T(8,128)(2,1)S(1)}, bf16[128,1024]{1,0:T(8,128)(2,1)}, u32[]{:S(2)}) copy-start(bf16[128,1024]{1,0:T(8,128)(2,1)} %param.29) | copy-start | bytes 786436
  109.1 32.7 %all-to-all-start.4 = ((bf16[8,128,528]{1,2,0:T(8,128)(2,1)}), bf16[8,128,528]{1,2,0:T(8,128)(2,1)}, u32[]{:S(2)}, u32[]{:S(2)}) async-start(bf16[8,128,528]{1,2,0:T(8,128)(2,1)} %pad_maximum_fusion.2), calls=%async_computation.4 | async-start | bytes 2162688 | tf_op jit(solution)/shard_map/all_to_all | solution.py:372
  136.0 16.7 %copy-start.15 = (bf16[128,2,4,128]{0,3,2,1:T(8,128)(2,1)S(1)}, bf16[128,2,4,128]{0,3,2,1:T(8,128)(2,1)}, u32[]{:S(2)}) copy-start(bf16[128,2,4,128]{0,3,2,1:T(8,128)(2,1)} %get-tuple-element.1095) | copy-start | bytes 786436
  141.8 46.7 %all-to-all-start.3 = ((bf16[8,128,768]{1,2,0:T(8,128)(2,1)}), bf16[8,128,768]{1,2,0:T(8,128)(2,1)S(1)}, u32[]{:S(2)}, u32[]{:S(2)}) async-start(bf16[8,128,768]{1,2,0:T(8,128)(2,1)} %pad_maximum_fusion), calls=%async_computation.3 | async-start | bytes 3145728 | tf_op jit(solution)/shard_map/all_to_all | solution.py:352
  154.7 2.8 %collective-permute-start.1 = (f32[128,256]{0,1:T(8,128)S(1)}, f32[128,256]{0,1:T(8,128)S(1)}, u32[]{:S(2)}, u32[]{:S(2)}) collective-permute-start(f32[128,256]{0,1:T(8,128)S(1)} %slice.109), channel_id=1, source_target_pairs={{0,1},{1,0},{2,3},{3,2},{4,5},{5,4},{6,7},{7,6},{8,9},{9,8},{10,11... | collective-permute-start | bytes 393224 | tf_op jit(solution)/shard_map/ppermute | solution.py:384
  (54 other events, 162.9 us)

commit v16 on v11

--- a/solution.py
+++ b/solution.py
@@ -10,7 +10,7 @@
 TOK_SPAN = 128
 
 
-precise = lax.Precision.HIGH
+precise = lax.Precision.DEFAULT
 big_negative = -1e30
 
 

time: 183 us -> 171 us (0.934)
  matrix products: 28.5 us -> 18.8 us
  starting transfers between devices: 34.3 us -> 25.9 us
  waiting for transfers between devices: 66.9 us -> 75 us
  local copies, waits for them, and re-layouts: 32.8 us -> 28.3 us
  other arithmetic: 18.5 us -> 20.7 us
    all_to_all x1, starting transfers between devices: 12.4 us -> 3.58 us  [on_device(): lax.all_to_all(jnp.concatenate([kv_terms.reshape(seq_count, tokens, kv_wi...]
    all_to_all x2, waiting for transfers between devices: 36.7 us -> 43.8 us  [on_device(): got = lax.all_to_all(sent, 'seq', split_axis=0, concat_axis=0, tiled=True)]
    dot_general x3, matrix products: 5.8 us -> 3.02 us  [mixer_stretch(): inner = jnp.einsum('hts,shp->thp', kernel, inputs, precision=precise)]
    dot_general x3, matrix products: 5.6 us -> 3.12 us  [mixer_whole(): state_in = jnp.einsum('kjh,jhnp->khnp', reach, summary, precision=precise)]
    unnamed x60 -> x90, local copies, waits for them, and re-layouts: 8.6 us -> 8.54 us
  transfers between devices with their start and end apart: 6 -> 6, of which waited for: 4 -> 4; matrix products, arithmetic and copies ran while one was open for 41% -> 36% of each run, Pallas kernels for 0% -> 0%
where the time goes in v16:
time: 171 us; the launch traced here: 170 us
  waiting for transfers between devices  75 us (44%)
  local copies, waits for them, and re-layouts  28.3 us (17%)
  starting transfers between devices  25.9 us (15%)
  other arithmetic  20.7 us (12%)
  matrix products  18.8 us (11%)
    all_to_all x2, waiting for transfers between devices, on_device(): got = lax.all_to_all(sent, 'seq', split_axis=0, concat_axis=0, tiled=True)  43.8 us
    all_to_all x1, waiting for transfers between devices, on_device(): lax.all_to_all(jnp.concatenate([kv_terms.reshape(seq_count, tokens, kv_wi...  29.8 us
    all_to_all x2, starting transfers between devices, on_device(): got = lax.all_to_all(sent, 'seq', split_axis=0, concat_axis=0, tiled=True)  10.4 us
    unnamed x90, local copies, waits for them, and re-layouts  8.54 us
    all_to_all x1, starting transfers between devices, mamba_by_heads(): lax.all_to_all(decay_log, 'seq', split_axis=0, concat_axis=1, tiled=True)  7.45 us
    all_to_all x1, starting transfers between devices, on_device(): lax.all_to_all(kv_sent, 'seq', split_axis=0, concat_axis=0, tiled=True)  4.43 us
    dot_general x3, matrix products, local_state(): jnp.einsum('hs,sn,shp->hnp', weights, b_float, inputs, precision=precise)  3.94 us
    another operation x1, other arithmetic, mixer_whole(): cumulated = jnp.cumsum(dec, axis=2)  3.76 us
  transfers between devices with their start and end apart: 6, of which 4 were waited for; matrix products, arithmetic and copies ran while one was open for 36% of the time, Pallas kernels for 0%

profile of v16, /device:TPU:0, one launch (start us, length us, event | category | flops | bytes accessed | tf_op | source)
XLA Modules:
  0.0 170.5 jit_solution(5798908458190703420)
XLA Ops:
  0.7 7.5 %all-to-all-start.2 = ((f32[8,2,128]{2,1,0:T(2,128)}), f32[8,2,128]{2,1,0:T(2,128)S(1)}, u32[]{:S(2)}, u32[]{:S(2)}) async-start(f32[8,2,128]{2,1,0:T(2,128)} %bitcast.334), calls=%async_computation.2 | async-start | bytes 16384 | tf_op jit(solution)/shard_map/all_to_all | solution.py:117
  9.6 1.3 copy.429
  11.8 1.3 pad_maximum_fusion
  13.2 1.5 all-to-all-done.2
  14.6 4.6 %all-to-all-start.1 = ((bf16[8,128,768]{2,1,0:T(8,128)(2,1)}), bf16[8,128,768]{2,1,0:T(8,128)(2,1)S(1)}, u32[]{:S(2)}, u32[]{:S(2)}) async-start(bf16[8,128,768]{2,1,0:T(8,128)(2,1)} %pad_maximum_fusion), calls=%async_computation.1 | async-start | bytes 3145728 | tf_op jit(solution)/shard_map/all_to_all | solution.py:211
  22.7 33.0 %all-to-all-done.1 = bf16[8,128,768]{2,1,0:T(8,128)(2,1)S(1)} async-done(((bf16[8,128,768]{2,1,0:T(8,128)(2,1)}), bf16[8,128,768]{2,1,0:T(8,128)(2,1)S(1)}, u32[]{:S(2)}, u32[]{:S(2)}) %all-to-all-start.1) | async-done | bytes 1572896 | tf_op jit(solution)/shard_map/all_to_all | solution.py:211
  55.6 1.1 broadcast_in_dim.265
  56.7 4.4 %all-to-all-start = ((bf16[8,128,512]{1,2,0:T(8,128)(2,1)}), bf16[8,128,512]{1,2,0:T(8,128)(2,1)}, u32[]{:S(2)}, u32[]{:S(2)}) async-start(bf16[8,128,512]{1,2,0:T(8,128)(2,1)} %broadcast_in_dim.265), calls=%async_computation | async-start | bytes 2097152 | tf_op jit(solution)/shard_map/all_to_all | solution.py:217
  64.3 1.4 convolution_bitcast_fusion.1
  66.5 2.4 %fusion.53 = (f32[8,128,2]{1,2,0:T(2,128)S(1)}, f32[8,2,128,128]{3,2,1,0:T(8,128)}) fusion(f32[8,128,128]{1,2,0:T(8,128)} %copy.544, bf16[8,128,2,128]{1,3,2,0:T(8,128)(2,1)S(1)} %bitcast.303, bf16[8,2,128,128]{3,0,2,1:T(8,128)(2,1)S(1)} %convolution_bitcast_fusion.1), kind=kOutput, calls=%fused_computation.88 | convolution fusion | flops 67631104 | bytes 2629632 | tf_op jit(solution)/shard_map/transpose(jvp(vmap(hs,sn,shp->hnp)))/dot_general | solution.py:53
  70.3 1.2 convolution_bitcast_fusion.3
  72.0 2.1 %copy.442 = bf16[8,2,128,128]{2,3,1,0:T(8,128)(2,1)} copy(bf16[8,2,128,128]{3,0,2,1:T(8,128)(2,1)} %convolution_bitcast_fusion.3) | data formatting | bytes 1048576 | tf_op jit(solution)/shard_map/jvp(kjh,jhnp->khnp)/transpose | solution.py:102
  74.2 2.2 %fusion.48 = f32[8,128,128]{1,2,0:T(8,128)} fusion(bf16[8,2,128,128]{2,3,1,0:T(8,128)(2,1)} %copy.442, bf16[8,128,2,128]{1,3,2,0:T(8,128)(2,1)S(1)} %bitcast.297, f32[8,128,2]{1,2,0:T(2,128)S(1)} %copy.437), kind=kOutput, calls=%fused_computation.76 | convolution fusion | flops 67633152 | bytes 1581056 | tf_op jit(solution)/shard_map/transpose(jvp(vmap(tn,hnp->thp)))/dot_general | solution.py:69
  79.2 1.8 %fusion.63 = (f32[8,2,128]{2,1,0:T(2,128)S(1)}, f32[8,2,128]{2,1,0:T(2,128)S(1)}, bf16[8,128,128]{2,1,0:T(8,128)(2,1)S(1)}) fusion(f32[8,128,128]{2,1,0:T(8,128)S(1)} %fusion.83, f32[8,2,128]{2,1,0:T(2,128)} %copy.434, pred[8,128,128]{2,1,0:T(8,128)(4,1)S(1)} %compare_and_fusion.3, bf16[8,2,128,128]{3,2,1,0:T(8,128)(2,1)S(1)} %bitcast.298, ...), kind=kOutput, calls=%fused_computation.99 | convolution fusion | flops 69332992 | bytes 1990656 | tf_op jit(solution)/shard_map/transpose(jvp(vmap(hts,shp->thp)))/dot_general | solution.py:67
  81.1 1.3 fusion.51
  83.2 3.2 %reduce_window_sum.46 = f32[8,2,128]{2,0,1:T(8,128)S(1)} reduce-window(f32[8,2,128]{2,0,1:T(8,128)} %get-tuple-element.1117, f32[]{:T(128)} %constant.152.clone.1), window={size=1x1x128 pad=0_0x0_0x0_127}, to_apply=%region_28.29 | reduce-window | flops 260096 | bytes 16388 | tf_op jit(solution)/shard_map/transpose(jvp(vmap(jit(cumsum))))/reduce_window_sum | solution.py:45
  86.3 3.8 %reduce_window_sum.47 = f32[8,2,128]{2,0,1:T(8,128)} reduce-window(f32[8,2,128]{2,0,1:T(8,128)} %get-tuple-element.1116, f32[]{:T(128)} %constant.152.clone.1), window={size=1x1x128 pad=0_0x0_0x0_127}, to_apply=%region_36.37 | reduce-window | flops 260096 | bytes 16388 | tf_op jit(solution)/shard_map/transpose(jvp(jit(cumsum)))/reduce_window_sum | solution.py:91
  90.8 1.4 fusion.52
  95.5 5.8 %all-to-all-start.4 = ((bf16[8,128,528]{1,2,0:T(8,128)(2,1)}), bf16[8,128,528]{1,2,0:T(8,128)(2,1)}, u32[]{:S(2)}, u32[]{:S(2)}) async-start(bf16[8,128,528]{1,2,0:T(8,128)(2,1)} %pad_maximum_fusion.2), calls=%async_computation.4 | async-start | bytes 2162688 | tf_op jit(solution)/shard_map/all_to_all | solution.py:362
  101.9 1.5 copy.419
  104.1 1.7 while.51
  104.1 1.6 conditional.9
  105.8 1.7 while.52
  105.9 1.6 conditional.10
  109.2 3.7 %while.53 = (s32[]{:T(128)}, f32[128,2,4,128]{0,3,2,1:T(8,128)S(1)}, bf16[1024,256]{0,1:T(8,128)(2,1)S(1)}, bf16[1024,256]{0,1:T(8,128)(2,1)}, s32[]{:T(128)}, /...) while((s32[]{:T(128)}, ...), condition=%wide.region_21.22_spmd.clone, body=%wide.region_16.21_spmd.clone.sunk | while | flops 675616896 | bytes 19289092 | solution.py:333
  109.2 3.7 %conditional.11 = ((f32[128,2,4,128]{0,3,2,1:T(8,128)S(1)}, bf16[1024,256]{0,1:T(8,128)(2,1)S(1)}, bf16[1024,256]{0,1:T(8,128)(2,1)})) conditional(s32[]{:T(128)} %convert_element_type.254, (f32[128,2,4,128]{0,3,2,1:T(8,128)S(1)}, bf16[1024,256]{0,1:T(8,128)(2,1)S(1)}, bf16[1024,256]{0,1:T(8,128)(2,1)}) %tuple.203, (s32[]{:T(128)}, ...), branch_computations={%region_17.17_spmd, %region_18.20_spmd} | conditional | flops 675616896 | bytes 19288270 | solution.py:261
  113.0 1.4 copy_bitcast_fusion
  115.1 1.3 pad_maximum_fusion.1
  116.4 10.8 %all-to-all-done.4 = bf16[8,128,528]{1,2,0:T(8,128)(2,1)} async-done(((bf16[8,128,528]{1,2,0:T(8,128)(2,1)}), bf16[8,128,528]{1,2,0:T(8,128)(2,1)}, u32[]{:S(2)}, u32[]{:S(2)}) %all-to-all-start.4) | async-done | bytes 1081376 | tf_op jit(solution)/shard_map/all_to_all | solution.py:362
  127.2 3.6 %all-to-all-start.3 = ((bf16[8,128,768]{1,2,0:T(8,128)(2,1)}), bf16[8,128,768]{1,2,0:T(8,128)(2,1)S(1)}, u32[]{:S(2)}, u32[]{:S(2)}) async-start(bf16[8,128,768]{1,2,0:T(8,128)(2,1)} %pad_maximum_fusion.1), calls=%async_computation.3 | async-start | bytes 3145728 | tf_op jit(solution)/shard_map/all_to_all | solution.py:342
  132.6 1.1 convert_reduce_fusion.4
  138.0 29.8 %all-to-all-done.3 = bf16[8,128,768]{1,2,0:T(8,128)(2,1)S(1)} async-done(((bf16[8,128,768]{1,2,0:T(8,128)(2,1)}), bf16[8,128,768]{1,2,0:T(8,128)(2,1)S(1)}, u32[]{:S(2)}, u32[]{:S(2)}) %all-to-all-start.3) | async-done | bytes 1572896 | tf_op jit(solution)/shard_map/all_to_all | solution.py:342
  (232 shorter events, 38.0 us)
Async XLA Ops:
  0.6 10.6 %copy-start.9 = (bf16[128,2048]{1,0:T(8,128)(2,1)S(1)}, bf16[128,2048]{1,0:T(8,128)(2,1)}, u32[]{:S(2)}) copy-start(bf16[128,2048]{1,0:T(8,128)(2,1)} %param.32) | copy-start | bytes 1572868
  0.7 14.0 %all-to-all-start.2 = ((f32[8,2,128]{2,1,0:T(2,128)}), f32[8,2,128]{2,1,0:T(2,128)S(1)}, u32[]{:S(2)}, u32[]{:S(2)}) async-start(f32[8,2,128]{2,1,0:T(2,128)} %bitcast.334), calls=%async_computation.2 | async-start | bytes 16384 | tf_op jit(solution)/shard_map/all_to_all | solution.py:117
  9.6 2.1 %copy-start.27 = (bf16[128,128]{1,0:T(8,128)(2,1)S(1)}, bf16[128,128]{1,0:T(8,128)(2,1)}, u32[]{:S(2)}) copy-start(bf16[128,128]{1,0:T(8,128)(2,1)} %param.24) | copy-start | bytes 98308
  9.6 2.2 %copy-start.28 = (bf16[128,128]{1,0:T(8,128)(2,1)S(1)}, bf16[128,128]{1,0:T(8,128)(2,1)}, u32[]{:S(2)}) copy-start(bf16[128,128]{1,0:T(8,128)(2,1)} %param.25) | copy-start | bytes 98308
  13.1 6.2 %copy-start.37 = (f32[16]{0:T(128)S(1)}, f32[16]{0:T(128)}, u32[]{:S(2)}) copy-start(f32[16]{0:T(128)} %param.27) | copy-start | bytes 196
  14.6 41.0 %all-to-all-start.1 = ((bf16[8,128,768]{2,1,0:T(8,128)(2,1)}), bf16[8,128,768]{2,1,0:T(8,128)(2,1)S(1)}, u32[]{:S(2)}, u32[]{:S(2)}) async-start(bf16[8,128,768]{2,1,0:T(8,128)(2,1)} %pad_maximum_fusion), calls=%async_computation.1 | async-start | bytes 3145728 | tf_op jit(solution)/shard_map/all_to_all | solution.py:211
  20.5 1.4 copy-start.25
  20.5 48.4 %copy-start.23 = (f32[8,128]{1,0:T(8,128)}, f32[8,128]{1,0:T(8,128)S(1)}, u32[]{:S(2)}) copy-start(f32[8,128]{1,0:T(8,128)S(1)} %get-tuple-element.1125) | copy-start | bytes 12292
  20.8 72.2 %copy-start.15 = (pred[8,128,128]{2,1,0:T(8,128)(4,1)}, pred[8,128,128]{2,1,0:T(8,128)(4,1)S(1)}, u32[]{:S(2)}) copy-start(pred[8,128,128]{2,1,0:T(8,128)(4,1)S(1)} %compare_and_fusion.3) | copy-start | bytes 393220
  22.0 52.2 %copy-start.17 = (f32[8,128,2]{1,2,0:T(2,128)}, f32[8,128,2]{1,2,0:T(2,128)S(1)}, u32[]{:S(2)}) copy-start(f32[8,128,2]{1,2,0:T(2,128)S(1)} %copy.437) | copy-start | bytes 24580
  22.2 55.3 %copy-start.31 = (f32[8,2]{0,1:T(2,128)}, f32[8,2]{0,1:T(2,128)S(1)}, u32[]{:S(2)}) copy-start(f32[8,2]{0,1:T(2,128)S(1)} %slice_reduce_fusion) | copy-start | bytes 196
  56.7 38.7 %all-to-all-start = ((bf16[8,128,512]{1,2,0:T(8,128)(2,1)}), bf16[8,128,512]{1,2,0:T(8,128)(2,1)}, u32[]{:S(2)}, u32[]{:S(2)}) async-start(bf16[8,128,512]{1,2,0:T(8,128)(2,1)} %broadcast_in_dim.265), calls=%async_computation | async-start | bytes 2097152 | tf_op jit(solution)/shard_map/all_to_all | solution.py:217
  66.5 5.0 %copy-start.4 = (bf16[2,128,128,8]{2,3,1,0:T(8,128)(2,1)S(1)}, bf16[2,128,128,8]{2,3,1,0:T(8,128)(2,1)}, u32[]{:S(2)}) copy-start(bf16[2,128,128,8]{2,3,1,0:T(8,128)(2,1)} %copy.450) | copy-start | bytes 1572868
  79.2 3.2 %copy-start.10 = (f32[8,128,128]{2,1,0:T(8,128)}, f32[8,128,128]{2,1,0:T(8,128)S(1)}, u32[]{:S(2)}) copy-start(f32[8,128,128]{2,1,0:T(8,128)S(1)} %fusion.83) | copy-start | bytes 1572868
  79.2 1.9 %copy-start.2 = (bf16[8,2,128,128]{2,3,1,0:T(8,128)(2,1)S(1)}, bf16[8,2,128,128]{2,3,1,0:T(8,128)(2,1)}, u32[]{:S(2)}) copy-start(bf16[8,2,128,128]{2,3,1,0:T(8,128)(2,1)} %copy.442) | copy-start | bytes 1572868
  90.1 2.5 %copy-start.3 = (f32[8,128,128]{1,2,0:T(8,128)S(1)}, f32[8,128,128]{1,2,0:T(8,128)}, u32[]{:S(2)}) copy-start(f32[8,128,128]{1,2,0:T(8,128)} %fusion.48) | copy-start | bytes 1572868
  90.8 2.1 %copy-start.11 = (f32[8,128,128]{2,1,0:T(8,128)S(1)}, f32[8,128,128]{2,1,0:T(8,128)}, u32[]{:S(2)}) copy-start(f32[8,128,128]{2,1,0:T(8,128)} %copy-done.10) | copy-start | bytes 1572868
  90.8 2.1 %copy-start.33 = (f32[8,2,128]{2,1,0:T(2,128)S(1)}, f32[8,2,128]{2,1,0:T(2,128)}, u32[]{:S(2)}) copy-start(f32[8,2,128]{2,1,0:T(2,128)} %copy.434) | copy-start | bytes 24580
  90.8 2.1 %copy-start.39 = (f32[2]{0:T(128)S(1)}, f32[2]{0:T(128)}, u32[]{:S(2)}) copy-start(f32[2]{0:T(128)} %dynamic_slice.18) | copy-start | bytes 28
  94.4 6.9 %copy-start.13 = (bf16[128,1024]{1,0:T(8,128)(2,1)S(1)}, bf16[128,1024]{1,0:T(8,128)(2,1)}, u32[]{:S(2)}) copy-start(bf16[128,1024]{1,0:T(8,128)(2,1)} %param.29) | copy-start | bytes 786436
  95.4 6.2 %copy-start.14 = (bf16[128,1024]{1,0:T(8,128)(2,1)S(1)}, bf16[128,1024]{1,0:T(8,128)(2,1)}, u32[]{:S(2)}) copy-start(bf16[128,1024]{1,0:T(8,128)(2,1)} %param.33) | copy-start | bytes 786436
  95.4 6.4 %copy-start.36 = (s32[4,1]{0,1:T(1,128)S(1)}, s32[4,1]{0,1:T(1,128)}, u32[]{:S(2)}) copy-start(s32[4,1]{0,1:T(1,128)} %copy-done.35) | copy-start | bytes 52
  95.5 31.7 %all-to-all-start.4 = ((bf16[8,128,528]{1,2,0:T(8,128)(2,1)}), bf16[8,128,528]{1,2,0:T(8,128)(2,1)}, u32[]{:S(2)}, u32[]{:S(2)}) async-start(bf16[8,128,528]{1,2,0:T(8,128)(2,1)} %pad_maximum_fusion.2), calls=%async_computation.4 | async-start | bytes 2162688 | tf_op jit(solution)/shard_map/all_to_all | solution.py:362
  112.9 1.5 copy-start.7
  112.9 1.5 copy-start.12
  112.9 1.5 copy-start.16
  112.9 1.5 copy-start.18
  112.9 1.5 copy-start.34
  112.9 1.5 copy-start.40
  116.4 15.3 %copy-start.8 = (bf16[128,2,4,128]{0,3,2,1:T(8,128)(2,1)S(1)}, bf16[128,2,4,128]{0,3,2,1:T(8,128)(2,1)}, u32[]{:S(2)}) copy-start(bf16[128,2,4,128]{0,3,2,1:T(8,128)(2,1)} %get-tuple-element.1095) | copy-start | bytes 786436
  127.2 40.6 %all-to-all-start.3 = ((bf16[8,128,768]{1,2,0:T(8,128)(2,1)}), bf16[8,128,768]{1,2,0:T(8,128)(2,1)S(1)}, u32[]{:S(2)}, u32[]{:S(2)}) async-start(bf16[8,128,768]{1,2,0:T(8,128)(2,1)} %pad_maximum_fusion.1), calls=%async_computation.3 | async-start | bytes 3145728 | tf_op jit(solution)/shard_map/all_to_all | solution.py:342
  133.7 2.8 %collective-permute-start = (f32[128,256]{0,1:T(8,128)S(1)}, f32[128,256]{0,1:T(8,128)S(1)}, u32[]{:S(2)}, u32[]{:S(2)}) collective-permute-start(f32[128,256]{0,1:T(8,128)S(1)} %slice.114), channel_id=1, source_target_pairs={{0,1},{1,0},{2,3},{3,2},{4,5},{5,4},{6,7},{7,6},{8,9},{9,8},{10,11... | collective-permute-start | bytes 393224 | tf_op jit(solution)/shard_map/ppermute | solution.py:374
  (15 other events, 16.6 us)

commit v17 on v16

--- a/solution.py
+++ b/solution.py
@@ -108,13 +108,12 @@
     return outputs.reshape(count * width, heads, P_SIZE)
 
 
-def mamba_by_heads(x_all, cot_all, b_all, c_all, decay_log, skip_gain, doc_lengths):
+def mamba_by_heads(x_all, cot_all, b_all, c_all, decay, skip_gain, doc_lengths):
     seq_count = lax.axis_size("seq")
     place = lax.axis_index("seq")
     heads_here = skip_gain.shape[0]
     own = heads_here // seq_count
     total = x_all.shape[0]
-    decay = lax.all_to_all(decay_log, "seq", split_axis=0, concat_axis=1, tiled=True)
     gains = lax.dynamic_slice_in_dim(skip_gain, place * own, own)
     segment = doc_index(jnp.arange(total, dtype=jnp.int32), doc_lengths)
     inputs = x_all.astype(jnp.float32).reshape(total, own, P_SIZE)
@@ -205,14 +204,35 @@
         def spread(a):
             return jnp.broadcast_to(a[None], (seq_count,) + a.shape)
 
+        decay_parts = []
+        rest = decay_log
+        for scale in (2.0**8, 2.0**16, 2.0**24, 2.0**32):
+            part = jnp.round(rest * scale) / scale
+            rest = rest - part
+            decay_parts.append(part)
+        decay_sent = jnp.concatenate(decay_parts, axis=0).astype(jnp.bfloat16)
+        decay_sent = decay_sent.reshape(len(decay_parts), seq_count, heads_here // seq_count, tokens)
+        decay_sent = decay_sent.transpose(1, 3, 0, 2).reshape(seq_count, tokens, -1)
         sent = jnp.concatenate(
-            [by_owner(x_input), by_owner(mixer_cot), spread(b_rows), spread(c_rows)], axis=2
+            [
+                by_owner(x_input),
+                by_owner(mixer_cot),
+                spread(b_rows),
+                spread(c_rows),
+                decay_sent,
+            ],
+            axis=2,
         )
         got = lax.all_to_all(sent, "seq", split_axis=0, concat_axis=0, tiled=True)
         x_all = got[:, :, :own_width].reshape(total_len, own_width)
         cot_all = got[:, :, own_width : 2 * own_width].reshape(total_len, own_width)
         b_all = got[:, :, 2 * own_width : 2 * own_width + state_width].reshape(total_len, -1)
-        c_all = got[:, :, 2 * own_width + state_width :].reshape(total_len, -1)
+        c_all = got[:, :, 2 * own_width + state_width : 2 * own_width + 2 * state_width]
+        c_all = c_all.reshape(total_len, -1)
+        decay_got = got[:, :, 2 * own_width + 2 * state_width :].astype(jnp.float32)
+        decay_got = decay_got.reshape(total_len, 4, heads_here // seq_count)
+        decay_own = ((decay_got[:, 0] + decay_got[:, 1]) + decay_got[:, 2]) + decay_got[:, 3]
+        decay_own = decay_own.T
         kv_sent = spread(jnp.concatenate([attention_key_rows, values], axis=1))
         gathered = lax.all_to_all(kv_sent, "seq", split_axis=0, concat_axis=0, tiled=True)
         gathered = gathered.reshape(total_len, 2 * key_width)
@@ -223,7 +243,7 @@
     key_all, value_all = gathered[:, :key_width], gathered[:, key_width : 2 * key_width]
     if by_heads:
         mixed_own, x_grad_own, bc_part = mamba_by_heads(
-            x_all, cot_all, b_all, c_all, decay_log, skip_gain, doc_lengths
+            x_all, cot_all, b_all, c_all, decay_own, skip_gain, doc_lengths
         )
     else:
         mixer_out, x_grad, grad_b, grad_c, grad_decay = mamba_by_stretch(

time: 171 us -> 176 us (1.029)
  waiting for transfers between devices: 75 us -> 67.7 us
  local copies, waits for them, and re-layouts: 28.3 us -> 34.4 us
  starting transfers between devices: 25.9 us -> 31.9 us
  other arithmetic: 20.7 us -> 16.8 us
  matrix products: 18.8 us -> 22.5 us
    all_to_all x1, starting transfers between devices: 3.58 us -> 14.4 us  [on_device(): lax.all_to_all(jnp.concatenate([kv_terms.reshape(seq_count, tokens, kv_wi...]
    all_to_all x1 -> x0, starting transfers between devices: 7.45 us -> none  [mamba_by_heads(): lax.all_to_all(decay_log, 'seq', split_axis=0, concat_axis=1, tiled=True)]
    all_to_all x2, waiting for transfers between devices: 43.8 us -> 37.1 us  [on_device(): got = lax.all_to_all(sent, 'seq', split_axis=0, concat_axis=0, tiled=True)]
    unnamed x90 -> x61, local copies, waits for them, and re-layouts: 8.54 us -> 14 us
    all_to_all x2, starting transfers between devices: 10.4 us -> 13.2 us  [on_device(): got = lax.all_to_all(sent, 'seq', split_axis=0, concat_axis=0, tiled=True)]
    dot_general x1, matrix products: 0.99 us -> 2.77 us  [output_step(): jnp.einsum('grtk,kgd->tgrd', weights, value_blk, preferred_element_type=j...]
  transfers between devices with their start and end apart: 6 -> 5, of which waited for: 4 -> 4; matrix products, arithmetic and copies ran while one was open for 36% -> 34% of each run, Pallas kernels for 0% -> 0%
where the time goes in v17:
time: 176 us; the launch traced here: 175 us
  waiting for transfers between devices  67.7 us (38%)
  local copies, waits for them, and re-layouts  34.4 us (20%)
  starting transfers between devices  31.9 us (18%)
  matrix products  22.5 us (13%)
  other arithmetic  16.8 us (10%)
    all_to_all x2, waiting for transfers between devices, on_device(): got = lax.all_to_all(sent, 'seq', split_axis=0, concat_axis=0, tiled=True)  37.1 us
    all_to_all x1, waiting for transfers between devices, on_device(): lax.all_to_all(jnp.concatenate([kv_terms.reshape(seq_count, tokens, kv_wi...  30 us
    all_to_all x1, starting transfers between devices, on_device(): lax.all_to_all(jnp.concatenate([kv_terms.reshape(seq_count, tokens, kv_wi...  14.4 us
    unnamed x61, local copies, waits for them, and re-layouts  14 us
    all_to_all x2, starting transfers between devices, on_device(): got = lax.all_to_all(sent, 'seq', split_axis=0, concat_axis=0, tiled=True)  13.2 us
    all_to_all x1, starting transfers between devices, on_device(): lax.all_to_all(kv_sent, 'seq', split_axis=0, concat_axis=0, tiled=True)  4.24 us
    dot_general x3, matrix products, mixer_stretch(): inner = jnp.einsum('hts,shp->thp', kernel, inputs, precision=precise)  4.14 us
    dot_general x3, matrix products, local_state(): jnp.einsum('hs,sn,shp->hnp', weights, b_float, inputs, precision=precise)  3.95 us
  transfers between devices with their start and end apart: 5, of which 4 were waited for; matrix products, arithmetic and copies ran while one was open for 34% of the time, Pallas kernels for 0%

profile of v17, /device:TPU:0, one launch (start us, length us, event | category | flops | bytes accessed | tf_op | source)
XLA Modules:
  0.0 175.0 jit_solution(15023264520340893234)
XLA Ops:
  3.1 1.3 copy.435
  4.5 1.3 copy.436
  9.7 7.3 %all-to-all-start.1 = ((bf16[8,128,776]{1,2,0:T(8,128)(2,1)}), bf16[8,128,776]{1,2,0:T(8,128)(2,1)S(1)}, u32[]{:S(2)}, u32[]{:S(2)}) async-start(bf16[8,128,776]{1,2,0:T(8,128)(2,1)} %copy_dynamic-update-slice_fusion), calls=%async_computation.1 | async-start | bytes 3178496 | tf_op jit(solution)/shard_map/all_to_all | solution.py:226
  19.2 35.2 %all-to-all-done.1 = bf16[8,128,776]{1,2,0:T(8,128)(2,1)S(1)} async-done(((bf16[8,128,776]{1,2,0:T(8,128)(2,1)}), bf16[8,128,776]{1,2,0:T(8,128)(2,1)S(1)}, u32[]{:S(2)}, u32[]{:S(2)}) %all-to-all-start.1) | async-done | bytes 1589280 | tf_op jit(solution)/shard_map/all_to_all | solution.py:226
  55.5 4.2 %all-to-all-start = ((bf16[8,128,512]{1,2,0:T(8,128)(2,1)}), bf16[8,128,512]{1,2,0:T(8,128)(2,1)}, u32[]{:S(2)}, u32[]{:S(2)}) async-start(bf16[8,128,512]{1,2,0:T(8,128)(2,1)} %broadcast_in_dim.265), calls=%async_computation | async-start | bytes 2097152 | tf_op jit(solution)/shard_map/all_to_all | solution.py:237
  63.3 2.1 %copy.456 = bf16[2,128,128,8]{2,3,1,0:T(8,128)(2,1)} copy(bf16[2,128,128,8]{1,2,0,3:T(8,128)(2,1)} %convolution_bitcast_fusion.2) | data formatting | bytes 1048576 | tf_op jit(solution)/shard_map/transpose(jvp(kjh,jhnp->khnp))/transpose;transpose(jvp(vmap(tn,hnp->thp)))/transpose | solution.py:102
  65.6 1.4 convolution_bitcast_fusion.1
  67.0 2.4 %fusion.53 = (f32[8,128,2]{1,2,0:T(2,128)S(1)}, f32[8,2,128,128]{3,2,1,0:T(8,128)}) fusion(f32[8,128,128]{1,2,0:T(8,128)} %copy.552, bf16[8,128,2,128]{1,3,2,0:T(8,128)(2,1)S(1)} %bitcast.316, bf16[8,2,128,128]{3,0,2,1:T(8,128)(2,1)S(1)} %convolution_bitcast_fusion.1), kind=kOutput, calls=%fused_computation.87 | convolution fusion | flops 67631104 | bytes 2629632 | tf_op jit(solution)/shard_map/transpose(jvp(vmap(hs,sn,shp->hnp)))/dot_general | solution.py:53
  72.3 1.4 copy.451
  74.9 2.3 %fusion.48 = f32[8,128,128]{1,2,0:T(8,128)} fusion(bf16[8,2,128,128]{2,3,1,0:T(8,128)(2,1)S(1)} %copy.451, bf16[8,128,2,128]{1,3,2,0:T(8,128)(2,1)} %bitcast.321, f32[8,128,2]{1,2,0:T(2,128)S(1)} %copy.446), kind=kOutput, calls=%fused_computation.75 | convolution fusion | flops 67633152 | bytes 1581056 | tf_op jit(solution)/shard_map/transpose(jvp(vmap(tn,hnp->thp)))/dot_general | solution.py:69
  77.5 2.0 %fusion.63 = (f32[8,2,128]{2,1,0:T(2,128)S(1)}, f32[8,2,128]{2,1,0:T(2,128)S(1)}, bf16[8,128,128]{2,1,0:T(8,128)(2,1)S(1)}) fusion(f32[8,128,128]{2,1,0:T(8,128)S(1)} %fusion.85, f32[8,2,128]{2,1,0:T(2,128)S(1)} %copy.442, pred[8,128,128]{2,1,0:T(8,128)(4,1)} %compare_and_fusion.3, bf16[8,2,128,128]{3,2,1,0:T(8,128)(2,1)S(1)} %bitcast.322, ...), kind=kOutput, calls=%fused_computation.98 | convolution fusion | flops 69332992 | bytes 1990656 | tf_op jit(solution)/shard_map/transpose(jvp(vmap(hts,shp->thp)))/dot_general | solution.py:67
  79.5 1.3 fusion.51
  80.9 2.5 %reduce_window_sum.47 = f32[8,2,128]{2,0,1:T(8,128)S(1)} reduce-window(f32[8,2,128]{2,0,1:T(8,128)S(1)} %get-tuple-element.1116, f32[]{:T(128)} %constant.160.clone.1), window={size=1x1x128 pad=0_0x0_0x0_127}, to_apply=%region_36.37 | reduce-window | flops 260096 | bytes 16388 | tf_op jit(solution)/shard_map/transpose(jvp(jit(cumsum)))/reduce_window_sum | solution.py:91
  83.4 2.5 %reduce_window_sum.46 = f32[8,2,128]{2,0,1:T(8,128)S(1)} reduce-window(f32[8,2,128]{2,0,1:T(8,128)S(1)} %get-tuple-element.1117, f32[]{:T(128)} %constant.160.clone.1), window={size=1x1x128 pad=0_0x0_0x0_127}, to_apply=%region_28.29 | reduce-window | flops 260096 | bytes 16388 | tf_op jit(solution)/shard_map/transpose(jvp(vmap(jit(cumsum))))/reduce_window_sum | solution.py:45
  85.9 1.5 fusion.52
  90.4 5.9 %all-to-all-start.3 = ((bf16[8,128,528]{1,2,0:T(8,128)(2,1)}), bf16[8,128,528]{1,2,0:T(8,128)(2,1)S(1)}, u32[]{:S(2)}, u32[]{:S(2)}) async-start(bf16[8,128,528]{1,2,0:T(8,128)(2,1)} %pad_maximum_fusion.1), calls=%async_computation.3 | async-start | bytes 2162688 | tf_op jit(solution)/shard_map/all_to_all | solution.py:382
  97.0 1.5 copy.425
  99.3 1.2 copy.434
  100.8 1.7 while.51
  100.8 1.6 conditional.9
  103.4 3.3 %while.52 = (s32[]{:T(128)}, f32[128,2,4,128]{0,3,2,1:T(8,128)}, s32[]{:T(128)}, bf16[1024,256]{0,1:T(8,128)(2,1)S(1)}, s32[4]{0:T(128)S(1)}, /*index=5*/s32[128...) while((s32[]{:T(128)}, f32[128,2,4,128]{0,3,2,1:T(8,128)}, ...), condition=%wide.region_15.16_spmd.clone, body=%wide.region_10.15_spmd.clone.sunk | while | flops 271390848 | bytes 3031901 | solution.py:315
  103.4 3.3 %conditional.10 = (f32[128,2,4,128]{0,3,2,1:T(8,128)}) conditional(s32[]{:T(128)} %convert_element_type.260, f32[128,2,4,128]{0,3,2,1:T(8,128)} %get-tuple-element.1423, (s32[]{:T(128)}, bf16[1024,256]{0,1:T(8,128)(2,1)S(1)}, s32[]{:T(128)}, s32[4]{0:T(128)S(1)}, s32[128]{0:T(128)S(1)}, /*index=5*/bf16[1024,256]{0,1:T(8,128)(2,1)S(1)}, ...), branch_computations={%region_11.11_spmd, %region_12.14_spmd} | conditional | flops 271390848 | bytes 3031158 | solution.py:281
  104.0 2.8 %fusion.13 = f32[128,2,4,128]{0,3,2,1:T(8,128)} fusion(f32[128,2,4,128]{0,3,2,1:T(8,128)} %get-tuple-element.621, bf16[512,2,128,1]{0,2,3,1:T(8,128)(2,1)S(1)} %bitcast.314, bf16[512,2,128,1]{0,2,3,1:T(8,128)(2,1)S(1)} %bitcast.313, bf16[128,2,4,128]{3,0,2,1:T(8,128)(2,1)S(1)} %get-tuple-element.628, f32[2,4,128]{2,1,0:T(4,128)S(1)} %get-tuple-element.629, ...), kind=kOutput, calls=%fused_computation.19 | convolution fusion | flops 271187968 | bytes 1904640 | tf_op jit(solution)/shard_map/while/body/eval_jaxpr/cond/branch_1_fun/grtk,kgd->tgrd/dot_general | solution.py:311
  106.8 1.8 %fusion.64 = (f32[2,4,128]{2,1,0:T(4,128)S(1)}, bf16[128,2,4,128]{0,3,2,1:T(8,128)(2,1)}) fusion(bf16[128,1024]{0,1:T(8,128)(2,1)S(1)} %copy.429, f32[128,2,4,128]{0,3,2,1:T(8,128)} %get-tuple-element.689), kind=kLoop, calls=%fused_computation.102 | loop fusion | flops 654336 | bytes 1052672 | tf_op jit(solution)/shard_map/bkfh,bkfh->kfb/dot_general | solution.py:321
  110.3 5.2 %while.53 = (s32[]{:T(128)}, f32[128,2,4,128]{0,3,2,1:T(8,128)S(1)}, bf16[1024,256]{0,1:T(8,128)(2,1)}, bf16[1024,256]{0,1:T(8,128)(2,1)}, s32[]{:T(128)}, /*ind...) while((s32[]{:T(128)}, ...), condition=%wide.region_21.22_spmd.clone, body=%wide.region_16.21_spmd.clone.sunk | while | flops 675616896 | bytes 23483460 | solution.py:353
  110.4 5.2 %conditional.11 = ((f32[128,2,4,128]{0,3,2,1:T(8,128)S(1)}, bf16[1024,256]{0,1:T(8,128)(2,1)}, bf16[1024,256]{0,1:T(8,128)(2,1)})) conditional(s32[]{:T(128)} %convert_element_type.261, (f32[128,2,4,128]{0,3,2,1:T(8,128)S(1)}, bf16[1024,256]{0,1:T(8,128)(2,1)}, bf16[1024,256]{0,1:T(8,128)(2,1)}) %tuple.206, (s32[]{:T(128)}, ...), branch_computations={%region_17.17_spmd, %region_18.20_spmd} | conditional | flops 675616896 | bytes 23482630 | solution.py:281
  115.6 1.6 copy_bitcast_fusion
  117.4 1.6 fusion.43
  119.0 1.3 pad_maximum_fusion
  120.2 1.9 %all-to-all-done.3 = bf16[8,128,528]{1,2,0:T(8,128)(2,1)S(1)} async-done(((bf16[8,128,528]{1,2,0:T(8,128)(2,1)}), bf16[8,128,528]{1,2,0:T(8,128)(2,1)S(1)}, u32[]{:S(2)}, u32[]{:S(2)}) %all-to-all-start.3) | async-done | bytes 1081376 | tf_op jit(solution)/shard_map/all_to_all | solution.py:382
  122.1 14.4 %all-to-all-start.2 = ((bf16[8,128,768]{1,2,0:T(8,128)(2,1)}), bf16[8,128,768]{1,2,0:T(8,128)(2,1)S(1)}, u32[]{:S(2)}, u32[]{:S(2)}) async-start(bf16[8,128,768]{1,2,0:T(8,128)(2,1)} %pad_maximum_fusion), calls=%async_computation.2 | async-start | bytes 3145728 | tf_op jit(solution)/shard_map/all_to_all | solution.py:362
  142.3 30.0 %all-to-all-done.2 = bf16[8,128,768]{1,2,0:T(8,128)(2,1)S(1)} async-done(((bf16[8,128,768]{1,2,0:T(8,128)(2,1)}), bf16[8,128,768]{1,2,0:T(8,128)(2,1)S(1)}, u32[]{:S(2)}, u32[]{:S(2)}) %all-to-all-start.2) | async-done | bytes 1572896 | tf_op jit(solution)/shard_map/all_to_all | solution.py:362
  (205 shorter events, 40.9 us)
Async XLA Ops:
  7.6 9.4 %copy-start.23 = (s32[4]{0:T(128)S(1)}, s32[4]{0:T(128)}, u32[]{:S(2)}) copy-start(s32[4]{0:T(128)} %param.28) | copy-start | bytes 52
  7.6 9.6 %copy-start.20 = (bf16[128,256]{1,0:T(8,128)(2,1)S(1)}, bf16[128,256]{1,0:T(8,128)(2,1)}, u32[]{:S(2)}) copy-start(bf16[128,256]{1,0:T(8,128)(2,1)} %param.31) | copy-start | bytes 196612
  7.6 9.6 %copy-start.21 = (bf16[128,256]{1,0:T(8,128)(2,1)S(1)}, bf16[128,256]{1,0:T(8,128)(2,1)}, u32[]{:S(2)}) copy-start(bf16[128,256]{1,0:T(8,128)(2,1)} %param.30) | copy-start | bytes 196612
  8.3 9.0 %copy-start.22 = (f32[16]{0:T(128)S(1)}, f32[16]{0:T(128)}, u32[]{:S(2)}) copy-start(f32[16]{0:T(128)} %param.27) | copy-start | bytes 196
  9.7 44.7 %all-to-all-start.1 = ((bf16[8,128,776]{1,2,0:T(8,128)(2,1)}), bf16[8,128,776]{1,2,0:T(8,128)(2,1)S(1)}, u32[]{:S(2)}, u32[]{:S(2)}) async-start(bf16[8,128,776]{1,2,0:T(8,128)(2,1)} %copy_dynamic-update-slice_fusion), calls=%async_computation.1 | async-start | bytes 3178496 | tf_op jit(solution)/shard_map/all_to_all | solution.py:226
  55.5 34.9 %all-to-all-start = ((bf16[8,128,512]{1,2,0:T(8,128)(2,1)}), bf16[8,128,512]{1,2,0:T(8,128)(2,1)}, u32[]{:S(2)}, u32[]{:S(2)}) async-start(bf16[8,128,512]{1,2,0:T(8,128)(2,1)} %broadcast_in_dim.265), calls=%async_computation | async-start | bytes 2097152 | tf_op jit(solution)/shard_map/all_to_all | solution.py:237
  62.1 3.4 %copy-start.3 = (bf16[8,128,256]{1,2,0:T(8,128)(2,1)}, bf16[8,128,256]{1,2,0:T(8,128)(2,1)S(1)}, u32[]{:S(2)}) copy-start(bf16[8,128,256]{1,2,0:T(8,128)(2,1)S(1)} %get-tuple-element.1108) | copy-start | bytes 1572868
  62.2 7.5 %copy-start = (bf16[8,128,256]{1,2,0:T(8,128)(2,1)}, bf16[8,128,256]{1,2,0:T(8,128)(2,1)S(1)}, u32[]{:S(2)}) copy-start(bf16[8,128,256]{1,2,0:T(8,128)(2,1)S(1)} %get-tuple-element.1109) | copy-start | bytes 1572868
  67.0 3.4 %copy-start.7 = (bf16[2,128,128,8]{2,3,1,0:T(8,128)(2,1)S(1)}, bf16[2,128,128,8]{2,3,1,0:T(8,128)(2,1)}, u32[]{:S(2)}) copy-start(bf16[2,128,128,8]{2,3,1,0:T(8,128)(2,1)} %copy.456) | copy-start | bytes 1572868
  74.9 2.6 %copy-start.1 = (bf16[8,128,256]{1,2,0:T(8,128)(2,1)S(1)}, bf16[8,128,256]{1,2,0:T(8,128)(2,1)}, u32[]{:S(2)}) copy-start(bf16[8,128,256]{1,2,0:T(8,128)(2,1)} %copy-done) | copy-start | bytes 1572868
  74.9 2.6 %copy-start.4 = (bf16[8,128,256]{1,2,0:T(8,128)(2,1)S(1)}, bf16[8,128,256]{1,2,0:T(8,128)(2,1)}, u32[]{:S(2)}) copy-start(bf16[8,128,256]{1,2,0:T(8,128)(2,1)} %copy-done.3) | copy-start | bytes 1572868
  77.5 3.3 %copy-start.14 = (f32[8,128,128]{2,1,0:T(8,128)}, f32[8,128,128]{2,1,0:T(8,128)S(1)}, u32[]{:S(2)}) copy-start(f32[8,128,128]{2,1,0:T(8,128)S(1)} %fusion.85) | copy-start | bytes 1572868
  80.8 6.8 %copy-start.6 = (f32[8,128,128]{1,2,0:T(8,128)S(1)}, f32[8,128,128]{1,2,0:T(8,128)}, u32[]{:S(2)}) copy-start(f32[8,128,128]{1,2,0:T(8,128)} %fusion.48) | copy-start | bytes 1572868
  85.9 2.1 %copy-start.5 = (bf16[8,128,256]{1,2,0:T(8,128)(2,1)S(1)}, bf16[8,128,256]{1,2,0:T(8,128)(2,1)}, u32[]{:S(2)}) copy-start(bf16[8,128,256]{1,2,0:T(8,128)(2,1)} %copy-done.3) | copy-start | bytes 1572868
  85.9 2.1 %copy-start.15 = (f32[8,128,128]{2,1,0:T(8,128)S(1)}, f32[8,128,128]{2,1,0:T(8,128)}, u32[]{:S(2)}) copy-start(f32[8,128,128]{2,1,0:T(8,128)} %copy-done.14) | copy-start | bytes 1572868
  85.9 2.1 %copy-start.19 = (pred[8,128,128]{2,1,0:T(8,128)(4,1)S(1)}, pred[8,128,128]{2,1,0:T(8,128)(4,1)}, u32[]{:S(2)}) copy-start(pred[8,128,128]{2,1,0:T(8,128)(4,1)} %compare_and_fusion.3) | copy-start | bytes 393220
  89.3 7.0 %copy-start.17 = (bf16[128,1024]{1,0:T(8,128)(2,1)S(1)}, bf16[128,1024]{1,0:T(8,128)(2,1)}, u32[]{:S(2)}) copy-start(bf16[128,1024]{1,0:T(8,128)(2,1)} %param.33) | copy-start | bytes 786436
  89.3 7.1 %copy-start.18 = (bf16[128,1024]{1,0:T(8,128)(2,1)S(1)}, bf16[128,1024]{1,0:T(8,128)(2,1)}, u32[]{:S(2)}) copy-start(bf16[128,1024]{1,0:T(8,128)(2,1)} %param.29) | copy-start | bytes 786436
  90.4 31.7 %all-to-all-start.3 = ((bf16[8,128,528]{1,2,0:T(8,128)(2,1)}), bf16[8,128,528]{1,2,0:T(8,128)(2,1)S(1)}, u32[]{:S(2)}, u32[]{:S(2)}) async-start(bf16[8,128,528]{1,2,0:T(8,128)(2,1)} %pad_maximum_fusion.1), calls=%async_computation.3 | async-start | bytes 2162688 | tf_op jit(solution)/shard_map/all_to_all | solution.py:382
  112.7 1.0 copy-start.8
  112.7 1.2 copy-start.10
  114.0 0.8 copy-start.9
  114.8 0.8 copy-start.11
  115.6 1.6 copy-start.2
  115.6 1.7 copy-start.12
  115.6 1.8 %copy-start.16 = (f32[8,128,128]{2,1,0:T(8,128)S(1)}, f32[8,128,128]{2,1,0:T(8,128)}, u32[]{:S(2)}) copy-start(f32[8,128,128]{2,1,0:T(8,128)} %copy-done.14) | copy-start | bytes 1572868
  120.2 16.3 %copy-start.13 = (bf16[128,2,4,128]{0,3,2,1:T(8,128)(2,1)S(1)}, bf16[128,2,4,128]{0,3,2,1:T(8,128)(2,1)}, u32[]{:S(2)}) copy-start(bf16[128,2,4,128]{0,3,2,1:T(8,128)(2,1)} %get-tuple-element.1095) | copy-start | bytes 786436
  122.1 50.2 %all-to-all-start.2 = ((bf16[8,128,768]{1,2,0:T(8,128)(2,1)}), bf16[8,128,768]{1,2,0:T(8,128)(2,1)S(1)}, u32[]{:S(2)}, u32[]{:S(2)}) async-start(bf16[8,128,768]{1,2,0:T(8,128)(2,1)} %pad_maximum_fusion), calls=%async_computation.2 | async-start | bytes 3145728 | tf_op jit(solution)/shard_map/all_to_all | solution.py:362
  139.4 1.4 collective-permute-start

commit v18 on v9

--- a/solution.py
+++ b/solution.py
@@ -10,7 +10,7 @@
 TOK_SPAN = 128
 
 
-precise = lax.Precision.HIGH
+precise = lax.Precision.DEFAULT
 big_negative = -1e30
 
 

time: 184 us -> 172 us (0.935)
  waiting for transfers between devices: 66.5 us -> 75.5 us
  local copies, waits for them, and re-layouts: 36 us -> 27.8 us
  matrix products: 28.8 us -> 22.8 us
  other arithmetic: 22.4 us -> 17.5 us
    all_to_all x2, waiting for transfers between devices: 43.8 us -> 52.1 us  [on_device(): got = lax.all_to_all(sent, 'seq', split_axis=0, concat_axis=0, tiled=True)]
    unnamed x142 -> x38, local copies, waits for them, and re-layouts: 12.2 us -> 8.58 us
    and x3, other arithmetic: 2.56 us -> 0.61 us  [block_view(): (key_pos[None, :] <= positions[:, None]) & (doc_index(key_pos, doc_length...]
  transfers between devices with their start and end apart: 6 -> 6, of which waited for: 4 -> 4; matrix products, arithmetic and copies ran while one was open for 45% -> 38% of each run, Pallas kernels for 0% -> 0%
where the time goes in v18:
time: 172 us; the launch traced here: 171 us
  waiting for transfers between devices  75.5 us (44%)
  local copies, waits for them, and re-layouts  27.8 us (16%)
  starting transfers between devices  25.8 us (15%)
  matrix products  22.8 us (13%)
  other arithmetic  17.5 us (10%)
    all_to_all x2, waiting for transfers between devices, on_device(): got = lax.all_to_all(sent, 'seq', split_axis=0, concat_axis=0, tiled=True)  52.1 us
    all_to_all x1, waiting for transfers between devices, on_device(): lax.all_to_all(kv_sent, 'seq', split_axis=0, concat_axis=0, tiled=True)  17.9 us
    all_to_all x2, starting transfers between devices, on_device(): got = lax.all_to_all(sent, 'seq', split_axis=0, concat_axis=0, tiled=True)  10.2 us
    unnamed x38, local copies, waits for them, and re-layouts  8.58 us
    all_to_all x1, starting transfers between devices, mamba_by_heads(): lax.all_to_all(decay_log, 'seq', split_axis=0, concat_axis=1, tiled=True)  7.45 us
    all_to_all x1, waiting for transfers between devices, mamba_by_heads(): lax.all_to_all(decay_log, 'seq', split_axis=0, concat_axis=1, tiled=True)  5.5 us
    dot_general x3, matrix products, mixer_stretch(): jnp.dot(c_float, b_float.T, precision=precise)[None]  5.28 us
    all_to_all x1, starting transfers between devices, on_device(): lax.all_to_all(kv_terms.reshape(seq_count, tokens, kv_width), 'seq', spli...  4.41 us
  transfers between devices with their start and end apart: 6, of which 4 were waited for; matrix products, arithmetic and copies ran while one was open for 38% of the time, Pallas kernels for 0%

profile of v18, /device:TPU:0, one launch (start us, length us, event | category | flops | bytes accessed | tf_op | source)
XLA Modules:
  0.0 171.0 jit_solution(17119782504772212155)
XLA Ops:
  0.7 7.5 %all-to-all-start.1 = ((f32[8,2,128]{2,1,0:T(2,128)}), f32[8,2,128]{2,1,0:T(2,128)S(1)}, u32[]{:S(2)}, u32[]{:S(2)}) async-start(f32[8,2,128]{2,1,0:T(2,128)} %bitcast.324), calls=%async_computation.1 | async-start | bytes 16384 | tf_op jit(solution)/shard_map/all_to_all | solution.py:117
  9.1 5.5 %all-to-all-done.1 = f32[8,2,128]{2,1,0:T(2,128)S(1)} async-done(((f32[8,2,128]{2,1,0:T(2,128)}), f32[8,2,128]{2,1,0:T(2,128)S(1)}, u32[]{:S(2)}, u32[]{:S(2)}) %all-to-all-start.1) | async-done | bytes 8224 | tf_op jit(solution)/shard_map/all_to_all | solution.py:117
  15.7 3.7 %all-to-all-start.3 = ((bf16[8,128,512]{1,2,0:T(8,128)(2,1)}), bf16[8,128,512]{1,2,0:T(8,128)(2,1)S(1)}, u32[]{:S(2)}, u32[]{:S(2)}) async-start(bf16[8,128,512]{1,2,0:T(8,128)(2,1)} %broadcast_in_dim.296), calls=%async_computation.3 | async-start | bytes 2097152 | tf_op jit(solution)/shard_map/all_to_all | solution.py:217
  20.7 1.3 copy.413
  23.9 2.3 %pad_maximum_fusion = bf16[8,128,768]{2,1,0:T(8,128)(2,1)} fusion(bf16[8,128,128]{2,1,0:T(8,128)(2,1)S(1)} %broadcast_in_dim.265, bf16[8,128,128]{2,1,0:T(8,128)(2,1)S(1)} %broadcast_in_dim.264, bf16[8,128,256]{2,1,0:T(8,128)(2,1)} %bitcast.301, bf16[8,128,256]{2,1,0:T(8,128)(2,1)S(1)} %bitcast.300), kind=kLoop, calls=%fused_computation.54 | loop fusion | flops 6291456 | bytes 3145728 | tf_op jit(solution)/shard_map/concatenate | solution.py:208
  26.3 17.9 %all-to-all-done.3 = bf16[8,128,512]{1,2,0:T(8,128)(2,1)S(1)} async-done(((bf16[8,128,512]{1,2,0:T(8,128)(2,1)}), bf16[8,128,512]{1,2,0:T(8,128)(2,1)S(1)}, u32[]{:S(2)}, u32[]{:S(2)}) %all-to-all-start.3) | async-done | bytes 1048608 | tf_op jit(solution)/shard_map/all_to_all | solution.py:217
  44.2 4.3 %all-to-all-start = ((bf16[8,128,768]{2,1,0:T(8,128)(2,1)}), bf16[8,128,768]{2,1,0:T(8,128)(2,1)}, u32[]{:S(2)}, u32[]{:S(2)}) async-start(bf16[8,128,768]{2,1,0:T(8,128)(2,1)} %pad_maximum_fusion), calls=%async_computation | async-start | bytes 3145728 | tf_op jit(solution)/shard_map/all_to_all | solution.py:211
  50.8 1.3 copy.455
  53.9 1.7 %while.51 = (s32[]{:T(128)}, f32[2,4,128]{2,1,0:T(4,128)S(1)}, f32[2,4,128]{2,1,0:T(4,128)S(1)}, s32[]{:T(128)}, s32[4]{0:T(128)S(1)}, /*index=5*/s32[128]{0:T(1...) while((s32[]{:T(128)}, f32[2,4,128]{2,1,0:T(4,128)S(1)}, ...), condition=%wide.region_24.25_spmd.clone, body=%wide.region_17.24_spmd.clone.sunk | while | flops 138616976 | bytes 5505893 | solution.py:278
  53.9 1.6 conditional.9
  55.7 1.7 while.52
  55.7 1.6 conditional.10
  58.3 4.9 %while.53 = (s32[]{:T(128)}, f32[128,2,4,128]{0,3,2,1:T(8,128)S(1)}, bf16[1024,256]{0,1:T(8,128)(2,1)S(1)}, bf16[1024,256]{0,1:T(8,128)(2,1)S(1)}, s32[]{:T(128)...) while((s32[]{:T(128)}, ...), condition=%wide.region_37.38_spmd.clone, body=%wide.region_32.37_spmd.clone.sunk | while | flops 675616896 | bytes 15094733 | solution.py:333
  58.8 3.8 %conditional.11 = ((f32[128,2,4,128]{0,3,2,1:T(8,128)S(1)}, bf16[1024,256]{0,1:T(8,128)(2,1)S(1)}, bf16[1024,256]{0,1:T(8,128)(2,1)S(1)})) conditional(s32[]{:T(128)} %convert_element_type.254, (f32[128,2,4,128]{0,3,2,1:T(8,128)S(1)}, bf16[1024,256]{0,1:T(8,128)(2,1)S(1)}, bf16[1024,256]{0,1:T(8,128)(2,1)S(1)}) %tuple.203, (s32[]{:T(128)}, ...), branch_computations={%region_33.33_spmd, %region_34.36_spmd} | conditional | flops 675616896 | bytes 15093910 | solution.py:261
  63.7 1.3 copy.470
  65.0 19.9 %all-to-all-done = bf16[8,128,768]{2,1,0:T(8,128)(2,1)} async-done(((bf16[8,128,768]{2,1,0:T(8,128)(2,1)}), bf16[8,128,768]{2,1,0:T(8,128)(2,1)}, u32[]{:S(2)}, u32[]{:S(2)}) %all-to-all-start) | async-done | bytes 1572896 | tf_op jit(solution)/shard_map/all_to_all | solution.py:211
  84.9 4.4 %all-to-all-start.4 = ((bf16[8,128,512]{1,2,0:T(8,128)(2,1)}), bf16[8,128,512]{1,2,0:T(8,128)(2,1)}, u32[]{:S(2)}, u32[]{:S(2)}) async-start(bf16[8,128,512]{1,2,0:T(8,128)(2,1)} %copy.470), calls=%async_computation.4 | async-start | bytes 2097152 | tf_op jit(solution)/shard_map/all_to_all | solution.py:351
  94.7 1.4 convolution_bitcast_fusion.1
  96.1 1.3 fusion.55
  101.4 1.4 copy.424
  102.8 1.3 fusion.85
  104.2 1.9 %fusion.65 = (f32[8,2,128]{2,1,0:T(2,128)S(1)}, f32[8,2,128]{2,1,0:T(2,128)S(1)}, bf16[8,128,128]{2,1,0:T(8,128)(2,1)S(1)}) fusion(f32[8,128,128]{2,1,0:T(8,128)S(1)} %fusion.85, f32[8,2,128]{2,1,0:T(2,128)S(1)} %copy.416, pred[8,128,128]{2,1,0:T(8,128)(4,1)} %compare_and_fusion.3, bf16[8,2,128,128]{3,2,1,0:T(8,128)(2,1)S(1)} %bitcast.285, ...), kind=kOutput, calls=%fused_computation.100 | convolution fusion | flops 69332992 | bytes 1990656 | tf_op jit(solution)/shard_map/transpose(jvp(vmap(hts,shp->thp)))/dot_general | solution.py:67
  106.7 1.5 fusion.44
  109.5 1.5 fusion.43
  111.0 2.5 %reduce_window_sum.46 = f32[8,2,128]{2,0,1:T(8,128)S(1)} reduce-window(f32[8,2,128]{2,0,1:T(8,128)S(1)} %get-tuple-element.1119, f32[]{:T(128)} %constant.152.clone.1), window={size=1x1x128 pad=0_0x0_0x0_127}, to_apply=%region_7.8 | reduce-window | flops 260096 | bytes 16388 | tf_op jit(solution)/shard_map/transpose(jvp(vmap(jit(cumsum))))/reduce_window_sum | solution.py:45
  113.5 2.5 %reduce_window_sum.47 = f32[8,2,128]{2,0,1:T(8,128)S(1)} reduce-window(f32[8,2,128]{2,0,1:T(8,128)S(1)} %get-tuple-element.1118, f32[]{:T(128)} %constant.152.clone.1), window={size=1x1x128 pad=0_0x0_0x0_127}, to_apply=%region_15.16 | reduce-window | flops 260096 | bytes 16388 | tf_op jit(solution)/shard_map/transpose(jvp(jit(cumsum)))/reduce_window_sum | solution.py:91
  116.0 2.0 %constant_dynamic-update-slice_fusion.3 = bf16[8,128,784]{1,2,0:T(8,128)(2,1)} fusion(bf16[8,128,256]{1,2,0:T(8,128)(2,1)} %bitcast.312), kind=kLoop, calls=%fused_computation.141 | loop fusion | bytes 1048576
  119.4 2.0 %fusion.50 = bf16[8,128,784]{1,2,0:T(8,128)(2,1)} fusion(bf16[8,128,784]{1,2,0:T(8,128)(2,1)} %constant_dynamic-update-slice_fusion.2, f32[8,128,128]{1,2,0:T(8,128)S(1)} %fusion.54, bf16[8,128,128]{2,1,0:T(8,128)(2,1)S(1)} %get-tuple-element.1008, bf16[8,128,768]{2,1,0:T(8,128)(2,1)} %all-to-all-done), kind=kOutput, calls=%fused_computation.79 | convolution fusion | flops 33816576 | bytes 1310720 | tf_op jit(solution)/shard_map/transpose(jvp(vmap()))/dot_general | solution.py:66
  121.3 2.0 %fusion.52 = bf16[8,128,784]{1,2,0:T(8,128)(2,1)} fusion(bf16[8,128,784]{1,2,0:T(8,128)(2,1)} %fusion.50, f32[8,128,128]{1,2,0:T(8,128)S(1)} %fusion.48, bf16[8,128,128]{2,1,0:T(8,128)(2,1)S(1)} %get-tuple-element.1008, bf16[8,128,768]{2,1,0:T(8,128)(2,1)} %all-to-all-done), kind=kOutput, calls=%fused_computation.81 | convolution fusion | flops 33816576 | bytes 1310720 | tf_op jit(solution)/shard_map/transpose(jvp(vmap()))/dot_general | solution.py:66
  123.9 5.9 %all-to-all-start.2 = ((bf16[8,128,784]{1,2,0:T(8,128)(2,1)}), bf16[8,128,784]{1,2,0:T(8,128)(2,1)S(1)}, u32[]{:S(2)}, u32[]{:S(2)}) async-start(bf16[8,128,784]{1,2,0:T(8,128)(2,1)} %bitcast_dynamic-update-slice_fusion), calls=%async_computation.2 | async-start | bytes 3211264 | tf_op jit(solution)/shard_map/all_to_all | solution.py:350
  131.6 1.4 convert_reduce_fusion.3
  134.5 32.2 %all-to-all-done.2 = bf16[8,128,784]{1,2,0:T(8,128)(2,1)S(1)} async-done(((bf16[8,128,784]{1,2,0:T(8,128)(2,1)}), bf16[8,128,784]{1,2,0:T(8,128)(2,1)S(1)}, u32[]{:S(2)}, u32[]{:S(2)}) %all-to-all-start.2) | async-done | bytes 1605664 | tf_op jit(solution)/shard_map/all_to_all | solution.py:350
  (176 shorter events, 39.4 us)
Async XLA Ops:
  0.6 18.8 %copy-start.11 = (s32[4]{0:T(128)S(1)}, s32[4]{0:T(128)}, u32[]{:S(2)}) copy-start(s32[4]{0:T(128)} %param.28) | copy-start | bytes 52
  0.7 19.0 %copy-start.5 = (bf16[128,1024]{1,0:T(8,128)(2,1)S(1)}, bf16[128,1024]{1,0:T(8,128)(2,1)}, u32[]{:S(2)}) copy-start(bf16[128,1024]{1,0:T(8,128)(2,1)} %param.29) | copy-start | bytes 786436
  0.7 14.0 %all-to-all-start.1 = ((f32[8,2,128]{2,1,0:T(2,128)}), f32[8,2,128]{2,1,0:T(2,128)S(1)}, u32[]{:S(2)}, u32[]{:S(2)}) async-start(f32[8,2,128]{2,1,0:T(2,128)} %bitcast.324), calls=%async_computation.1 | async-start | bytes 16384 | tf_op jit(solution)/shard_map/all_to_all | solution.py:117
  9.1 10.9 %copy-start.6 = (bf16[128,1024]{1,0:T(8,128)(2,1)S(1)}, bf16[128,1024]{1,0:T(8,128)(2,1)}, u32[]{:S(2)}) copy-start(bf16[128,1024]{1,0:T(8,128)(2,1)} %param.33) | copy-start | bytes 786436
  15.7 4.4 %copy-start.4 = (bf16[128,2048]{1,0:T(8,128)(2,1)S(1)}, bf16[128,2048]{1,0:T(8,128)(2,1)}, u32[]{:S(2)}) copy-start(bf16[128,2048]{1,0:T(8,128)(2,1)} %param.23) | copy-start | bytes 1572868
  15.7 28.4 %all-to-all-start.3 = ((bf16[8,128,512]{1,2,0:T(8,128)(2,1)}), bf16[8,128,512]{1,2,0:T(8,128)(2,1)S(1)}, u32[]{:S(2)}, u32[]{:S(2)}) async-start(bf16[8,128,512]{1,2,0:T(8,128)(2,1)} %broadcast_in_dim.296), calls=%async_computation.3 | async-start | bytes 2097152 | tf_op jit(solution)/shard_map/all_to_all | solution.py:217
  20.2 2.9 %copy-start.10 = (f32[16]{0:T(128)S(1)}, f32[16]{0:T(128)}, u32[]{:S(2)}) copy-start(f32[16]{0:T(128)} %param.27) | copy-start | bytes 196
  20.2 3.6 %copy-start.8 = (bf16[128,128]{1,0:T(8,128)(2,1)S(1)}, bf16[128,128]{1,0:T(8,128)(2,1)}, u32[]{:S(2)}) copy-start(bf16[128,128]{1,0:T(8,128)(2,1)} %param.24) | copy-start | bytes 98308
  20.2 3.7 %copy-start.9 = (bf16[128,128]{1,0:T(8,128)(2,1)S(1)}, bf16[128,128]{1,0:T(8,128)(2,1)}, u32[]{:S(2)}) copy-start(bf16[128,128]{1,0:T(8,128)(2,1)} %param.25) | copy-start | bytes 98308
  44.2 40.7 %all-to-all-start = ((bf16[8,128,768]{2,1,0:T(8,128)(2,1)}), bf16[8,128,768]{2,1,0:T(8,128)(2,1)}, u32[]{:S(2)}, u32[]{:S(2)}) async-start(bf16[8,128,768]{2,1,0:T(8,128)(2,1)} %pad_maximum_fusion), calls=%async_computation | async-start | bytes 3145728 | tf_op jit(solution)/shard_map/all_to_all | solution.py:211
  84.9 39.0 %all-to-all-start.4 = ((bf16[8,128,512]{1,2,0:T(8,128)(2,1)}), bf16[8,128,512]{1,2,0:T(8,128)(2,1)}, u32[]{:S(2)}, u32[]{:S(2)}) async-start(bf16[8,128,512]{1,2,0:T(8,128)(2,1)} %copy.470), calls=%async_computation.4 | async-start | bytes 2097152 | tf_op jit(solution)/shard_map/all_to_all | solution.py:351
  96.1 2.3 %copy-start.2 = (bf16[2,128,128,8]{2,3,1,0:T(8,128)(2,1)S(1)}, bf16[2,128,128,8]{2,3,1,0:T(8,128)(2,1)}, u32[]{:S(2)}) copy-start(bf16[2,128,128,8]{2,3,1,0:T(8,128)(2,1)} %copy.428) | copy-start | bytes 1572868
  104.2 1.9 %copy-start.7 = (pred[8,128,128]{2,1,0:T(8,128)(4,1)S(1)}, pred[8,128,128]{2,1,0:T(8,128)(4,1)}, u32[]{:S(2)}) copy-start(pred[8,128,128]{2,1,0:T(8,128)(4,1)} %compare_and_fusion.3) | copy-start | bytes 393220
  109.5 8.5 %copy-start.1 = (bf16[8,128,2,128]{1,3,2,0:T(8,128)(2,1)S(1)}, bf16[8,128,2,128]{1,3,2,0:T(8,128)(2,1)}, u32[]{:S(2)}) copy-start(bf16[8,128,2,128]{1,3,2,0:T(8,128)(2,1)} %fusion.44) | copy-start | bytes 1572868
  110.9 7.9 %copy-start = (f32[8,2,128,128]{3,2,1,0:T(8,128)S(1)}, f32[8,2,128,128]{3,2,1,0:T(8,128)}, u32[]{:S(2)}) copy-start(f32[8,2,128,128]{3,2,1,0:T(8,128)} %get-tuple-element.1131) | copy-start | bytes 3145732
  123.9 6.8 %copy-start.3 = (bf16[128,2,4,128]{0,3,2,1:T(8,128)(2,1)S(1)}, bf16[128,2,4,128]{0,3,2,1:T(8,128)(2,1)}, u32[]{:S(2)}) copy-start(bf16[128,2,4,128]{0,3,2,1:T(8,128)(2,1)} %get-tuple-element.1090) | copy-start | bytes 786436
  123.9 42.7 %all-to-all-start.2 = ((bf16[8,128,784]{1,2,0:T(8,128)(2,1)}), bf16[8,128,784]{1,2,0:T(8,128)(2,1)S(1)}, u32[]{:S(2)}, u32[]{:S(2)}) async-start(bf16[8,128,784]{1,2,0:T(8,128)(2,1)} %bitcast_dynamic-update-slice_fusion), calls=%async_computation.2 | async-start | bytes 3211264 | tf_op jit(solution)/shard_map/all_to_all | solution.py:350
  166.7 2.8 %collective-permute-start = (f32[128,256]{0,1:T(8,128)S(1)}, f32[128,256]{0,1:T(8,128)S(1)}, u32[]{:S(2)}, u32[]{:S(2)}) collective-permute-start(f32[128,256]{0,1:T(8,128)S(1)} %slice.110), channel_id=1, source_target_pairs={{0,1},{1,0},{2,3},{3,2},{4,5},{5,4},{6,7},{7,6},{8,9},{9,8},{10,11... | collective-permute-start | bytes 393224 | tf_op jit(solution)/shard_map/ppermute | solution.py:369
